TPU v7x, 512 devices: a whole 4x4x16 slice. The times are simulated.
512 devices in a mesh: pipe: 4 (over y_hi, core), ctx: 16 (over z), dp: 8 (over y_lo, x).
Axes of the slice: x: 4, y: 4 (y_hi: 2, y_lo: 2; y = y_hi * 2 + y_lo), z: 16, core: 2. Of those that a mesh axis runs over, the one named last changes fastest.
Arguments:
- clean_latent: float32 [2, 8, 1024, 64], P(None, 'dp', 'ctx'), may hold values from -6 to 6
- noise_latent: float32 [2, 8, 1024, 64], P(None, 'dp', 'ctx'), may hold values from -6 to 6
- time_index: int32 [2, 8], P(None, 'dp'), may hold values from 0 to 999
- frame_ids: int32 [2, 8, 1024], P(None, 'dp'), may hold values from 0 to 15, never falling along the last dimension, each value on 1 to 128 neighbouring positions
- embed_weight: bfloat16 [64, 1536], replicated, may hold values from -0.75 to 0.75
- time_vector: float32 [1536], replicated, may hold values from -5 to 5
- query_weight: bfloat16 [4, 1536, 1536], P('pipe', 'dp'), may hold values from -1 to 41
- key_weight: bfloat16 [4, 1536, 1536], P('pipe', 'dp'), may hold values from -1 to 3
- norm_gain: float32 [4, 1536], P('pipe'), may hold values from 0.1 to 1.9
- head_gain: float32 [1536], replicated, may hold values from 0.1 to 1.9
- head_weight: bfloat16 [1536, 64], P(None, 'pipe'), may hold values from -0.15625 to 0.15625
Outputs:
- velocity: float32 [2, 8, 1024, 64], P(None, 'dp', 'ctx', 'pipe')
- head_grad: float32 [1536, 64], P('dp', 'pipe')
Inputs may be any that keep to these rules, and one draw needn't show every extreme that they name: `frame_ids`: along each sequence the frame number never falls and starts at 0; each frame holds 1 to 128 patches, and some frame holds exactly 128.
All inputs are finite; a program needn't handle non-finite values.
Results may differ from a plain program's by a relative error of at most 0.014.
The roundings to bfloat16 on the way count: a program that leaves them out, or rounds other values in their place, can miss the bound.
Values may be sent and summed in bfloat16 or wider, within the bound.
No kernel may reach another device: no remote copies, remote signals or barrier semaphores. Data moves between devices by JAX's collectives and lax.ppermute only.
A program may use at most 128 MiB of HBM per device.

v0:
```python
import jax
import jax.numpy as jnp
from jax import lax
from jax.sharding import PartitionSpec as P

HEAD = 96


epsilon = 1e-06


def shifted(value, axis, steps):
    count = lax.axis_size(axis)
    first, last = (max(0, -steps), min(count, count - steps))
    return lax.ppermute(value, axis, [(source, source + steps) for source in range(first, last)])


def broadcast(value, axis, source):
    kept = jnp.where(lax.axis_index(axis) == source, value, 0).astype(value.dtype)
    return lax.psum(kept, axis)


def rms_scale(values, gain_row):
    return (
        values * lax.rsqrt(jnp.mean(values * values, axis=-1, keepdims=True) + epsilon) * gain_row
    )


def on_device(
    clean_latent,
    noise_latent,
    time_index,
    frame_ids,
    embed_weight,
    time_vector,
    query_weight,
    key_weight,
    norm_gain,
    head_gain,
    head_weight,
):
    phase_index = lax.axis_index("pipe")
    phase_count = lax.axis_size("pipe")
    cycle_size = lax.axis_size("ctx")
    micro_count = clean_latent.shape[0]
    local_rows = clean_latent.shape[2]
    model_width = embed_weight.shape[1]
    head_count = model_width // HEAD
    local_heads = head_count // cycle_size
    local_width = local_heads * HEAD
    seq_total = local_rows * cycle_size
    block_rows = min(512, seq_total)
    block_count = seq_total // block_rows
    score_scale = HEAD ** (-0.5)
    flow_time = ((time_index.astype(jnp.float32) + 0.5) / 1000.0)[:, :, None, None]
    noisy_input = ((1.0 - flow_time) * noise_latent + flow_time * clean_latent).astype(jnp.bfloat16)
    target = clean_latent - noise_latent
    embedded = jnp.einsum(
        "mbsp,pd->mbsd", noisy_input, embed_weight, preferred_element_type=jnp.float32
    )
    embedded = (embedded + flow_time * time_vector).astype(jnp.bfloat16)
    gathered = (
        lax.all_gather(query_weight, "dp", axis=1, tiled=True),
        lax.all_gather(key_weight, "dp", axis=1, tiled=True),
    )
    full_query = gathered[0][0]
    full_key = gathered[1][0]
    section_gain = norm_gain[0]
    block_starts = jnp.arange(block_count, dtype=jnp.int32) * block_rows

    def attention(by_heads, frame_row):
        query_all = by_heads[0].reshape(seq_total, local_heads, HEAD)
        key_all = by_heads[1].reshape(seq_total, local_heads, HEAD)
        value_all = by_heads[2].reshape(seq_total, local_heads, HEAD)

        def attend_block(query_start):
            query_heads = lax.dynamic_slice_in_dim(query_all, query_start, block_rows, 0)
            query_ids = lax.dynamic_slice_in_dim(frame_row, query_start, block_rows, 0)
            last_frame = query_ids[block_rows - 1]
            start_state = (
                jnp.full((local_heads, block_rows), -1e30, jnp.float32),
                jnp.zeros((local_heads, block_rows), jnp.float32),
                jnp.zeros((local_heads, block_rows, HEAD), jnp.float32),
            )

            def absorb(running, key_start):
                key_heads = lax.dynamic_slice_in_dim(key_all, key_start, block_rows, 0)
                value_heads = lax.dynamic_slice_in_dim(value_all, key_start, block_rows, 0)
                key_ids = lax.dynamic_slice_in_dim(frame_row, key_start, block_rows, 0)
                allowed = key_ids[None, :] <= query_ids[:, None]

                def update(state_in):
                    row_max, row_sum, mixed_sum = state_in
                    scores = (
                        jnp.einsum(
                            "shd,khd->hsk",
                            query_heads,
                            key_heads,
                            preferred_element_type=jnp.float32,
                        )
                        * score_scale
                    )
                    scores = jnp.where(allowed[None], scores, -1e30)
                    new_max = jnp.maximum(row_max, jnp.max(scores, axis=-1))
                    weights = jnp.where(allowed[None], jnp.exp(scores - new_max[..., None]), 0.0)
                    rescale = jnp.exp(row_max - new_max)
                    new_sum = row_sum * rescale + jnp.sum(weights, axis=-1)
                    new_mixed = mixed_sum * rescale[..., None] + jnp.einsum(
                        "hsk,khd->hsd",
                        weights.astype(jnp.bfloat16),
                        value_heads,
                        preferred_element_type=jnp.float32,
                    )
                    return (new_max, new_sum, new_mixed)

                def unchanged(state_in):
                    return state_in

                return (lax.cond(key_ids[0] <= last_frame, update, unchanged, running), None)

            final_state, _ = lax.scan(absorb, start_state, block_starts)
            row_max, row_sum, mixed_sum = final_state
            return (
                (mixed_sum / row_sum[..., None])
                .transpose(1, 0, 2)
                .reshape(block_rows, local_width)
                .astype(jnp.bfloat16)
            )

        return lax.map(attend_block, block_starts).reshape(seq_total, local_width)

    incoming = jnp.zeros((1, local_rows, model_width), jnp.bfloat16)
    finals = []
    moment_count = micro_count + phase_count - 1
    for moment in range(moment_count):
        micro_slot = jnp.clip(moment - phase_index, 0, micro_count - 1)
        active = jnp.logical_and(moment >= phase_index, moment - phase_index < micro_count)
        current = jnp.where(phase_index == 0, embedded[min(moment, micro_count - 1)], incoming)
        frame_row = lax.dynamic_index_in_dim(frame_ids, micro_slot, 0, keepdims=False)[0]
        wide_state = current.astype(jnp.float32)
        normed = rms_scale(wide_state, section_gain).astype(jnp.bfloat16)[0]

        def project(source):
            queries = jnp.dot(source, full_query, preferred_element_type=jnp.float32).astype(
                jnp.bfloat16
            )
            keys = jnp.dot(source, full_key, preferred_element_type=jnp.float32).astype(
                jnp.bfloat16
            )
            return jnp.stack((queries, keys, source), axis=0)

        def blank_triple(source):
            return jnp.zeros((3,) + source.shape, jnp.bfloat16)

        triple = lax.cond(active, project, blank_triple, normed)
        section_by_heads = lax.all_to_all(triple, "ctx", split_axis=2, concat_axis=1, tiled=True)

        def run_attention(arrived):
            return attention(arrived, frame_row)

        def blank_heads(arrived):
            return jnp.zeros((seq_total, local_width), jnp.bfloat16)

        mixed_heads = lax.cond(active, run_attention, blank_heads, section_by_heads)
        mixed = lax.all_to_all(mixed_heads, "ctx", split_axis=0, concat_axis=1, tiled=True)
        result = (wide_state + mixed.astype(jnp.float32)[None]).astype(jnp.bfloat16)
        if moment + 1 < moment_count:
            incoming = shifted(result, "pipe", 1)
        if moment >= phase_count - 1:
            finals.append(result)
    final_state = jnp.stack(finals, axis=0)
    final_state = broadcast(final_state, "pipe", phase_count - 1)
    head_cols = head_weight.shape[1]
    final_norm = rms_scale(final_state.astype(jnp.float32), head_gain).astype(jnp.bfloat16)
    velocity = jnp.einsum(
        "mbsd,dp->mbsp", final_norm, head_weight, preferred_element_type=jnp.float32
    )
    goal_cols = lax.dynamic_slice_in_dim(target, phase_index * head_cols, head_cols, 3)
    residue = velocity - goal_cols
    grad_term = jnp.einsum(
        "mbsd,mbsp->dp", final_norm.astype(jnp.float32), residue, precision=lax.Precision.HIGHEST
    ) / float(seq_total)
    summed = lax.psum(grad_term.astype(jnp.bfloat16), "ctx")
    gradient = lax.psum_scatter(summed, "dp", scatter_dimension=0, tiled=True).astype(jnp.float32)
    return (velocity, gradient)


def solution(mesh):
    placed = (
        P(None, "dp", "ctx", None),
        P(None, "dp", "ctx", None),
        P(None, "dp"),
        P(None, "dp", None),
        P(),
        P(),
        P("pipe", "dp", None),
        P("pipe", "dp", None),
        P("pipe", None),
        P(),
        P(None, "pipe"),
    )
    return jax.shard_map(
        on_device,
        mesh=mesh,
        in_specs=placed,
        out_specs=(P(None, "dp", "ctx", "pipe"), P("dp", "pipe")),
        check_vma=False,
    )
```

profile of v0, /device:TPU:1, one launch (start us, length us, event | category | flops | bytes accessed | tf_op | source)
XLA Modules:
  0.0 778.6 jit_solution(16003102793598724875)
XLA Ops:
  11.5 1.2 fusion.113
  13.1 67.5 %all-gather.3.cloned.1.call-done = bf16[1,1536,1536]{2,1,0:T(8,128)(2,1)} async-done(((bf16[1,192,1536]{2,1,0:T(8,128)(2,1)}), bf16[1,1536,1536]{2,1,0:T(8,128)(2,1)}) %all-gather.3.cloned.1.call-update) | async-done | bytes 4718608 | tf_op jit(solution)/shard_map/all_gather | solution.py:63
  80.6 66.1 %all-gather.5.cloned.1.call-done = bf16[1,1536,1536]{2,1,0:T(8,128)(2,1)} async-done(((bf16[1,192,1536]{2,1,0:T(8,128)(2,1)}), bf16[1,1536,1536]{2,1,0:T(8,128)(2,1)}) %all-gather.5.cloned.1.call-update) | async-done | bytes 4718608 | tf_op jit(solution)/shard_map/all_gather | solution.py:64
  146.8 1.0 copy.79
  147.8 1.9 reshape.611
  149.7 12.0 %all-to-all-start = ((bf16[16,2,9216]{2,1,0:T(2,128)(2,1)}), bf16[16,2,9216]{2,1,0:T(2,128)(2,1)S(1)}, u32[]{:S(2)}, u32[]{:S(2)}) async-start(bf16[16,2,9216]{2,1,0:T(2,128)(2,1)} %reshape.611), calls=%async_computation | async-start | bytes 1179648 | tf_op jit(solution)/shard_map/all_to_all | solution.py:156
  161.7 22.1 %all-to-all-done = bf16[16,2,9216]{2,1,0:T(2,128)(2,1)S(1)} async-done(((bf16[16,2,9216]{2,1,0:T(2,128)(2,1)}), bf16[16,2,9216]{2,1,0:T(2,128)(2,1)S(1)}, u32[]{:S(2)}, u32[]{:S(2)}) %all-to-all-start) | async-done | bytes 589856 | tf_op jit(solution)/shard_map/all_to_all | solution.py:156
  185.9 25.6 %all_to_all.145 = bf16[16,64,96]{2,1,0:T(8,128)(2,1)S(1)} all-to-all(bf16[16,64,96]{2,1,0:T(8,128)(2,1)S(1)} %bitcast.415), channel_id=1, replica_groups=mesh['pipe'=4,'ctx'=16,'dp'=8] {'ctx'}, dimensions={0} | all-to-all | bytes 393216 | tf_op jit(solution)/shard_map/all_to_all | solution.py:165
  212.1 13.8 %collective-permute-start = (bf16[1,64,1536]{2,1,0:T(8,128)(2,1)S(1)}, bf16[1,64,1536]{2,1,0:T(8,128)(2,1)S(1)}, u32[]{:S(2)}, u32[]{:S(2)}) collective-permute-start(bf16[1,64,1536]{2,1,0:T(8,128)(2,1)S(1)} %fusion.138), channel_id=1, source_target_pairs={{0,128},{128,256},{256,384},{1,129},{129,257},{257,385},{2,130},{1... | collective-permute-start | bytes 589832 | tf_op jit(solution)/shard_map/ppermute | solution.py:15
  225.9 24.0 %collective-permute-done = bf16[1,64,1536]{2,1,0:T(8,128)(2,1)S(1)} collective-permute-done((bf16[1,64,1536]{2,1,0:T(8,128)(2,1)S(1)}, bf16[1,64,1536]{2,1,0:T(8,128)(2,1)S(1)}, u32[]{:S(2)}, u32[]{:S(2)}) %collective-permute-start) | collective-permute-done | bytes 196640 | tf_op jit(solution)/shard_map/ppermute | solution.py:15
  250.2 4.8 conditional.17
  250.2 3.4 fusion.21
  255.0 1.0 copy.83
  256.0 1.9 reshape.613
  257.9 5.8 all-to-all-start.2
  263.7 26.1 %all-to-all-done.2 = bf16[16,2,9216]{2,1,0:T(2,128)(2,1)S(1)} async-done(((bf16[16,2,9216]{2,1,0:T(2,128)(2,1)}), bf16[16,2,9216]{2,1,0:T(2,128)(2,1)S(1)}, u32[]{:S(2)}, u32[]{:S(2)}) %all-to-all-start.2) | async-done | bytes 589856 | tf_op jit(solution)/shard_map/all_to_all | solution.py:156
  290.8 1.0 copy.103
  291.8 30.7 %conditional.18 = (bf16[1024,96]{1,0:T(8,128)(2,1)S(1)}) conditional(s32[]{:T(128)} %convert_element_type.296, () %tuple.177, (bf16[3,16,64,96]{3,1,2,0:T(8,128)(2,1)S(1)}, s32[]{:T(128)}, s32[2,1,1024]{2,1,0:T(1,128)S(1)}, s32[2]{0:T(128)S(1)}, s32[2]{0:T(128)S(1)}) %tuple.461), branch_computations={%region_16.17_spmd, %region_17.26_spmd} | conditional | flops 104006672 | bytes 8522588 | solution.py:164
  292.7 29.6 %while.130 = (s32[]{:T(128)}, bf16[2,512,96]{1,2,0:T(8,128)(2,1)S(1)}, s32[2]{0:T(128)S(1)}, s32[1024]{0:T(1024)S(1)}, bf16[1024,1,96]{0,2,1:T(8,128)(2,1)S(1)},...) while((s32[]{:T(128)}, ...), condition=%wide.region_25.25_spmd, body=%wide.region_18.24_spmd.sunk | while | flops 104006672 | bytes 4582064 | solution.py:130
  296.4 11.1 %while.143 = (s32[]{:T(128)}, f32[1,512]{1,0:T(1,128)S(1)}, f32[1,512]{1,0:T(1,128)S(1)}, f32[1,512,96]{1,2,0:T(8,128)S(1)}, s32[2]{0:T(128)S(1)}, /*index=5*/s3...) while((s32[]{:T(128)}, f32[1,512]{1,0:T(1,128)S(1)}, ...), condition=%wide.region_24.23_spmd, body=%wide.region_19.22_spmd.sunk | while | flops 103908360 | bytes 3883349 | solution.py:121
  300.8 1.1 conditional.33
  306.4 1.1 conditional.33
  311.2 11.1 %while.143 = (s32[]{:T(128)}, f32[1,512]{1,0:T(1,128)S(1)}, f32[1,512]{1,0:T(1,128)S(1)}, f32[1,512,96]{1,2,0:T(8,128)S(1)}, s32[2]{0:T(128)S(1)}, /*index=5*/s3...) while((s32[]{:T(128)}, f32[1,512]{1,0:T(1,128)S(1)}, ...), condition=%wide.region_24.23_spmd, body=%wide.region_19.22_spmd.sunk | while | flops 103908360 | bytes 3883349 | solution.py:121
  315.6 1.1 conditional.33
  321.2 1.1 conditional.33
  322.5 25.8 %all_to_all.146 = bf16[16,64,96]{2,1,0:T(8,128)(2,1)S(1)} all-to-all(bf16[16,64,96]{2,1,0:T(8,128)(2,1)S(1)} %bitcast.417), channel_id=1, replica_groups=mesh['pipe'=4,'ctx'=16,'dp'=8] {'ctx'}, dimensions={0} | all-to-all | bytes 393216 | tf_op jit(solution)/shard_map/all_to_all | solution.py:165
  349.0 1.9 collective-permute-start.1
  350.9 5.7 collective-permute-done.1
  356.9 4.8 conditional.19
  357.0 3.4 fusion.44
  361.7 1.0 copy.87
  362.8 1.9 reshape.615
  364.6 7.2 all-to-all-start.4
  371.9 27.0 %all-to-all-done.4 = bf16[16,2,9216]{2,1,0:T(2,128)(2,1)S(1)} async-done(((bf16[16,2,9216]{2,1,0:T(2,128)(2,1)}), bf16[16,2,9216]{2,1,0:T(2,128)(2,1)S(1)}, u32[]{:S(2)}, u32[]{:S(2)}) %all-to-all-start.4) | async-done | bytes 589856 | tf_op jit(solution)/shard_map/all_to_all | solution.py:156
  400.8 30.6 %conditional.20 = (bf16[1024,96]{1,0:T(8,128)(2,1)S(1)}) conditional(s32[]{:T(128)} %convert_element_type.303, () %tuple.181, (bf16[3,16,64,96]{3,1,2,0:T(8,128)(2,1)S(1)}, s32[]{:T(128)}, s32[2,1,1024]{2,1,0:T(1,128)S(1)}, s32[2]{0:T(128)S(1)}, s32[2]{0:T(128)S(1)}) %tuple.462), branch_computations={%region_29.30_spmd, %region_30.39_spmd} | conditional | flops 104006672 | bytes 8522588 | solution.py:164
  401.5 29.6 %while.133 = (s32[]{:T(128)}, bf16[2,512,96]{1,2,0:T(8,128)(2,1)S(1)}, s32[2]{0:T(128)S(1)}, s32[1024]{0:T(1024)S(1)}, bf16[1024,1,96]{0,2,1:T(8,128)(2,1)S(1)},...) while((s32[]{:T(128)}, ...), condition=%wide.region_38.38_spmd, body=%wide.region_31.37_spmd.sunk | while | flops 104006672 | bytes 4582064 | solution.py:130
  405.2 11.1 %while.142 = (s32[]{:T(128)}, f32[1,512]{1,0:T(1,128)S(1)}, f32[1,512]{1,0:T(1,128)S(1)}, f32[1,512,96]{1,2,0:T(8,128)S(1)}, s32[2]{0:T(128)S(1)}, /*index=5*/s3...) while((s32[]{:T(128)}, f32[1,512]{1,0:T(1,128)S(1)}, ...), condition=%wide.region_37.36_spmd, body=%wide.region_32.35_spmd.sunk | while | flops 103908360 | bytes 3883349 | solution.py:121
  409.6 1.1 conditional.32
  415.2 1.1 conditional.32
  420.0 11.1 %while.142 = (s32[]{:T(128)}, f32[1,512]{1,0:T(1,128)S(1)}, f32[1,512]{1,0:T(1,128)S(1)}, f32[1,512,96]{1,2,0:T(8,128)S(1)}, s32[2]{0:T(128)S(1)}, /*index=5*/s3...) while((s32[]{:T(128)}, f32[1,512]{1,0:T(1,128)S(1)}, ...), condition=%wide.region_37.36_spmd, body=%wide.region_32.35_spmd.sunk | while | flops 103908360 | bytes 3883349 | solution.py:121
  424.4 1.1 conditional.32
  430.0 1.1 conditional.32
  431.3 18.8 %all_to_all.147 = bf16[16,64,96]{2,1,0:T(8,128)(2,1)S(1)} all-to-all(bf16[16,64,96]{2,1,0:T(8,128)(2,1)S(1)} %bitcast.419), channel_id=1, replica_groups=mesh['pipe'=4,'ctx'=16,'dp'=8] {'ctx'}, dimensions={0} | all-to-all | bytes 393216 | tf_op jit(solution)/shard_map/all_to_all | solution.py:165
  450.7 1.9 collective-permute-start.2
  452.7 2.6 collective-permute-done.2
  455.6 1.0 copy.91
  456.7 1.9 reshape.617
  458.6 5.8 all-to-all-start.6
  464.3 32.2 %all-to-all-done.6 = bf16[16,2,9216]{2,1,0:T(2,128)(2,1)S(1)} async-done(((bf16[16,2,9216]{2,1,0:T(2,128)(2,1)}), bf16[16,2,9216]{2,1,0:T(2,128)(2,1)S(1)}, u32[]{:S(2)}, u32[]{:S(2)}) %all-to-all-start.6) | async-done | bytes 589856 | tf_op jit(solution)/shard_map/all_to_all | solution.py:156
  498.5 19.7 %all_to_all.148 = bf16[16,64,96]{2,1,0:T(8,128)(2,1)S(1)} all-to-all(bf16[16,64,96]{2,1,0:T(8,128)(2,1)S(1)} %bitcast.421), channel_id=1, replica_groups=mesh['pipe'=4,'ctx'=16,'dp'=8] {'ctx'}, dimensions={0} | all-to-all | bytes 393216 | tf_op jit(solution)/shard_map/all_to_all | solution.py:165
  518.9 37.8 %collective-permute-start.3 = (bf16[1,64,1536]{2,1,0:T(8,128)(2,1)S(1)}, bf16[1,64,1536]{2,1,0:T(8,128)(2,1)S(1)}, u32[]{:S(2)}, u32[]{:S(2)}) collective-permute-start(bf16[1,64,1536]{2,1,0:T(8,128)(2,1)S(1)} %fusion.130), channel_id=1, source_target_pairs={{0,128},{128,256},{256,384},{1,129},{129,257},{257,385},{2,130},{1... | collective-permute-start | bytes 589832 | tf_op jit(solution)/shard_map/ppermute | solution.py:15
  556.7 2.6 collective-permute-done.3
  559.7 1.0 copy.95
  560.7 1.8 reshape.619
  562.6 4.8 all-to-all-start.8
  567.4 23.6 %all-to-all-done.8 = bf16[16,2,9216]{2,1,0:T(2,128)(2,1)S(1)} async-done(((bf16[16,2,9216]{2,1,0:T(2,128)(2,1)}), bf16[16,2,9216]{2,1,0:T(2,128)(2,1)S(1)}, u32[]{:S(2)}, u32[]{:S(2)}) %all-to-all-start.8) | async-done | bytes 589856 | tf_op jit(solution)/shard_map/all_to_all | solution.py:156
  593.7 6.8 all-to-all-start.9
  600.6 12.7 %all-to-all-done.9 = bf16[16,64,96]{2,1,0:T(8,128)(2,1)S(1)} async-done(((bf16[16,64,96]{2,1,0:T(8,128)(2,1)}), bf16[16,64,96]{2,1,0:T(8,128)(2,1)S(1)}, u32[]{:S(2)}, u32[]{:S(2)}) %all-to-all-start.9) | async-done | bytes 196640 | tf_op jit(solution)/shard_map/all_to_all | solution.py:165
  615.1 86.8 %all-reduce.2.cloned.1.call-done = bf16[2,1,64,1536]{3,2,1,0:T(8,128)(2,1)} async-done(((bf16[2,1,64,1536]{3,2,1,0:T(8,128)(2,1)}), bf16[2,1,64,1536]{3,2,1,0:T(8,128)(2,1)}) %all-reduce.2.cloned.1.call-update) | async-done | bytes 393232 | tf_op jit(solution)/shard_map/psum | solution.py:20
  701.9 1.2 fusion.116
  703.1 1.3 fusion.144
  704.4 1.4 fusion.115
  706.8 39.4 %reduce-scatter.4.cloned.1.call-done = bf16[192,16]{1,0:T(8,128)(2,1)} async-done(((bf16[1536,16]{1,0:T(8,128)(2,1)}), bf16[192,16]{1,0:T(8,128)(2,1)}) %reduce-scatter.4.cloned.1.call-update) | async-done | bytes 6160
  747.1 24.4 %psum.16 = bf16[192,16]{0,1:T(8,128)(2,1)S(1)} all-reduce(bf16[192,16]{0,1:T(8,128)(2,1)S(1)} %copy.108), channel_id=1, replica_groups=mesh['pipe'=4,'ctx'=16,'dp'=8] {'ctx'}, use_global_device_ids=true, to_apply=%region_67.68 | all-reduce | flops 3072 | bytes 12288 | tf_op jit(solution)/shard_map/psum | solution.py:183
  (222 shorter events, 52.1 us)
Async XLA Ops:
  7.2 4.3 copy-start
  7.2 73.4 %all-gather.3.cloned.1.call-start = ((), (), s32[]{:S(2)}) async-start(), calls=%async_computation.11 | async-start | bytes 5308416 | tf_op jit(solution)/shard_map/all_gather | solution.py:63
  7.9 138.8 %all-gather.5.cloned.1.call-start = ((), (), s32[]{:S(2)}) async-start(), calls=%async_computation.12 | async-start | bytes 5308416 | tf_op jit(solution)/shard_map/all_gather | solution.py:64
  146.8 39.0 %copy-start.9 = (s32[2,1,1024]{2,1,0:T(1,128)S(1)}, s32[2,1,1024]{2,1,0:T(1,128)}, u32[]{:S(2)}) copy-start(s32[2,1,1024]{2,1,0:T(1,128)} %param.64) | copy-start | bytes 24580
  149.7 34.2 %all-to-all-start = ((bf16[16,2,9216]{2,1,0:T(2,128)(2,1)}), bf16[16,2,9216]{2,1,0:T(2,128)(2,1)S(1)}, u32[]{:S(2)}, u32[]{:S(2)}) async-start(bf16[16,2,9216]{2,1,0:T(2,128)(2,1)} %reshape.611), calls=%async_computation | async-start | bytes 1179648 | tf_op jit(solution)/shard_map/all_to_all | solution.py:156
  212.1 37.8 %collective-permute-start = (bf16[1,64,1536]{2,1,0:T(8,128)(2,1)S(1)}, bf16[1,64,1536]{2,1,0:T(8,128)(2,1)S(1)}, u32[]{:S(2)}, u32[]{:S(2)}) collective-permute-start(bf16[1,64,1536]{2,1,0:T(8,128)(2,1)S(1)} %fusion.138), channel_id=1, source_target_pairs={{0,128},{128,256},{256,384},{1,129},{129,257},{257,385},{2,130},{1... | collective-permute-start | bytes 589832 | tf_op jit(solution)/shard_map/ppermute | solution.py:15
  250.2 3.8 copy-start.3
  257.9 31.9 %all-to-all-start.2 = ((bf16[16,2,9216]{2,1,0:T(2,128)(2,1)}), bf16[16,2,9216]{2,1,0:T(2,128)(2,1)S(1)}, u32[]{:S(2)}, u32[]{:S(2)}) async-start(bf16[16,2,9216]{2,1,0:T(2,128)(2,1)} %reshape.613), calls=%async_computation.2 | async-start | bytes 1179648 | tf_op jit(solution)/shard_map/all_to_all | solution.py:156
  349.0 7.6 collective-permute-start.1
  357.0 3.8 copy-start.4
  364.6 34.2 %all-to-all-start.4 = ((bf16[16,2,9216]{2,1,0:T(2,128)(2,1)}), bf16[16,2,9216]{2,1,0:T(2,128)(2,1)S(1)}, u32[]{:S(2)}, u32[]{:S(2)}) async-start(bf16[16,2,9216]{2,1,0:T(2,128)(2,1)} %reshape.615), calls=%async_computation.4 | async-start | bytes 1179648 | tf_op jit(solution)/shard_map/all_to_all | solution.py:156
  450.7 4.5 collective-permute-start.2
  458.6 38.0 %all-to-all-start.6 = ((bf16[16,2,9216]{2,1,0:T(2,128)(2,1)}), bf16[16,2,9216]{2,1,0:T(2,128)(2,1)S(1)}, u32[]{:S(2)}, u32[]{:S(2)}) async-start(bf16[16,2,9216]{2,1,0:T(2,128)(2,1)} %reshape.617), calls=%async_computation.6 | async-start | bytes 1179648 | tf_op jit(solution)/shard_map/all_to_all | solution.py:156
  518.9 40.4 %collective-permute-start.3 = (bf16[1,64,1536]{2,1,0:T(8,128)(2,1)S(1)}, bf16[1,64,1536]{2,1,0:T(8,128)(2,1)S(1)}, u32[]{:S(2)}, u32[]{:S(2)}) collective-permute-start(bf16[1,64,1536]{2,1,0:T(8,128)(2,1)S(1)} %fusion.130), channel_id=1, source_target_pairs={{0,128},{128,256},{256,384},{1,129},{129,257},{257,385},{2,130},{1... | collective-permute-start | bytes 589832 | tf_op jit(solution)/shard_map/ppermute | solution.py:15
  562.6 28.4 %all-to-all-start.8 = ((bf16[16,2,9216]{2,1,0:T(2,128)(2,1)}), bf16[16,2,9216]{2,1,0:T(2,128)(2,1)S(1)}, u32[]{:S(2)}, u32[]{:S(2)}) async-start(bf16[16,2,9216]{2,1,0:T(2,128)(2,1)} %reshape.619), calls=%async_computation.8 | async-start | bytes 1179648 | tf_op jit(solution)/shard_map/all_to_all | solution.py:156
  593.7 21.1 %copy-start.7 = (f32[2,1,64,64]{3,2,1,0:T(8,128)S(1)}, f32[2,1,64,64]{3,2,1,0:T(8,128)}, u32[]{:S(2)}) copy-start(f32[2,1,64,64]{3,2,1,0:T(8,128)} %param.61) | copy-start | bytes 98308
  593.7 21.1 %copy-start.8 = (f32[2,1,64,64]{3,2,1,0:T(8,128)S(1)}, f32[2,1,64,64]{3,2,1,0:T(8,128)}, u32[]{:S(2)}) copy-start(f32[2,1,64,64]{3,2,1,0:T(8,128)} %param.62) | copy-start | bytes 98308
  593.7 109.4 %copy-start.10 = (bf16[1536,16]{0,1:T(8,128)(2,1)S(1)}, bf16[1536,16]{0,1:T(8,128)(2,1)}, u32[]{:S(2)}) copy-start(bf16[1536,16]{0,1:T(8,128)(2,1)} %param.71) | copy-start | bytes 147460
  593.7 109.4 %copy-start.11 = (f32[1536]{0:T(1024)S(1)}, f32[1536]{0:T(1024)}, u32[]{:S(2)}) copy-start(f32[1536]{0:T(1024)} %param.70) | copy-start | bytes 18436
  593.7 178.4 %copy-start.1 = (bf16[64,1536]{1,0:T(8,128)(2,1)S(1)}, bf16[64,1536]{1,0:T(8,128)(2,1)}, u32[]{:S(2)}) copy-start(bf16[64,1536]{1,0:T(8,128)(2,1)} %param.65) | copy-start | bytes 589828
  593.7 19.6 %all-to-all-start.9 = ((bf16[16,64,96]{2,1,0:T(8,128)(2,1)}), bf16[16,64,96]{2,1,0:T(8,128)(2,1)S(1)}, u32[]{:S(2)}, u32[]{:S(2)}) async-start(bf16[16,64,96]{2,1,0:T(8,128)(2,1)} %bitcast.134), calls=%async_computation.9 | async-start | bytes 524288 | tf_op jit(solution)/shard_map/all_to_all | solution.py:165
  600.5 101.4 %all-reduce.2.cloned.1.call-start = ((), (), s32[]{:S(2)}) async-start(), calls=%async_computation.13 | async-start | bytes 786432 | tf_op jit(solution)/shard_map/psum | solution.py:20
  614.8 131.5 %reduce-scatter.4.cloned.1.call-start = ((), (), s32[]{:S(2)}) async-start(), calls=%async_computation.14 | async-start | bytes 442368
  704.4 67.7 %copy-start.12 = (f32[2,64,16]{1,2,0:T(8,128)}, f32[2,64,16]{1,2,0:T(8,128)S(1)}, u32[]{:S(2)}) copy-start(f32[2,64,16]{1,2,0:T(8,128)S(1)} %fusion.144) | copy-start | bytes 24580
Sparse Core Ops, SparseCore 0:
  10.1 70.4 all-gather.2
  82.7 64.0 all-gather.4
  614.9 86.9 all-reduce.1
  706.9 39.2 reduce-scatter.3
where the time goes:
time: 791 us; the launch traced here: 779 us
  waiting for transfers between devices  440 us (56%)
  blocking collectives  114 us (14%)
  starting transfers between devices  98 us (12%)
  local copies, waits for them, and re-layouts  48 us (6%)
  loops' own time  35.3 us (4%)
  matrix products  19.1 us (2%)
  between operations  14.4 us (2%)
  other arithmetic  9.72 us (1%)
    all_to_all x5, waiting for transfers between devices, on_device(): lax.all_to_all(triple, 'ctx', split_axis=2, concat_axis=1, tiled=True)  131 us
    all_to_all x4, blocking collectives, on_device(): lax.all_to_all(mixed_heads, 'ctx', split_axis=0, concat_axis=1, tiled=True)  89.8 us
    psum x1, waiting for transfers between devices, broadcast(): return lax.psum(kept, axis)  86.8 us
    all_gather x1, waiting for transfers between devices, on_device(): lax.all_gather(query_weight, 'dp', axis=1, tiled=True)  67.5 us
    all_gather x1, waiting for transfers between devices, on_device(): lax.all_gather(key_weight, 'dp', axis=1, tiled=True)  66.1 us
    ppermute x4, starting transfers between devices, shifted(): lax.ppermute(value, axis, [(source, source + steps) for source in range(f...  55.4 us
    unnamed x5, waiting for transfers between devices  40.9 us
    all_to_all x5, starting transfers between devices, on_device(): lax.all_to_all(triple, 'ctx', split_axis=2, concat_axis=1, tiled=True)  35.6 us
  transfers between devices with their start and end apart: 14, of which 14 were waited for; matrix products, arithmetic and copies ran while one was open for 1% of the time, Pallas kernels for 0%

commit v1 on v0

--- a/solution.py
+++ b/solution.py
@@ -49,8 +49,6 @@
     local_heads = head_count // cycle_size
     local_width = local_heads * HEAD
     seq_total = local_rows * cycle_size
-    block_rows = min(512, seq_total)
-    block_count = seq_total // block_rows
     score_scale = HEAD ** (-0.5)
     flow_time = ((time_index.astype(jnp.float32) + 0.5) / 1000.0)[:, :, None, None]
     noisy_input = ((1.0 - flow_time) * noise_latent + flow_time * clean_latent).astype(jnp.bfloat16)
@@ -63,71 +61,31 @@
         lax.all_gather(query_weight, "dp", axis=1, tiled=True),
         lax.all_gather(key_weight, "dp", axis=1, tiled=True),
     )
+    head_full = lax.all_gather(head_weight, "pipe", axis=1, tiled=True)
     full_query = gathered[0][0]
     full_key = gathered[1][0]
     section_gain = norm_gain[0]
-    block_starts = jnp.arange(block_count, dtype=jnp.int32) * block_rows
 
     def attention(by_heads, frame_row):
         query_all = by_heads[0].reshape(seq_total, local_heads, HEAD)
         key_all = by_heads[1].reshape(seq_total, local_heads, HEAD)
         value_all = by_heads[2].reshape(seq_total, local_heads, HEAD)
-
-        def attend_block(query_start):
-            query_heads = lax.dynamic_slice_in_dim(query_all, query_start, block_rows, 0)
-            query_ids = lax.dynamic_slice_in_dim(frame_row, query_start, block_rows, 0)
-            last_frame = query_ids[block_rows - 1]
-            start_state = (
-                jnp.full((local_heads, block_rows), -1e30, jnp.float32),
-                jnp.zeros((local_heads, block_rows), jnp.float32),
-                jnp.zeros((local_heads, block_rows, HEAD), jnp.float32),
-            )
-
-            def absorb(running, key_start):
-                key_heads = lax.dynamic_slice_in_dim(key_all, key_start, block_rows, 0)
-                value_heads = lax.dynamic_slice_in_dim(value_all, key_start, block_rows, 0)
-                key_ids = lax.dynamic_slice_in_dim(frame_row, key_start, block_rows, 0)
-                allowed = key_ids[None, :] <= query_ids[:, None]
-
-                def update(state_in):
-                    row_max, row_sum, mixed_sum = state_in
-                    scores = (
-                        jnp.einsum(
-                            "shd,khd->hsk",
-                            query_heads,
-                            key_heads,
-                            preferred_element_type=jnp.float32,
-                        )
-                        * score_scale
-                    )
-                    scores = jnp.where(allowed[None], scores, -1e30)
-                    new_max = jnp.maximum(row_max, jnp.max(scores, axis=-1))
-                    weights = jnp.where(allowed[None], jnp.exp(scores - new_max[..., None]), 0.0)
-                    rescale = jnp.exp(row_max - new_max)
-                    new_sum = row_sum * rescale + jnp.sum(weights, axis=-1)
-                    new_mixed = mixed_sum * rescale[..., None] + jnp.einsum(
-                        "hsk,khd->hsd",
-                        weights.astype(jnp.bfloat16),
-                        value_heads,
-                        preferred_element_type=jnp.float32,
-                    )
-                    return (new_max, new_sum, new_mixed)
-
-                def unchanged(state_in):
-                    return state_in
-
-                return (lax.cond(key_ids[0] <= last_frame, update, unchanged, running), None)
-
-            final_state, _ = lax.scan(absorb, start_state, block_starts)
-            row_max, row_sum, mixed_sum = final_state
-            return (
-                (mixed_sum / row_sum[..., None])
-                .transpose(1, 0, 2)
-                .reshape(block_rows, local_width)
-                .astype(jnp.bfloat16)
-            )
-
-        return lax.map(attend_block, block_starts).reshape(seq_total, local_width)
+        allowed = frame_row[None, :] <= frame_row[:, None]
+        scores = (
+            jnp.einsum("shd,khd->hsk", query_all, key_all, preferred_element_type=jnp.float32)
+            * score_scale
+        )
+        scores = jnp.where(allowed[None], scores, -1e30)
+        row_max = jnp.max(scores, axis=-1, keepdims=True)
+        weights = jnp.where(allowed[None], jnp.exp(scores - row_max), 0.0)
+        row_sum = jnp.sum(weights, axis=-1)
+        mixed = jnp.einsum(
+            "hsk,khd->hsd",
+            weights.astype(jnp.bfloat16),
+            value_all,
+            preferred_element_type=jnp.float32,
+        ) / row_sum[..., None]
+        return mixed.transpose(1, 0, 2).reshape(seq_total, local_width).astype(jnp.bfloat16)
 
     incoming = jnp.zeros((1, local_rows, model_width), jnp.bfloat16)
     finals = []
@@ -169,19 +127,33 @@
         if moment >= phase_count - 1:
             finals.append(result)
     final_state = jnp.stack(finals, axis=0)
-    final_state = broadcast(final_state, "pipe", phase_count - 1)
+    last_phase = phase_count - 1
+    is_last = phase_index == last_phase
     head_cols = head_weight.shape[1]
     final_norm = rms_scale(final_state.astype(jnp.float32), head_gain).astype(jnp.bfloat16)
-    velocity = jnp.einsum(
-        "mbsd,dp->mbsp", final_norm, head_weight, preferred_element_type=jnp.float32
+    velocity_all = jnp.einsum(
+        "mbsd,dp->mbsp", final_norm, head_full, preferred_element_type=jnp.float32
     )
-    goal_cols = lax.dynamic_slice_in_dim(target, phase_index * head_cols, head_cols, 3)
-    residue = velocity - goal_cols
-    grad_term = jnp.einsum(
+    residue = velocity_all - target
+    grad_all = jnp.einsum(
         "mbsd,mbsp->dp", final_norm.astype(jnp.float32), residue, precision=lax.Precision.HIGHEST
     ) / float(seq_total)
-    summed = lax.psum(grad_term.astype(jnp.bfloat16), "ctx")
-    gradient = lax.psum_scatter(summed, "dp", scatter_dimension=0, tiled=True).astype(jnp.float32)
+    arrived = jnp.zeros(velocity_all.shape[:3] + (head_cols,), jnp.float32)
+    for target_phase in range(last_phase):
+        piece = velocity_all[..., target_phase * head_cols : (target_phase + 1) * head_cols]
+        arrived = arrived + lax.ppermute(piece, "pipe", [(last_phase, target_phase)])
+    own_piece = velocity_all[..., last_phase * head_cols :]
+    velocity = jnp.where(is_last, own_piece, arrived)
+    dp_count = lax.axis_size("dp")
+    grad_rows = model_width // dp_count
+    kept = jnp.where(is_last, grad_all, 0.0)
+    blocks = (
+        kept.reshape(dp_count, grad_rows, phase_count, head_cols)
+        .transpose(0, 2, 1, 3)
+        .reshape(dp_count * phase_count, grad_rows, head_cols)
+    )
+    scattered = lax.psum_scatter(blocks, ("dp", "pipe"), scatter_dimension=0, tiled=True)
+    gradient = lax.psum(scattered.reshape(grad_rows, head_cols), "ctx")
     return (velocity, gradient)
 
 

time: 791 us -> 736 us (0.930)
  the two profiles are of different devices: /device:TPU:1 before, /device:TPU:32 now
where the time goes in v1:
time: 736 us; the launch traced here: 727 us
  waiting for transfers between devices  403 us (55%)
  blocking collectives  187 us (25%)
  starting transfers between devices  66.6 us (9%)
  local copies, waits for them, and re-layouts  31 us (4%)
  matrix products  14.6 us (2%)
  between operations  14.6 us (2%)
  other arithmetic  8.79 us (1%)
    all_to_all x5, waiting for transfers between devices, on_device(): lax.all_to_all(triple, 'ctx', split_axis=2, concat_axis=1, tiled=True)  127 us
    reduce_scatter x1, waiting for transfers between devices, on_device(): lax.psum_scatter(blocks, ('dp', 'pipe'), scatter_dimension=0, tiled=True)  126 us
    all_to_all x4, blocking collectives, on_device(): lax.all_to_all(mixed_heads, 'ctx', split_axis=0, concat_axis=1, tiled=True)  110 us
    all_gather x1, waiting for transfers between devices, on_device(): lax.all_gather(query_weight, 'dp', axis=1, tiled=True)  66.3 us
    all_gather x1, waiting for transfers between devices, on_device(): lax.all_gather(key_weight, 'dp', axis=1, tiled=True)  66.1 us
    psum x1, blocking collectives, on_device(): gradient = lax.psum(scattered.reshape(grad_rows, head_cols), 'ctx')  56 us
    all_to_all x5, starting transfers between devices, on_device(): lax.all_to_all(triple, 'ctx', split_axis=2, concat_axis=1, tiled=True)  36.9 us
    all_gather x1, blocking collectives, on_device(): head_full = lax.all_gather(head_weight, 'pipe', axis=1, tiled=True)  21.2 us
  transfers between devices with their start and end apart: 16, of which 13 were waited for; matrix products, arithmetic and copies ran while one was open for 1% of the time, Pallas kernels for 0%

profile of v1, /device:TPU:32, one launch (start us, length us, event | category | flops | bytes accessed | tf_op | source)
XLA Modules:
  0.0 727.0 jit_solution(17154873010605061578)
XLA Ops:
  11.5 1.2 fusion.88
  13.1 66.3 %all-gather.3.cloned.1.call-done = bf16[1,1536,1536]{2,1,0:T(8,128)(2,1)} async-done(((bf16[1,192,1536]{2,1,0:T(8,128)(2,1)}), bf16[1,1536,1536]{2,1,0:T(8,128)(2,1)}) %all-gather.3.cloned.1.call-update) | async-done | bytes 4718608 | tf_op jit(solution)/shard_map/all_gather | solution.py:61
  79.4 66.1 %all-gather.5.cloned.1.call-done = bf16[1,1536,1536]{2,1,0:T(8,128)(2,1)} async-done(((bf16[1,192,1536]{2,1,0:T(8,128)(2,1)}), bf16[1,1536,1536]{2,1,0:T(8,128)(2,1)}) %all-gather.5.cloned.1.call-update) | async-done | bytes 4718608 | tf_op jit(solution)/shard_map/all_gather | solution.py:62
  145.5 4.8 conditional.10
  145.5 3.4 fusion
  149.3 0.9 fusion.1
  150.3 1.0 copy.41
  151.4 1.8 reshape.565
  153.2 12.7 %all-to-all-start = ((bf16[16,2,9216]{2,1,0:T(2,128)(2,1)}), bf16[16,2,9216]{2,1,0:T(2,128)(2,1)S(1)}, u32[]{:S(2)}, u32[]{:S(2)}) async-start(bf16[16,2,9216]{2,1,0:T(2,128)(2,1)} %reshape.565), calls=%async_computation | async-start | bytes 1179648 | tf_op jit(solution)/shard_map/all_to_all | solution.py:114
  165.9 25.3 %all-to-all-done = bf16[16,2,9216]{2,1,0:T(2,128)(2,1)S(1)} async-done(((bf16[16,2,9216]{2,1,0:T(2,128)(2,1)}), bf16[16,2,9216]{2,1,0:T(2,128)(2,1)S(1)}, u32[]{:S(2)}, u32[]{:S(2)}) %all-to-all-start) | async-done | bytes 589856 | tf_op jit(solution)/shard_map/all_to_all | solution.py:114
  191.1 0.9 reshape.566
  192.1 1.0 copy.70
  193.1 3.8 conditional.11
  194.1 1.5 fusion.3
  195.7 1.2 fusion.10
  197.1 23.0 %all_to_all.145 = bf16[16,64,96]{2,1,0:T(8,128)(2,1)S(1)} all-to-all(bf16[16,64,96]{2,1,0:T(8,128)(2,1)S(1)} %bitcast.192), channel_id=1, replica_groups=mesh['pipe'=4,'ctx'=16,'dp'=8] {'ctx'}, dimensions={0} | all-to-all | bytes 393216 | tf_op jit(solution)/shard_map/all_to_all | solution.py:123
  220.7 1.3 collective-permute-start
  222.0 1.0 collective-permute-done
  223.4 4.8 conditional.12
  223.4 3.4 fusion.16
  227.2 0.9 fusion.17
  228.2 1.0 copy.46
  229.2 1.8 reshape.567
  231.1 5.0 all-to-all-start.2
  236.1 26.3 %all-to-all-done.2 = bf16[16,2,9216]{2,1,0:T(2,128)(2,1)S(1)} async-done(((bf16[16,2,9216]{2,1,0:T(2,128)(2,1)}), bf16[16,2,9216]{2,1,0:T(2,128)(2,1)S(1)}, u32[]{:S(2)}, u32[]{:S(2)}) %all-to-all-start.2) | async-done | bytes 589856 | tf_op jit(solution)/shard_map/all_to_all | solution.py:114
  262.4 0.9 reshape.568
  263.3 1.0 copy.71
  264.3 4.3 conditional.13
  265.8 1.5 fusion.21
  267.4 1.2 fusion.28
  268.8 30.6 %all_to_all.146 = bf16[16,64,96]{2,1,0:T(8,128)(2,1)S(1)} all-to-all(bf16[16,64,96]{2,1,0:T(8,128)(2,1)S(1)} %bitcast.193), channel_id=1, replica_groups=mesh['pipe'=4,'ctx'=16,'dp'=8] {'ctx'}, dimensions={0} | all-to-all | bytes 393216 | tf_op jit(solution)/shard_map/all_to_all | solution.py:123
  300.1 2.0 collective-permute-start.1
  302.1 1.0 collective-permute-done.1
  303.5 1.0 copy.51
  304.5 1.8 reshape.569
  306.4 6.6 all-to-all-start.4
  313.0 26.2 %all-to-all-done.4 = bf16[16,2,9216]{2,1,0:T(2,128)(2,1)S(1)} async-done(((bf16[16,2,9216]{2,1,0:T(2,128)(2,1)}), bf16[16,2,9216]{2,1,0:T(2,128)(2,1)S(1)}, u32[]{:S(2)}, u32[]{:S(2)}) %all-to-all-start.4) | async-done | bytes 589856 | tf_op jit(solution)/shard_map/all_to_all | solution.py:114
  339.2 0.9 reshape.570
  340.1 1.0 copy.72
  341.3 26.5 %all_to_all.147 = bf16[16,64,96]{2,1,0:T(8,128)(2,1)S(1)} all-to-all(bf16[16,64,96]{2,1,0:T(8,128)(2,1)S(1)} %bitcast.194), channel_id=1, replica_groups=mesh['pipe'=4,'ctx'=16,'dp'=8] {'ctx'}, dimensions={0} | all-to-all | bytes 393216 | tf_op jit(solution)/shard_map/all_to_all | solution.py:123
  368.4 6.6 collective-permute-start.2
  375.0 1.0 collective-permute-done.2
  376.6 1.0 copy.56
  377.6 1.8 reshape.571
  379.5 6.0 all-to-all-start.6
  385.5 27.4 %all-to-all-done.6 = bf16[16,2,9216]{2,1,0:T(2,128)(2,1)S(1)} async-done(((bf16[16,2,9216]{2,1,0:T(2,128)(2,1)}), bf16[16,2,9216]{2,1,0:T(2,128)(2,1)S(1)}, u32[]{:S(2)}, u32[]{:S(2)}) %all-to-all-start.6) | async-done | bytes 589856 | tf_op jit(solution)/shard_map/all_to_all | solution.py:114
  412.9 0.9 reshape.572
  413.8 1.0 copy.73
  415.0 29.6 %all_to_all.148 = bf16[16,64,96]{2,1,0:T(8,128)(2,1)S(1)} all-to-all(bf16[16,64,96]{2,1,0:T(8,128)(2,1)S(1)} %bitcast.195), channel_id=1, replica_groups=mesh['pipe'=4,'ctx'=16,'dp'=8] {'ctx'}, dimensions={0} | all-to-all | bytes 393216 | tf_op jit(solution)/shard_map/all_to_all | solution.py:123
  445.3 2.0 collective-permute-start.3
  447.3 1.0 collective-permute-done.3
  448.7 1.0 copy.61
  449.7 1.8 reshape.573
  451.6 6.6 all-to-all-start.8
  458.2 21.4 %all-to-all-done.8 = bf16[16,2,9216]{2,1,0:T(2,128)(2,1)S(1)} async-done(((bf16[16,2,9216]{2,1,0:T(2,128)(2,1)}), bf16[16,2,9216]{2,1,0:T(2,128)(2,1)S(1)}, u32[]{:S(2)}, u32[]{:S(2)}) %all-to-all-start.8) | async-done | bytes 589856 | tf_op jit(solution)/shard_map/all_to_all | solution.py:114
  479.5 0.9 reshape.574
  480.5 1.0 copy.74
  482.6 15.2 %all-to-all-start.9 = ((bf16[16,64,96]{2,1,0:T(8,128)(2,1)}), bf16[16,64,96]{2,1,0:T(8,128)(2,1)S(1)}, u32[]{:S(2)}, u32[]{:S(2)}) async-start(bf16[16,64,96]{2,1,0:T(8,128)(2,1)} %bitcast.58), calls=%async_computation.9 | async-start | bytes 524288 | tf_op jit(solution)/shard_map/all_to_all | solution.py:123
  498.1 21.2 %all_gather.11 = bf16[1536,64]{0,1:T(8,128)(2,1)S(1)} all-gather(bf16[1536,16]{0,1:T(8,128)(2,1)S(1)} %copy-done.10), channel_id=1, replica_groups=mesh['pipe'=4,'ctx'=16,'dp'=8] {'pipe'}, dimensions={1}, use_global_device_ids=true | all-gather | bytes 245760 | tf_op jit(solution)/shard_map/all_gather | solution.py:64
  521.1 1.0 copy.68
  522.1 1.3 collective-permute-start.4
  524.8 12.4 %collective-permute-done.4 = f32[2,1,64,16]{2,3,0,1:T(8,128)S(1)} collective-permute-done((f32[2,1,64,16]{2,3,0,1:T(8,128)S(1)}, f32[2,1,64,16]{2,3,0,1:T(8,128)S(1)}, u32[]{:S(2)}, u32[]{:S(2)}) %collective-permute-start.4) | collective-permute-done | bytes 8224 | tf_op jit(solution)/shard_map/ppermute | solution.py:144
  537.8 126.5 %reduce-scatter.2.cloned.1.call-done = f32[1,192,16]{1,2,0:T(8,128)} async-done(((f32[32,192,16]{1,2,0:T(8,128)}), f32[1,192,16]{1,2,0:T(8,128)}) %reduce-scatter.2.cloned.1.call-update) | async-done | bytes 12304 | tf_op jit(solution)/shard_map/reduce_scatter | solution.py:155
  664.2 56.0 %psum.7 = f32[192,16]{0,1:T(8,128)} all-reduce(f32[192,16]{0,1:T(8,128)} %bitcast.228), channel_id=1, replica_groups=mesh['pipe'=4,'ctx'=16,'dp'=8] {'ctx'}, use_global_device_ids=true, to_apply=%region_37.38 | all-reduce | flops 3072 | bytes 24576 | tf_op jit(solution)/shard_map/psum | solution.py:156
  (105 shorter events, 17.6 us)
Async XLA Ops:
  7.2 4.3 copy-start
  7.2 72.2 %all-gather.3.cloned.1.call-start = ((), (), s32[]{:S(2)}) async-start(), calls=%async_computation.11 | async-start | bytes 5308416 | tf_op jit(solution)/shard_map/all_gather | solution.py:61
  7.9 137.6 %all-gather.5.cloned.1.call-start = ((), (), s32[]{:S(2)}) async-start(), calls=%async_computation.12 | async-start | bytes 5308416 | tf_op jit(solution)/shard_map/all_gather | solution.py:62
  145.5 3.8 copy-start.2
  151.4 41.7 %copy-start.9 = (s32[2,1,1024]{2,1,0:T(1,128)S(1)}, s32[2,1,1024]{2,1,0:T(1,128)}, u32[]{:S(2)}) copy-start(s32[2,1,1024]{2,1,0:T(1,128)} %param.34) | copy-start | bytes 24580
  153.2 37.9 %all-to-all-start = ((bf16[16,2,9216]{2,1,0:T(2,128)(2,1)}), bf16[16,2,9216]{2,1,0:T(2,128)(2,1)S(1)}, u32[]{:S(2)}, u32[]{:S(2)}) async-start(bf16[16,2,9216]{2,1,0:T(2,128)(2,1)} %reshape.565), calls=%async_computation | async-start | bytes 1179648 | tf_op jit(solution)/shard_map/all_to_all | solution.py:114
  220.7 2.4 collective-permute-start
  223.4 3.8 copy-start.3
  231.1 31.3 %all-to-all-start.2 = ((bf16[16,2,9216]{2,1,0:T(2,128)(2,1)}), bf16[16,2,9216]{2,1,0:T(2,128)(2,1)S(1)}, u32[]{:S(2)}, u32[]{:S(2)}) async-start(bf16[16,2,9216]{2,1,0:T(2,128)(2,1)} %reshape.567), calls=%async_computation.2 | async-start | bytes 1179648 | tf_op jit(solution)/shard_map/all_to_all | solution.py:114
  300.1 3.0 collective-permute-start.1
  306.4 32.8 %all-to-all-start.4 = ((bf16[16,2,9216]{2,1,0:T(2,128)(2,1)}), bf16[16,2,9216]{2,1,0:T(2,128)(2,1)S(1)}, u32[]{:S(2)}, u32[]{:S(2)}) async-start(bf16[16,2,9216]{2,1,0:T(2,128)(2,1)} %reshape.569), calls=%async_computation.4 | async-start | bytes 1179648 | tf_op jit(solution)/shard_map/all_to_all | solution.py:114
  368.4 7.6 %collective-permute-start.2 = (bf16[1,64,1536]{2,1,0:T(8,128)(2,1)S(1)}, bf16[1,64,1536]{2,1,0:T(8,128)(2,1)S(1)}, u32[]{:S(2)}, u32[]{:S(2)}) collective-permute-start(bf16[1,64,1536]{2,1,0:T(8,128)(2,1)S(1)} %fusion.98), channel_id=1, source_target_pairs={{0,128},{128,256},{256,384},{1,129},{129,257},{257,385},{2,130},{1... | collective-permute-start | bytes 589832 | tf_op jit(solution)/shard_map/ppermute | solution.py:15
  379.5 33.4 %all-to-all-start.6 = ((bf16[16,2,9216]{2,1,0:T(2,128)(2,1)}), bf16[16,2,9216]{2,1,0:T(2,128)(2,1)S(1)}, u32[]{:S(2)}, u32[]{:S(2)}) async-start(bf16[16,2,9216]{2,1,0:T(2,128)(2,1)} %reshape.571), calls=%async_computation.6 | async-start | bytes 1179648 | tf_op jit(solution)/shard_map/all_to_all | solution.py:114
  445.3 3.0 collective-permute-start.3
  451.6 28.0 %all-to-all-start.8 = ((bf16[16,2,9216]{2,1,0:T(2,128)(2,1)}), bf16[16,2,9216]{2,1,0:T(2,128)(2,1)S(1)}, u32[]{:S(2)}, u32[]{:S(2)}) async-start(bf16[16,2,9216]{2,1,0:T(2,128)(2,1)} %reshape.573), calls=%async_computation.8 | async-start | bytes 1179648 | tf_op jit(solution)/shard_map/all_to_all | solution.py:114
  481.5 16.4 %copy-start.7 = (f32[2,1,64,64]{3,2,1,0:T(8,128)S(1)}, f32[2,1,64,64]{3,2,1,0:T(8,128)}, u32[]{:S(2)}) copy-start(f32[2,1,64,64]{3,2,1,0:T(8,128)} %param.31) | copy-start | bytes 98308
  481.5 16.4 %copy-start.8 = (f32[2,1,64,64]{3,2,1,0:T(8,128)S(1)}, f32[2,1,64,64]{3,2,1,0:T(8,128)}, u32[]{:S(2)}) copy-start(f32[2,1,64,64]{3,2,1,0:T(8,128)} %param.32) | copy-start | bytes 98308
  481.5 16.5 %copy-start.10 = (bf16[1536,16]{0,1:T(8,128)(2,1)S(1)}, bf16[1536,16]{0,1:T(8,128)(2,1)}, u32[]{:S(2)}) copy-start(bf16[1536,16]{0,1:T(8,128)(2,1)} %param.41) | copy-start | bytes 147460
  481.8 38.3 %copy-start.11 = (f32[1536]{0:T(1024)S(1)}, f32[1536]{0:T(1024)}, u32[]{:S(2)}) copy-start(f32[1536]{0:T(1024)} %param.40) | copy-start | bytes 18436
  482.6 36.7 %all-to-all-start.9 = ((bf16[16,64,96]{2,1,0:T(8,128)(2,1)}), bf16[16,64,96]{2,1,0:T(8,128)(2,1)S(1)}, u32[]{:S(2)}, u32[]{:S(2)}) async-start(bf16[16,64,96]{2,1,0:T(8,128)(2,1)} %bitcast.58), calls=%async_computation.9 | async-start | bytes 524288 | tf_op jit(solution)/shard_map/all_to_all | solution.py:123
  497.8 166.4 %reduce-scatter.2.cloned.1.call-start = ((), (), s32[]{:S(2)}) async-start(), calls=%async_computation.13 | async-start | bytes 540672 | tf_op jit(solution)/shard_map/reduce_scatter | solution.py:155
  519.3 201.0 %copy-start.1 = (bf16[64,1536]{1,0:T(8,128)(2,1)S(1)}, bf16[64,1536]{1,0:T(8,128)(2,1)}, u32[]{:S(2)}) copy-start(bf16[64,1536]{1,0:T(8,128)(2,1)} %param.35) | copy-start | bytes 589828
  522.1 15.0 %collective-permute-start.4 = (f32[2,1,64,16]{2,3,0,1:T(8,128)S(1)}, f32[2,1,64,16]{2,3,0,1:T(8,128)S(1)}, u32[]{:S(2)}, u32[]{:S(2)}) collective-permute-start(f32[2,1,64,16]{2,3,0,1:T(8,128)S(1)} %get-tuple-element.294), channel_id=1, source_target_pairs={{384,0},{385,1},{386,2},{387,3},{388,4},{389,5},{390,6},{391,7},{3... | collective-permute-start | bytes 24584 | tf_op jit(solution)/shard_map/ppermute | solution.py:144
  523.4 13.7 %collective-permute-start.5 = (f32[2,1,64,16]{2,3,0,1:T(8,128)S(1)}, f32[2,1,64,16]{2,3,0,1:T(8,128)S(1)}, u32[]{:S(2)}, u32[]{:S(2)}) collective-permute-start(f32[2,1,64,16]{2,3,0,1:T(8,128)S(1)} %get-tuple-element.292), channel_id=1, source_target_pairs={{384,128},{385,129},{386,130},{387,131},{388,132},{389,133},{390,1... | collective-permute-start | bytes 24584 | tf_op jit(solution)/shard_map/ppermute | solution.py:144
  524.1 13.0 %collective-permute-start.6 = (f32[2,1,64,16]{2,3,0,1:T(8,128)S(1)}, f32[2,1,64,16]{2,3,0,1:T(8,128)S(1)}, u32[]{:S(2)}, u32[]{:S(2)}) collective-permute-start(f32[2,1,64,16]{2,3,0,1:T(8,128)S(1)} %get-tuple-element.293), channel_id=1, source_target_pairs={{384,256},{385,257},{386,258},{387,259},{388,260},{389,261},{390,2... | collective-permute-start | bytes 24584 | tf_op jit(solution)/shard_map/ppermute | solution.py:144
Sparse Core Ops, SparseCore 0:
  10.1 69.2 all-gather.2
  81.5 64.0 all-gather.4
  522.2 141.9 reduce-scatter.1

commit v2 on v1

--- a/solution.py
+++ b/solution.py
@@ -13,11 +13,6 @@
     count = lax.axis_size(axis)
     first, last = (max(0, -steps), min(count, count - steps))
     return lax.ppermute(value, axis, [(source, source + steps) for source in range(first, last)])
-
-
-def broadcast(value, axis, source):
-    kept = jnp.where(lax.axis_index(axis) == source, value, 0).astype(value.dtype)
-    return lax.psum(kept, axis)
 
 
 def rms_scale(values, gain_row):
@@ -41,7 +36,9 @@
 ):
     phase_index = lax.axis_index("pipe")
     phase_count = lax.axis_size("pipe")
+    cycle_index = lax.axis_index("ctx")
     cycle_size = lax.axis_size("ctx")
+    dp_count = lax.axis_size("dp")
     micro_count = clean_latent.shape[0]
     local_rows = clean_latent.shape[2]
     model_width = embed_weight.shape[1]
@@ -57,19 +54,18 @@
         "mbsp,pd->mbsd", noisy_input, embed_weight, preferred_element_type=jnp.float32
     )
     embedded = (embedded + flow_time * time_vector).astype(jnp.bfloat16)
-    gathered = (
-        lax.all_gather(query_weight, "dp", axis=1, tiled=True),
-        lax.all_gather(key_weight, "dp", axis=1, tiled=True),
-    )
+    column_start = cycle_index * local_width
+    query_cols = lax.dynamic_slice_in_dim(query_weight[0], column_start, local_width, 1)
+    key_cols = lax.dynamic_slice_in_dim(key_weight[0], column_start, local_width, 1)
+    head_query = lax.all_gather(query_cols, "dp", axis=0, tiled=True)
+    head_key = lax.all_gather(key_cols, "dp", axis=0, tiled=True)
     head_full = lax.all_gather(head_weight, "pipe", axis=1, tiled=True)
-    full_query = gathered[0][0]
-    full_key = gathered[1][0]
     section_gain = norm_gain[0]
 
-    def attention(by_heads, frame_row):
-        query_all = by_heads[0].reshape(seq_total, local_heads, HEAD)
-        key_all = by_heads[1].reshape(seq_total, local_heads, HEAD)
-        value_all = by_heads[2].reshape(seq_total, local_heads, HEAD)
+    def attention(query_all, key_all, value_all, frame_row):
+        query_all = query_all.reshape(seq_total, local_heads, HEAD)
+        key_all = key_all.reshape(seq_total, local_heads, HEAD)
+        value_all = value_all.reshape(seq_total, local_heads, HEAD)
         allowed = frame_row[None, :] <= frame_row[:, None]
         scores = (
             jnp.einsum("shd,khd->hsk", query_all, key_all, preferred_element_type=jnp.float32)
@@ -87,6 +83,19 @@
         ) / row_sum[..., None]
         return mixed.transpose(1, 0, 2).reshape(seq_total, local_width).astype(jnp.bfloat16)
 
+    def mix_heads(rows_all, frame_row):
+        queries = jnp.dot(rows_all, head_query, preferred_element_type=jnp.float32).astype(
+            jnp.bfloat16
+        )
+        keys = jnp.dot(rows_all, head_key, preferred_element_type=jnp.float32).astype(
+            jnp.bfloat16
+        )
+        values = lax.dynamic_slice_in_dim(rows_all, column_start, local_width, 1)
+        return attention(queries, keys, values, frame_row)
+
+    def blank_heads(rows_all, frame_row):
+        return jnp.zeros((seq_total, local_width), jnp.bfloat16)
+
     incoming = jnp.zeros((1, local_rows, model_width), jnp.bfloat16)
     finals = []
     moment_count = micro_count + phase_count - 1
@@ -97,29 +106,8 @@
         frame_row = lax.dynamic_index_in_dim(frame_ids, micro_slot, 0, keepdims=False)[0]
         wide_state = current.astype(jnp.float32)
         normed = rms_scale(wide_state, section_gain).astype(jnp.bfloat16)[0]
-
-        def project(source):
-            queries = jnp.dot(source, full_query, preferred_element_type=jnp.float32).astype(
-                jnp.bfloat16
-            )
-            keys = jnp.dot(source, full_key, preferred_element_type=jnp.float32).astype(
-                jnp.bfloat16
-            )
-            return jnp.stack((queries, keys, source), axis=0)
-
-        def blank_triple(source):
-            return jnp.zeros((3,) + source.shape, jnp.bfloat16)
-
-        triple = lax.cond(active, project, blank_triple, normed)
-        section_by_heads = lax.all_to_all(triple, "ctx", split_axis=2, concat_axis=1, tiled=True)
-
-        def run_attention(arrived):
-            return attention(arrived, frame_row)
-
-        def blank_heads(arrived):
-            return jnp.zeros((seq_total, local_width), jnp.bfloat16)
-
-        mixed_heads = lax.cond(active, run_attention, blank_heads, section_by_heads)
+        rows_all = lax.all_gather(normed, "ctx", axis=0, tiled=True)
+        mixed_heads = lax.cond(active, mix_heads, blank_heads, rows_all, frame_row)
         mixed = lax.all_to_all(mixed_heads, "ctx", split_axis=0, concat_axis=1, tiled=True)
         result = (wide_state + mixed.astype(jnp.float32)[None]).astype(jnp.bfloat16)
         if moment + 1 < moment_count:
@@ -138,22 +126,18 @@
     grad_all = jnp.einsum(
         "mbsd,mbsp->dp", final_norm.astype(jnp.float32), residue, precision=lax.Precision.HIGHEST
     ) / float(seq_total)
-    arrived = jnp.zeros(velocity_all.shape[:3] + (head_cols,), jnp.float32)
+    grad_rows = lax.psum_scatter(grad_all, "dp", scatter_dimension=0, tiled=True)
+    grad_rows = lax.psum(grad_rows, "ctx")
+    velocity_in = jnp.zeros(velocity_all.shape[:3] + (head_cols,), jnp.float32)
+    gradient_in = jnp.zeros((grad_rows.shape[0], head_cols), jnp.float32)
     for target_phase in range(last_phase):
-        piece = velocity_all[..., target_phase * head_cols : (target_phase + 1) * head_cols]
-        arrived = arrived + lax.ppermute(piece, "pipe", [(last_phase, target_phase)])
-    own_piece = velocity_all[..., last_phase * head_cols :]
-    velocity = jnp.where(is_last, own_piece, arrived)
-    dp_count = lax.axis_size("dp")
-    grad_rows = model_width // dp_count
-    kept = jnp.where(is_last, grad_all, 0.0)
-    blocks = (
-        kept.reshape(dp_count, grad_rows, phase_count, head_cols)
-        .transpose(0, 2, 1, 3)
-        .reshape(dp_count * phase_count, grad_rows, head_cols)
-    )
-    scattered = lax.psum_scatter(blocks, ("dp", "pipe"), scatter_dimension=0, tiled=True)
-    gradient = lax.psum(scattered.reshape(grad_rows, head_cols), "ctx")
+        cols = slice(target_phase * head_cols, (target_phase + 1) * head_cols)
+        pair = [(last_phase, target_phase)]
+        velocity_in = velocity_in + lax.ppermute(velocity_all[..., cols], "pipe", pair)
+        gradient_in = gradient_in + lax.ppermute(grad_rows[:, cols], "pipe", pair)
+    own_cols = slice(last_phase * head_cols, phase_count * head_cols)
+    velocity = jnp.where(is_last, velocity_all[..., own_cols], velocity_in)
+    gradient = jnp.where(is_last, grad_rows[:, own_cols], gradient_in)
     return (velocity, gradient)
 
 

time: 736 us -> 700 us (0.951)
  the two profiles are of different devices: /device:TPU:32 before, /device:TPU:1 now
where the time goes in v2:
time: 700 us; the launch traced here: 699 us
  waiting for transfers between devices  370 us (53%)
  blocking collectives  191 us (27%)
  starting transfers between devices  74.6 us (11%)
  matrix products  26.3 us (4%)
  other arithmetic  15.5 us (2%)
  between operations  14.6 us (2%)
  local copies, waits for them, and re-layouts  7.73 us (1%)
    all_gather x5, waiting for transfers between devices, on_device(): rows_all = lax.all_gather(normed, 'ctx', axis=0, tiled=True)  274 us
    all_to_all x4, blocking collectives, on_device(): lax.all_to_all(mixed_heads, 'ctx', split_axis=0, concat_axis=1, tiled=True)  79.6 us
    ppermute x4, starting transfers between devices, shifted(): lax.ppermute(value, axis, [(source, source + steps) for source in range(f...  62.6 us
    psum x1, blocking collectives, on_device(): grad_rows = lax.psum(grad_rows, 'ctx')  42.6 us
    unnamed x7, waiting for transfers between devices  40.9 us
    ppermute x4, waiting for transfers between devices, shifted(): lax.ppermute(value, axis, [(source, source + steps) for source in range(f...  30.7 us
    all_gather x1, blocking collectives, on_device(): head_key = lax.all_gather(key_cols, 'dp', axis=0, tiled=True)  23.5 us
    ppermute x3, waiting for transfers between devices, on_device(): gradient_in = gradient_in + lax.ppermute(grad_rows[:, cols], 'pipe', pair)  23.4 us
  transfers between devices with their start and end apart: 17, of which 11 were waited for; matrix products, arithmetic and copies ran while one was open for 0% of the time, Pallas kernels for 0%

profile of v2, /device:TPU:1, one launch (start us, length us, event | category | flops | bytes accessed | tf_op | source)
XLA Modules:
  0.0 699.2 jit_solution(15485403225246856169)
XLA Ops:
  7.2 0.7 multiply_bitcast_fusion
  7.9 0.7 broadcast_subtract_fusion
  8.6 0.8 broadcast_multiply_fusion
  9.4 1.3 fusion.85
  10.8 0.7 reduce.36
  11.6 0.8 fusion.91
  12.5 1.0 constant_dynamic-slice_fusion.6
  13.5 23.5 %all-gather.1 = bf16[1,1536,96]{2,1,0:T(8,128)(2,1)S(1)} all-gather(bf16[1,192,96]{2,1,0:T(8,128)(2,1)S(1)} %constant_dynamic-slice_fusion.5), channel_id=3, replica_groups=mesh['pipe'=4,'ctx'=16,'dp'=8] {'dp'}, dimensions={1}, use_global_device_ids=true | all-gather | bytes 331776 | tf_op jit(solution)/shard_map/all_gather | solution.py:61
  37.1 23.0 %all-gather = bf16[1,1536,96]{2,1,0:T(8,128)(2,1)S(1)} all-gather(bf16[1,192,96]{2,1,0:T(8,128)(2,1)S(1)} %constant_dynamic-slice_fusion.6), channel_id=2, replica_groups=mesh['pipe'=4,'ctx'=16,'dp'=8] {'dp'}, dimensions={1}, use_global_device_ids=true | all-gather | bytes 331776 | tf_op jit(solution)/shard_map/all_gather | solution.py:60
  60.1 25.4 %all-gather.12.cloned.1.call-done = bf16[1024,1536]{1,0:T(8,128)(2,1)} async-done(((bf16[64,1536]{1,0:T(8,128)(2,1)}), bf16[1024,1536]{1,0:T(8,128)(2,1)}) %all-gather.12.cloned.1.call-update) | async-done | bytes 3145744 | tf_op jit(solution)/shard_map/all_gather | solution.py:109
  85.7 19.4 %all_to_all.65 = bf16[16,64,96]{2,1,0:T(8,128)(2,1)S(1)} all-to-all(bf16[16,64,96]{2,1,0:T(8,128)(2,1)S(1)} %bitcast.100), channel_id=1, replica_groups=mesh['pipe'=4,'ctx'=16,'dp'=8] {'ctx'}, dimensions={0} | all-to-all | bytes 393216 | tf_op jit(solution)/shard_map/all_to_all | solution.py:111
  105.1 0.3 copy.35
  105.7 15.7 %collective-permute-start = (bf16[1,64,1536]{2,1,0:T(8,128)(2,1)S(1)}, bf16[1,64,1536]{2,1,0:T(8,128)(2,1)S(1)}, u32[]{:S(2)}, u32[]{:S(2)}) collective-permute-start(bf16[1,64,1536]{2,1,0:T(8,128)(2,1)S(1)} %fusion.88), channel_id=1, source_target_pairs={{0,128},{128,256},{256,384},{1,129},{129,257},{257,385},{2,130},{1... | collective-permute-start | bytes 589832 | tf_op jit(solution)/shard_map/ppermute | solution.py:15
  121.4 13.5 %collective-permute-done = bf16[1,64,1536]{2,1,0:T(8,128)(2,1)S(1)} collective-permute-done((bf16[1,64,1536]{2,1,0:T(8,128)(2,1)S(1)}, bf16[1,64,1536]{2,1,0:T(8,128)(2,1)S(1)}, u32[]{:S(2)}, u32[]{:S(2)}) %collective-permute-start) | collective-permute-done | bytes 196640 | tf_op jit(solution)/shard_map/ppermute | solution.py:15
  135.1 0.8 fusion.94
  136.0 61.1 %all-gather.14.cloned.1.call-done = bf16[1,1024,1536]{2,1,0:T(8,128)(2,1)} async-done(((bf16[1,64,1536]{2,1,0:T(8,128)(2,1)}), bf16[1,1024,1536]{2,1,0:T(8,128)(2,1)}) %all-gather.14.cloned.1.call-update) | async-done | bytes 3145744 | tf_op jit(solution)/shard_map/all_gather | solution.py:109
  197.1 15.1 %conditional.6 = (bf16[1024,96]{0,1:T(8,128)(2,1)S(1)}) conditional(s32[]{:T(128)} %convert_element_type.287, () %tuple.50, (s32[]{:T(128)}, s32[2,1,1024]{2,1,0:T(1,128)S(1)}, bf16[1024,1536]{1,0:T(8,128)(2,1)}, bf16[1536,96]{1,0:T(8,128)(2,1)S(1)}, bf16[1536,96]{1,0:T(8,128)(2,1)S(1)}, /*index=5*/s32[]{:T(128)}) %tuple.111), branch_computations={%region_6.7_spmd, %region_7.10_spmd} | conditional | flops 1023801344 | bytes 20361290 | solution.py:110
  197.1 3.0 convolution_convert_fusion.2
  200.1 5.6 fusion.17
  205.6 3.0 fusion.18
  208.7 3.6 fusion.26
  212.4 19.1 %all_to_all.66 = bf16[16,64,96]{2,1,0:T(8,128)(2,1)S(1)} all-to-all(bf16[16,64,96]{2,1,0:T(8,128)(2,1)S(1)} %bitcast.101), channel_id=1, replica_groups=mesh['pipe'=4,'ctx'=16,'dp'=8] {'ctx'}, dimensions={0} | all-to-all | bytes 393216 | tf_op jit(solution)/shard_map/all_to_all | solution.py:111
  231.6 0.3 copy.37
  232.2 1.9 collective-permute-start.1
  234.1 12.0 %collective-permute-done.1 = bf16[1,64,1536]{2,1,0:T(8,128)(2,1)S(1)} collective-permute-done((bf16[1,64,1536]{2,1,0:T(8,128)(2,1)S(1)}, bf16[1,64,1536]{2,1,0:T(8,128)(2,1)S(1)}, u32[]{:S(2)}, u32[]{:S(2)}) %collective-permute-start.1) | collective-permute-done | bytes 196640 | tf_op jit(solution)/shard_map/ppermute | solution.py:15
  246.3 0.8 fusion.98
  247.2 60.8 %all-gather.16.cloned.1.call-done = bf16[1,1024,1536]{2,1,0:T(8,128)(2,1)} async-done(((bf16[1,64,1536]{2,1,0:T(8,128)(2,1)}), bf16[1,1024,1536]{2,1,0:T(8,128)(2,1)}) %all-gather.16.cloned.1.call-update) | async-done | bytes 3145744 | tf_op jit(solution)/shard_map/all_gather | solution.py:109
  308.0 15.1 %conditional.7 = (bf16[1024,96]{0,1:T(8,128)(2,1)S(1)}) conditional(s32[]{:T(128)} %convert_element_type.294, () %tuple.52, (s32[]{:T(128)}, s32[2,1,1024]{2,1,0:T(1,128)S(1)}, bf16[1024,1536]{1,0:T(8,128)(2,1)}, bf16[1536,96]{1,0:T(8,128)(2,1)S(1)}, bf16[1536,96]{1,0:T(8,128)(2,1)S(1)}, /*index=5*/s32[]{:T(128)}) %tuple.112), branch_computations={%region_11.12_spmd, %region_12.15_spmd} | conditional | flops 1023801344 | bytes 20361290 | solution.py:110
  308.0 3.0 convolution_convert_fusion.4
  311.0 5.6 fusion.34
  316.6 3.0 fusion.35
  319.6 3.6 fusion.43
  323.4 21.9 %all_to_all.67 = bf16[16,64,96]{2,1,0:T(8,128)(2,1)S(1)} all-to-all(bf16[16,64,96]{2,1,0:T(8,128)(2,1)S(1)} %bitcast.102), channel_id=1, replica_groups=mesh['pipe'=4,'ctx'=16,'dp'=8] {'ctx'}, dimensions={0} | all-to-all | bytes 393216 | tf_op jit(solution)/shard_map/all_to_all | solution.py:111
  345.3 0.3 copy.39
  345.9 13.5 %collective-permute-start.2 = (bf16[1,64,1536]{2,1,0:T(8,128)(2,1)S(1)}, bf16[1,64,1536]{2,1,0:T(8,128)(2,1)S(1)}, u32[]{:S(2)}, u32[]{:S(2)}) collective-permute-start(bf16[1,64,1536]{2,1,0:T(8,128)(2,1)S(1)} %fusion.99), channel_id=1, source_target_pairs={{0,128},{128,256},{256,384},{1,129},{129,257},{257,385},{2,130},{1... | collective-permute-start | bytes 589832 | tf_op jit(solution)/shard_map/ppermute | solution.py:15
  359.4 2.6 collective-permute-done.2
  362.2 0.8 fusion.102
  363.1 63.5 %all-gather.18.cloned.1.call-done = bf16[1,1024,1536]{2,1,0:T(8,128)(2,1)} async-done(((bf16[1,64,1536]{2,1,0:T(8,128)(2,1)}), bf16[1,1024,1536]{2,1,0:T(8,128)(2,1)}) %all-gather.18.cloned.1.call-update) | async-done | bytes 3145744 | tf_op jit(solution)/shard_map/all_gather | solution.py:109
  426.8 19.2 %all_to_all.68 = bf16[16,64,96]{2,1,0:T(8,128)(2,1)S(1)} all-to-all(bf16[16,64,96]{2,1,0:T(8,128)(2,1)S(1)} %bitcast.103), channel_id=1, replica_groups=mesh['pipe'=4,'ctx'=16,'dp'=8] {'ctx'}, dimensions={0} | all-to-all | bytes 393216 | tf_op jit(solution)/shard_map/all_to_all | solution.py:111
  446.1 0.3 copy.41
  446.7 31.4 %collective-permute-start.3 = (bf16[1,64,1536]{2,1,0:T(8,128)(2,1)S(1)}, bf16[1,64,1536]{2,1,0:T(8,128)(2,1)S(1)}, u32[]{:S(2)}, u32[]{:S(2)}) collective-permute-start(bf16[1,64,1536]{2,1,0:T(8,128)(2,1)S(1)} %fusion.103), channel_id=1, source_target_pairs={{0,128},{128,256},{256,384},{1,129},{129,257},{257,385},{2,130},{1... | collective-permute-start | bytes 589832 | tf_op jit(solution)/shard_map/ppermute | solution.py:15
  478.0 2.6 collective-permute-done.3
  480.8 0.8 fusion.106
  481.6 63.6 %all-gather.20.cloned.1.call-done = bf16[1,1024,1536]{2,1,0:T(8,128)(2,1)} async-done(((bf16[1,64,1536]{2,1,0:T(8,128)(2,1)}), bf16[1,1024,1536]{2,1,0:T(8,128)(2,1)}) %all-gather.20.cloned.1.call-update) | async-done | bytes 3145744 | tf_op jit(solution)/shard_map/all_gather | solution.py:109
  545.2 0.2 conditional.9
  545.5 0.8 copy.42
  546.3 6.6 all-to-all-start.4
  553.2 21.8 %all_gather.31 = bf16[1536,64]{0,1:T(8,128)(2,1)S(1)} all-gather(bf16[1536,16]{0,1:T(8,128)(2,1)S(1)} %copy-done.4), channel_id=1, replica_groups=mesh['pipe'=4,'ctx'=16,'dp'=8] {'pipe'}, dimensions={1}, use_global_device_ids=true | all-gather | bytes 245760 | tf_op jit(solution)/shard_map/all_gather | solution.py:62
  575.1 0.3 copy.43
  575.8 0.4 convolution_bitcast_fusion.1
  576.2 0.4 fusion.86
  576.7 1.2 copy.47
  577.9 0.7 collective-permute-start.4
  578.5 1.3 collective-permute-start.5
  579.8 0.7 collective-permute-start.6
  580.5 40.8 %reduce-scatter.4.cloned.1.call-done = f32[192,64]{1,0:T(8,128)} async-done(((f32[1536,64]{1,0:T(8,128)}), f32[192,64]{1,0:T(8,128)}) %reduce-scatter.4.cloned.1.call-update) | async-done | bytes 49168
  621.3 1.0 copy.48
  622.3 42.6 %psum.7 = f32[192,64]{0,1:T(8,128)S(1)} all-reduce(f32[192,64]{0,1:T(8,128)S(1)} %copy.48), channel_id=1, replica_groups=mesh['pipe'=4,'ctx'=16,'dp'=8] {'ctx'}, use_global_device_ids=true, to_apply=%region_27.28 | all-reduce | flops 12288 | bytes 98304 | tf_op jit(solution)/shard_map/psum | solution.py:130
  665.0 0.7 collective-permute-start.7
  665.6 1.3 collective-permute-start.8
  667.0 0.7 collective-permute-start.9
  667.6 0.6 fusion.117
  668.3 23.4 %collective-permute-done.8 = f32[192,16]{0,1:T(8,128)S(1)} collective-permute-done((f32[192,16]{0,1:T(8,128)S(1)}, f32[192,16]{0,1:T(8,128)S(1)}, u32[]{:S(2)}, u32[]{:S(2)}) %collective-permute-start.8) | collective-permute-done | bytes 12320 | tf_op jit(solution)/shard_map/ppermute | solution.py:137
  691.7 0.6 slice_select_fusion.1
  (73 shorter events, 4.1 us)
Async XLA Ops:
  7.2 5.3 copy-start
  7.2 78.3 %all-gather.12.cloned.1.call-start = ((), (), s32[]{:S(2)}) async-start(), calls=%async_computation.6 | async-start | bytes 3342336 | tf_op jit(solution)/shard_map/all_gather | solution.py:109
  12.4 184.7 %all-gather.14.cloned.1.call-start = ((), (), s32[]{:S(2)}) async-start(), calls=%async_computation.7 | async-start | bytes 3342336 | tf_op jit(solution)/shard_map/all_gather | solution.py:109
  85.5 111.6 %copy-start.3 = (s32[2,1,1024]{2,1,0:T(1,128)S(1)}, s32[2,1,1024]{2,1,0:T(1,128)}, u32[]{:S(2)}) copy-start(s32[2,1,1024]{2,1,0:T(1,128)} %param.24) | copy-start | bytes 24580
  105.7 29.2 %collective-permute-start = (bf16[1,64,1536]{2,1,0:T(8,128)(2,1)S(1)}, bf16[1,64,1536]{2,1,0:T(8,128)(2,1)S(1)}, u32[]{:S(2)}, u32[]{:S(2)}) collective-permute-start(bf16[1,64,1536]{2,1,0:T(8,128)(2,1)S(1)} %fusion.88), channel_id=1, source_target_pairs={{0,128},{128,256},{256,384},{1,129},{129,257},{257,385},{2,130},{1... | collective-permute-start | bytes 589832 | tf_op jit(solution)/shard_map/ppermute | solution.py:15
  135.9 172.1 %all-gather.16.cloned.1.call-start = ((), (), s32[]{:S(2)}) async-start(), calls=%async_computation.8 | async-start | bytes 3342336 | tf_op jit(solution)/shard_map/all_gather | solution.py:109
  232.2 14.0 %collective-permute-start.1 = (bf16[1,64,1536]{2,1,0:T(8,128)(2,1)S(1)}, bf16[1,64,1536]{2,1,0:T(8,128)(2,1)S(1)}, u32[]{:S(2)}, u32[]{:S(2)}) collective-permute-start(bf16[1,64,1536]{2,1,0:T(8,128)(2,1)S(1)} %fusion.95), channel_id=1, source_target_pairs={{0,128},{128,256},{256,384},{1,129},{129,257},{257,385},{2,130},{1... | collective-permute-start | bytes 589832 | tf_op jit(solution)/shard_map/ppermute | solution.py:15
  247.2 179.5 %all-gather.18.cloned.1.call-start = ((), (), s32[]{:S(2)}) async-start(), calls=%async_computation.9 | async-start | bytes 3342336 | tf_op jit(solution)/shard_map/all_gather | solution.py:109
  345.9 16.1 %collective-permute-start.2 = (bf16[1,64,1536]{2,1,0:T(8,128)(2,1)S(1)}, bf16[1,64,1536]{2,1,0:T(8,128)(2,1)S(1)}, u32[]{:S(2)}, u32[]{:S(2)}) collective-permute-start(bf16[1,64,1536]{2,1,0:T(8,128)(2,1)S(1)} %fusion.99), channel_id=1, source_target_pairs={{0,128},{128,256},{256,384},{1,129},{129,257},{257,385},{2,130},{1... | collective-permute-start | bytes 589832 | tf_op jit(solution)/shard_map/ppermute | solution.py:15
  363.0 182.2 %all-gather.20.cloned.1.call-start = ((), (), s32[]{:S(2)}) async-start(), calls=%async_computation.10 | async-start | bytes 3342336 | tf_op jit(solution)/shard_map/all_gather | solution.py:109
  446.7 34.0 %collective-permute-start.3 = (bf16[1,64,1536]{2,1,0:T(8,128)(2,1)S(1)}, bf16[1,64,1536]{2,1,0:T(8,128)(2,1)S(1)}, u32[]{:S(2)}, u32[]{:S(2)}) collective-permute-start(bf16[1,64,1536]{2,1,0:T(8,128)(2,1)S(1)} %fusion.103), channel_id=1, source_target_pairs={{0,128},{128,256},{256,384},{1,129},{129,257},{257,385},{2,130},{1... | collective-permute-start | bytes 589832 | tf_op jit(solution)/shard_map/ppermute | solution.py:15
  545.2 7.7 %copy-start.1 = (f32[2,1,64,64]{3,2,1,0:T(8,128)S(1)}, f32[2,1,64,64]{3,2,1,0:T(8,128)}, u32[]{:S(2)}) copy-start(f32[2,1,64,64]{3,2,1,0:T(8,128)} %param.21) | copy-start | bytes 98308
  545.2 7.8 %copy-start.2 = (f32[2,1,64,64]{3,2,1,0:T(8,128)S(1)}, f32[2,1,64,64]{3,2,1,0:T(8,128)}, u32[]{:S(2)}) copy-start(f32[2,1,64,64]{3,2,1,0:T(8,128)} %param.22) | copy-start | bytes 98308
  545.2 7.9 %copy-start.4 = (bf16[1536,16]{0,1:T(8,128)(2,1)S(1)}, bf16[1536,16]{0,1:T(8,128)(2,1)}, u32[]{:S(2)}) copy-start(bf16[1536,16]{0,1:T(8,128)(2,1)} %param.31) | copy-start | bytes 147460
  545.5 30.3 %copy-start.5 = (f32[1536]{0:T(1024)S(1)}, f32[1536]{0:T(1024)}, u32[]{:S(2)}) copy-start(f32[1536]{0:T(1024)} %param.30) | copy-start | bytes 18436
  546.3 28.7 %all-to-all-start.4 = ((bf16[16,64,96]{2,1,0:T(8,128)(2,1)}), bf16[16,64,96]{2,1,0:T(8,128)(2,1)S(1)}, u32[]{:S(2)}, u32[]{:S(2)}) async-start(bf16[16,64,96]{2,1,0:T(8,128)(2,1)} %bitcast.23), calls=%async_computation.4 | async-start | bytes 524288 | tf_op jit(solution)/shard_map/all_to_all | solution.py:111
  552.9 68.4 %reduce-scatter.4.cloned.1.call-start = ((), (), s32[]{:S(2)}) async-start(), calls=%async_computation.11 | async-start | bytes 884736
  577.9 89.1 %collective-permute-start.4 = (f32[2,1,64,16]{2,3,0,1:T(8,128)S(1)}, f32[2,1,64,16]{2,3,0,1:T(8,128)S(1)}, u32[]{:S(2)}, u32[]{:S(2)}) collective-permute-start(f32[2,1,64,16]{2,3,0,1:T(8,128)S(1)} %get-tuple-element.251), channel_id=1, source_target_pairs={{384,0},{385,1},{386,2},{387,3},{388,4},{389,5},{390,6},{391,7},{3... | collective-permute-start | bytes 24584 | tf_op jit(solution)/shard_map/ppermute | solution.py:136
  578.5 89.1 %collective-permute-start.5 = (f32[2,1,64,16]{2,3,0,1:T(8,128)S(1)}, f32[2,1,64,16]{2,3,0,1:T(8,128)S(1)}, u32[]{:S(2)}, u32[]{:S(2)}) collective-permute-start(f32[2,1,64,16]{2,3,0,1:T(8,128)S(1)} %get-tuple-element.249), channel_id=1, source_target_pairs={{384,128},{385,129},{386,130},{387,131},{388,132},{389,133},{390,1... | collective-permute-start | bytes 24584 | tf_op jit(solution)/shard_map/ppermute | solution.py:136
  579.8 87.8 %collective-permute-start.6 = (f32[2,1,64,16]{2,3,0,1:T(8,128)S(1)}, f32[2,1,64,16]{2,3,0,1:T(8,128)S(1)}, u32[]{:S(2)}, u32[]{:S(2)}) collective-permute-start(f32[2,1,64,16]{2,3,0,1:T(8,128)S(1)} %get-tuple-element.250), channel_id=1, source_target_pairs={{384,256},{385,257},{386,258},{387,259},{388,260},{389,261},{390,2... | collective-permute-start | bytes 24584 | tf_op jit(solution)/shard_map/ppermute | solution.py:136
  665.0 3.3 collective-permute-start.7
  665.6 26.1 %collective-permute-start.8 = (f32[192,16]{0,1:T(8,128)S(1)}, f32[192,16]{0,1:T(8,128)S(1)}, u32[]{:S(2)}, u32[]{:S(2)}) collective-permute-start(f32[192,16]{0,1:T(8,128)S(1)} %get-tuple-element.246), channel_id=1, source_target_pairs={{384,128},{385,129},{386,130},{387,131},{388,132},{389,133},{390,1... | collective-permute-start | bytes 36872 | tf_op jit(solution)/shard_map/ppermute | solution.py:137
  667.0 24.8 %collective-permute-start.9 = (f32[192,16]{0,1:T(8,128)S(1)}, f32[192,16]{0,1:T(8,128)S(1)}, u32[]{:S(2)}, u32[]{:S(2)}) collective-permute-start(f32[192,16]{0,1:T(8,128)S(1)} %get-tuple-element.247), channel_id=1, source_target_pairs={{384,256},{385,257},{386,258},{387,259},{388,260},{389,261},{390,2... | collective-permute-start | bytes 36872 | tf_op jit(solution)/shard_map/ppermute | solution.py:137
Sparse Core Ops, SparseCore 0:
  12.5 72.9 all-gather.11
  136.1 60.9 all-gather.13
  247.3 60.7 all-gather.15
  363.2 63.4 all-gather.17
  481.8 63.4 all-gather.19
  578.0 43.3 reduce-scatter.3

commit v3 on v1

--- a/solution.py
+++ b/solution.py
@@ -57,13 +57,22 @@
         "mbsp,pd->mbsd", noisy_input, embed_weight, preferred_element_type=jnp.float32
     )
     embedded = (embedded + flow_time * time_vector).astype(jnp.bfloat16)
-    gathered = (
-        lax.all_gather(query_weight, "dp", axis=1, tiled=True),
-        lax.all_gather(key_weight, "dp", axis=1, tiled=True),
-    )
+    dp_count = lax.axis_size("dp")
+    column_start = lax.axis_index("ctx") * local_width
+
+    def gather_whole(weight):
+        piece = lax.dynamic_slice_in_dim(weight[0], column_start, local_width, 1)
+        pieces = lax.all_gather(piece, ("dp", "ctx"), axis=0, tiled=False)
+        rows = pieces.shape[1]
+        return (
+            pieces.reshape(dp_count, cycle_size, rows, local_width)
+            .transpose(0, 2, 1, 3)
+            .reshape(dp_count * rows, cycle_size * local_width)
+        )
+
+    full_query = gather_whole(query_weight)
+    full_key = gather_whole(key_weight)
     head_full = lax.all_gather(head_weight, "pipe", axis=1, tiled=True)
-    full_query = gathered[0][0]
-    full_key = gathered[1][0]
     section_gain = norm_gain[0]
 
     def attention(by_heads, frame_row):
@@ -138,22 +147,17 @@
     grad_all = jnp.einsum(
         "mbsd,mbsp->dp", final_norm.astype(jnp.float32), residue, precision=lax.Precision.HIGHEST
     ) / float(seq_total)
-    arrived = jnp.zeros(velocity_all.shape[:3] + (head_cols,), jnp.float32)
+    grad_rows = lax.psum_scatter(grad_all, "dp", scatter_dimension=0, tiled=True)
+    velocity_in = jnp.zeros(velocity_all.shape[:3] + (head_cols,), jnp.float32)
+    gradient_in = jnp.zeros((grad_rows.shape[0], head_cols), jnp.float32)
     for target_phase in range(last_phase):
-        piece = velocity_all[..., target_phase * head_cols : (target_phase + 1) * head_cols]
-        arrived = arrived + lax.ppermute(piece, "pipe", [(last_phase, target_phase)])
-    own_piece = velocity_all[..., last_phase * head_cols :]
-    velocity = jnp.where(is_last, own_piece, arrived)
-    dp_count = lax.axis_size("dp")
-    grad_rows = model_width // dp_count
-    kept = jnp.where(is_last, grad_all, 0.0)
-    blocks = (
-        kept.reshape(dp_count, grad_rows, phase_count, head_cols)
-        .transpose(0, 2, 1, 3)
-        .reshape(dp_count * phase_count, grad_rows, head_cols)
-    )
-    scattered = lax.psum_scatter(blocks, ("dp", "pipe"), scatter_dimension=0, tiled=True)
-    gradient = lax.psum(scattered.reshape(grad_rows, head_cols), "ctx")
+        cols = slice(target_phase * head_cols, (target_phase + 1) * head_cols)
+        pair = [(last_phase, target_phase)]
+        velocity_in = velocity_in + lax.ppermute(velocity_all[..., cols], "pipe", pair)
+        gradient_in = gradient_in + lax.ppermute(grad_rows[:, cols], "pipe", pair)
+    own_cols = slice(last_phase * head_cols, phase_count * head_cols)
+    velocity = jnp.where(is_last, velocity_all[..., own_cols], velocity_in)
+    gradient = lax.psum(jnp.where(is_last, grad_rows[:, own_cols], gradient_in), "ctx")
     return (velocity, gradient)
 
 

time: 736 us -> 1720 us (2.34)
  the two profiles are of different devices: /device:TPU:32 before, /device:TPU:1 now
where the time goes in v3:
time: 1720 us; the launch traced here: 1700 us
  waiting for transfers between devices  1280 us (74%)
  starting transfers between devices  156 us (9%)
  blocking collectives  153 us (9%)
  local copies, waits for them, and re-layouts  77 us (4%)
    all_gather x2, waiting for transfers between devices, gather_whole(): pieces = lax.all_gather(piece, ('dp', 'ctx'), axis=0, tiled=False)  1090 us
    all_to_all x5, waiting for transfers between devices, on_device(): lax.all_to_all(triple, 'ctx', split_axis=2, concat_axis=1, tiled=True)  122 us
    ppermute x4, starting transfers between devices, shifted(): lax.ppermute(value, axis, [(source, source + steps) for source in range(f...  117 us
    all_to_all x4, blocking collectives, on_device(): lax.all_to_all(mixed_heads, 'ctx', split_axis=0, concat_axis=1, tiled=True)  90.6 us
    psum x1, blocking collectives, on_device(): lax.psum(jnp.where(is_last, grad_rows[:, own_cols], gradient_in), 'ctx')  43.4 us
    unnamed x4, waiting for transfers between devices  41.2 us
  transfers between devices with their start and end apart: 19, of which 13 were waited for; matrix products, arithmetic and copies ran while one was open for 2% of the time, Pallas kernels for 0%

profile of v3, /device:TPU:1, one launch (start us, length us, event | category | flops | bytes accessed | tf_op | source)
XLA Modules:
  0.0 1702.6 jit_solution(15035644398884848655)
XLA Ops:
  7.2 1.0 copy-done
  9.0 1.6 constant_dynamic-slice_fusion.5
  13.5 1.3 fusion.88
  15.2 513.8 %all-gather.3.cloned.1.call-done = bf16[128,192,96]{2,1,0:T(8,128)(2,1)} async-done(((bf16[1,192,96]{2,1,0:T(8,128)(2,1)}), bf16[128,192,96]{2,1,0:T(8,128)(2,1)}) %all-gather.3.cloned.1.call-update) | async-done | bytes 4718608 | tf_op jit(solution)/shard_map/all_gather | solution.py:65
  529.0 9.4 copy.43
  538.4 11.2 reshape.559
  549.6 572.4 %all-gather.5.cloned.1.call-done = bf16[128,192,96]{2,1,0:T(8,128)(2,1)} async-done(((bf16[1,192,96]{2,1,0:T(8,128)(2,1)}), bf16[128,192,96]{2,1,0:T(8,128)(2,1)}) %all-gather.5.cloned.1.call-update) | async-done | bytes 4718608 | tf_op jit(solution)/shard_map/all_gather | solution.py:65
  1122.0 9.4 copy.44
  1131.5 11.2 reshape.561
  1142.9 1.0 copy.45
  1143.9 1.8 reshape.575
  1145.8 3.6 all-to-all-start
  1149.4 18.6 %all-to-all-done = bf16[16,2,9216]{2,1,0:T(2,128)(2,1)S(1)} async-done(((bf16[16,2,9216]{2,1,0:T(2,128)(2,1)}), bf16[16,2,9216]{2,1,0:T(2,128)(2,1)S(1)}, u32[]{:S(2)}, u32[]{:S(2)}) %all-to-all-start) | async-done | bytes 589856 | tf_op jit(solution)/shard_map/all_to_all | solution.py:123
  1168.9 1.0 copy.73
  1170.2 20.6 %all_to_all.145 = bf16[16,64,96]{2,1,0:T(8,128)(2,1)S(1)} all-to-all(bf16[16,64,96]{2,1,0:T(8,128)(2,1)S(1)} %bitcast.184), channel_id=1, replica_groups=mesh['pipe'=4,'ctx'=16,'dp'=8] {'ctx'}, dimensions={0} | all-to-all | bytes 393216 | tf_op jit(solution)/shard_map/all_to_all | solution.py:132
  1191.5 96.6 %collective-permute-start = (bf16[1,64,1536]{2,1,0:T(8,128)(2,1)S(1)}, bf16[1,64,1536]{2,1,0:T(8,128)(2,1)S(1)}, u32[]{:S(2)}, u32[]{:S(2)}) collective-permute-start(bf16[1,64,1536]{2,1,0:T(8,128)(2,1)S(1)} %fusion.109), channel_id=1, source_target_pairs={{0,128},{128,256},{256,384},{1,129},{129,257},{257,385},{2,130},{1... | collective-permute-start | bytes 589832 | tf_op jit(solution)/shard_map/ppermute | solution.py:15
  1288.1 6.5 collective-permute-done
  1294.8 4.8 conditional.12
  1294.8 3.4 fusion.16
  1299.6 1.0 copy.50
  1300.7 1.8 reshape.577
  1302.5 5.8 all-to-all-start.2
  1308.3 26.1 %all-to-all-done.2 = bf16[16,2,9216]{2,1,0:T(2,128)(2,1)S(1)} async-done(((bf16[16,2,9216]{2,1,0:T(2,128)(2,1)}), bf16[16,2,9216]{2,1,0:T(2,128)(2,1)S(1)}, u32[]{:S(2)}, u32[]{:S(2)}) %all-to-all-start.2) | async-done | bytes 589856 | tf_op jit(solution)/shard_map/all_to_all | solution.py:123
  1335.4 1.0 copy.74
  1336.4 4.0 conditional.13
  1337.7 1.5 fusion.21
  1339.2 1.2 fusion.28
  1340.6 25.8 %all_to_all.146 = bf16[16,64,96]{2,1,0:T(8,128)(2,1)S(1)} all-to-all(bf16[16,64,96]{2,1,0:T(8,128)(2,1)S(1)} %bitcast.185), channel_id=1, replica_groups=mesh['pipe'=4,'ctx'=16,'dp'=8] {'ctx'}, dimensions={0} | all-to-all | bytes 393216 | tf_op jit(solution)/shard_map/all_to_all | solution.py:132
  1367.1 1.9 collective-permute-start.1
  1369.0 5.7 collective-permute-done.1
  1375.0 4.8 conditional.14
  1375.0 3.4 fusion.34
  1379.8 1.0 copy.55
  1380.9 1.8 reshape.579
  1382.7 7.2 all-to-all-start.4
  1389.9 27.0 %all-to-all-done.4 = bf16[16,2,9216]{2,1,0:T(2,128)(2,1)S(1)} async-done(((bf16[16,2,9216]{2,1,0:T(2,128)(2,1)}), bf16[16,2,9216]{2,1,0:T(2,128)(2,1)S(1)}, u32[]{:S(2)}, u32[]{:S(2)}) %all-to-all-start.4) | async-done | bytes 589856 | tf_op jit(solution)/shard_map/all_to_all | solution.py:123
  1417.8 1.0 copy.75
  1418.8 3.8 conditional.15
  1419.9 1.5 fusion.39
  1421.4 1.2 fusion.46
  1422.8 21.4 %all_to_all.147 = bf16[16,64,96]{2,1,0:T(8,128)(2,1)S(1)} all-to-all(bf16[16,64,96]{2,1,0:T(8,128)(2,1)S(1)} %bitcast.186), channel_id=1, replica_groups=mesh['pipe'=4,'ctx'=16,'dp'=8] {'ctx'}, dimensions={0} | all-to-all | bytes 393216 | tf_op jit(solution)/shard_map/all_to_all | solution.py:132
  1444.9 4.0 collective-permute-start.2
  1449.0 2.6 collective-permute-done.2
  1452.3 1.0 copy.60
  1453.4 1.8 reshape.581
  1455.2 5.8 all-to-all-start.6
  1461.0 27.5 %all-to-all-done.6 = bf16[16,2,9216]{2,1,0:T(2,128)(2,1)S(1)} async-done(((bf16[16,2,9216]{2,1,0:T(2,128)(2,1)}), bf16[16,2,9216]{2,1,0:T(2,128)(2,1)S(1)}, u32[]{:S(2)}, u32[]{:S(2)}) %all-to-all-start.6) | async-done | bytes 589856 | tf_op jit(solution)/shard_map/all_to_all | solution.py:123
  1489.5 1.0 copy.76
  1490.7 22.7 %all_to_all.148 = bf16[16,64,96]{2,1,0:T(8,128)(2,1)S(1)} all-to-all(bf16[16,64,96]{2,1,0:T(8,128)(2,1)S(1)} %bitcast.187), channel_id=1, replica_groups=mesh['pipe'=4,'ctx'=16,'dp'=8] {'ctx'}, dimensions={0} | all-to-all | bytes 393216 | tf_op jit(solution)/shard_map/all_to_all | solution.py:132
  1514.0 14.0 collective-permute-start.3
  1528.1 2.6 collective-permute-done.3
  1531.1 1.0 copy.65
  1532.1 1.8 reshape.583
  1533.9 4.7 all-to-all-start.8
  1538.6 23.0 %all-to-all-done.8 = bf16[16,2,9216]{2,1,0:T(2,128)(2,1)S(1)} async-done(((bf16[16,2,9216]{2,1,0:T(2,128)(2,1)}), bf16[16,2,9216]{2,1,0:T(2,128)(2,1)S(1)}, u32[]{:S(2)}, u32[]{:S(2)}) %all-to-all-start.8) | async-done | bytes 589856 | tf_op jit(solution)/shard_map/all_to_all | solution.py:123
  1564.6 6.9 all-to-all-start.9
  1571.8 19.2 %all_gather.13 = bf16[1536,64]{0,1:T(8,128)(2,1)S(1)} all-gather(bf16[1536,16]{0,1:T(8,128)(2,1)S(1)} %copy-done.10), channel_id=1, replica_groups=mesh['pipe'=4,'ctx'=16,'dp'=8] {'pipe'}, dimensions={1}, use_global_device_ids=true | all-gather | bytes 245760 | tf_op jit(solution)/shard_map/all_gather | solution.py:75
  1592.7 1.2 copy.78
  1593.9 1.3 collective-permute-start.5
  1596.5 41.1 %reduce-scatter.4.cloned.1.call-done = f32[192,64]{1,0:T(8,128)} async-done(((f32[1536,64]{1,0:T(8,128)}), f32[192,64]{1,0:T(8,128)}) %reduce-scatter.4.cloned.1.call-update) | async-done | bytes 49168
  1637.7 1.2 fusion.130
  1640.5 1.3 collective-permute-start.8
  1642.5 10.0 collective-permute-done.8
  1652.5 43.4 %psum.7 = f32[192,16]{0,1:T(8,128)} all-reduce(f32[192,16]{0,1:T(8,128)S(1)} %add_select_fusion), channel_id=1, replica_groups=mesh['pipe'=4,'ctx'=16,'dp'=8] {'ctx'}, use_global_device_ids=true, to_apply=%region_37.38 | all-reduce | flops 3072 | bytes 24576 | tf_op jit(solution)/shard_map/psum | solution.py:160
  (122 shorter events, 26.2 us)
Async XLA Ops:
  7.2 1.1 copy-start
  7.2 521.8 %all-gather.3.cloned.1.call-start = ((), (), s32[]{:S(2)}) async-start(), calls=%async_computation.11 | async-start | bytes 6340608 | tf_op jit(solution)/shard_map/all_gather | solution.py:65
  9.0 1113.0 %all-gather.5.cloned.1.call-start = ((), (), s32[]{:S(2)}) async-start(), calls=%async_computation.12 | async-start | bytes 6340608 | tf_op jit(solution)/shard_map/all_gather | solution.py:65
  1143.9 26.0 %copy-start.9 = (s32[2,1,1024]{2,1,0:T(1,128)S(1)}, s32[2,1,1024]{2,1,0:T(1,128)}, u32[]{:S(2)}) copy-start(s32[2,1,1024]{2,1,0:T(1,128)} %param.34) | copy-start | bytes 24580
  1145.8 22.2 %all-to-all-start = ((bf16[16,2,9216]{2,1,0:T(2,128)(2,1)}), bf16[16,2,9216]{2,1,0:T(2,128)(2,1)S(1)}, u32[]{:S(2)}, u32[]{:S(2)}) async-start(bf16[16,2,9216]{2,1,0:T(2,128)(2,1)} %reshape.575), calls=%async_computation | async-start | bytes 1179648 | tf_op jit(solution)/shard_map/all_to_all | solution.py:123
  1191.5 103.0 %collective-permute-start = (bf16[1,64,1536]{2,1,0:T(8,128)(2,1)S(1)}, bf16[1,64,1536]{2,1,0:T(8,128)(2,1)S(1)}, u32[]{:S(2)}, u32[]{:S(2)}) collective-permute-start(bf16[1,64,1536]{2,1,0:T(8,128)(2,1)S(1)} %fusion.109), channel_id=1, source_target_pairs={{0,128},{128,256},{256,384},{1,129},{129,257},{257,385},{2,130},{1... | collective-permute-start | bytes 589832 | tf_op jit(solution)/shard_map/ppermute | solution.py:15
  1294.8 3.8 copy-start.3
  1302.5 31.9 %all-to-all-start.2 = ((bf16[16,2,9216]{2,1,0:T(2,128)(2,1)}), bf16[16,2,9216]{2,1,0:T(2,128)(2,1)S(1)}, u32[]{:S(2)}, u32[]{:S(2)}) async-start(bf16[16,2,9216]{2,1,0:T(2,128)(2,1)} %reshape.577), calls=%async_computation.2 | async-start | bytes 1179648 | tf_op jit(solution)/shard_map/all_to_all | solution.py:123
  1367.1 7.6 collective-permute-start.1
  1375.0 3.8 copy-start.4
  1382.7 34.2 %all-to-all-start.4 = ((bf16[16,2,9216]{2,1,0:T(2,128)(2,1)}), bf16[16,2,9216]{2,1,0:T(2,128)(2,1)S(1)}, u32[]{:S(2)}, u32[]{:S(2)}) async-start(bf16[16,2,9216]{2,1,0:T(2,128)(2,1)} %reshape.579), calls=%async_computation.4 | async-start | bytes 1179648 | tf_op jit(solution)/shard_map/all_to_all | solution.py:123
  1444.9 6.6 collective-permute-start.2
  1455.2 33.3 %all-to-all-start.6 = ((bf16[16,2,9216]{2,1,0:T(2,128)(2,1)}), bf16[16,2,9216]{2,1,0:T(2,128)(2,1)S(1)}, u32[]{:S(2)}, u32[]{:S(2)}) async-start(bf16[16,2,9216]{2,1,0:T(2,128)(2,1)} %reshape.581), calls=%async_computation.6 | async-start | bytes 1179648 | tf_op jit(solution)/shard_map/all_to_all | solution.py:123
  1514.0 16.6 collective-permute-start.3
  1533.9 27.6 %all-to-all-start.8 = ((bf16[16,2,9216]{2,1,0:T(2,128)(2,1)}), bf16[16,2,9216]{2,1,0:T(2,128)(2,1)S(1)}, u32[]{:S(2)}, u32[]{:S(2)}) async-start(bf16[16,2,9216]{2,1,0:T(2,128)(2,1)} %reshape.583), calls=%async_computation.8 | async-start | bytes 1179648 | tf_op jit(solution)/shard_map/all_to_all | solution.py:123
  1563.5 8.1 copy-start.7
  1563.5 8.2 copy-start.8
  1563.5 8.3 copy-start.10
  1563.7 28.1 %copy-start.11 = (f32[1536]{0:T(1024)S(1)}, f32[1536]{0:T(1024)}, u32[]{:S(2)}) copy-start(f32[1536]{0:T(1024)} %param.40) | copy-start | bytes 18436
  1564.6 26.4 %all-to-all-start.9 = ((bf16[16,64,96]{2,1,0:T(8,128)(2,1)}), bf16[16,64,96]{2,1,0:T(8,128)(2,1)S(1)}, u32[]{:S(2)}, u32[]{:S(2)}) async-start(bf16[16,64,96]{2,1,0:T(8,128)(2,1)} %bitcast.60), calls=%async_computation.9 | async-start | bytes 524288 | tf_op jit(solution)/shard_map/all_to_all | solution.py:132
  1571.5 66.2 %reduce-scatter.4.cloned.1.call-start = ((), (), s32[]{:S(2)}) async-start(), calls=%async_computation.13 | async-start | bytes 884736
  1591.1 104.8 %copy-start.1 = (bf16[1,192,1536]{2,1,0:T(8,128)(2,1)S(1)}, bf16[1,192,1536]{2,1,0:T(8,128)(2,1)}, u32[]{:S(2)}) copy-start(bf16[1,192,1536]{2,1,0:T(8,128)(2,1)} %param.37) | copy-start | bytes 1769476
  1593.9 46.6 %collective-permute-start.5 = (f32[2,1,64,16]{2,3,0,1:T(8,128)S(1)}, f32[2,1,64,16]{2,3,0,1:T(8,128)S(1)}, u32[]{:S(2)}, u32[]{:S(2)}) collective-permute-start(f32[2,1,64,16]{2,3,0,1:T(8,128)S(1)} %get-tuple-element.296), channel_id=1, source_target_pairs={{384,128},{385,129},{386,130},{387,131},{388,132},{389,133},{390,1... | collective-permute-start | bytes 24584 | tf_op jit(solution)/shard_map/ppermute | solution.py:156
  1595.2 46.6 %collective-permute-start.6 = (f32[2,1,64,16]{2,3,0,1:T(8,128)S(1)}, f32[2,1,64,16]{2,3,0,1:T(8,128)S(1)}, u32[]{:S(2)}, u32[]{:S(2)}) collective-permute-start(f32[2,1,64,16]{2,3,0,1:T(8,128)S(1)} %get-tuple-element.297), channel_id=1, source_target_pairs={{384,256},{385,257},{386,258},{387,259},{388,260},{389,261},{390,2... | collective-permute-start | bytes 24584 | tf_op jit(solution)/shard_map/ppermute | solution.py:156
  1595.9 45.9 %collective-permute-start.4 = (f32[2,1,64,16]{2,3,0,1:T(8,128)S(1)}, f32[2,1,64,16]{2,3,0,1:T(8,128)S(1)}, u32[]{:S(2)}, u32[]{:S(2)}) collective-permute-start(f32[2,1,64,16]{2,3,0,1:T(8,128)S(1)} %get-tuple-element.298), channel_id=1, source_target_pairs={{384,0},{385,1},{386,2},{387,3},{388,4},{389,5},{390,6},{391,7},{3... | collective-permute-start | bytes 24584 | tf_op jit(solution)/shard_map/ppermute | solution.py:156
  1639.1 3.3 collective-permute-start.9
  1639.8 2.7 collective-permute-start.7
  1640.5 12.0 collective-permute-start.8
Sparse Core Ops, SparseCore 0:
  10.1 518.8 all-gather.2
  531.0 590.9 all-gather.4
  1594.0 43.6 reduce-scatter.3

commit v4 on v3

--- a/solution.py
+++ b/solution.py
@@ -13,11 +13,6 @@
     count = lax.axis_size(axis)
     first, last = (max(0, -steps), min(count, count - steps))
     return lax.ppermute(value, axis, [(source, source + steps) for source in range(first, last)])
-
-
-def broadcast(value, axis, source):
-    kept = jnp.where(lax.axis_index(axis) == source, value, 0).astype(value.dtype)
-    return lax.psum(kept, axis)
 
 
 def rms_scale(values, gain_row):
@@ -57,21 +52,16 @@
         "mbsp,pd->mbsd", noisy_input, embed_weight, preferred_element_type=jnp.float32
     )
     embedded = (embedded + flow_time * time_vector).astype(jnp.bfloat16)
+    dp_index = lax.axis_index("dp")
     dp_count = lax.axis_size("dp")
-    column_start = lax.axis_index("ctx") * local_width
-
-    def gather_whole(weight):
-        piece = lax.dynamic_slice_in_dim(weight[0], column_start, local_width, 1)
-        pieces = lax.all_gather(piece, ("dp", "ctx"), axis=0, tiled=False)
-        rows = pieces.shape[1]
-        return (
-            pieces.reshape(dp_count, cycle_size, rows, local_width)
-            .transpose(0, 2, 1, 3)
-            .reshape(dp_count * rows, cycle_size * local_width)
-        )
-
-    full_query = gather_whole(query_weight)
-    full_key = gather_whole(key_weight)
+    full_query = lax.all_gather(query_weight[0], "dp", axis=0, tiled=True)
+    key_blocks = [key_weight[0]]
+    for step in range(1, dp_count):
+        pairs = [(source, (source + step) % dp_count) for source in range(dp_count)]
+        key_blocks.append(lax.ppermute(key_weight[0], "dp", pairs))
+    by_step = jnp.stack(key_blocks, axis=0)
+    source_step = (dp_index - jnp.arange(dp_count, dtype=jnp.int32)) % dp_count
+    full_key = jnp.take(by_step, source_step, axis=0).reshape(model_width, model_width)
     head_full = lax.all_gather(head_weight, "pipe", axis=1, tiled=True)
     section_gain = norm_gain[0]
 
@@ -148,6 +138,7 @@
         "mbsd,mbsp->dp", final_norm.astype(jnp.float32), residue, precision=lax.Precision.HIGHEST
     ) / float(seq_total)
     grad_rows = lax.psum_scatter(grad_all, "dp", scatter_dimension=0, tiled=True)
+    grad_rows = lax.psum(grad_rows, "ctx")
     velocity_in = jnp.zeros(velocity_all.shape[:3] + (head_cols,), jnp.float32)
     gradient_in = jnp.zeros((grad_rows.shape[0], head_cols), jnp.float32)
     for target_phase in range(last_phase):
@@ -157,7 +148,7 @@
         gradient_in = gradient_in + lax.ppermute(grad_rows[:, cols], "pipe", pair)
     own_cols = slice(last_phase * head_cols, phase_count * head_cols)
     velocity = jnp.where(is_last, velocity_all[..., own_cols], velocity_in)
-    gradient = lax.psum(jnp.where(is_last, grad_rows[:, own_cols], gradient_in), "ctx")
+    gradient = jnp.where(is_last, grad_rows[:, own_cols], gradient_in)
     return (velocity, gradient)
 
 

time: 1720 us -> 638 us (0.37)
  waiting for transfers between devices: 1280 us -> 273 us
  starting transfers between devices: 156 us -> 108 us
  local copies, waits for them, and re-layouts: 77 us -> 47.7 us
    all_gather x2 -> x1, waiting for transfers between devices: 1090 us -> 6.14 us  [on_device(): full_query = lax.all_gather(query_weight[0], 'dp', axis=0, tiled=True)]
    ppermute x4, starting transfers between devices: 117 us -> 33.9 us  [shifted(): lax.ppermute(value, axis, [(source, source + steps) for source in range(f...]
    ppermute x0 -> x7, waiting for transfers between devices: none -> 60.5 us  [on_device(): key_blocks.append(lax.ppermute(key_weight[0], 'dp', pairs))]
    ppermute x0 -> x7, starting transfers between devices: none -> 22.9 us  [on_device(): key_blocks.append(lax.ppermute(key_weight[0], 'dp', pairs))]
    reshape x2 -> x0, local copies, waits for them, and re-layouts: 22.4 us -> none  [gather_whole(): return pieces.reshape(dp_count, cycle_size, rows, local_width).transpose(...]
    transpose x2 -> x0, local copies, waits for them, and re-layouts: 18.9 us -> none  [gather_whole(): return pieces.reshape(dp_count, cycle_size, rows, local_width).transpose(...]
    unnamed x4 -> x3, waiting for transfers between devices: 41.2 us -> 45 us
  transfers between devices with their start and end apart: 19 -> 25, of which waited for: 13 -> 16; matrix products, arithmetic and copies ran while one was open for 2% -> 4% of each run, Pallas kernels for 0% -> 0%
where the time goes in v4:
time: 638 us; the launch traced here: 628 us
  waiting for transfers between devices  273 us (43%)
  blocking collectives  154 us (24%)
  starting transfers between devices  108 us (17%)
  local copies, waits for them, and re-layouts  47.7 us (7%)
  between operations  15.1 us (2%)
  matrix products  14.6 us (2%)
  other arithmetic  14.5 us (2%)
    all_to_all x5, waiting for transfers between devices, on_device(): lax.all_to_all(triple, 'ctx', split_axis=2, concat_axis=1, tiled=True)  127 us
    all_to_all x4, blocking collectives, on_device(): lax.all_to_all(mixed_heads, 'ctx', split_axis=0, concat_axis=1, tiled=True)  91.9 us
    ppermute x7, waiting for transfers between devices, on_device(): key_blocks.append(lax.ppermute(key_weight[0], 'dp', pairs))  60.5 us
    unnamed x3, waiting for transfers between devices  45 us
    psum x1, blocking collectives, on_device(): grad_rows = lax.psum(grad_rows, 'ctx')  42.6 us
    all_to_all x5, starting transfers between devices, on_device(): lax.all_to_all(triple, 'ctx', split_axis=2, concat_axis=1, tiled=True)  39.3 us
    ppermute x4, starting transfers between devices, shifted(): lax.ppermute(value, axis, [(source, source + steps) for source in range(f...  33.9 us
    unnamed x37, local copies, waits for them, and re-layouts  25.5 us
  transfers between devices with their start and end apart: 25, of which 16 were waited for; matrix products, arithmetic and copies ran while one was open for 4% of the time, Pallas kernels for 0%

profile of v4, /device:TPU:1, one launch (start us, length us, event | category | flops | bytes accessed | tf_op | source)
XLA Modules:
  0.0 628.5 jit_solution(4667838016200467648)
XLA Ops:
  7.9 4.0 collective-permute-start
  11.9 4.4 collective-permute-start.1
  16.3 4.1 collective-permute-start.2
  20.3 2.1 collective-permute-start.3
  22.4 3.2 collective-permute-start.4
  28.5 1.2 fusion.88
  29.8 1.9 constant_dynamic-update-slice_fusion
  32.2 3.3 collective-permute-start.5
  35.6 1.9 bitcast_dynamic-update-slice_fusion.6
  37.5 12.0 %collective-permute-done.1 = bf16[192,1536]{1,0:T(8,128)(2,1)} collective-permute-done((bf16[192,1536]{1,0:T(8,128)(2,1)}, bf16[192,1536]{1,0:T(8,128)(2,1)}, u32[]{:S(2)}, u32[]{:S(2)}) %collective-permute-start.1) | collective-permute-done | bytes 589856 | tf_op jit(solution)/shard_map/ppermute | solution.py:61
  49.5 1.9 collective-permute-start.6
  51.4 1.9 bitcast_dynamic-update-slice_fusion.5
  54.2 29.7 %collective-permute-done.3 = bf16[192,1536]{1,0:T(8,128)(2,1)S(1)} collective-permute-done((bf16[192,1536]{1,0:T(8,128)(2,1)}, bf16[192,1536]{1,0:T(8,128)(2,1)S(1)}, u32[]{:S(2)}, u32[]{:S(2)}) %collective-permute-start.3) | collective-permute-done | bytes 589856 | tf_op jit(solution)/shard_map/ppermute | solution.py:61
  85.6 10.5 %collective-permute-done.5 = bf16[192,1536]{1,0:T(8,128)(2,1)S(1)} collective-permute-done((bf16[192,1536]{1,0:T(8,128)(2,1)}, bf16[192,1536]{1,0:T(8,128)(2,1)S(1)}, u32[]{:S(2)}, u32[]{:S(2)}) %collective-permute-start.5) | collective-permute-done | bytes 589856 | tf_op jit(solution)/shard_map/ppermute | solution.py:61
  97.0 8.4 %collective-permute-done.6 = bf16[192,1536]{1,0:T(8,128)(2,1)S(1)} collective-permute-done((bf16[192,1536]{1,0:T(8,128)(2,1)S(1)}, bf16[192,1536]{1,0:T(8,128)(2,1)S(1)}, u32[]{:S(2)}, u32[]{:S(2)}) %collective-permute-start.6) | collective-permute-done | bytes 589856 | tf_op jit(solution)/shard_map/ppermute | solution.py:61
  106.2 5.5 gather_fusion
  111.7 5.1 bitcast_select_fusion
  116.7 6.1 all-gather.3.cloned.1.call-done
  122.9 1.0 copy.39
  124.0 1.8 reshape.621
  125.8 15.6 %all-to-all-start = ((bf16[16,2,9216]{2,1,0:T(2,128)(2,1)}), bf16[16,2,9216]{2,1,0:T(2,128)(2,1)S(1)}, u32[]{:S(2)}, u32[]{:S(2)}) async-start(bf16[16,2,9216]{2,1,0:T(2,128)(2,1)} %reshape.621), calls=%async_computation | async-start | bytes 1179648 | tf_op jit(solution)/shard_map/all_to_all | solution.py:113
  141.5 22.1 %all-to-all-done = bf16[16,2,9216]{2,1,0:T(2,128)(2,1)S(1)} async-done(((bf16[16,2,9216]{2,1,0:T(2,128)(2,1)}), bf16[16,2,9216]{2,1,0:T(2,128)(2,1)S(1)}, u32[]{:S(2)}, u32[]{:S(2)}) %all-to-all-start) | async-done | bytes 589856 | tf_op jit(solution)/shard_map/all_to_all | solution.py:113
  165.7 25.5 %all_to_all.145 = bf16[16,64,96]{2,1,0:T(8,128)(2,1)S(1)} all-to-all(bf16[16,64,96]{2,1,0:T(8,128)(2,1)S(1)} %bitcast.197), channel_id=1, replica_groups=mesh['pipe'=4,'ctx'=16,'dp'=8] {'ctx'}, dimensions={0} | all-to-all | bytes 393216 | tf_op jit(solution)/shard_map/all_to_all | solution.py:122
  191.9 13.9 %collective-permute-start.7 = (bf16[1,64,1536]{2,1,0:T(8,128)(2,1)S(1)}, bf16[1,64,1536]{2,1,0:T(8,128)(2,1)S(1)}, u32[]{:S(2)}, u32[]{:S(2)}) collective-permute-start(bf16[1,64,1536]{2,1,0:T(8,128)(2,1)S(1)} %fusion.109), channel_id=1, source_target_pairs={{0,128},{128,256},{256,384},{1,129},{129,257},{257,385},{2,130},{1... | collective-permute-start | bytes 589832 | tf_op jit(solution)/shard_map/ppermute | solution.py:15
  205.8 2.6 collective-permute-done.7
  208.7 5.3 conditional.12
  208.8 3.4 fusion.16
  215.0 1.8 reshape.623
  216.9 5.6 all-to-all-start.2
  222.5 27.1 %all-to-all-done.2 = bf16[16,2,9216]{2,1,0:T(2,128)(2,1)S(1)} async-done(((bf16[16,2,9216]{2,1,0:T(2,128)(2,1)}), bf16[16,2,9216]{2,1,0:T(2,128)(2,1)S(1)}, u32[]{:S(2)}, u32[]{:S(2)}) %all-to-all-start.2) | async-done | bytes 589856 | tf_op jit(solution)/shard_map/all_to_all | solution.py:113
  251.5 3.8 conditional.13
  252.6 1.5 fusion.21
  254.1 1.2 fusion.28
  255.5 22.3 %all_to_all.146 = bf16[16,64,96]{2,1,0:T(8,128)(2,1)S(1)} all-to-all(bf16[16,64,96]{2,1,0:T(8,128)(2,1)S(1)} %bitcast.198), channel_id=1, replica_groups=mesh['pipe'=4,'ctx'=16,'dp'=8] {'ctx'}, dimensions={0} | all-to-all | bytes 393216 | tf_op jit(solution)/shard_map/all_to_all | solution.py:122
  278.4 1.9 collective-permute-start.8
  280.4 3.8 collective-permute-done.8
  284.5 4.8 conditional.14
  284.5 3.4 fusion.34
  290.3 1.8 reshape.625
  292.2 7.6 %all-to-all-start.4 = ((bf16[16,2,9216]{2,1,0:T(2,128)(2,1)}), bf16[16,2,9216]{2,1,0:T(2,128)(2,1)S(1)}, u32[]{:S(2)}, u32[]{:S(2)}) async-start(bf16[16,2,9216]{2,1,0:T(2,128)(2,1)} %reshape.625), calls=%async_computation.4 | async-start | bytes 1179648 | tf_op jit(solution)/shard_map/all_to_all | solution.py:113
  299.7 27.0 %all-to-all-done.4 = bf16[16,2,9216]{2,1,0:T(2,128)(2,1)S(1)} async-done(((bf16[16,2,9216]{2,1,0:T(2,128)(2,1)}), bf16[16,2,9216]{2,1,0:T(2,128)(2,1)S(1)}, u32[]{:S(2)}, u32[]{:S(2)}) %all-to-all-start.4) | async-done | bytes 589856 | tf_op jit(solution)/shard_map/all_to_all | solution.py:113
  328.6 4.0 conditional.15
  329.9 1.5 fusion.39
  331.4 1.2 fusion.46
  332.8 21.4 %all_to_all.147 = bf16[16,64,96]{2,1,0:T(8,128)(2,1)S(1)} all-to-all(bf16[16,64,96]{2,1,0:T(8,128)(2,1)S(1)} %bitcast.199), channel_id=1, replica_groups=mesh['pipe'=4,'ctx'=16,'dp'=8] {'ctx'}, dimensions={0} | all-to-all | bytes 393216 | tf_op jit(solution)/shard_map/all_to_all | solution.py:122
  354.9 4.0 collective-permute-start.9
  358.9 2.6 collective-permute-done.9
  362.9 1.8 reshape.627
  364.8 5.8 all-to-all-start.6
  370.6 27.5 %all-to-all-done.6 = bf16[16,2,9216]{2,1,0:T(2,128)(2,1)S(1)} async-done(((bf16[16,2,9216]{2,1,0:T(2,128)(2,1)}), bf16[16,2,9216]{2,1,0:T(2,128)(2,1)S(1)}, u32[]{:S(2)}, u32[]{:S(2)}) %all-to-all-start.6) | async-done | bytes 589856 | tf_op jit(solution)/shard_map/all_to_all | solution.py:113
  400.2 22.7 %all_to_all.148 = bf16[16,64,96]{2,1,0:T(8,128)(2,1)S(1)} all-to-all(bf16[16,64,96]{2,1,0:T(8,128)(2,1)S(1)} %bitcast.200), channel_id=1, replica_groups=mesh['pipe'=4,'ctx'=16,'dp'=8] {'ctx'}, dimensions={0} | all-to-all | bytes 393216 | tf_op jit(solution)/shard_map/all_to_all | solution.py:122
  423.6 14.1 %collective-permute-start.10 = (bf16[1,64,1536]{2,1,0:T(8,128)(2,1)S(1)}, bf16[1,64,1536]{2,1,0:T(8,128)(2,1)S(1)}, u32[]{:S(2)}, u32[]{:S(2)}) collective-permute-start(bf16[1,64,1536]{2,1,0:T(8,128)(2,1)S(1)} %fusion.101), channel_id=1, source_target_pairs={{0,128},{128,256},{256,384},{1,129},{129,257},{257,385},{2,130},{1... | collective-permute-start | bytes 589832 | tf_op jit(solution)/shard_map/ppermute | solution.py:15
  437.7 2.6 collective-permute-done.10
  441.9 1.8 reshape.629
  443.7 4.7 all-to-all-start.8
  448.4 23.0 %all-to-all-done.8 = bf16[16,2,9216]{2,1,0:T(2,128)(2,1)S(1)} async-done(((bf16[16,2,9216]{2,1,0:T(2,128)(2,1)}), bf16[16,2,9216]{2,1,0:T(2,128)(2,1)S(1)}, u32[]{:S(2)}, u32[]{:S(2)}) %all-to-all-start.8) | async-done | bytes 589856 | tf_op jit(solution)/shard_map/all_to_all | solution.py:113
  474.2 6.9 %all-to-all-start.9 = ((bf16[16,64,96]{2,1,0:T(8,128)(2,1)}), bf16[16,64,96]{2,1,0:T(8,128)(2,1)S(1)}, u32[]{:S(2)}, u32[]{:S(2)}) async-start(bf16[16,64,96]{2,1,0:T(8,128)(2,1)} %bitcast.67), calls=%async_computation.9 | async-start | bytes 524288 | tf_op jit(solution)/shard_map/all_to_all | solution.py:122
  481.4 19.2 %all_gather.7 = bf16[1536,64]{0,1:T(8,128)(2,1)S(1)} all-gather(bf16[1536,16]{0,1:T(8,128)(2,1)S(1)} %copy-done.11), channel_id=1, replica_groups=mesh['pipe'=4,'ctx'=16,'dp'=8] {'pipe'}, dimensions={1}, use_global_device_ids=true | all-gather | bytes 245760 | tf_op jit(solution)/shard_map/all_gather | solution.py:65
  502.3 1.2 copy.72
  504.2 1.3 collective-permute-start.12
  506.1 44.3 %reduce-scatter.4.cloned.1.call-done = f32[192,64]{1,0:T(8,128)} async-done(((f32[1536,64]{1,0:T(8,128)}), f32[192,64]{1,0:T(8,128)}) %reduce-scatter.4.cloned.1.call-update) | async-done | bytes 49168
  551.4 42.6 %psum.7 = f32[192,64]{0,1:T(8,128)S(1)} all-reduce(f32[192,64]{0,1:T(8,128)S(1)} %copy.73), channel_id=1, replica_groups=mesh['pipe'=4,'ctx'=16,'dp'=8] {'ctx'}, use_global_device_ids=true, to_apply=%region_37.38 | all-reduce | flops 12288 | bytes 98304 | tf_op jit(solution)/shard_map/psum | solution.py:141
  594.7 1.3 collective-permute-start.15
  597.4 23.4 %collective-permute-done.15 = f32[192,16]{0,1:T(8,128)S(1)} collective-permute-done((f32[192,16]{0,1:T(8,128)S(1)}, f32[192,16]{0,1:T(8,128)S(1)}, u32[]{:S(2)}, u32[]{:S(2)}) %collective-permute-start.15) | collective-permute-done | bytes 12320 | tf_op jit(solution)/shard_map/ppermute | solution.py:148
  (141 shorter events, 39.6 us)
Async XLA Ops:
  7.2 21.3 %copy-start = (bf16[64,1536]{1,0:T(8,128)(2,1)S(1)}, bf16[64,1536]{1,0:T(8,128)(2,1)}, u32[]{:S(2)}) copy-start(bf16[64,1536]{1,0:T(8,128)(2,1)} %param.35) | copy-start | bytes 589828
  7.2 42.3 %copy-start.7 = (bf16[1,192,1536]{2,1,0:T(8,128)(2,1)S(1)}, bf16[1,192,1536]{2,1,0:T(8,128)(2,1)}, u32[]{:S(2)}) copy-start(bf16[1,192,1536]{2,1,0:T(8,128)(2,1)} %param.38) | copy-start | bytes 1769476
  7.2 115.7 %all-gather.3.cloned.1.call-start = ((), (), s32[]{:S(2)}) async-start(), calls=%async_computation.11 | async-start | bytes 5308416 | tf_op jit(solution)/shard_map/all_gather | solution.py:57
  7.9 24.3 %collective-permute-start = (bf16[192,1536]{1,0:T(8,128)(2,1)}, bf16[192,1536]{1,0:T(8,128)(2,1)}, u32[]{:S(2)}, u32[]{:S(2)}) collective-permute-start(bf16[192,1536]{1,0:T(8,128)(2,1)} %bitcast.203), channel_id=1, source_target_pairs={{0,1},{1,2},{2,3},{3,4},{4,5},{5,6},{6,7},{7,0},{8,9},{9,10},{10,1... | collective-permute-start | bytes 1769480 | tf_op jit(solution)/shard_map/ppermute | solution.py:61
  11.9 37.6 %collective-permute-start.1 = (bf16[192,1536]{1,0:T(8,128)(2,1)}, bf16[192,1536]{1,0:T(8,128)(2,1)}, u32[]{:S(2)}, u32[]{:S(2)}) collective-permute-start(bf16[192,1536]{1,0:T(8,128)(2,1)} %bitcast.204), channel_id=1, source_target_pairs={{0,2},{1,3},{2,4},{3,5},{4,6},{5,7},{6,0},{7,1},{8,10},{9,11},{10,... | collective-permute-start | bytes 1769480 | tf_op jit(solution)/shard_map/ppermute | solution.py:61
  16.3 37.1 %collective-permute-start.2 = (bf16[192,1536]{1,0:T(8,128)(2,1)}, bf16[192,1536]{1,0:T(8,128)(2,1)S(1)}, u32[]{:S(2)}, u32[]{:S(2)}) collective-permute-start(bf16[192,1536]{1,0:T(8,128)(2,1)} %bitcast.205), channel_id=1, source_target_pairs={{0,3},{1,4},{2,5},{3,6},{4,7},{5,0},{6,1},{7,2},{8,11},{9,12},{10,... | collective-permute-start | bytes 1769480 | tf_op jit(solution)/shard_map/ppermute | solution.py:61
  20.3 63.5 %collective-permute-start.3 = (bf16[192,1536]{1,0:T(8,128)(2,1)}, bf16[192,1536]{1,0:T(8,128)(2,1)S(1)}, u32[]{:S(2)}, u32[]{:S(2)}) collective-permute-start(bf16[192,1536]{1,0:T(8,128)(2,1)} %bitcast.206), channel_id=1, source_target_pairs={{0,4},{1,5},{2,6},{3,7},{4,0},{5,1},{6,2},{7,3},{8,12},{9,13},{10,... | collective-permute-start | bytes 1769480 | tf_op jit(solution)/shard_map/ppermute | solution.py:61
  22.4 62.2 %collective-permute-start.4 = (bf16[192,1536]{1,0:T(8,128)(2,1)}, bf16[192,1536]{1,0:T(8,128)(2,1)S(1)}, u32[]{:S(2)}, u32[]{:S(2)}) collective-permute-start(bf16[192,1536]{1,0:T(8,128)(2,1)} %bitcast.207), channel_id=1, source_target_pairs={{0,5},{1,6},{2,7},{3,0},{4,1},{5,2},{6,3},{7,4},{8,13},{9,14},{10,... | collective-permute-start | bytes 1769480 | tf_op jit(solution)/shard_map/ppermute | solution.py:61
  32.2 63.8 %collective-permute-start.5 = (bf16[192,1536]{1,0:T(8,128)(2,1)}, bf16[192,1536]{1,0:T(8,128)(2,1)S(1)}, u32[]{:S(2)}, u32[]{:S(2)}) collective-permute-start(bf16[192,1536]{1,0:T(8,128)(2,1)} %bitcast.208), channel_id=1, source_target_pairs={{0,6},{1,7},{2,0},{3,1},{4,2},{5,3},{6,4},{7,5},{8,14},{9,15},{10,... | collective-permute-start | bytes 1769480 | tf_op jit(solution)/shard_map/ppermute | solution.py:61
  49.5 55.9 %collective-permute-start.6 = (bf16[192,1536]{1,0:T(8,128)(2,1)S(1)}, bf16[192,1536]{1,0:T(8,128)(2,1)S(1)}, u32[]{:S(2)}, u32[]{:S(2)}) collective-permute-start(bf16[192,1536]{1,0:T(8,128)(2,1)S(1)} %bitcast.209), channel_id=1, source_target_pairs={{0,7},{1,0},{2,1},{3,2},{4,3},{5,4},{6,5},{7,6},{8,15},{9,8},{10,9... | collective-permute-start | bytes 1769480 | tf_op jit(solution)/shard_map/ppermute | solution.py:61
  124.0 41.5 %copy-start.10 = (s32[2,1,1024]{2,1,0:T(1,128)S(1)}, s32[2,1,1024]{2,1,0:T(1,128)}, u32[]{:S(2)}) copy-start(s32[2,1,1024]{2,1,0:T(1,128)} %param.34) | copy-start | bytes 24580
  125.8 37.7 %all-to-all-start = ((bf16[16,2,9216]{2,1,0:T(2,128)(2,1)}), bf16[16,2,9216]{2,1,0:T(2,128)(2,1)S(1)}, u32[]{:S(2)}, u32[]{:S(2)}) async-start(bf16[16,2,9216]{2,1,0:T(2,128)(2,1)} %reshape.621), calls=%async_computation | async-start | bytes 1179648 | tf_op jit(solution)/shard_map/all_to_all | solution.py:113
  191.9 16.5 %collective-permute-start.7 = (bf16[1,64,1536]{2,1,0:T(8,128)(2,1)S(1)}, bf16[1,64,1536]{2,1,0:T(8,128)(2,1)S(1)}, u32[]{:S(2)}, u32[]{:S(2)}) collective-permute-start(bf16[1,64,1536]{2,1,0:T(8,128)(2,1)S(1)} %fusion.109), channel_id=1, source_target_pairs={{0,128},{128,256},{256,384},{1,129},{129,257},{257,385},{2,130},{1... | collective-permute-start | bytes 589832 | tf_op jit(solution)/shard_map/ppermute | solution.py:15
  208.7 3.8 copy-start.3
  216.9 32.7 %all-to-all-start.2 = ((bf16[16,2,9216]{2,1,0:T(2,128)(2,1)}), bf16[16,2,9216]{2,1,0:T(2,128)(2,1)S(1)}, u32[]{:S(2)}, u32[]{:S(2)}) async-start(bf16[16,2,9216]{2,1,0:T(2,128)(2,1)} %reshape.623), calls=%async_computation.2 | async-start | bytes 1179648 | tf_op jit(solution)/shard_map/all_to_all | solution.py:113
  278.4 5.8 collective-permute-start.8
  284.5 3.8 copy-start.4
  292.2 34.5 %all-to-all-start.4 = ((bf16[16,2,9216]{2,1,0:T(2,128)(2,1)}), bf16[16,2,9216]{2,1,0:T(2,128)(2,1)S(1)}, u32[]{:S(2)}, u32[]{:S(2)}) async-start(bf16[16,2,9216]{2,1,0:T(2,128)(2,1)} %reshape.625), calls=%async_computation.4 | async-start | bytes 1179648 | tf_op jit(solution)/shard_map/all_to_all | solution.py:113
  354.9 6.6 %collective-permute-start.9 = (bf16[1,64,1536]{2,1,0:T(8,128)(2,1)S(1)}, bf16[1,64,1536]{2,1,0:T(8,128)(2,1)S(1)}, u32[]{:S(2)}, u32[]{:S(2)}) collective-permute-start(bf16[1,64,1536]{2,1,0:T(8,128)(2,1)S(1)} %fusion.97), channel_id=1, source_target_pairs={{0,128},{128,256},{256,384},{1,129},{129,257},{257,385},{2,130},{1... | collective-permute-start | bytes 589832 | tf_op jit(solution)/shard_map/ppermute | solution.py:15
  364.8 33.3 %all-to-all-start.6 = ((bf16[16,2,9216]{2,1,0:T(2,128)(2,1)}), bf16[16,2,9216]{2,1,0:T(2,128)(2,1)S(1)}, u32[]{:S(2)}, u32[]{:S(2)}) async-start(bf16[16,2,9216]{2,1,0:T(2,128)(2,1)} %reshape.627), calls=%async_computation.6 | async-start | bytes 1179648 | tf_op jit(solution)/shard_map/all_to_all | solution.py:113
  423.6 16.7 %collective-permute-start.10 = (bf16[1,64,1536]{2,1,0:T(8,128)(2,1)S(1)}, bf16[1,64,1536]{2,1,0:T(8,128)(2,1)S(1)}, u32[]{:S(2)}, u32[]{:S(2)}) collective-permute-start(bf16[1,64,1536]{2,1,0:T(8,128)(2,1)S(1)} %fusion.101), channel_id=1, source_target_pairs={{0,128},{128,256},{256,384},{1,129},{129,257},{257,385},{2,130},{1... | collective-permute-start | bytes 589832 | tf_op jit(solution)/shard_map/ppermute | solution.py:15
  443.7 27.6 %all-to-all-start.8 = ((bf16[16,2,9216]{2,1,0:T(2,128)(2,1)}), bf16[16,2,9216]{2,1,0:T(2,128)(2,1)S(1)}, u32[]{:S(2)}, u32[]{:S(2)}) async-start(bf16[16,2,9216]{2,1,0:T(2,128)(2,1)} %reshape.629), calls=%async_computation.8 | async-start | bytes 1179648 | tf_op jit(solution)/shard_map/all_to_all | solution.py:113
  473.3 7.9 %copy-start.8 = (f32[2,1,64,64]{3,2,1,0:T(8,128)S(1)}, f32[2,1,64,64]{3,2,1,0:T(8,128)}, u32[]{:S(2)}) copy-start(f32[2,1,64,64]{3,2,1,0:T(8,128)} %param.31) | copy-start | bytes 98308
  473.3 8.0 %copy-start.9 = (f32[2,1,64,64]{3,2,1,0:T(8,128)S(1)}, f32[2,1,64,64]{3,2,1,0:T(8,128)}, u32[]{:S(2)}) copy-start(f32[2,1,64,64]{3,2,1,0:T(8,128)} %param.32) | copy-start | bytes 98308
  473.3 8.1 %copy-start.11 = (bf16[1536,16]{0,1:T(8,128)(2,1)S(1)}, bf16[1536,16]{0,1:T(8,128)(2,1)}, u32[]{:S(2)}) copy-start(bf16[1536,16]{0,1:T(8,128)(2,1)} %param.41) | copy-start | bytes 147460
  473.4 28.1 %copy-start.12 = (f32[1536]{0:T(1024)S(1)}, f32[1536]{0:T(1024)}, u32[]{:S(2)}) copy-start(f32[1536]{0:T(1024)} %param.40) | copy-start | bytes 18436
  474.2 26.4 %all-to-all-start.9 = ((bf16[16,64,96]{2,1,0:T(8,128)(2,1)}), bf16[16,64,96]{2,1,0:T(8,128)(2,1)S(1)}, u32[]{:S(2)}, u32[]{:S(2)}) async-start(bf16[16,64,96]{2,1,0:T(8,128)(2,1)} %bitcast.67), calls=%async_computation.9 | async-start | bytes 524288 | tf_op jit(solution)/shard_map/all_to_all | solution.py:122
  481.1 69.3 %reduce-scatter.4.cloned.1.call-start = ((), (), s32[]{:S(2)}) async-start(), calls=%async_computation.12 | async-start | bytes 884736
  500.6 120.8 %copy-start.1 = (bf16[64,1536]{1,0:T(8,128)(2,1)S(1)}, bf16[64,1536]{1,0:T(8,128)(2,1)}, u32[]{:S(2)}) copy-start(bf16[64,1536]{1,0:T(8,128)(2,1)} %param.35) | copy-start | bytes 589828
  503.5 92.6 %collective-permute-start.11 = (f32[2,1,64,16]{2,3,0,1:T(8,128)S(1)}, f32[2,1,64,16]{2,3,0,1:T(8,128)S(1)}, u32[]{:S(2)}, u32[]{:S(2)}) collective-permute-start(f32[2,1,64,16]{2,3,0,1:T(8,128)S(1)} %get-tuple-element.297), channel_id=1, source_target_pairs={{384,0},{385,1},{386,2},{387,3},{388,4},{389,5},{390,6},{391,7},{3... | collective-permute-start | bytes 24584 | tf_op jit(solution)/shard_map/ppermute | solution.py:147
  504.2 92.6 %collective-permute-start.12 = (f32[2,1,64,16]{2,3,0,1:T(8,128)S(1)}, f32[2,1,64,16]{2,3,0,1:T(8,128)S(1)}, u32[]{:S(2)}, u32[]{:S(2)}) collective-permute-start(f32[2,1,64,16]{2,3,0,1:T(8,128)S(1)} %get-tuple-element.295), channel_id=1, source_target_pairs={{384,128},{385,129},{386,130},{387,131},{388,132},{389,133},{390,1... | collective-permute-start | bytes 24584 | tf_op jit(solution)/shard_map/ppermute | solution.py:147
  505.5 91.3 %collective-permute-start.13 = (f32[2,1,64,16]{2,3,0,1:T(8,128)S(1)}, f32[2,1,64,16]{2,3,0,1:T(8,128)S(1)}, u32[]{:S(2)}, u32[]{:S(2)}) collective-permute-start(f32[2,1,64,16]{2,3,0,1:T(8,128)S(1)} %get-tuple-element.296), channel_id=1, source_target_pairs={{384,256},{385,257},{386,258},{387,259},{388,260},{389,261},{390,2... | collective-permute-start | bytes 24584 | tf_op jit(solution)/shard_map/ppermute | solution.py:147
  594.1 3.3 collective-permute-start.14
  594.7 26.1 %collective-permute-start.15 = (f32[192,16]{0,1:T(8,128)S(1)}, f32[192,16]{0,1:T(8,128)S(1)}, u32[]{:S(2)}, u32[]{:S(2)}) collective-permute-start(f32[192,16]{0,1:T(8,128)S(1)} %get-tuple-element.292), channel_id=1, source_target_pairs={{384,128},{385,129},{386,130},{387,131},{388,132},{389,133},{390,1... | collective-permute-start | bytes 36872 | tf_op jit(solution)/shard_map/ppermute | solution.py:148
  596.1 24.7 %collective-permute-start.16 = (f32[192,16]{0,1:T(8,128)S(1)}, f32[192,16]{0,1:T(8,128)S(1)}, u32[]{:S(2)}, u32[]{:S(2)}) collective-permute-start(f32[192,16]{0,1:T(8,128)S(1)} %get-tuple-element.293), channel_id=1, source_target_pairs={{384,256},{385,257},{386,258},{387,259},{388,260},{389,261},{390,2... | collective-permute-start | bytes 36872 | tf_op jit(solution)/shard_map/ppermute | solution.py:148
Sparse Core Ops, SparseCore 0:
  10.1 112.7 all-gather.2
  503.6 46.8 reduce-scatter.3

commit v5 on v4

--- a/solution.py
+++ b/solution.py
@@ -54,15 +54,38 @@
     embedded = (embedded + flow_time * time_vector).astype(jnp.bfloat16)
     dp_index = lax.axis_index("dp")
     dp_count = lax.axis_size("dp")
-    full_query = lax.all_gather(query_weight[0], "dp", axis=0, tiled=True)
-    key_blocks = [key_weight[0]]
-    for step in range(1, dp_count):
-        pairs = [(source, (source + step) % dp_count) for source in range(dp_count)]
-        key_blocks.append(lax.ppermute(key_weight[0], "dp", pairs))
-    by_step = jnp.stack(key_blocks, axis=0)
     source_step = (dp_index - jnp.arange(dp_count, dtype=jnp.int32)) % dp_count
-    full_key = jnp.take(by_step, source_step, axis=0).reshape(model_width, model_width)
-    head_full = lax.all_gather(head_weight, "pipe", axis=1, tiled=True)
+    first_phases = list(range(0, phase_count, 2))
+    later_phases = list(range(1, phase_count, 2))
+
+    def gather_rows(block, phases):
+        pieces = [block]
+        for step in range(1, dp_count):
+            pairs = [
+                (phase * dp_count + source, phase * dp_count + (source + step) % dp_count)
+                for phase in phases
+                for source in range(dp_count)
+            ]
+            pieces.append(lax.ppermute(block, ("pipe", "dp"), pairs))
+        by_step = jnp.stack(pieces, axis=0)
+        by_source = jnp.take(by_step, source_step, axis=0)
+        return by_source.transpose(1, 0, 2, 3).reshape(2, model_width, model_width)
+
+    weight_block = jnp.stack((query_weight[0], key_weight[0]), axis=0)
+    early_weights = gather_rows(weight_block, first_phases)
+    takes_early = phase_index % 2 == 0
+    ready_pairs = [(phase, phase + 1) for phase in first_phases if phase + 1 < phase_count]
+    ready = lax.ppermute(early_weights[0, :8, :128], "pipe", ready_pairs)
+    late_block, ready = lax.optimization_barrier((weight_block, ready))
+    late_weights = gather_rows(late_block, later_phases)
+    last_phase = phase_count - 1
+    head_pieces = []
+    for source_phase in range(phase_count):
+        if source_phase == last_phase:
+            head_pieces.append(head_weight)
+        else:
+            head_pieces.append(lax.ppermute(head_weight, "pipe", [(source_phase, last_phase)]))
+    head_full = jnp.concatenate(head_pieces, axis=1)
     section_gain = norm_gain[0]
 
     def attention(by_heads, frame_row):
@@ -97,11 +120,16 @@
         wide_state = current.astype(jnp.float32)
         normed = rms_scale(wide_state, section_gain).astype(jnp.bfloat16)[0]
 
-        def project(source):
-            queries = jnp.dot(source, full_query, preferred_element_type=jnp.float32).astype(
+        if moment == 0:
+            weights_now = early_weights
+        else:
+            weights_now = jnp.where(takes_early, early_weights, late_weights)
+
+        def project(source, weights_now=weights_now):
+            queries = jnp.dot(source, weights_now[0], preferred_element_type=jnp.float32).astype(
                 jnp.bfloat16
             )
-            keys = jnp.dot(source, full_key, preferred_element_type=jnp.float32).astype(
+            keys = jnp.dot(source, weights_now[1], preferred_element_type=jnp.float32).astype(
                 jnp.bfloat16
             )
             return jnp.stack((queries, keys, source), axis=0)
@@ -126,7 +154,6 @@
         if moment >= phase_count - 1:
             finals.append(result)
     final_state = jnp.stack(finals, axis=0)
-    last_phase = phase_count - 1
     is_last = phase_index == last_phase
     head_cols = head_weight.shape[1]
     final_norm = rms_scale(final_state.astype(jnp.float32), head_gain).astype(jnp.bfloat16)

time: 638 us -> 702 us (1.10)
  local copies, waits for them, and re-layouts: 47.7 us -> 93.9 us
  blocking collectives: 154 us -> 113 us
  starting transfers between devices: 108 us -> 138 us
  other arithmetic: 14.5 us -> 32.5 us
  waiting for transfers between devices: 273 us -> 282 us
    ppermute x7 -> x17, starting transfers between devices: 22.9 us -> 52.5 us  [the longest x14 30 us: gather_rows(): pieces.append(lax.ppermute(block, ('pipe', 'dp'), pairs))]
    all_to_all x4 -> x3, blocking collectives: 91.9 us -> 69.5 us  [on_device(): lax.all_to_all(mixed_heads, 'ctx', split_axis=0, concat_axis=1, tiled=True)]
    all_gather x1 -> x0, blocking collectives: 19.2 us -> none  [on_device(): head_full = lax.all_gather(head_weight, 'pipe', axis=1, tiled=True)]
    transpose x0 -> x2, local copies, waits for them, and re-layouts: none -> 16.3 us  [gather_rows(): return by_source.transpose(1, 0, 2, 3).reshape(2, model_width, model_width)]
    transpose x0 -> x1, other arithmetic: none -> 14.5 us  [gather_rows(): return by_source.transpose(1, 0, 2, 3).reshape(2, model_width, model_width)]
    unnamed x37 -> x49, local copies, waits for them, and re-layouts: 25.5 us -> 39.3 us
    ppermute x7 -> x17, waiting for transfers between devices: 60.5 us -> 73.6 us  [the longest x14 73.6 us: gather_rows(): pieces.append(lax.ppermute(block, ('pipe', 'dp'), pairs))]
    gather x1 -> x2, local copies, waits for them, and re-layouts: 5.46 us -> 17.7 us  [gather_rows(): by_source = jnp.take(by_step, source_step, axis=0)]
  transfers between devices with their start and end apart: 25 -> 35, of which waited for: 16 -> 14; matrix products, arithmetic and copies ran while one was open for 4% -> 8% of each run, Pallas kernels for 0% -> 0%
where the time goes in v5:
time: 702 us; the launch traced here: 693 us
  waiting for transfers between devices  282 us (40%)
  starting transfers between devices  138 us (20%)
  blocking collectives  113 us (16%)
  local copies, waits for them, and re-layouts  93.9 us (13%)
  other arithmetic  32.5 us (5%)
  matrix products  18.1 us (3%)
  between operations  15.2 us (2%)
    all_to_all x5, waiting for transfers between devices, on_device(): lax.all_to_all(triple, 'ctx', split_axis=2, concat_axis=1, tiled=True)  124 us
    ppermute x14, waiting for transfers between devices, gather_rows(): pieces.append(lax.ppermute(block, ('pipe', 'dp'), pairs))  73.6 us
    all_to_all x3, blocking collectives, on_device(): lax.all_to_all(mixed_heads, 'ctx', split_axis=0, concat_axis=1, tiled=True)  69.5 us
    unnamed x2, waiting for transfers between devices  45.3 us
    all_to_all x5, starting transfers between devices, on_device(): lax.all_to_all(triple, 'ctx', split_axis=2, concat_axis=1, tiled=True)  43.3 us
    psum x1, blocking collectives, on_device(): grad_rows = lax.psum(grad_rows, 'ctx')  43 us
    unnamed x49, local copies, waits for them, and re-layouts  39.3 us
    ppermute x14, starting transfers between devices, gather_rows(): pieces.append(lax.ppermute(block, ('pipe', 'dp'), pairs))  30 us
  transfers between devices with their start and end apart: 35, of which 14 were waited for; matrix products, arithmetic and copies ran while one was open for 8% of the time, Pallas kernels for 0%

profile of v5, /device:TPU:1, one launch (start us, length us, event | category | flops | bytes accessed | tf_op | source)
XLA Modules:
  0.0 693.1 jit_solution(1676488106090476014)
XLA Ops:
  9.6 4.0 collective-permute-start.8
  13.5 4.4 collective-permute-start.9
  17.9 4.1 collective-permute-start.10
  22.0 2.1 collective-permute-start.11
  24.1 3.2 collective-permute-start.12
  30.4 3.3 collective-permute-start.13
  33.8 2.4 bitcast_dynamic-update-slice_fusion.6
  36.1 16.9 %collective-permute-done.9 = bf16[2,192,1536]{2,1,0:T(8,128)(2,1)} collective-permute-done((bf16[2,192,1536]{2,1,0:T(8,128)(2,1)S(1)}, bf16[2,192,1536]{2,1,0:T(8,128)(2,1)}, u32[]{:S(2)}, u32[]{:S(2)}) %collective-permute-start.9) | collective-permute-done | bytes 1179680 | tf_op jit(solution)/shard_map/ppermute | solution.py:69
  53.0 1.9 collective-permute-start.14
  55.0 2.4 bitcast_dynamic-update-slice_fusion.5
  57.4 4.6 collective-permute-done.10
  62.8 2.4 bitcast_dynamic-update-slice_fusion.4
  65.1 52.1 %collective-permute-done.11 = bf16[2,192,1536]{2,1,0:T(8,128)(2,1)} collective-permute-done((bf16[2,192,1536]{2,1,0:T(8,128)(2,1)S(1)}, bf16[2,192,1536]{2,1,0:T(8,128)(2,1)}, u32[]{:S(2)}, u32[]{:S(2)}) %collective-permute-start.11) | collective-permute-done | bytes 1179680 | tf_op jit(solution)/shard_map/ppermute | solution.py:69
  117.9 2.4 bitcast_dynamic-update-slice_fusion.3
  125.8 1.7 collective-permute-start.5
  128.7 1.7 collective-permute-start.6
  133.7 8.9 %gather_fusion.1 = bf16[8,2,192,1536]{3,2,1,0:T(8,128)(2,1)} fusion(bf16[8,2,192,1536]{3,2,1,0:T(8,128)(2,1)} %bitcast_dynamic-update-slice_fusion, s32[1024]{0:T(1024)S(1)} %pad_clamp_fusion), kind=kCustom, calls=%fused_computation.1.clone | custom fusion | bytes 18874400 | tf_op jit(solution)/shard_map/jit(_take)/gather | solution.py:71
  143.7 2.5 bitcast_dynamic-update-slice_fusion.9
  146.2 2.5 bitcast_dynamic-update-slice_fusion.8
  148.6 8.8 %gather_fusion = bf16[8,2,192,1536]{3,2,1,0:T(8,128)(2,1)} fusion(bf16[8,2,192,1536]{3,2,1,0:T(8,128)(2,1)} %bitcast_dynamic-update-slice_fusion.8, s32[1024]{0:T(1024)S(1)} %pad_clamp_fusion), kind=kCustom, calls=%fused_computation.clone | custom fusion | bytes 18874400 | tf_op jit(solution)/shard_map/jit(_take)/gather | solution.py:71
  157.5 14.5 %select_bitcast_fusion = (bf16[2,8,192,1536]{3,2,0,1:T(8,128)(2,1)}, bf16[2,8,192,1536]{3,2,0,1:T(8,128)(2,1)}) fusion(bf16[8,2,192,1536]{3,2,1,0:T(8,128)(2,1)} %gather_fusion.1, pred[8]{0:T(512)(128)(4,1)S(1)} %compare_and_fusion, bf16[8,2,192,1536]{3,2,1,0:T(8,128)(2,1)} %gather_fusion), kind=kLoop, calls=%fused_computation.126 | loop fusion | flops 9437184 | bytes 37748744 | tf_op jit(solution)/shard_map/transpose | solution.py:72
  171.9 8.2 %copy.43 = bf16[2,8,192,1536]{3,2,1,0:T(8,128)(2,1)} copy(bf16[2,8,192,1536]{3,2,0,1:T(8,128)(2,1)} %get-tuple-element.285) | data formatting | bytes 18874368 | tf_op jit(solution)/shard_map/transpose | solution.py:72
  181.2 1.8 reshape.590
  183.1 14.9 %all-to-all-start = ((bf16[16,2,9216]{2,1,0:T(2,128)(2,1)}), bf16[16,2,9216]{2,1,0:T(2,128)(2,1)S(1)}, u32[]{:S(2)}, u32[]{:S(2)}) async-start(bf16[16,2,9216]{2,1,0:T(2,128)(2,1)} %reshape.590), calls=%async_computation | async-start | bytes 1179648 | tf_op jit(solution)/shard_map/all_to_all | solution.py:141
  198.0 24.9 %all-to-all-done = bf16[16,2,9216]{2,1,0:T(2,128)(2,1)S(1)} async-done(((bf16[16,2,9216]{2,1,0:T(2,128)(2,1)}), bf16[16,2,9216]{2,1,0:T(2,128)(2,1)S(1)}, u32[]{:S(2)}, u32[]{:S(2)}) %all-to-all-start) | async-done | bytes 589856 | tf_op jit(solution)/shard_map/all_to_all | solution.py:141
  226.2 6.7 all-to-all-start.1
  233.0 8.2 %copy.49 = bf16[2,8,192,1536]{3,2,1,0:T(8,128)(2,1)} copy(bf16[2,8,192,1536]{3,2,0,1:T(8,128)(2,1)} %get-tuple-element.284) | data formatting | bytes 18874368 | tf_op jit(solution)/shard_map/transpose | solution.py:72
  241.1 4.6 all-to-all-done.1
  246.4 1.9 collective-permute-start.7
  248.3 11.2 %bitcast_select_fusion = bf16[2,1536,1536]{2,1,0:T(8,128)(2,1)} fusion(bf16[2,8,192,1536]{3,2,1,0:T(8,128)(2,1)} %copy.49, pred[]{:T(512)S(6)} %eq.19, bf16[2,8,192,1536]{3,2,1,0:T(8,128)(2,1)} %copy.43), kind=kLoop, calls=%fused_computation.125 | loop fusion | flops 4718592 | bytes 28311552 | tf_op jit(solution)/shard_map/jit(_where)/select_n | solution.py:126
  259.9 6.6 conditional.12
  259.9 3.3 fusion.44
  263.1 3.3 fusion.47
  267.5 1.8 reshape.592
  269.4 10.7 %all-to-all-start.2 = ((bf16[16,2,9216]{2,1,0:T(2,128)(2,1)}), bf16[16,2,9216]{2,1,0:T(2,128)(2,1)S(1)}, u32[]{:S(2)}, u32[]{:S(2)}) async-start(bf16[16,2,9216]{2,1,0:T(2,128)(2,1)} %reshape.592), calls=%async_computation.2 | async-start | bytes 1179648 | tf_op jit(solution)/shard_map/all_to_all | solution.py:141
  280.0 25.4 %all-to-all-done.2 = bf16[16,2,9216]{2,1,0:T(2,128)(2,1)S(1)} async-done(((bf16[16,2,9216]{2,1,0:T(2,128)(2,1)}), bf16[16,2,9216]{2,1,0:T(2,128)(2,1)S(1)}, u32[]{:S(2)}, u32[]{:S(2)}) %all-to-all-start.2) | async-done | bytes 589856 | tf_op jit(solution)/shard_map/all_to_all | solution.py:141
  307.4 3.8 conditional.13
  311.4 25.9 %all_to_all.145 = bf16[16,64,96]{2,1,0:T(8,128)(2,1)S(1)} all-to-all(bf16[16,64,96]{2,1,0:T(8,128)(2,1)S(1)} %bitcast.273), channel_id=1, replica_groups=mesh['pipe'=4,'ctx'=16,'dp'=8] {'ctx'}, dimensions={0} | all-to-all | bytes 393216 | tf_op jit(solution)/shard_map/all_to_all | solution.py:150
  337.9 1.9 collective-permute-start.15
  339.9 6.3 collective-permute-done.15
  346.5 6.6 conditional.14
  346.6 3.3 fusion.78
  349.8 3.3 fusion.81
  354.2 1.8 reshape.594
  356.0 7.2 %all-to-all-start.4 = ((bf16[16,2,9216]{2,1,0:T(2,128)(2,1)}), bf16[16,2,9216]{2,1,0:T(2,128)(2,1)S(1)}, u32[]{:S(2)}, u32[]{:S(2)}) async-start(bf16[16,2,9216]{2,1,0:T(2,128)(2,1)} %reshape.594), calls=%async_computation.4 | async-start | bytes 1179648 | tf_op jit(solution)/shard_map/all_to_all | solution.py:141
  363.3 24.6 %all-to-all-done.4 = bf16[16,2,9216]{2,1,0:T(2,128)(2,1)S(1)} async-done(((bf16[16,2,9216]{2,1,0:T(2,128)(2,1)}), bf16[16,2,9216]{2,1,0:T(2,128)(2,1)S(1)}, u32[]{:S(2)}, u32[]{:S(2)}) %all-to-all-start.4) | async-done | bytes 589856 | tf_op jit(solution)/shard_map/all_to_all | solution.py:141
  389.8 3.8 conditional.15
  393.8 22.2 %all_to_all.146 = bf16[16,64,96]{2,1,0:T(8,128)(2,1)S(1)} all-to-all(bf16[16,64,96]{2,1,0:T(8,128)(2,1)S(1)} %bitcast.274), channel_id=1, replica_groups=mesh['pipe'=4,'ctx'=16,'dp'=8] {'ctx'}, dimensions={0} | all-to-all | bytes 393216 | tf_op jit(solution)/shard_map/all_to_all | solution.py:150
  416.6 2.0 collective-permute-start.16
  418.6 2.6 collective-permute-done.16
  422.6 1.8 reshape.596
  424.4 5.8 all-to-all-start.6
  430.2 27.9 %all-to-all-done.6 = bf16[16,2,9216]{2,1,0:T(2,128)(2,1)S(1)} async-done(((bf16[16,2,9216]{2,1,0:T(2,128)(2,1)}), bf16[16,2,9216]{2,1,0:T(2,128)(2,1)S(1)}, u32[]{:S(2)}, u32[]{:S(2)}) %all-to-all-start.6) | async-done | bytes 589856 | tf_op jit(solution)/shard_map/all_to_all | solution.py:141
  460.6 21.5 %all_to_all.147 = bf16[16,64,96]{2,1,0:T(8,128)(2,1)S(1)} all-to-all(bf16[16,64,96]{2,1,0:T(8,128)(2,1)S(1)} %bitcast.275), channel_id=1, replica_groups=mesh['pipe'=4,'ctx'=16,'dp'=8] {'ctx'}, dimensions={0} | all-to-all | bytes 393216 | tf_op jit(solution)/shard_map/all_to_all | solution.py:150
  482.7 16.6 %collective-permute-start.17 = (bf16[1,64,1536]{2,1,0:T(8,128)(2,1)S(1)}, bf16[1,64,1536]{2,1,0:T(8,128)(2,1)S(1)}, u32[]{:S(2)}, u32[]{:S(2)}) collective-permute-start(bf16[1,64,1536]{2,1,0:T(8,128)(2,1)S(1)} %fusion.181), channel_id=1, source_target_pairs={{0,128},{128,256},{256,384},{1,129},{129,257},{257,385},{2,130},{1... | collective-permute-start | bytes 589832 | tf_op jit(solution)/shard_map/ppermute | solution.py:15
  499.4 2.6 collective-permute-done.17
  503.4 1.8 reshape.598
  505.2 4.7 all-to-all-start.8
  509.9 20.9 %all-to-all-done.8 = bf16[16,2,9216]{2,1,0:T(2,128)(2,1)S(1)} async-done(((bf16[16,2,9216]{2,1,0:T(2,128)(2,1)}), bf16[16,2,9216]{2,1,0:T(2,128)(2,1)S(1)}, u32[]{:S(2)}, u32[]{:S(2)}) %all-to-all-start.8) | async-done | bytes 589856 | tf_op jit(solution)/shard_map/all_to_all | solution.py:141
  533.6 7.6 %all-to-all-start.9 = ((bf16[16,64,96]{2,1,0:T(8,128)(2,1)}), bf16[16,64,96]{2,1,0:T(8,128)(2,1)S(1)}, u32[]{:S(2)}, u32[]{:S(2)}) async-start(bf16[16,64,96]{2,1,0:T(8,128)(2,1)} %bitcast.86), calls=%async_computation.9 | async-start | bytes 524288 | tf_op jit(solution)/shard_map/all_to_all | solution.py:150
  541.8 21.2 %collective-permute-start.19 = (bf16[1536,16]{0,1:T(8,128)(2,1)S(1)}, bf16[1536,16]{0,1:T(8,128)(2,1)S(1)}, u32[]{:S(2)}, u32[]{:S(2)}) collective-permute-start(bf16[1536,16]{0,1:T(8,128)(2,1)S(1)} %copy-done.7), channel_id=1, source_target_pairs={{128,384},{129,385},{130,386},{131,387},{132,388},{133,389},{134,3... | collective-permute-start | bytes 147464 | tf_op jit(solution)/shard_map/ppermute | solution.py:87
  569.5 45.3 %reduce-scatter.4.cloned.1.call-done = f32[192,64]{1,0:T(8,128)} async-done(((f32[1536,64]{1,0:T(8,128)}), f32[192,64]{1,0:T(8,128)}) %reduce-scatter.4.cloned.1.call-update) | async-done | bytes 49168
  615.7 43.0 %psum.7 = f32[192,64]{0,1:T(8,128)S(1)} all-reduce(f32[192,64]{0,1:T(8,128)S(1)} %copy.79), channel_id=1, replica_groups=mesh['pipe'=4,'ctx'=16,'dp'=8] {'ctx'}, use_global_device_ids=true, to_apply=%region_37.39 | all-reduce | flops 12288 | bytes 98304 | tf_op jit(solution)/shard_map/psum | solution.py:168
  662.0 23.4 %collective-permute-done.25 = f32[192,16]{0,1:T(8,128)S(1)} collective-permute-done((f32[192,16]{0,1:T(8,128)S(1)}, f32[192,16]{0,1:T(8,128)S(1)}, u32[]{:S(2)}, u32[]{:S(2)}) %collective-permute-start.25) | collective-permute-done | bytes 12320 | tf_op jit(solution)/shard_map/ppermute | solution.py:175
  (170 shorter events, 59.3 us)
Async XLA Ops:
  7.2 22.5 %copy-start = (bf16[64,1536]{1,0:T(8,128)(2,1)S(1)}, bf16[64,1536]{1,0:T(8,128)(2,1)}, u32[]{:S(2)}) copy-start(bf16[64,1536]{1,0:T(8,128)(2,1)} %param.37) | copy-start | bytes 589828
  7.2 22.3 %copy-start.9 = (s32[2,1]{0,1:T(1,128)S(1)}, s32[2,1]{0,1:T(1,128)}, u32[]{:S(2)}) copy-start(s32[2,1]{0,1:T(1,128)} %param.35) | copy-start | bytes 28
  7.2 22.3 %copy-start.5 = (f32[1536]{0:T(1024)S(1)}, f32[1536]{0:T(1024)}, u32[]{:S(2)}) copy-start(f32[1536]{0:T(1024)} %param.38) | copy-start | bytes 18436
  7.2 22.4 %copy-start.2 = (f32[2,1,64,64]{3,2,1,0:T(8,128)S(1)}, f32[2,1,64,64]{3,2,1,0:T(8,128)}, u32[]{:S(2)}) copy-start(f32[2,1,64,64]{3,2,1,0:T(8,128)} %param.33) | copy-start | bytes 98308
  7.2 22.4 %copy-start.3 = (f32[2,1,64,64]{3,2,1,0:T(8,128)S(1)}, f32[2,1,64,64]{3,2,1,0:T(8,128)}, u32[]{:S(2)}) copy-start(f32[2,1,64,64]{3,2,1,0:T(8,128)} %param.34) | copy-start | bytes 98308
  7.2 22.9 %copy-start.6 = (f32[1,1536]{1,0:T(1,128)S(1)}, f32[1,1536]{1,0:T(1,128)}, u32[]{:S(2)}) copy-start(f32[1,1536]{1,0:T(1,128)} %param.41) | copy-start | bytes 18436
  9.6 20.9 %collective-permute-start.8 = (bf16[2,192,1536]{2,1,0:T(8,128)(2,1)S(1)}, bf16[2,192,1536]{2,1,0:T(8,128)(2,1)}, u32[]{:S(2)}, u32[]{:S(2)}) collective-permute-start(bf16[2,192,1536]{2,1,0:T(8,128)(2,1)S(1)} %constant_dynamic-update-slice_fusion), channel_id=1, source_target_pairs={{128,129},{129,130},{130,131},{131,132},{132,133},{133,134},{134,1... | collective-permute-start | bytes 3538952 | tf_op jit(solution)/shard_map/ppermute | solution.py:69
  13.5 39.5 %collective-permute-start.9 = (bf16[2,192,1536]{2,1,0:T(8,128)(2,1)S(1)}, bf16[2,192,1536]{2,1,0:T(8,128)(2,1)}, u32[]{:S(2)}, u32[]{:S(2)}) collective-permute-start(bf16[2,192,1536]{2,1,0:T(8,128)(2,1)S(1)} %constant_dynamic-update-slice_fusion), channel_id=1, source_target_pairs={{128,130},{129,131},{130,132},{131,133},{132,134},{133,135},{134,1... | collective-permute-start | bytes 3538952 | tf_op jit(solution)/shard_map/ppermute | solution.py:69
  17.9 44.1 %collective-permute-start.10 = (bf16[2,192,1536]{2,1,0:T(8,128)(2,1)S(1)}, bf16[2,192,1536]{2,1,0:T(8,128)(2,1)}, u32[]{:S(2)}, u32[]{:S(2)}) collective-permute-start(bf16[2,192,1536]{2,1,0:T(8,128)(2,1)S(1)} %constant_dynamic-update-slice_fusion), channel_id=1, source_target_pairs={{128,131},{129,132},{130,133},{131,134},{132,135},{133,128},{134,1... | collective-permute-start | bytes 3538952 | tf_op jit(solution)/shard_map/ppermute | solution.py:69
  22.0 95.2 %collective-permute-start.11 = (bf16[2,192,1536]{2,1,0:T(8,128)(2,1)S(1)}, bf16[2,192,1536]{2,1,0:T(8,128)(2,1)}, u32[]{:S(2)}, u32[]{:S(2)}) collective-permute-start(bf16[2,192,1536]{2,1,0:T(8,128)(2,1)S(1)} %constant_dynamic-update-slice_fusion), channel_id=1, source_target_pairs={{128,132},{129,133},{130,134},{131,135},{132,128},{133,129},{134,1... | collective-permute-start | bytes 3538952 | tf_op jit(solution)/shard_map/ppermute | solution.py:69
  24.1 96.2 %collective-permute-start.12 = (bf16[2,192,1536]{2,1,0:T(8,128)(2,1)S(1)}, bf16[2,192,1536]{2,1,0:T(8,128)(2,1)S(1)}, u32[]{:S(2)}, u32[]{:S(2)}) collective-permute-start(bf16[2,192,1536]{2,1,0:T(8,128)(2,1)S(1)} %constant_dynamic-update-slice_fusion), channel_id=1, source_target_pairs={{128,133},{129,134},{130,135},{131,128},{132,129},{133,130},{134,1... | collective-permute-start | bytes 3538952 | tf_op jit(solution)/shard_map/ppermute | solution.py:69
  30.4 91.7 %collective-permute-start.13 = (bf16[2,192,1536]{2,1,0:T(8,128)(2,1)S(1)}, bf16[2,192,1536]{2,1,0:T(8,128)(2,1)S(1)}, u32[]{:S(2)}, u32[]{:S(2)}) collective-permute-start(bf16[2,192,1536]{2,1,0:T(8,128)(2,1)S(1)} %constant_dynamic-update-slice_fusion), channel_id=1, source_target_pairs={{128,134},{129,135},{130,128},{131,129},{132,130},{133,131},{134,1... | collective-permute-start | bytes 3538952 | tf_op jit(solution)/shard_map/ppermute | solution.py:69
  53.0 71.0 %collective-permute-start.14 = (bf16[2,192,1536]{2,1,0:T(8,128)(2,1)S(1)}, bf16[2,192,1536]{2,1,0:T(8,128)(2,1)S(1)}, u32[]{:S(2)}, u32[]{:S(2)}) collective-permute-start(bf16[2,192,1536]{2,1,0:T(8,128)(2,1)S(1)} %constant_dynamic-update-slice_fusion), channel_id=1, source_target_pairs={{128,135},{129,128},{130,129},{131,130},{132,131},{133,132},{134,1... | collective-permute-start | bytes 3538952 | tf_op jit(solution)/shard_map/ppermute | solution.py:69
  62.0 63.8 %collective-permute-start = (bf16[2,192,1536]{2,1,0:T(8,128)(2,1)S(1)}, bf16[2,192,1536]{2,1,0:T(8,128)(2,1)S(1)}, u32[]{:S(2)}, u32[]{:S(2)}) collective-permute-start(bf16[2,192,1536]{2,1,0:T(8,128)(2,1)S(1)} %constant_dynamic-update-slice_fusion), channel_id=1, source_target_pairs={{0,1},{1,2},{2,3},{3,4},{4,5},{5,6},{6,7},{7,0},{256,257},{257,258... | collective-permute-start | bytes 3538952 | tf_op jit(solution)/shard_map/ppermute | solution.py:69
  117.2 11.5 %collective-permute-start.1 = (bf16[2,192,1536]{2,1,0:T(8,128)(2,1)S(1)}, bf16[2,192,1536]{2,1,0:T(8,128)(2,1)S(1)}, u32[]{:S(2)}, u32[]{:S(2)}) collective-permute-start(bf16[2,192,1536]{2,1,0:T(8,128)(2,1)S(1)} %constant_dynamic-update-slice_fusion), channel_id=1, source_target_pairs={{0,2},{1,3},{2,4},{3,5},{4,6},{5,7},{6,0},{7,1},{256,258},{257,259... | collective-permute-start | bytes 3538952 | tf_op jit(solution)/shard_map/ppermute | solution.py:69
  120.3 11.2 %collective-permute-start.2 = (bf16[2,192,1536]{2,1,0:T(8,128)(2,1)S(1)}, bf16[2,192,1536]{2,1,0:T(8,128)(2,1)S(1)}, u32[]{:S(2)}, u32[]{:S(2)}) collective-permute-start(bf16[2,192,1536]{2,1,0:T(8,128)(2,1)S(1)} %constant_dynamic-update-slice_fusion), channel_id=1, source_target_pairs={{0,3},{1,4},{2,5},{3,6},{4,7},{5,0},{6,1},{7,2},{256,259},{257,260... | collective-permute-start | bytes 3538952 | tf_op jit(solution)/shard_map/ppermute | solution.py:69
  122.1 10.4 %collective-permute-start.3 = (bf16[2,192,1536]{2,1,0:T(8,128)(2,1)S(1)}, bf16[2,192,1536]{2,1,0:T(8,128)(2,1)S(1)}, u32[]{:S(2)}, u32[]{:S(2)}) collective-permute-start(bf16[2,192,1536]{2,1,0:T(8,128)(2,1)S(1)} %constant_dynamic-update-slice_fusion), channel_id=1, source_target_pairs={{0,4},{1,5},{2,6},{3,7},{4,0},{5,1},{6,2},{7,3},{256,260},{257,261... | collective-permute-start | bytes 3538952 | tf_op jit(solution)/shard_map/ppermute | solution.py:69
  124.0 18.6 %collective-permute-start.4 = (bf16[2,192,1536]{2,1,0:T(8,128)(2,1)S(1)}, bf16[2,192,1536]{2,1,0:T(8,128)(2,1)S(1)}, u32[]{:S(2)}, u32[]{:S(2)}) collective-permute-start(bf16[2,192,1536]{2,1,0:T(8,128)(2,1)S(1)} %constant_dynamic-update-slice_fusion), channel_id=1, source_target_pairs={{0,5},{1,6},{2,7},{3,0},{4,1},{5,2},{6,3},{7,4},{256,261},{257,262... | collective-permute-start | bytes 3538952 | tf_op jit(solution)/shard_map/ppermute | solution.py:69
  125.8 17.9 %collective-permute-start.5 = (bf16[2,192,1536]{2,1,0:T(8,128)(2,1)S(1)}, bf16[2,192,1536]{2,1,0:T(8,128)(2,1)}, u32[]{:S(2)}, u32[]{:S(2)}) collective-permute-start(bf16[2,192,1536]{2,1,0:T(8,128)(2,1)S(1)} %constant_dynamic-update-slice_fusion), channel_id=1, source_target_pairs={{0,6},{1,7},{2,0},{3,1},{4,2},{5,3},{6,4},{7,5},{256,262},{257,263... | collective-permute-start | bytes 3538952 | tf_op jit(solution)/shard_map/ppermute | solution.py:69
  128.7 17.5 %collective-permute-start.6 = (bf16[2,192,1536]{2,1,0:T(8,128)(2,1)S(1)}, bf16[2,192,1536]{2,1,0:T(8,128)(2,1)}, u32[]{:S(2)}, u32[]{:S(2)}) collective-permute-start(bf16[2,192,1536]{2,1,0:T(8,128)(2,1)S(1)} %constant_dynamic-update-slice_fusion), channel_id=1, source_target_pairs={{0,7},{1,0},{2,1},{3,2},{4,3},{5,4},{6,5},{7,6},{256,263},{257,256... | collective-permute-start | bytes 3538952 | tf_op jit(solution)/shard_map/ppermute | solution.py:69
  181.2 43.6 %copy-start.4 = (s32[2,1,1024]{2,1,0:T(1,128)S(1)}, s32[2,1,1024]{2,1,0:T(1,128)}, u32[]{:S(2)}) copy-start(s32[2,1,1024]{2,1,0:T(1,128)} %param.36) | copy-start | bytes 24580
  183.1 39.8 %all-to-all-start = ((bf16[16,2,9216]{2,1,0:T(2,128)(2,1)}), bf16[16,2,9216]{2,1,0:T(2,128)(2,1)S(1)}, u32[]{:S(2)}, u32[]{:S(2)}) async-start(bf16[16,2,9216]{2,1,0:T(2,128)(2,1)} %reshape.590), calls=%async_computation | async-start | bytes 1179648 | tf_op jit(solution)/shard_map/all_to_all | solution.py:141
  226.2 19.5 %all-to-all-start.1 = ((bf16[16,64,96]{2,1,0:T(8,128)(2,1)}), bf16[16,64,96]{2,1,0:T(8,128)(2,1)S(1)}, u32[]{:S(2)}, u32[]{:S(2)}) async-start(bf16[16,64,96]{2,1,0:T(8,128)(2,1)} %bitcast.60), calls=%async_computation.1 | async-start | bytes 524288 | tf_op jit(solution)/shard_map/all_to_all | solution.py:150
  246.4 13.2 %collective-permute-start.7 = (bf16[1,64,1536]{2,1,0:T(8,128)(2,1)S(1)}, bf16[1,64,1536]{2,1,0:T(8,128)(2,1)S(1)}, u32[]{:S(2)}, u32[]{:S(2)}) collective-permute-start(bf16[1,64,1536]{2,1,0:T(8,128)(2,1)S(1)} %fusion.189), channel_id=1, source_target_pairs={{0,128},{128,256},{256,384},{1,129},{129,257},{257,385},{2,130},{1... | collective-permute-start | bytes 589832 | tf_op jit(solution)/shard_map/ppermute | solution.py:15
  269.4 36.1 %all-to-all-start.2 = ((bf16[16,2,9216]{2,1,0:T(2,128)(2,1)}), bf16[16,2,9216]{2,1,0:T(2,128)(2,1)S(1)}, u32[]{:S(2)}, u32[]{:S(2)}) async-start(bf16[16,2,9216]{2,1,0:T(2,128)(2,1)} %reshape.592), calls=%async_computation.2 | async-start | bytes 1179648 | tf_op jit(solution)/shard_map/all_to_all | solution.py:141
  337.9 8.3 %collective-permute-start.15 = (bf16[1,64,1536]{2,1,0:T(8,128)(2,1)S(1)}, bf16[1,64,1536]{2,1,0:T(8,128)(2,1)S(1)}, u32[]{:S(2)}, u32[]{:S(2)}) collective-permute-start(bf16[1,64,1536]{2,1,0:T(8,128)(2,1)S(1)} %fusion.173), channel_id=1, source_target_pairs={{0,128},{128,256},{256,384},{1,129},{129,257},{257,385},{2,130},{1... | collective-permute-start | bytes 589832 | tf_op jit(solution)/shard_map/ppermute | solution.py:15
  356.0 31.8 %all-to-all-start.4 = ((bf16[16,2,9216]{2,1,0:T(2,128)(2,1)}), bf16[16,2,9216]{2,1,0:T(2,128)(2,1)S(1)}, u32[]{:S(2)}, u32[]{:S(2)}) async-start(bf16[16,2,9216]{2,1,0:T(2,128)(2,1)} %reshape.594), calls=%async_computation.4 | async-start | bytes 1179648 | tf_op jit(solution)/shard_map/all_to_all | solution.py:141
  416.6 4.6 collective-permute-start.16
  424.4 33.8 %all-to-all-start.6 = ((bf16[16,2,9216]{2,1,0:T(2,128)(2,1)}), bf16[16,2,9216]{2,1,0:T(2,128)(2,1)S(1)}, u32[]{:S(2)}, u32[]{:S(2)}) async-start(bf16[16,2,9216]{2,1,0:T(2,128)(2,1)} %reshape.596), calls=%async_computation.6 | async-start | bytes 1179648 | tf_op jit(solution)/shard_map/all_to_all | solution.py:141
  482.7 19.2 %collective-permute-start.17 = (bf16[1,64,1536]{2,1,0:T(8,128)(2,1)S(1)}, bf16[1,64,1536]{2,1,0:T(8,128)(2,1)S(1)}, u32[]{:S(2)}, u32[]{:S(2)}) collective-permute-start(bf16[1,64,1536]{2,1,0:T(8,128)(2,1)S(1)} %fusion.181), channel_id=1, source_target_pairs={{0,128},{128,256},{256,384},{1,129},{129,257},{257,385},{2,130},{1... | collective-permute-start | bytes 589832 | tf_op jit(solution)/shard_map/ppermute | solution.py:15
  505.2 25.5 %all-to-all-start.8 = ((bf16[16,2,9216]{2,1,0:T(2,128)(2,1)}), bf16[16,2,9216]{2,1,0:T(2,128)(2,1)S(1)}, u32[]{:S(2)}, u32[]{:S(2)}) async-start(bf16[16,2,9216]{2,1,0:T(2,128)(2,1)} %reshape.598), calls=%async_computation.8 | async-start | bytes 1179648 | tf_op jit(solution)/shard_map/all_to_all | solution.py:141
  532.7 8.5 %copy-start.7 = (bf16[1536,16]{0,1:T(8,128)(2,1)S(1)}, bf16[1536,16]{0,1:T(8,128)(2,1)}, u32[]{:S(2)}) copy-start(bf16[1536,16]{0,1:T(8,128)(2,1)} %param.43) | copy-start | bytes 147460
  532.7 32.1 %copy-start.8 = (f32[1536]{0:T(1024)S(1)}, f32[1536]{0:T(1024)}, u32[]{:S(2)}) copy-start(f32[1536]{0:T(1024)} %param.42) | copy-start | bytes 18436
  533.6 30.4 %all-to-all-start.9 = ((bf16[16,64,96]{2,1,0:T(8,128)(2,1)}), bf16[16,64,96]{2,1,0:T(8,128)(2,1)S(1)}, u32[]{:S(2)}, u32[]{:S(2)}) async-start(bf16[16,64,96]{2,1,0:T(8,128)(2,1)} %bitcast.86), calls=%async_computation.9 | async-start | bytes 524288 | tf_op jit(solution)/shard_map/all_to_all | solution.py:150
  541.1 73.7 %reduce-scatter.4.cloned.1.call-start = ((), (), s32[]{:S(2)}) async-start(), calls=%async_computation.11 | async-start | bytes 884736
  541.2 23.6 %collective-permute-start.18 = (bf16[1536,16]{0,1:T(8,128)(2,1)S(1)}, bf16[1536,16]{0,1:T(8,128)(2,1)S(1)}, u32[]{:S(2)}, u32[]{:S(2)}) collective-permute-start(bf16[1536,16]{0,1:T(8,128)(2,1)S(1)} %copy-done.7), channel_id=1, source_target_pairs={{0,384},{1,385},{2,386},{3,387},{4,388},{5,389},{6,390},{7,391},{8... | collective-permute-start | bytes 147464 | tf_op jit(solution)/shard_map/ppermute | solution.py:87
  541.8 22.9 %collective-permute-start.19 = (bf16[1536,16]{0,1:T(8,128)(2,1)S(1)}, bf16[1536,16]{0,1:T(8,128)(2,1)S(1)}, u32[]{:S(2)}, u32[]{:S(2)}) collective-permute-start(bf16[1536,16]{0,1:T(8,128)(2,1)S(1)} %copy-done.7), channel_id=1, source_target_pairs={{128,384},{129,385},{130,386},{131,387},{132,388},{133,389},{134,3... | collective-permute-start | bytes 147464 | tf_op jit(solution)/shard_map/ppermute | solution.py:87
  563.1 1.7 collective-permute-start.20
  563.9 122.1 %copy-start.1 = (bf16[64,1536]{1,0:T(8,128)(2,1)S(1)}, bf16[64,1536]{1,0:T(8,128)(2,1)}, u32[]{:S(2)}) copy-start(bf16[64,1536]{1,0:T(8,128)(2,1)} %param.37) | copy-start | bytes 589828
  566.8 93.9 %collective-permute-start.21 = (f32[2,1,64,16]{2,3,0,1:T(8,128)S(1)}, f32[2,1,64,16]{2,3,0,1:T(8,128)S(1)}, u32[]{:S(2)}, u32[]{:S(2)}) collective-permute-start(f32[2,1,64,16]{2,3,0,1:T(8,128)S(1)} %get-tuple-element.283), channel_id=1, source_target_pairs={{384,0},{385,1},{386,2},{387,3},{388,4},{389,5},{390,6},{391,7},{3... | collective-permute-start | bytes 24584 | tf_op jit(solution)/shard_map/ppermute | solution.py:174
  567.5 93.9 %collective-permute-start.22 = (f32[2,1,64,16]{2,3,0,1:T(8,128)S(1)}, f32[2,1,64,16]{2,3,0,1:T(8,128)S(1)}, u32[]{:S(2)}, u32[]{:S(2)}) collective-permute-start(f32[2,1,64,16]{2,3,0,1:T(8,128)S(1)} %get-tuple-element.281), channel_id=1, source_target_pairs={{384,128},{385,129},{386,130},{387,131},{388,132},{389,133},{390,1... | collective-permute-start | bytes 24584 | tf_op jit(solution)/shard_map/ppermute | solution.py:174
  568.8 92.6 %collective-permute-start.23 = (f32[2,1,64,16]{2,3,0,1:T(8,128)S(1)}, f32[2,1,64,16]{2,3,0,1:T(8,128)S(1)}, u32[]{:S(2)}, u32[]{:S(2)}) collective-permute-start(f32[2,1,64,16]{2,3,0,1:T(8,128)S(1)} %get-tuple-element.282), channel_id=1, source_target_pairs={{384,256},{385,257},{386,258},{387,259},{388,260},{389,261},{390,2... | collective-permute-start | bytes 24584 | tf_op jit(solution)/shard_map/ppermute | solution.py:174
  658.7 3.3 collective-permute-start.24
  659.4 26.0 %collective-permute-start.25 = (f32[192,16]{0,1:T(8,128)S(1)}, f32[192,16]{0,1:T(8,128)S(1)}, u32[]{:S(2)}, u32[]{:S(2)}) collective-permute-start(f32[192,16]{0,1:T(8,128)S(1)} %get-tuple-element.278), channel_id=1, source_target_pairs={{384,128},{385,129},{386,130},{387,131},{388,132},{389,133},{390,1... | collective-permute-start | bytes 36872 | tf_op jit(solution)/shard_map/ppermute | solution.py:175
  660.7 24.7 %collective-permute-start.26 = (f32[192,16]{0,1:T(8,128)S(1)}, f32[192,16]{0,1:T(8,128)S(1)}, u32[]{:S(2)}, u32[]{:S(2)}) collective-permute-start(f32[192,16]{0,1:T(8,128)S(1)} %get-tuple-element.279), channel_id=1, source_target_pairs={{384,256},{385,257},{386,258},{387,259},{388,260},{389,261},{390,2... | collective-permute-start | bytes 36872 | tf_op jit(solution)/shard_map/ppermute | solution.py:175
Sparse Core Ops, SparseCore 0:
  566.9 47.7 reduce-scatter.3

commit v6 on v4

--- a/solution.py
+++ b/solution.py
@@ -59,10 +59,16 @@
     for step in range(1, dp_count):
         pairs = [(source, (source + step) % dp_count) for source in range(dp_count)]
         key_blocks.append(lax.ppermute(key_weight[0], "dp", pairs))
-    by_step = jnp.stack(key_blocks, axis=0)
-    source_step = (dp_index - jnp.arange(dp_count, dtype=jnp.int32)) % dp_count
-    full_key = jnp.take(by_step, source_step, axis=0).reshape(model_width, model_width)
-    head_full = lax.all_gather(head_weight, "pipe", axis=1, tiled=True)
+    key_by_step = jnp.stack(key_blocks, axis=0).reshape(model_width, model_width)
+    source_block = (dp_index - jnp.arange(dp_count, dtype=jnp.int32)) % dp_count
+    last_phase = phase_count - 1
+    head_pieces = []
+    for source_phase in range(phase_count):
+        if source_phase == last_phase:
+            head_pieces.append(head_weight)
+        else:
+            head_pieces.append(lax.ppermute(head_weight, "pipe", [(source_phase, last_phase)]))
+    head_full = jnp.concatenate(head_pieces, axis=1)
     section_gain = norm_gain[0]
 
     def attention(by_heads, frame_row):
@@ -101,7 +107,10 @@
             queries = jnp.dot(source, full_query, preferred_element_type=jnp.float32).astype(
                 jnp.bfloat16
             )
-            keys = jnp.dot(source, full_key, preferred_element_type=jnp.float32).astype(
+            block_rows = model_width // dp_count
+            by_block = source.reshape(local_rows, dp_count, block_rows)
+            in_step_order = jnp.take(by_block, source_block, axis=1).reshape(local_rows, model_width)
+            keys = jnp.dot(in_step_order, key_by_step, preferred_element_type=jnp.float32).astype(
                 jnp.bfloat16
             )
             return jnp.stack((queries, keys, source), axis=0)
@@ -126,7 +135,6 @@
         if moment >= phase_count - 1:
             finals.append(result)
     final_state = jnp.stack(finals, axis=0)
-    last_phase = phase_count - 1
     is_last = phase_index == last_phase
     head_cols = head_weight.shape[1]
     final_norm = rms_scale(final_state.astype(jnp.float32), head_gain).astype(jnp.bfloat16)

time: 638 us -> 644 us (level)
  starting transfers between devices: 108 us -> 139 us
  blocking collectives: 154 us -> 136 us
    ppermute x0 -> x3, starting transfers between devices: none -> 24.8 us  [on_device(): lax.ppermute(head_weight, 'pipe', [(source_phase, last_phase)])]
    all_gather x1 -> x0, blocking collectives: 19.2 us -> none  [on_device(): head_full = lax.all_gather(head_weight, 'pipe', axis=1, tiled=True)]
    all_gather x1, waiting for transfers between devices: 6.14 us -> 16.7 us  [on_device(): full_query = lax.all_gather(query_weight[0], 'dp', axis=0, tiled=True)]
    all_to_all x5, waiting for transfers between devices: 127 us -> 117 us  [on_device(): lax.all_to_all(triple, 'ctx', split_axis=2, concat_axis=1, tiled=True)]
  transfers between devices with their start and end apart: 25 -> 28, of which waited for: 16 -> 16; matrix products, arithmetic and copies ran while one was open for 4% -> 3% of each run, Pallas kernels for 0% -> 0%
where the time goes in v6:
time: 644 us; the launch traced here: 634 us
  waiting for transfers between devices  273 us (42%)
  starting transfers between devices  139 us (22%)
  blocking collectives  136 us (21%)
  local copies, waits for them, and re-layouts  45.7 us (7%)
  between operations  15.1 us (2%)
  matrix products  14.6 us (2%)
  other arithmetic  9.66 us (2%)
    all_to_all x5, waiting for transfers between devices, on_device(): lax.all_to_all(triple, 'ctx', split_axis=2, concat_axis=1, tiled=True)  117 us
    all_to_all x4, blocking collectives, on_device(): lax.all_to_all(mixed_heads, 'ctx', split_axis=0, concat_axis=1, tiled=True)  93.4 us
    ppermute x7, waiting for transfers between devices, on_device(): key_blocks.append(lax.ppermute(key_weight[0], 'dp', pairs))  59.6 us
    unnamed x3, waiting for transfers between devices  44.8 us
    psum x1, blocking collectives, on_device(): grad_rows = lax.psum(grad_rows, 'ctx')  42.7 us
    all_to_all x5, starting transfers between devices, on_device(): lax.all_to_all(triple, 'ctx', split_axis=2, concat_axis=1, tiled=True)  39.3 us
    ppermute x4, starting transfers between devices, shifted(): lax.ppermute(value, axis, [(source, source + steps) for source in range(f...  38.4 us
    unnamed x37, local copies, waits for them, and re-layouts  26.6 us
  transfers between devices with their start and end apart: 28, of which 16 were waited for; matrix products, arithmetic and copies ran while one was open for 3% of the time, Pallas kernels for 0%

profile of v6, /device:TPU:1, one launch (start us, length us, event | category | flops | bytes accessed | tf_op | source)
XLA Modules:
  0.0 634.0 jit_solution(727981323686134716)
XLA Ops:
  7.9 4.0 collective-permute-start
  11.9 4.4 collective-permute-start.1
  16.3 4.1 collective-permute-start.2
  20.3 2.1 collective-permute-start.3
  22.4 3.2 collective-permute-start.4
  28.5 1.2 fusion.84
  29.9 1.9 constant_dynamic-update-slice_fusion
  32.0 3.3 collective-permute-start.5
  35.4 1.9 bitcast_dynamic-update-slice_fusion.6
  37.3 12.2 %collective-permute-done.1 = bf16[192,1536]{1,0:T(8,128)(2,1)} collective-permute-done((bf16[192,1536]{1,0:T(8,128)(2,1)}, bf16[192,1536]{1,0:T(8,128)(2,1)}, u32[]{:S(2)}, u32[]{:S(2)}) %collective-permute-start.1) | collective-permute-done | bytes 589856 | tf_op jit(solution)/shard_map/ppermute | solution.py:61
  49.5 1.9 collective-permute-start.6
  51.4 1.9 bitcast_dynamic-update-slice_fusion.5
  53.3 1.9 bitcast_dynamic-update-slice_fusion.4
  55.2 28.6 %collective-permute-done.3 = bf16[192,1536]{1,0:T(8,128)(2,1)S(1)} collective-permute-done((bf16[192,1536]{1,0:T(8,128)(2,1)}, bf16[192,1536]{1,0:T(8,128)(2,1)S(1)}, u32[]{:S(2)}, u32[]{:S(2)}) %collective-permute-start.3) | collective-permute-done | bytes 589856 | tf_op jit(solution)/shard_map/ppermute | solution.py:61
  85.6 10.5 %collective-permute-done.5 = bf16[192,1536]{1,0:T(8,128)(2,1)S(1)} collective-permute-done((bf16[192,1536]{1,0:T(8,128)(2,1)}, bf16[192,1536]{1,0:T(8,128)(2,1)S(1)}, u32[]{:S(2)}, u32[]{:S(2)}) %collective-permute-start.5) | collective-permute-done | bytes 589856 | tf_op jit(solution)/shard_map/ppermute | solution.py:61
  97.0 8.4 %collective-permute-done.6 = bf16[192,1536]{1,0:T(8,128)(2,1)S(1)} collective-permute-done((bf16[192,1536]{1,0:T(8,128)(2,1)S(1)}, bf16[192,1536]{1,0:T(8,128)(2,1)S(1)}, u32[]{:S(2)}, u32[]{:S(2)}) %collective-permute-start.6) | collective-permute-done | bytes 589856 | tf_op jit(solution)/shard_map/ppermute | solution.py:61
  106.2 16.7 %all-gather.3.cloned.1.call-done = bf16[1,1536,1536]{2,1,0:T(8,128)(2,1)} async-done(((bf16[1,192,1536]{2,1,0:T(8,128)(2,1)}), bf16[1,1536,1536]{2,1,0:T(8,128)(2,1)}) %all-gather.3.cloned.1.call-update) | async-done | bytes 4718608 | tf_op jit(solution)/shard_map/all_gather | solution.py:57
  122.9 1.0 copy.77
  124.0 1.8 reshape.635
  125.8 15.6 %all-to-all-start = ((bf16[16,2,9216]{2,1,0:T(2,128)(2,1)}), bf16[16,2,9216]{2,1,0:T(2,128)(2,1)S(1)}, u32[]{:S(2)}, u32[]{:S(2)}) async-start(bf16[16,2,9216]{2,1,0:T(2,128)(2,1)} %reshape.635), calls=%async_computation | async-start | bytes 1179648 | tf_op jit(solution)/shard_map/all_to_all | solution.py:122
  141.5 21.6 %all-to-all-done = bf16[16,2,9216]{2,1,0:T(2,128)(2,1)S(1)} async-done(((bf16[16,2,9216]{2,1,0:T(2,128)(2,1)}), bf16[16,2,9216]{2,1,0:T(2,128)(2,1)S(1)}, u32[]{:S(2)}, u32[]{:S(2)}) %all-to-all-start) | async-done | bytes 589856 | tf_op jit(solution)/shard_map/all_to_all | solution.py:122
  165.2 26.0 %all_to_all.145 = bf16[16,64,96]{2,1,0:T(8,128)(2,1)S(1)} all-to-all(bf16[16,64,96]{2,1,0:T(8,128)(2,1)S(1)} %bitcast.205), channel_id=1, replica_groups=mesh['pipe'=4,'ctx'=16,'dp'=8] {'ctx'}, dimensions={0} | all-to-all | bytes 393216 | tf_op jit(solution)/shard_map/all_to_all | solution.py:131
  191.9 14.0 %collective-permute-start.7 = (bf16[1,64,1536]{2,1,0:T(8,128)(2,1)S(1)}, bf16[1,64,1536]{2,1,0:T(8,128)(2,1)S(1)}, u32[]{:S(2)}, u32[]{:S(2)}) collective-permute-start(bf16[1,64,1536]{2,1,0:T(8,128)(2,1)S(1)} %fusion.105), channel_id=1, source_target_pairs={{0,128},{128,256},{256,384},{1,129},{129,257},{257,385},{2,130},{1... | collective-permute-start | bytes 589832 | tf_op jit(solution)/shard_map/ppermute | solution.py:15
  205.8 2.6 collective-permute-done.7
  208.7 6.6 %conditional.12 = (bf16[3,64,1536]{2,1,0:T(8,128)(2,1)S(1)}) conditional(s32[]{:T(128)} %convert_element_type.285, () %tuple.84, (bf16[1,64,1536]{2,1,0:T(8,128)(2,1)S(1)}, bf16[1536,1536]{1,0:T(8,128)(2,1)}, s32[8]{0:T(128)S(1)}, bf16[1536,1536]{1,0:T(8,128)(2,1)}) %tuple.172), branch_computations={%region_8.10_spmd, %region_9.11_spmd} | conditional | flops 604865600 | bytes 32641236 | solution.py:121
  210.2 3.4 fusion.73
  215.4 1.0 copy.82
  216.4 1.8 reshape.637
  218.3 5.6 all-to-all-start.2
  223.9 27.1 %all-to-all-done.2 = bf16[16,2,9216]{2,1,0:T(2,128)(2,1)S(1)} async-done(((bf16[16,2,9216]{2,1,0:T(2,128)(2,1)}), bf16[16,2,9216]{2,1,0:T(2,128)(2,1)S(1)}, u32[]{:S(2)}, u32[]{:S(2)}) %all-to-all-start.2) | async-done | bytes 589856 | tf_op jit(solution)/shard_map/all_to_all | solution.py:122
  252.9 3.8 conditional.13
  254.0 1.5 fusion.15
  255.5 1.2 fusion.22
  256.9 22.3 %all_to_all.146 = bf16[16,64,96]{2,1,0:T(8,128)(2,1)S(1)} all-to-all(bf16[16,64,96]{2,1,0:T(8,128)(2,1)S(1)} %bitcast.206), channel_id=1, replica_groups=mesh['pipe'=4,'ctx'=16,'dp'=8] {'ctx'}, dimensions={0} | all-to-all | bytes 393216 | tf_op jit(solution)/shard_map/all_to_all | solution.py:131
  279.9 1.9 collective-permute-start.8
  281.8 3.8 collective-permute-done.8
  285.9 6.2 conditional.14
  287.3 3.4 fusion.76
  293.1 1.8 reshape.639
  294.9 7.6 %all-to-all-start.4 = ((bf16[16,2,9216]{2,1,0:T(2,128)(2,1)}), bf16[16,2,9216]{2,1,0:T(2,128)(2,1)S(1)}, u32[]{:S(2)}, u32[]{:S(2)}) async-start(bf16[16,2,9216]{2,1,0:T(2,128)(2,1)} %reshape.639), calls=%async_computation.4 | async-start | bytes 1179648 | tf_op jit(solution)/shard_map/all_to_all | solution.py:122
  302.5 25.2 %all-to-all-done.4 = bf16[16,2,9216]{2,1,0:T(2,128)(2,1)S(1)} async-done(((bf16[16,2,9216]{2,1,0:T(2,128)(2,1)}), bf16[16,2,9216]{2,1,0:T(2,128)(2,1)S(1)}, u32[]{:S(2)}, u32[]{:S(2)}) %all-to-all-start.4) | async-done | bytes 589856 | tf_op jit(solution)/shard_map/all_to_all | solution.py:122
  329.7 4.0 conditional.15
  331.0 1.5 fusion.29
  332.5 1.2 fusion.36
  333.9 21.9 %all_to_all.147 = bf16[16,64,96]{2,1,0:T(8,128)(2,1)S(1)} all-to-all(bf16[16,64,96]{2,1,0:T(8,128)(2,1)S(1)} %bitcast.207), channel_id=1, replica_groups=mesh['pipe'=4,'ctx'=16,'dp'=8] {'ctx'}, dimensions={0} | all-to-all | bytes 393216 | tf_op jit(solution)/shard_map/all_to_all | solution.py:131
  356.5 5.3 collective-permute-start.9
  361.7 2.6 collective-permute-done.9
  365.8 1.8 reshape.641
  367.6 5.8 all-to-all-start.6
  373.4 25.5 %all-to-all-done.6 = bf16[16,2,9216]{2,1,0:T(2,128)(2,1)S(1)} async-done(((bf16[16,2,9216]{2,1,0:T(2,128)(2,1)}), bf16[16,2,9216]{2,1,0:T(2,128)(2,1)S(1)}, u32[]{:S(2)}, u32[]{:S(2)}) %all-to-all-start.6) | async-done | bytes 589856 | tf_op jit(solution)/shard_map/all_to_all | solution.py:122
  401.0 23.2 %all_to_all.148 = bf16[16,64,96]{2,1,0:T(8,128)(2,1)S(1)} all-to-all(bf16[16,64,96]{2,1,0:T(8,128)(2,1)S(1)} %bitcast.208), channel_id=1, replica_groups=mesh['pipe'=4,'ctx'=16,'dp'=8] {'ctx'}, dimensions={0} | all-to-all | bytes 393216 | tf_op jit(solution)/shard_map/all_to_all | solution.py:131
  424.9 17.2 %collective-permute-start.10 = (bf16[1,64,1536]{2,1,0:T(8,128)(2,1)S(1)}, bf16[1,64,1536]{2,1,0:T(8,128)(2,1)S(1)}, u32[]{:S(2)}, u32[]{:S(2)}) collective-permute-start(bf16[1,64,1536]{2,1,0:T(8,128)(2,1)S(1)} %fusion.97), channel_id=1, source_target_pairs={{0,128},{128,256},{256,384},{1,129},{129,257},{257,385},{2,130},{1... | collective-permute-start | bytes 589832 | tf_op jit(solution)/shard_map/ppermute | solution.py:15
  442.1 2.4 collective-permute-done.10
  445.9 1.8 reshape.643
  447.7 4.7 all-to-all-start.8
  452.4 17.9 %all-to-all-done.8 = bf16[16,2,9216]{2,1,0:T(2,128)(2,1)S(1)} async-done(((bf16[16,2,9216]{2,1,0:T(2,128)(2,1)}), bf16[16,2,9216]{2,1,0:T(2,128)(2,1)S(1)}, u32[]{:S(2)}, u32[]{:S(2)}) %all-to-all-start.8) | async-done | bytes 589856 | tf_op jit(solution)/shard_map/all_to_all | solution.py:122
  473.2 7.9 %all-to-all-start.9 = ((bf16[16,64,96]{2,1,0:T(8,128)(2,1)}), bf16[16,64,96]{2,1,0:T(8,128)(2,1)S(1)}, u32[]{:S(2)}, u32[]{:S(2)}) async-start(bf16[16,64,96]{2,1,0:T(8,128)(2,1)} %bitcast.71), calls=%async_computation.9 | async-start | bytes 524288 | tf_op jit(solution)/shard_map/all_to_all | solution.py:131
  481.9 23.5 %collective-permute-start.12 = (bf16[1536,16]{0,1:T(8,128)(2,1)S(1)}, bf16[1536,16]{0,1:T(8,128)(2,1)S(1)}, u32[]{:S(2)}, u32[]{:S(2)}) collective-permute-start(bf16[1536,16]{0,1:T(8,128)(2,1)S(1)} %copy-done.11), channel_id=1, source_target_pairs={{128,384},{129,385},{130,386},{131,387},{132,388},{133,389},{134,3... | collective-permute-start | bytes 147464 | tf_op jit(solution)/shard_map/ppermute | solution.py:70
  508.0 1.2 copy.110
  509.9 1.3 collective-permute-start.15
  511.8 44.1 %reduce-scatter.4.cloned.1.call-done = f32[192,64]{1,0:T(8,128)} async-done(((f32[1536,64]{1,0:T(8,128)}), f32[192,64]{1,0:T(8,128)}) %reduce-scatter.4.cloned.1.call-update) | async-done | bytes 49168
  556.9 42.7 %psum.7 = f32[192,64]{0,1:T(8,128)S(1)} all-reduce(f32[192,64]{0,1:T(8,128)S(1)} %copy.111), channel_id=1, replica_groups=mesh['pipe'=4,'ctx'=16,'dp'=8] {'ctx'}, use_global_device_ids=true, to_apply=%region_37.39 | all-reduce | flops 12288 | bytes 98304 | tf_op jit(solution)/shard_map/psum | solution.py:149
  600.2 1.3 collective-permute-start.18
  602.9 23.4 %collective-permute-done.18 = f32[192,16]{0,1:T(8,128)S(1)} collective-permute-done((f32[192,16]{0,1:T(8,128)S(1)}, f32[192,16]{0,1:T(8,128)S(1)}, u32[]{:S(2)}, u32[]{:S(2)}) %collective-permute-start.18) | collective-permute-done | bytes 12320 | tf_op jit(solution)/shard_map/ppermute | solution.py:156
  (158 shorter events, 41.4 us)
Async XLA Ops:
  7.2 21.3 %copy-start = (bf16[64,1536]{1,0:T(8,128)(2,1)S(1)}, bf16[64,1536]{1,0:T(8,128)(2,1)}, u32[]{:S(2)}) copy-start(bf16[64,1536]{1,0:T(8,128)(2,1)} %param.37) | copy-start | bytes 589828
  7.2 42.3 %copy-start.7 = (bf16[1,192,1536]{2,1,0:T(8,128)(2,1)S(1)}, bf16[1,192,1536]{2,1,0:T(8,128)(2,1)}, u32[]{:S(2)}) copy-start(bf16[1,192,1536]{2,1,0:T(8,128)(2,1)} %param.40) | copy-start | bytes 1769476
  7.2 115.7 %all-gather.3.cloned.1.call-start = ((), (), s32[]{:S(2)}) async-start(), calls=%async_computation.11 | async-start | bytes 5308416 | tf_op jit(solution)/shard_map/all_gather | solution.py:57
  7.9 24.1 %collective-permute-start = (bf16[192,1536]{1,0:T(8,128)(2,1)}, bf16[192,1536]{1,0:T(8,128)(2,1)}, u32[]{:S(2)}, u32[]{:S(2)}) collective-permute-start(bf16[192,1536]{1,0:T(8,128)(2,1)} %bitcast.211), channel_id=1, source_target_pairs={{0,1},{1,2},{2,3},{3,4},{4,5},{5,6},{6,7},{7,0},{8,9},{9,10},{10,1... | collective-permute-start | bytes 1769480 | tf_op jit(solution)/shard_map/ppermute | solution.py:61
  11.9 37.6 %collective-permute-start.1 = (bf16[192,1536]{1,0:T(8,128)(2,1)}, bf16[192,1536]{1,0:T(8,128)(2,1)}, u32[]{:S(2)}, u32[]{:S(2)}) collective-permute-start(bf16[192,1536]{1,0:T(8,128)(2,1)} %bitcast.212), channel_id=1, source_target_pairs={{0,2},{1,3},{2,4},{3,5},{4,6},{5,7},{6,0},{7,1},{8,10},{9,11},{10,... | collective-permute-start | bytes 1769480 | tf_op jit(solution)/shard_map/ppermute | solution.py:61
  16.3 37.1 %collective-permute-start.2 = (bf16[192,1536]{1,0:T(8,128)(2,1)}, bf16[192,1536]{1,0:T(8,128)(2,1)}, u32[]{:S(2)}, u32[]{:S(2)}) collective-permute-start(bf16[192,1536]{1,0:T(8,128)(2,1)} %bitcast.213), channel_id=1, source_target_pairs={{0,3},{1,4},{2,5},{3,6},{4,7},{5,0},{6,1},{7,2},{8,11},{9,12},{10,... | collective-permute-start | bytes 1769480 | tf_op jit(solution)/shard_map/ppermute | solution.py:61
  20.3 63.5 %collective-permute-start.3 = (bf16[192,1536]{1,0:T(8,128)(2,1)}, bf16[192,1536]{1,0:T(8,128)(2,1)S(1)}, u32[]{:S(2)}, u32[]{:S(2)}) collective-permute-start(bf16[192,1536]{1,0:T(8,128)(2,1)} %bitcast.214), channel_id=1, source_target_pairs={{0,4},{1,5},{2,6},{3,7},{4,0},{5,1},{6,2},{7,3},{8,12},{9,13},{10,... | collective-permute-start | bytes 1769480 | tf_op jit(solution)/shard_map/ppermute | solution.py:61
  22.4 62.3 %collective-permute-start.4 = (bf16[192,1536]{1,0:T(8,128)(2,1)}, bf16[192,1536]{1,0:T(8,128)(2,1)S(1)}, u32[]{:S(2)}, u32[]{:S(2)}) collective-permute-start(bf16[192,1536]{1,0:T(8,128)(2,1)} %bitcast.215), channel_id=1, source_target_pairs={{0,5},{1,6},{2,7},{3,0},{4,1},{5,2},{6,3},{7,4},{8,13},{9,14},{10,... | collective-permute-start | bytes 1769480 | tf_op jit(solution)/shard_map/ppermute | solution.py:61
  32.0 64.0 %collective-permute-start.5 = (bf16[192,1536]{1,0:T(8,128)(2,1)}, bf16[192,1536]{1,0:T(8,128)(2,1)S(1)}, u32[]{:S(2)}, u32[]{:S(2)}) collective-permute-start(bf16[192,1536]{1,0:T(8,128)(2,1)} %bitcast.216), channel_id=1, source_target_pairs={{0,6},{1,7},{2,0},{3,1},{4,2},{5,3},{6,4},{7,5},{8,14},{9,15},{10,... | collective-permute-start | bytes 1769480 | tf_op jit(solution)/shard_map/ppermute | solution.py:61
  49.5 55.9 %collective-permute-start.6 = (bf16[192,1536]{1,0:T(8,128)(2,1)S(1)}, bf16[192,1536]{1,0:T(8,128)(2,1)S(1)}, u32[]{:S(2)}, u32[]{:S(2)}) collective-permute-start(bf16[192,1536]{1,0:T(8,128)(2,1)S(1)} %bitcast.217), channel_id=1, source_target_pairs={{0,7},{1,0},{2,1},{3,2},{4,3},{5,4},{6,5},{7,6},{8,15},{9,8},{10,9... | collective-permute-start | bytes 1769480 | tf_op jit(solution)/shard_map/ppermute | solution.py:61
  124.0 41.0 %copy-start.10 = (s32[2,1,1024]{2,1,0:T(1,128)S(1)}, s32[2,1,1024]{2,1,0:T(1,128)}, u32[]{:S(2)}) copy-start(s32[2,1,1024]{2,1,0:T(1,128)} %param.36) | copy-start | bytes 24580
  125.8 37.2 %all-to-all-start = ((bf16[16,2,9216]{2,1,0:T(2,128)(2,1)}), bf16[16,2,9216]{2,1,0:T(2,128)(2,1)S(1)}, u32[]{:S(2)}, u32[]{:S(2)}) async-start(bf16[16,2,9216]{2,1,0:T(2,128)(2,1)} %reshape.635), calls=%async_computation | async-start | bytes 1179648 | tf_op jit(solution)/shard_map/all_to_all | solution.py:122
  191.9 16.6 %collective-permute-start.7 = (bf16[1,64,1536]{2,1,0:T(8,128)(2,1)S(1)}, bf16[1,64,1536]{2,1,0:T(8,128)(2,1)S(1)}, u32[]{:S(2)}, u32[]{:S(2)}) collective-permute-start(bf16[1,64,1536]{2,1,0:T(8,128)(2,1)S(1)} %fusion.105), channel_id=1, source_target_pairs={{0,128},{128,256},{256,384},{1,129},{129,257},{257,385},{2,130},{1... | collective-permute-start | bytes 589832 | tf_op jit(solution)/shard_map/ppermute | solution.py:15
  210.1 3.8 copy-start.3
  218.3 32.7 %all-to-all-start.2 = ((bf16[16,2,9216]{2,1,0:T(2,128)(2,1)}), bf16[16,2,9216]{2,1,0:T(2,128)(2,1)S(1)}, u32[]{:S(2)}, u32[]{:S(2)}) async-start(bf16[16,2,9216]{2,1,0:T(2,128)(2,1)} %reshape.637), calls=%async_computation.2 | async-start | bytes 1179648 | tf_op jit(solution)/shard_map/all_to_all | solution.py:122
  279.9 5.7 collective-permute-start.8
  287.3 3.8 copy-start.4
  294.9 32.8 %all-to-all-start.4 = ((bf16[16,2,9216]{2,1,0:T(2,128)(2,1)}), bf16[16,2,9216]{2,1,0:T(2,128)(2,1)S(1)}, u32[]{:S(2)}, u32[]{:S(2)}) async-start(bf16[16,2,9216]{2,1,0:T(2,128)(2,1)} %reshape.639), calls=%async_computation.4 | async-start | bytes 1179648 | tf_op jit(solution)/shard_map/all_to_all | solution.py:122
  356.5 7.9 %collective-permute-start.9 = (bf16[1,64,1536]{2,1,0:T(8,128)(2,1)S(1)}, bf16[1,64,1536]{2,1,0:T(8,128)(2,1)S(1)}, u32[]{:S(2)}, u32[]{:S(2)}) collective-permute-start(bf16[1,64,1536]{2,1,0:T(8,128)(2,1)S(1)} %fusion.93), channel_id=1, source_target_pairs={{0,128},{128,256},{256,384},{1,129},{129,257},{257,385},{2,130},{1... | collective-permute-start | bytes 589832 | tf_op jit(solution)/shard_map/ppermute | solution.py:15
  367.6 31.3 %all-to-all-start.6 = ((bf16[16,2,9216]{2,1,0:T(2,128)(2,1)}), bf16[16,2,9216]{2,1,0:T(2,128)(2,1)S(1)}, u32[]{:S(2)}, u32[]{:S(2)}) async-start(bf16[16,2,9216]{2,1,0:T(2,128)(2,1)} %reshape.641), calls=%async_computation.6 | async-start | bytes 1179648 | tf_op jit(solution)/shard_map/all_to_all | solution.py:122
  424.9 19.6 %collective-permute-start.10 = (bf16[1,64,1536]{2,1,0:T(8,128)(2,1)S(1)}, bf16[1,64,1536]{2,1,0:T(8,128)(2,1)S(1)}, u32[]{:S(2)}, u32[]{:S(2)}) collective-permute-start(bf16[1,64,1536]{2,1,0:T(8,128)(2,1)S(1)} %fusion.97), channel_id=1, source_target_pairs={{0,128},{128,256},{256,384},{1,129},{129,257},{257,385},{2,130},{1... | collective-permute-start | bytes 589832 | tf_op jit(solution)/shard_map/ppermute | solution.py:15
  447.7 22.6 %all-to-all-start.8 = ((bf16[16,2,9216]{2,1,0:T(2,128)(2,1)}), bf16[16,2,9216]{2,1,0:T(2,128)(2,1)S(1)}, u32[]{:S(2)}, u32[]{:S(2)}) async-start(bf16[16,2,9216]{2,1,0:T(2,128)(2,1)} %reshape.643), calls=%async_computation.8 | async-start | bytes 1179648 | tf_op jit(solution)/shard_map/all_to_all | solution.py:122
  472.3 8.9 %copy-start.11 = (bf16[1536,16]{0,1:T(8,128)(2,1)S(1)}, bf16[1536,16]{0,1:T(8,128)(2,1)}, u32[]{:S(2)}) copy-start(bf16[1536,16]{0,1:T(8,128)(2,1)} %param.43) | copy-start | bytes 147460
  472.3 33.8 %copy-start.8 = (f32[2,1,64,64]{3,2,1,0:T(8,128)S(1)}, f32[2,1,64,64]{3,2,1,0:T(8,128)}, u32[]{:S(2)}) copy-start(f32[2,1,64,64]{3,2,1,0:T(8,128)} %param.33) | copy-start | bytes 98308
  472.3 33.9 %copy-start.9 = (f32[2,1,64,64]{3,2,1,0:T(8,128)S(1)}, f32[2,1,64,64]{3,2,1,0:T(8,128)}, u32[]{:S(2)}) copy-start(f32[2,1,64,64]{3,2,1,0:T(8,128)} %param.34) | copy-start | bytes 98308
  472.3 34.8 %copy-start.12 = (f32[1536]{0:T(1024)S(1)}, f32[1536]{0:T(1024)}, u32[]{:S(2)}) copy-start(f32[1536]{0:T(1024)} %param.42) | copy-start | bytes 18436
  473.2 33.0 %all-to-all-start.9 = ((bf16[16,64,96]{2,1,0:T(8,128)(2,1)}), bf16[16,64,96]{2,1,0:T(8,128)(2,1)S(1)}, u32[]{:S(2)}, u32[]{:S(2)}) async-start(bf16[16,64,96]{2,1,0:T(8,128)(2,1)} %bitcast.71), calls=%async_computation.9 | async-start | bytes 524288 | tf_op jit(solution)/shard_map/all_to_all | solution.py:131
  481.1 74.7 %reduce-scatter.4.cloned.1.call-start = ((), (), s32[]{:S(2)}) async-start(), calls=%async_computation.12 | async-start | bytes 884736
  481.2 25.9 %collective-permute-start.11 = (bf16[1536,16]{0,1:T(8,128)(2,1)S(1)}, bf16[1536,16]{0,1:T(8,128)(2,1)S(1)}, u32[]{:S(2)}, u32[]{:S(2)}) collective-permute-start(bf16[1536,16]{0,1:T(8,128)(2,1)S(1)} %copy-done.11), channel_id=1, source_target_pairs={{0,384},{1,385},{2,386},{3,387},{4,388},{5,389},{6,390},{7,391},{8... | collective-permute-start | bytes 147464 | tf_op jit(solution)/shard_map/ppermute | solution.py:70
  481.9 25.2 %collective-permute-start.12 = (bf16[1536,16]{0,1:T(8,128)(2,1)S(1)}, bf16[1536,16]{0,1:T(8,128)(2,1)S(1)}, u32[]{:S(2)}, u32[]{:S(2)}) collective-permute-start(bf16[1536,16]{0,1:T(8,128)(2,1)S(1)} %copy-done.11), channel_id=1, source_target_pairs={{128,384},{129,385},{130,386},{131,387},{132,388},{133,389},{134,3... | collective-permute-start | bytes 147464 | tf_op jit(solution)/shard_map/ppermute | solution.py:70
  505.4 1.7 collective-permute-start.13
  506.3 120.6 %copy-start.1 = (bf16[64,1536]{1,0:T(8,128)(2,1)S(1)}, bf16[64,1536]{1,0:T(8,128)(2,1)}, u32[]{:S(2)}) copy-start(bf16[64,1536]{1,0:T(8,128)(2,1)} %param.37) | copy-start | bytes 589828
  509.2 92.4 %collective-permute-start.14 = (f32[2,1,64,16]{2,3,0,1:T(8,128)S(1)}, f32[2,1,64,16]{2,3,0,1:T(8,128)S(1)}, u32[]{:S(2)}, u32[]{:S(2)}) collective-permute-start(f32[2,1,64,16]{2,3,0,1:T(8,128)S(1)} %get-tuple-element.330), channel_id=1, source_target_pairs={{384,0},{385,1},{386,2},{387,3},{388,4},{389,5},{390,6},{391,7},{3... | collective-permute-start | bytes 24584 | tf_op jit(solution)/shard_map/ppermute | solution.py:155
  509.9 92.4 %collective-permute-start.15 = (f32[2,1,64,16]{2,3,0,1:T(8,128)S(1)}, f32[2,1,64,16]{2,3,0,1:T(8,128)S(1)}, u32[]{:S(2)}, u32[]{:S(2)}) collective-permute-start(f32[2,1,64,16]{2,3,0,1:T(8,128)S(1)} %get-tuple-element.328), channel_id=1, source_target_pairs={{384,128},{385,129},{386,130},{387,131},{388,132},{389,133},{390,1... | collective-permute-start | bytes 24584 | tf_op jit(solution)/shard_map/ppermute | solution.py:155
  511.2 91.1 %collective-permute-start.16 = (f32[2,1,64,16]{2,3,0,1:T(8,128)S(1)}, f32[2,1,64,16]{2,3,0,1:T(8,128)S(1)}, u32[]{:S(2)}, u32[]{:S(2)}) collective-permute-start(f32[2,1,64,16]{2,3,0,1:T(8,128)S(1)} %get-tuple-element.329), channel_id=1, source_target_pairs={{384,256},{385,257},{386,258},{387,259},{388,260},{389,261},{390,2... | collective-permute-start | bytes 24584 | tf_op jit(solution)/shard_map/ppermute | solution.py:155
  599.6 3.3 collective-permute-start.17
  600.2 26.0 %collective-permute-start.18 = (f32[192,16]{0,1:T(8,128)S(1)}, f32[192,16]{0,1:T(8,128)S(1)}, u32[]{:S(2)}, u32[]{:S(2)}) collective-permute-start(f32[192,16]{0,1:T(8,128)S(1)} %get-tuple-element.325), channel_id=1, source_target_pairs={{384,128},{385,129},{386,130},{387,131},{388,132},{389,133},{390,1... | collective-permute-start | bytes 36872 | tf_op jit(solution)/shard_map/ppermute | solution.py:156
  601.5 24.7 %collective-permute-start.19 = (f32[192,16]{0,1:T(8,128)S(1)}, f32[192,16]{0,1:T(8,128)S(1)}, u32[]{:S(2)}, u32[]{:S(2)}) collective-permute-start(f32[192,16]{0,1:T(8,128)S(1)} %get-tuple-element.326), channel_id=1, source_target_pairs={{384,256},{385,257},{386,258},{387,259},{388,260},{389,261},{390,2... | collective-permute-start | bytes 36872 | tf_op jit(solution)/shard_map/ppermute | solution.py:156
Sparse Core Ops, SparseCore 0:
  10.1 112.7 all-gather.2
  509.3 46.5 reduce-scatter.3

commit v7 on v6

--- a/solution.py
+++ b/solution.py
@@ -145,18 +145,18 @@
     grad_all = jnp.einsum(
         "mbsd,mbsp->dp", final_norm.astype(jnp.float32), residue, precision=lax.Precision.HIGHEST
     ) / float(seq_total)
-    grad_rows = lax.psum_scatter(grad_all, "dp", scatter_dimension=0, tiled=True)
-    grad_rows = lax.psum(grad_rows, "ctx")
     velocity_in = jnp.zeros(velocity_all.shape[:3] + (head_cols,), jnp.float32)
-    gradient_in = jnp.zeros((grad_rows.shape[0], head_cols), jnp.float32)
+    gradient_in = jnp.zeros((model_width, head_cols), jnp.float32)
     for target_phase in range(last_phase):
         cols = slice(target_phase * head_cols, (target_phase + 1) * head_cols)
         pair = [(last_phase, target_phase)]
         velocity_in = velocity_in + lax.ppermute(velocity_all[..., cols], "pipe", pair)
-        gradient_in = gradient_in + lax.ppermute(grad_rows[:, cols], "pipe", pair)
+        gradient_in = gradient_in + lax.ppermute(grad_all[:, cols], "pipe", pair)
     own_cols = slice(last_phase * head_cols, phase_count * head_cols)
     velocity = jnp.where(is_last, velocity_all[..., own_cols], velocity_in)
-    gradient = jnp.where(is_last, grad_rows[:, own_cols], gradient_in)
+    gradient_cols = jnp.where(is_last, grad_all[:, own_cols], gradient_in)
+    gradient_rows = lax.psum_scatter(gradient_cols, "dp", scatter_dimension=0, tiled=True)
+    gradient = lax.psum(gradient_rows, "ctx")
     return (velocity, gradient)
 
 

time: 644 us -> 642 us (level)
  the two profiles are of different devices: /device:TPU:1 before, /device:TPU:16 now
where the time goes in v7:
time: 642 us; the launch traced here: 632 us
  waiting for transfers between devices  297 us (46%)
  blocking collectives  153 us (24%)
  starting transfers between devices  96.4 us (15%)
  local copies, waits for them, and re-layouts  45.8 us (7%)
  between operations  15.1 us (2%)
  matrix products  14.6 us (2%)
  other arithmetic  9.06 us (1%)
    all_to_all x5, waiting for transfers between devices, on_device(): lax.all_to_all(triple, 'ctx', split_axis=2, concat_axis=1, tiled=True)  138 us
    all_to_all x4, blocking collectives, on_device(): lax.all_to_all(mixed_heads, 'ctx', split_axis=0, concat_axis=1, tiled=True)  95.9 us
    psum x1, blocking collectives, on_device(): gradient = lax.psum(gradient_rows, 'ctx')  56.8 us
    ppermute x7, waiting for transfers between devices, on_device(): key_blocks.append(lax.ppermute(key_weight[0], 'dp', pairs))  55.3 us
    unnamed x3, waiting for transfers between devices  42.6 us
    all_to_all x5, starting transfers between devices, on_device(): lax.all_to_all(triple, 'ctx', split_axis=2, concat_axis=1, tiled=True)  40.5 us
    ppermute x4, waiting for transfers between devices, shifted(): lax.ppermute(value, axis, [(source, source + steps) for source in range(f...  31.5 us
    ppermute x7, starting transfers between devices, on_device(): key_blocks.append(lax.ppermute(key_weight[0], 'dp', pairs))  27.7 us
  transfers between devices with their start and end apart: 28, of which 19 were waited for; matrix products, arithmetic and copies ran while one was open for 3% of the time, Pallas kernels for 0%

profile of v7, /device:TPU:16, one launch (start us, length us, event | category | flops | bytes accessed | tf_op | source)
XLA Modules:
  0.0 632.0 jit_solution(2548463247191848409)
XLA Ops:
  7.9 3.4 collective-permute-start
  11.3 4.6 collective-permute-start.1
  16.0 4.1 collective-permute-start.2
  20.1 2.7 collective-permute-start.3
  22.7 3.2 collective-permute-start.4
  30.2 2.0 constant_dynamic-update-slice_fusion
  32.4 7.8 %collective-permute-start.5 = (bf16[192,1536]{1,0:T(8,128)(2,1)}, bf16[192,1536]{1,0:T(8,128)(2,1)S(1)}, u32[]{:S(2)}, u32[]{:S(2)}) collective-permute-start(bf16[192,1536]{1,0:T(8,128)(2,1)} %bitcast.216), channel_id=1, source_target_pairs={{0,6},{1,7},{2,0},{3,1},{4,2},{5,3},{6,4},{7,5},{8,14},{9,15},{10,... | collective-permute-start | bytes 1769480 | tf_op jit(solution)/shard_map/ppermute | solution.py:61
  40.2 1.9 bitcast_dynamic-update-slice_fusion.6
  42.2 9.9 %collective-permute-done.1 = bf16[192,1536]{1,0:T(8,128)(2,1)} collective-permute-done((bf16[192,1536]{1,0:T(8,128)(2,1)}, bf16[192,1536]{1,0:T(8,128)(2,1)}, u32[]{:S(2)}, u32[]{:S(2)}) %collective-permute-start.1) | collective-permute-done | bytes 589856 | tf_op jit(solution)/shard_map/ppermute | solution.py:61
  52.0 1.9 collective-permute-start.6
  53.9 2.0 bitcast_dynamic-update-slice_fusion.5
  55.9 5.1 collective-permute-done.2
  61.0 1.9 bitcast_dynamic-update-slice_fusion.4
  62.9 19.6 %collective-permute-done.3 = bf16[192,1536]{1,0:T(8,128)(2,1)S(1)} collective-permute-done((bf16[192,1536]{1,0:T(8,128)(2,1)}, bf16[192,1536]{1,0:T(8,128)(2,1)S(1)}, u32[]{:S(2)}, u32[]{:S(2)}) %collective-permute-start.3) | collective-permute-done | bytes 589856 | tf_op jit(solution)/shard_map/ppermute | solution.py:61
  84.3 10.7 %collective-permute-done.5 = bf16[192,1536]{1,0:T(8,128)(2,1)S(1)} collective-permute-done((bf16[192,1536]{1,0:T(8,128)(2,1)}, bf16[192,1536]{1,0:T(8,128)(2,1)S(1)}, u32[]{:S(2)}, u32[]{:S(2)}) %collective-permute-start.5) | collective-permute-done | bytes 589856 | tf_op jit(solution)/shard_map/ppermute | solution.py:61
  95.9 10.0 %collective-permute-done.6 = bf16[192,1536]{1,0:T(8,128)(2,1)S(1)} collective-permute-done((bf16[192,1536]{1,0:T(8,128)(2,1)S(1)}, bf16[192,1536]{1,0:T(8,128)(2,1)S(1)}, u32[]{:S(2)}, u32[]{:S(2)}) %collective-permute-start.6) | collective-permute-done | bytes 589856 | tf_op jit(solution)/shard_map/ppermute | solution.py:61
  106.8 16.2 %all-gather.3.cloned.1.call-done = bf16[1,1536,1536]{2,1,0:T(8,128)(2,1)} async-done(((bf16[1,192,1536]{2,1,0:T(8,128)(2,1)}), bf16[1,1536,1536]{2,1,0:T(8,128)(2,1)}) %all-gather.3.cloned.1.call-update) | async-done | bytes 4718608 | tf_op jit(solution)/shard_map/all_gather | solution.py:57
  124.1 1.8 reshape.635
  125.9 14.6 %all-to-all-start = ((bf16[16,2,9216]{2,1,0:T(2,128)(2,1)}), bf16[16,2,9216]{2,1,0:T(2,128)(2,1)S(1)}, u32[]{:S(2)}, u32[]{:S(2)}) async-start(bf16[16,2,9216]{2,1,0:T(2,128)(2,1)} %reshape.635), calls=%async_computation | async-start | bytes 1179648 | tf_op jit(solution)/shard_map/all_to_all | solution.py:122
  140.5 30.8 %all-to-all-done = bf16[16,2,9216]{2,1,0:T(2,128)(2,1)S(1)} async-done(((bf16[16,2,9216]{2,1,0:T(2,128)(2,1)}), bf16[16,2,9216]{2,1,0:T(2,128)(2,1)S(1)}, u32[]{:S(2)}, u32[]{:S(2)}) %all-to-all-start) | async-done | bytes 589856 | tf_op jit(solution)/shard_map/all_to_all | solution.py:122
  173.5 25.5 %all_to_all.145 = bf16[16,64,96]{2,1,0:T(8,128)(2,1)S(1)} all-to-all(bf16[16,64,96]{2,1,0:T(8,128)(2,1)S(1)} %bitcast.205), channel_id=1, replica_groups=mesh['pipe'=4,'ctx'=16,'dp'=8] {'ctx'}, dimensions={0} | all-to-all | bytes 393216 | tf_op jit(solution)/shard_map/all_to_all | solution.py:131
  199.6 1.9 collective-permute-start.7
  201.5 6.6 %collective-permute-done.7 = bf16[1,64,1536]{2,1,0:T(8,128)(2,1)S(1)} collective-permute-done((bf16[1,64,1536]{2,1,0:T(8,128)(2,1)S(1)}, bf16[1,64,1536]{2,1,0:T(8,128)(2,1)S(1)}, u32[]{:S(2)}, u32[]{:S(2)}) %collective-permute-start.7) | collective-permute-done | bytes 196640 | tf_op jit(solution)/shard_map/ppermute | solution.py:15
  210.0 1.8 reshape.637
  211.8 5.9 all-to-all-start.2
  217.7 26.1 %all-to-all-done.2 = bf16[16,2,9216]{2,1,0:T(2,128)(2,1)S(1)} async-done(((bf16[16,2,9216]{2,1,0:T(2,128)(2,1)}), bf16[16,2,9216]{2,1,0:T(2,128)(2,1)S(1)}, u32[]{:S(2)}, u32[]{:S(2)}) %all-to-all-start.2) | async-done | bytes 589856 | tf_op jit(solution)/shard_map/all_to_all | solution.py:122
  246.0 23.5 %all_to_all.146 = bf16[16,64,96]{2,1,0:T(8,128)(2,1)S(1)} all-to-all(bf16[16,64,96]{2,1,0:T(8,128)(2,1)S(1)} %bitcast.206), channel_id=1, replica_groups=mesh['pipe'=4,'ctx'=16,'dp'=8] {'ctx'}, dimensions={0} | all-to-all | bytes 393216 | tf_op jit(solution)/shard_map/all_to_all | solution.py:131
  270.1 1.9 collective-permute-start.8
  272.1 12.0 %collective-permute-done.8 = bf16[1,64,1536]{2,1,0:T(8,128)(2,1)S(1)} collective-permute-done((bf16[1,64,1536]{2,1,0:T(8,128)(2,1)S(1)}, bf16[1,64,1536]{2,1,0:T(8,128)(2,1)S(1)}, u32[]{:S(2)}, u32[]{:S(2)}) %collective-permute-start.8) | collective-permute-done | bytes 196640 | tf_op jit(solution)/shard_map/ppermute | solution.py:15
  284.4 6.2 conditional.14
  285.8 3.4 fusion.76
  291.6 1.8 reshape.639
  293.4 9.1 %all-to-all-start.4 = ((bf16[16,2,9216]{2,1,0:T(2,128)(2,1)}), bf16[16,2,9216]{2,1,0:T(2,128)(2,1)S(1)}, u32[]{:S(2)}, u32[]{:S(2)}) async-start(bf16[16,2,9216]{2,1,0:T(2,128)(2,1)} %reshape.639), calls=%async_computation.4 | async-start | bytes 1179648 | tf_op jit(solution)/shard_map/all_to_all | solution.py:122
  302.5 22.7 %all-to-all-done.4 = bf16[16,2,9216]{2,1,0:T(2,128)(2,1)S(1)} async-done(((bf16[16,2,9216]{2,1,0:T(2,128)(2,1)}), bf16[16,2,9216]{2,1,0:T(2,128)(2,1)S(1)}, u32[]{:S(2)}, u32[]{:S(2)}) %all-to-all-start.4) | async-done | bytes 589856 | tf_op jit(solution)/shard_map/all_to_all | solution.py:122
  327.2 4.0 conditional.15
  328.4 1.5 fusion.29
  330.0 1.2 fusion.36
  331.4 23.5 %all_to_all.147 = bf16[16,64,96]{2,1,0:T(8,128)(2,1)S(1)} all-to-all(bf16[16,64,96]{2,1,0:T(8,128)(2,1)S(1)} %bitcast.207), channel_id=1, replica_groups=mesh['pipe'=4,'ctx'=16,'dp'=8] {'ctx'}, dimensions={0} | all-to-all | bytes 393216 | tf_op jit(solution)/shard_map/all_to_all | solution.py:131
  355.5 1.9 collective-permute-start.9
  357.5 6.6 %collective-permute-done.9 = bf16[1,64,1536]{2,1,0:T(8,128)(2,1)S(1)} collective-permute-done((bf16[1,64,1536]{2,1,0:T(8,128)(2,1)S(1)}, bf16[1,64,1536]{2,1,0:T(8,128)(2,1)S(1)}, u32[]{:S(2)}, u32[]{:S(2)}) %collective-permute-start.9) | collective-permute-done | bytes 196640 | tf_op jit(solution)/shard_map/ppermute | solution.py:15
  364.3 6.2 conditional.16
  365.7 3.4 fusion.79
  371.6 1.8 reshape.641
  373.4 6.1 all-to-all-start.6
  379.5 26.1 %all-to-all-done.6 = bf16[16,2,9216]{2,1,0:T(2,128)(2,1)S(1)} async-done(((bf16[16,2,9216]{2,1,0:T(2,128)(2,1)}), bf16[16,2,9216]{2,1,0:T(2,128)(2,1)S(1)}, u32[]{:S(2)}, u32[]{:S(2)}) %all-to-all-start.6) | async-done | bytes 589856 | tf_op jit(solution)/shard_map/all_to_all | solution.py:122
  407.5 3.8 conditional.17
  408.6 1.5 fusion.43
  410.2 1.2 fusion.50
  411.5 23.5 %all_to_all.148 = bf16[16,64,96]{2,1,0:T(8,128)(2,1)S(1)} all-to-all(bf16[16,64,96]{2,1,0:T(8,128)(2,1)S(1)} %bitcast.208), channel_id=1, replica_groups=mesh['pipe'=4,'ctx'=16,'dp'=8] {'ctx'}, dimensions={0} | all-to-all | bytes 393216 | tf_op jit(solution)/shard_map/all_to_all | solution.py:131
  435.7 2.1 collective-permute-start.10
  437.8 6.3 %collective-permute-done.10 = bf16[1,64,1536]{2,1,0:T(8,128)(2,1)S(1)} collective-permute-done((bf16[1,64,1536]{2,1,0:T(8,128)(2,1)S(1)}, bf16[1,64,1536]{2,1,0:T(8,128)(2,1)S(1)}, u32[]{:S(2)}, u32[]{:S(2)}) %collective-permute-start.10) | collective-permute-done | bytes 196640 | tf_op jit(solution)/shard_map/ppermute | solution.py:15
  445.6 1.8 reshape.643
  447.4 4.9 all-to-all-start.8
  452.4 32.5 %all-to-all-done.8 = bf16[16,2,9216]{2,1,0:T(2,128)(2,1)S(1)} async-done(((bf16[16,2,9216]{2,1,0:T(2,128)(2,1)}), bf16[16,2,9216]{2,1,0:T(2,128)(2,1)S(1)}, u32[]{:S(2)}, u32[]{:S(2)}) %all-to-all-start.8) | async-done | bytes 589856 | tf_op jit(solution)/shard_map/all_to_all | solution.py:122
  487.8 6.8 %all-to-all-start.9 = ((bf16[16,64,96]{2,1,0:T(8,128)(2,1)}), bf16[16,64,96]{2,1,0:T(8,128)(2,1)S(1)}, u32[]{:S(2)}, u32[]{:S(2)}) async-start(bf16[16,64,96]{2,1,0:T(8,128)(2,1)} %bitcast.71), calls=%async_computation.9 | async-start | bytes 524288 | tf_op jit(solution)/shard_map/all_to_all | solution.py:131
  496.0 6.8 %collective-permute-start.13 = (bf16[1536,16]{0,1:T(8,128)(2,1)S(1)}, bf16[1536,16]{0,1:T(8,128)(2,1)S(1)}, u32[]{:S(2)}, u32[]{:S(2)}) collective-permute-start(bf16[1536,16]{0,1:T(8,128)(2,1)S(1)} %copy-done.11), channel_id=1, source_target_pairs={{256,384},{257,385},{258,386},{259,387},{260,388},{261,389},{262,3... | collective-permute-start | bytes 147464 | tf_op jit(solution)/shard_map/ppermute | solution.py:70
  503.0 5.5 all-to-all-done.9
  511.5 1.3 collective-permute-start.19
  514.2 1.3 collective-permute-start.16
  515.5 5.4 collective-permute-done.19
  520.9 1.2 copy.110
  522.1 2.6 collective-permute-done.16
  525.3 41.9 %reduce-scatter.4.cloned.1.call-done = f32[192,16]{1,0:T(8,128)} async-done(((f32[1536,16]{1,0:T(8,128)}), f32[192,16]{1,0:T(8,128)}) %reduce-scatter.4.cloned.1.call-update) | async-done | bytes 12304
  568.1 56.8 %psum.7 = f32[192,16]{0,1:T(8,128)} all-reduce(f32[192,16]{0,1:T(8,128)S(1)} %copy.111), channel_id=1, replica_groups=mesh['pipe'=4,'ctx'=16,'dp'=8] {'ctx'}, use_global_device_ids=true, to_apply=%region_37.39 | all-reduce | flops 3072 | bytes 24576 | tf_op jit(solution)/shard_map/psum | solution.py:159
  (158 shorter events, 44.6 us)
Async XLA Ops:
  7.2 21.6 %copy-start = (bf16[64,1536]{1,0:T(8,128)(2,1)S(1)}, bf16[64,1536]{1,0:T(8,128)(2,1)}, u32[]{:S(2)}) copy-start(bf16[64,1536]{1,0:T(8,128)(2,1)} %param.37) | copy-start | bytes 589828
  7.2 44.8 %copy-start.7 = (bf16[1,192,1536]{2,1,0:T(8,128)(2,1)S(1)}, bf16[1,192,1536]{2,1,0:T(8,128)(2,1)}, u32[]{:S(2)}) copy-start(bf16[1,192,1536]{2,1,0:T(8,128)(2,1)} %param.40) | copy-start | bytes 1769476
  7.2 115.8 %all-gather.3.cloned.1.call-start = ((), (), s32[]{:S(2)}) async-start(), calls=%async_computation.11 | async-start | bytes 5308416 | tf_op jit(solution)/shard_map/all_gather | solution.py:57
  7.9 24.4 %collective-permute-start = (bf16[192,1536]{1,0:T(8,128)(2,1)}, bf16[192,1536]{1,0:T(8,128)(2,1)}, u32[]{:S(2)}, u32[]{:S(2)}) collective-permute-start(bf16[192,1536]{1,0:T(8,128)(2,1)} %bitcast.211), channel_id=1, source_target_pairs={{0,1},{1,2},{2,3},{3,4},{4,5},{5,6},{6,7},{7,0},{8,9},{9,10},{10,1... | collective-permute-start | bytes 1769480 | tf_op jit(solution)/shard_map/ppermute | solution.py:61
  11.3 40.7 %collective-permute-start.1 = (bf16[192,1536]{1,0:T(8,128)(2,1)}, bf16[192,1536]{1,0:T(8,128)(2,1)}, u32[]{:S(2)}, u32[]{:S(2)}) collective-permute-start(bf16[192,1536]{1,0:T(8,128)(2,1)} %bitcast.212), channel_id=1, source_target_pairs={{0,2},{1,3},{2,4},{3,5},{4,6},{5,7},{6,0},{7,1},{8,10},{9,11},{10,... | collective-permute-start | bytes 1769480 | tf_op jit(solution)/shard_map/ppermute | solution.py:61
  16.0 45.0 %collective-permute-start.2 = (bf16[192,1536]{1,0:T(8,128)(2,1)}, bf16[192,1536]{1,0:T(8,128)(2,1)}, u32[]{:S(2)}, u32[]{:S(2)}) collective-permute-start(bf16[192,1536]{1,0:T(8,128)(2,1)} %bitcast.213), channel_id=1, source_target_pairs={{0,3},{1,4},{2,5},{3,6},{4,7},{5,0},{6,1},{7,2},{8,11},{9,12},{10,... | collective-permute-start | bytes 1769480 | tf_op jit(solution)/shard_map/ppermute | solution.py:61
  20.1 62.5 %collective-permute-start.3 = (bf16[192,1536]{1,0:T(8,128)(2,1)}, bf16[192,1536]{1,0:T(8,128)(2,1)S(1)}, u32[]{:S(2)}, u32[]{:S(2)}) collective-permute-start(bf16[192,1536]{1,0:T(8,128)(2,1)} %bitcast.214), channel_id=1, source_target_pairs={{0,4},{1,5},{2,6},{3,7},{4,0},{5,1},{6,2},{7,3},{8,12},{9,13},{10,... | collective-permute-start | bytes 1769480 | tf_op jit(solution)/shard_map/ppermute | solution.py:61
  22.7 60.7 %collective-permute-start.4 = (bf16[192,1536]{1,0:T(8,128)(2,1)}, bf16[192,1536]{1,0:T(8,128)(2,1)S(1)}, u32[]{:S(2)}, u32[]{:S(2)}) collective-permute-start(bf16[192,1536]{1,0:T(8,128)(2,1)} %bitcast.215), channel_id=1, source_target_pairs={{0,5},{1,6},{2,7},{3,0},{4,1},{5,2},{6,3},{7,4},{8,13},{9,14},{10,... | collective-permute-start | bytes 1769480 | tf_op jit(solution)/shard_map/ppermute | solution.py:61
  32.4 62.6 %collective-permute-start.5 = (bf16[192,1536]{1,0:T(8,128)(2,1)}, bf16[192,1536]{1,0:T(8,128)(2,1)S(1)}, u32[]{:S(2)}, u32[]{:S(2)}) collective-permute-start(bf16[192,1536]{1,0:T(8,128)(2,1)} %bitcast.216), channel_id=1, source_target_pairs={{0,6},{1,7},{2,0},{3,1},{4,2},{5,3},{6,4},{7,5},{8,14},{9,15},{10,... | collective-permute-start | bytes 1769480 | tf_op jit(solution)/shard_map/ppermute | solution.py:61
  52.0 53.9 %collective-permute-start.6 = (bf16[192,1536]{1,0:T(8,128)(2,1)S(1)}, bf16[192,1536]{1,0:T(8,128)(2,1)S(1)}, u32[]{:S(2)}, u32[]{:S(2)}) collective-permute-start(bf16[192,1536]{1,0:T(8,128)(2,1)S(1)} %bitcast.217), channel_id=1, source_target_pairs={{0,7},{1,0},{2,1},{3,2},{4,3},{5,4},{6,5},{7,6},{8,15},{9,8},{10,9... | collective-permute-start | bytes 1769480 | tf_op jit(solution)/shard_map/ppermute | solution.py:61
  124.1 49.2 %copy-start.10 = (s32[2,1,1024]{2,1,0:T(1,128)S(1)}, s32[2,1,1024]{2,1,0:T(1,128)}, u32[]{:S(2)}) copy-start(s32[2,1,1024]{2,1,0:T(1,128)} %param.36) | copy-start | bytes 24580
  125.9 45.4 %all-to-all-start = ((bf16[16,2,9216]{2,1,0:T(2,128)(2,1)}), bf16[16,2,9216]{2,1,0:T(2,128)(2,1)S(1)}, u32[]{:S(2)}, u32[]{:S(2)}) async-start(bf16[16,2,9216]{2,1,0:T(2,128)(2,1)} %reshape.635), calls=%async_computation | async-start | bytes 1179648 | tf_op jit(solution)/shard_map/all_to_all | solution.py:122
  199.6 8.5 %collective-permute-start.7 = (bf16[1,64,1536]{2,1,0:T(8,128)(2,1)S(1)}, bf16[1,64,1536]{2,1,0:T(8,128)(2,1)S(1)}, u32[]{:S(2)}, u32[]{:S(2)}) collective-permute-start(bf16[1,64,1536]{2,1,0:T(8,128)(2,1)S(1)} %fusion.105), channel_id=1, source_target_pairs={{0,128},{128,256},{256,384},{1,129},{129,257},{257,385},{2,130},{1... | collective-permute-start | bytes 589832 | tf_op jit(solution)/shard_map/ppermute | solution.py:15
  211.8 32.0 %all-to-all-start.2 = ((bf16[16,2,9216]{2,1,0:T(2,128)(2,1)}), bf16[16,2,9216]{2,1,0:T(2,128)(2,1)S(1)}, u32[]{:S(2)}, u32[]{:S(2)}) async-start(bf16[16,2,9216]{2,1,0:T(2,128)(2,1)} %reshape.637), calls=%async_computation.2 | async-start | bytes 1179648 | tf_op jit(solution)/shard_map/all_to_all | solution.py:122
  270.1 13.9 %collective-permute-start.8 = (bf16[1,64,1536]{2,1,0:T(8,128)(2,1)S(1)}, bf16[1,64,1536]{2,1,0:T(8,128)(2,1)S(1)}, u32[]{:S(2)}, u32[]{:S(2)}) collective-permute-start(bf16[1,64,1536]{2,1,0:T(8,128)(2,1)S(1)} %fusion.89), channel_id=1, source_target_pairs={{0,128},{128,256},{256,384},{1,129},{129,257},{257,385},{2,130},{1... | collective-permute-start | bytes 589832 | tf_op jit(solution)/shard_map/ppermute | solution.py:15
  285.8 3.8 copy-start.4
  293.4 31.8 %all-to-all-start.4 = ((bf16[16,2,9216]{2,1,0:T(2,128)(2,1)}), bf16[16,2,9216]{2,1,0:T(2,128)(2,1)S(1)}, u32[]{:S(2)}, u32[]{:S(2)}) async-start(bf16[16,2,9216]{2,1,0:T(2,128)(2,1)} %reshape.639), calls=%async_computation.4 | async-start | bytes 1179648 | tf_op jit(solution)/shard_map/all_to_all | solution.py:122
  355.5 8.5 %collective-permute-start.9 = (bf16[1,64,1536]{2,1,0:T(8,128)(2,1)S(1)}, bf16[1,64,1536]{2,1,0:T(8,128)(2,1)S(1)}, u32[]{:S(2)}, u32[]{:S(2)}) collective-permute-start(bf16[1,64,1536]{2,1,0:T(8,128)(2,1)S(1)} %fusion.93), channel_id=1, source_target_pairs={{0,128},{128,256},{256,384},{1,129},{129,257},{257,385},{2,130},{1... | collective-permute-start | bytes 589832 | tf_op jit(solution)/shard_map/ppermute | solution.py:15
  365.7 3.8 copy-start.5
  373.4 32.2 %all-to-all-start.6 = ((bf16[16,2,9216]{2,1,0:T(2,128)(2,1)}), bf16[16,2,9216]{2,1,0:T(2,128)(2,1)S(1)}, u32[]{:S(2)}, u32[]{:S(2)}) async-start(bf16[16,2,9216]{2,1,0:T(2,128)(2,1)} %reshape.641), calls=%async_computation.6 | async-start | bytes 1179648 | tf_op jit(solution)/shard_map/all_to_all | solution.py:122
  435.7 8.5 %collective-permute-start.10 = (bf16[1,64,1536]{2,1,0:T(8,128)(2,1)S(1)}, bf16[1,64,1536]{2,1,0:T(8,128)(2,1)S(1)}, u32[]{:S(2)}, u32[]{:S(2)}) collective-permute-start(bf16[1,64,1536]{2,1,0:T(8,128)(2,1)S(1)} %fusion.97), channel_id=1, source_target_pairs={{0,128},{128,256},{256,384},{1,129},{129,257},{257,385},{2,130},{1... | collective-permute-start | bytes 589832 | tf_op jit(solution)/shard_map/ppermute | solution.py:15
  447.4 37.4 %all-to-all-start.8 = ((bf16[16,2,9216]{2,1,0:T(2,128)(2,1)}), bf16[16,2,9216]{2,1,0:T(2,128)(2,1)S(1)}, u32[]{:S(2)}, u32[]{:S(2)}) async-start(bf16[16,2,9216]{2,1,0:T(2,128)(2,1)} %reshape.643), calls=%async_computation.8 | async-start | bytes 1179648 | tf_op jit(solution)/shard_map/all_to_all | solution.py:122
  486.8 7.8 %copy-start.11 = (bf16[1536,16]{0,1:T(8,128)(2,1)S(1)}, bf16[1536,16]{0,1:T(8,128)(2,1)}, u32[]{:S(2)}) copy-start(bf16[1536,16]{0,1:T(8,128)(2,1)} %param.43) | copy-start | bytes 147460
  486.8 15.9 %copy-start.8 = (f32[2,1,64,64]{3,2,1,0:T(8,128)S(1)}, f32[2,1,64,64]{3,2,1,0:T(8,128)}, u32[]{:S(2)}) copy-start(f32[2,1,64,64]{3,2,1,0:T(8,128)} %param.33) | copy-start | bytes 98308
  486.8 16.0 %copy-start.9 = (f32[2,1,64,64]{3,2,1,0:T(8,128)S(1)}, f32[2,1,64,64]{3,2,1,0:T(8,128)}, u32[]{:S(2)}) copy-start(f32[2,1,64,64]{3,2,1,0:T(8,128)} %param.34) | copy-start | bytes 98308
  486.9 22.4 %copy-start.12 = (f32[1536]{0:T(1024)S(1)}, f32[1536]{0:T(1024)}, u32[]{:S(2)}) copy-start(f32[1536]{0:T(1024)} %param.42) | copy-start | bytes 18436
  487.8 20.7 %all-to-all-start.9 = ((bf16[16,64,96]{2,1,0:T(8,128)(2,1)}), bf16[16,64,96]{2,1,0:T(8,128)(2,1)S(1)}, u32[]{:S(2)}, u32[]{:S(2)}) async-start(bf16[16,64,96]{2,1,0:T(8,128)(2,1)} %bitcast.71), calls=%async_computation.9 | async-start | bytes 524288 | tf_op jit(solution)/shard_map/all_to_all | solution.py:131
  494.6 72.6 %reduce-scatter.4.cloned.1.call-start = ((), (), s32[]{:S(2)}) async-start(), calls=%async_computation.12 | async-start | bytes 884736
  494.6 14.6 %collective-permute-start.11 = (bf16[1536,16]{0,1:T(8,128)(2,1)S(1)}, bf16[1536,16]{0,1:T(8,128)(2,1)S(1)}, u32[]{:S(2)}, u32[]{:S(2)}) collective-permute-start(bf16[1536,16]{0,1:T(8,128)(2,1)S(1)} %copy-done.11), channel_id=1, source_target_pairs={{0,384},{1,385},{2,386},{3,387},{4,388},{5,389},{6,390},{7,391},{8... | collective-permute-start | bytes 147464 | tf_op jit(solution)/shard_map/ppermute | solution.py:70
  495.3 14.0 %collective-permute-start.12 = (bf16[1536,16]{0,1:T(8,128)(2,1)S(1)}, bf16[1536,16]{0,1:T(8,128)(2,1)S(1)}, u32[]{:S(2)}, u32[]{:S(2)}) collective-permute-start(bf16[1536,16]{0,1:T(8,128)(2,1)S(1)} %copy-done.11), channel_id=1, source_target_pairs={{128,384},{129,385},{130,386},{131,387},{132,388},{133,389},{134,3... | collective-permute-start | bytes 147464 | tf_op jit(solution)/shard_map/ppermute | solution.py:70
  496.0 13.3 %collective-permute-start.13 = (bf16[1536,16]{0,1:T(8,128)(2,1)S(1)}, bf16[1536,16]{0,1:T(8,128)(2,1)S(1)}, u32[]{:S(2)}, u32[]{:S(2)}) collective-permute-start(bf16[1536,16]{0,1:T(8,128)(2,1)S(1)} %copy-done.11), channel_id=1, source_target_pairs={{256,384},{257,385},{258,386},{259,387},{260,388},{261,389},{262,3... | collective-permute-start | bytes 147464 | tf_op jit(solution)/shard_map/ppermute | solution.py:70
  508.5 116.5 %copy-start.1 = (bf16[64,1536]{1,0:T(8,128)(2,1)S(1)}, bf16[64,1536]{1,0:T(8,128)(2,1)}, u32[]{:S(2)}) copy-start(bf16[64,1536]{1,0:T(8,128)(2,1)} %param.37) | copy-start | bytes 589828
  510.2 4.0 collective-permute-start.17
  510.8 4.6 collective-permute-start.18
  511.5 9.4 %collective-permute-start.19 = (f32[1536,16]{0,1:T(8,128)S(1)}, f32[1536,16]{0,1:T(8,128)S(1)}, u32[]{:S(2)}, u32[]{:S(2)}) collective-permute-start(f32[1536,16]{0,1:T(8,128)S(1)} %get-tuple-element.326), channel_id=1, source_target_pairs={{384,256},{385,257},{386,258},{387,259},{388,260},{389,261},{390,2... | collective-permute-start | bytes 294920 | tf_op jit(solution)/shard_map/ppermute | solution.py:154
  512.8 9.3 %collective-permute-start.14 = (f32[2,1,64,16]{2,3,0,1:T(8,128)S(1)}, f32[2,1,64,16]{2,3,0,1:T(8,128)S(1)}, u32[]{:S(2)}, u32[]{:S(2)}) collective-permute-start(f32[2,1,64,16]{2,3,0,1:T(8,128)S(1)} %get-tuple-element.330), channel_id=1, source_target_pairs={{384,0},{385,1},{386,2},{387,3},{388,4},{389,5},{390,6},{391,7},{3... | collective-permute-start | bytes 24584 | tf_op jit(solution)/shard_map/ppermute | solution.py:153
  513.5 8.6 %collective-permute-start.15 = (f32[2,1,64,16]{2,3,0,1:T(8,128)S(1)}, f32[2,1,64,16]{2,3,0,1:T(8,128)S(1)}, u32[]{:S(2)}, u32[]{:S(2)}) collective-permute-start(f32[2,1,64,16]{2,3,0,1:T(8,128)S(1)} %get-tuple-element.328), channel_id=1, source_target_pairs={{384,128},{385,129},{386,130},{387,131},{388,132},{389,133},{390,1... | collective-permute-start | bytes 24584 | tf_op jit(solution)/shard_map/ppermute | solution.py:153
  514.2 10.5 %collective-permute-start.16 = (f32[2,1,64,16]{2,3,0,1:T(8,128)S(1)}, f32[2,1,64,16]{2,3,0,1:T(8,128)S(1)}, u32[]{:S(2)}, u32[]{:S(2)}) collective-permute-start(f32[2,1,64,16]{2,3,0,1:T(8,128)S(1)} %get-tuple-element.329), channel_id=1, source_target_pairs={{384,256},{385,257},{386,258},{387,259},{388,260},{389,261},{390,2... | collective-permute-start | bytes 24584 | tf_op jit(solution)/shard_map/ppermute | solution.py:153
Sparse Core Ops, SparseCore 0:
  10.1 112.8 all-gather.2
  522.2 44.9 reduce-scatter.3

commit v8 on v7

--- a/solution.py
+++ b/solution.py
@@ -146,17 +146,15 @@
         "mbsd,mbsp->dp", final_norm.astype(jnp.float32), residue, precision=lax.Precision.HIGHEST
     ) / float(seq_total)
     velocity_in = jnp.zeros(velocity_all.shape[:3] + (head_cols,), jnp.float32)
-    gradient_in = jnp.zeros((model_width, head_cols), jnp.float32)
     for target_phase in range(last_phase):
         cols = slice(target_phase * head_cols, (target_phase + 1) * head_cols)
         pair = [(last_phase, target_phase)]
         velocity_in = velocity_in + lax.ppermute(velocity_all[..., cols], "pipe", pair)
-        gradient_in = gradient_in + lax.ppermute(grad_all[:, cols], "pipe", pair)
     own_cols = slice(last_phase * head_cols, phase_count * head_cols)
     velocity = jnp.where(is_last, velocity_all[..., own_cols], velocity_in)
-    gradient_cols = jnp.where(is_last, grad_all[:, own_cols], gradient_in)
-    gradient_rows = lax.psum_scatter(gradient_cols, "dp", scatter_dimension=0, tiled=True)
-    gradient = lax.psum(gradient_rows, "ctx")
+    grad_rows = lax.psum_scatter(grad_all, "dp", scatter_dimension=0, tiled=True)
+    grad_rows = lax.psum(jnp.where(is_last, grad_rows, 0.0), ("ctx", "pipe"))
+    gradient = lax.dynamic_slice_in_dim(grad_rows, phase_index * head_cols, head_cols, 1)
     return (velocity, gradient)
 
 

time: 642 us -> 833 us (1.30)
  the two profiles are of different devices: /device:TPU:16 before, /device:TPU:1 now
where the time goes in v8:
time: 833 us; the launch traced here: 821 us
  blocking collectives  350 us (42%)
  waiting for transfers between devices  249 us (30%)
  starting transfers between devices  136 us (16%)
  local copies, waits for them, and re-layouts  46.4 us (6%)
  between operations  15.1 us (2%)
  matrix products  14.6 us (2%)
  other arithmetic  9.05 us (1%)
    psum x1, blocking collectives, on_device(): grad_rows = lax.psum(jnp.where(is_last, grad_rows, 0.0), ('ctx', 'pipe'))  256 us
    all_to_all x5, waiting for transfers between devices, on_device(): lax.all_to_all(triple, 'ctx', split_axis=2, concat_axis=1, tiled=True)  117 us
    all_to_all x4, blocking collectives, on_device(): lax.all_to_all(mixed_heads, 'ctx', split_axis=0, concat_axis=1, tiled=True)  93.4 us
    ppermute x7, waiting for transfers between devices, on_device(): key_blocks.append(lax.ppermute(key_weight[0], 'dp', pairs))  59.6 us
    all_to_all x5, starting transfers between devices, on_device(): lax.all_to_all(triple, 'ctx', split_axis=2, concat_axis=1, tiled=True)  39.3 us
    ppermute x4, starting transfers between devices, shifted(): lax.ppermute(value, axis, [(source, source + steps) for source in range(f...  38.4 us
    unnamed x3, waiting for transfers between devices  30.8 us
    unnamed x37, local copies, waits for them, and re-layouts  26.7 us
  transfers between devices with their start and end apart: 25, of which 16 were waited for; matrix products, arithmetic and copies ran while one was open for 2% of the time, Pallas kernels for 0%

profile of v8, /device:TPU:1, one launch (start us, length us, event | category | flops | bytes accessed | tf_op | source)
XLA Modules:
  0.0 820.5 jit_solution(14728570842247084500)
XLA Ops:
  7.9 4.0 collective-permute-start
  11.9 4.4 collective-permute-start.1
  16.3 4.1 collective-permute-start.2
  20.3 2.1 collective-permute-start.3
  22.4 3.2 collective-permute-start.4
  28.5 1.2 fusion.84
  29.9 1.9 constant_dynamic-update-slice_fusion
  32.0 3.3 collective-permute-start.5
  35.4 1.9 bitcast_dynamic-update-slice_fusion.6
  37.3 12.2 %collective-permute-done.1 = bf16[192,1536]{1,0:T(8,128)(2,1)} collective-permute-done((bf16[192,1536]{1,0:T(8,128)(2,1)}, bf16[192,1536]{1,0:T(8,128)(2,1)}, u32[]{:S(2)}, u32[]{:S(2)}) %collective-permute-start.1) | collective-permute-done | bytes 589856 | tf_op jit(solution)/shard_map/ppermute | solution.py:61
  49.5 1.9 collective-permute-start.6
  51.4 1.9 bitcast_dynamic-update-slice_fusion.5
  53.3 1.9 bitcast_dynamic-update-slice_fusion.4
  55.2 28.6 %collective-permute-done.3 = bf16[192,1536]{1,0:T(8,128)(2,1)S(1)} collective-permute-done((bf16[192,1536]{1,0:T(8,128)(2,1)}, bf16[192,1536]{1,0:T(8,128)(2,1)S(1)}, u32[]{:S(2)}, u32[]{:S(2)}) %collective-permute-start.3) | collective-permute-done | bytes 589856 | tf_op jit(solution)/shard_map/ppermute | solution.py:61
  85.6 10.5 %collective-permute-done.5 = bf16[192,1536]{1,0:T(8,128)(2,1)S(1)} collective-permute-done((bf16[192,1536]{1,0:T(8,128)(2,1)}, bf16[192,1536]{1,0:T(8,128)(2,1)S(1)}, u32[]{:S(2)}, u32[]{:S(2)}) %collective-permute-start.5) | collective-permute-done | bytes 589856 | tf_op jit(solution)/shard_map/ppermute | solution.py:61
  97.0 8.4 %collective-permute-done.6 = bf16[192,1536]{1,0:T(8,128)(2,1)S(1)} collective-permute-done((bf16[192,1536]{1,0:T(8,128)(2,1)S(1)}, bf16[192,1536]{1,0:T(8,128)(2,1)S(1)}, u32[]{:S(2)}, u32[]{:S(2)}) %collective-permute-start.6) | collective-permute-done | bytes 589856 | tf_op jit(solution)/shard_map/ppermute | solution.py:61
  106.2 16.7 %all-gather.3.cloned.1.call-done = bf16[1,1536,1536]{2,1,0:T(8,128)(2,1)} async-done(((bf16[1,192,1536]{2,1,0:T(8,128)(2,1)}), bf16[1,1536,1536]{2,1,0:T(8,128)(2,1)}) %all-gather.3.cloned.1.call-update) | async-done | bytes 4718608 | tf_op jit(solution)/shard_map/all_gather | solution.py:57
  122.9 1.0 copy.77
  124.0 1.9 reshape.635
  125.9 15.6 %all-to-all-start = ((bf16[16,2,9216]{2,1,0:T(2,128)(2,1)}), bf16[16,2,9216]{2,1,0:T(2,128)(2,1)S(1)}, u32[]{:S(2)}, u32[]{:S(2)}) async-start(bf16[16,2,9216]{2,1,0:T(2,128)(2,1)} %reshape.635), calls=%async_computation | async-start | bytes 1179648 | tf_op jit(solution)/shard_map/all_to_all | solution.py:122
  141.5 21.6 %all-to-all-done = bf16[16,2,9216]{2,1,0:T(2,128)(2,1)S(1)} async-done(((bf16[16,2,9216]{2,1,0:T(2,128)(2,1)}), bf16[16,2,9216]{2,1,0:T(2,128)(2,1)S(1)}, u32[]{:S(2)}, u32[]{:S(2)}) %all-to-all-start) | async-done | bytes 589856 | tf_op jit(solution)/shard_map/all_to_all | solution.py:122
  165.2 26.0 %all_to_all.145 = bf16[16,64,96]{2,1,0:T(8,128)(2,1)S(1)} all-to-all(bf16[16,64,96]{2,1,0:T(8,128)(2,1)S(1)} %bitcast.205), channel_id=1, replica_groups=mesh['pipe'=4,'ctx'=16,'dp'=8] {'ctx'}, dimensions={0} | all-to-all | bytes 393216 | tf_op jit(solution)/shard_map/all_to_all | solution.py:131
  191.9 14.0 %collective-permute-start.7 = (bf16[1,64,1536]{2,1,0:T(8,128)(2,1)S(1)}, bf16[1,64,1536]{2,1,0:T(8,128)(2,1)S(1)}, u32[]{:S(2)}, u32[]{:S(2)}) collective-permute-start(bf16[1,64,1536]{2,1,0:T(8,128)(2,1)S(1)} %fusion.105), channel_id=1, source_target_pairs={{0,128},{128,256},{256,384},{1,129},{129,257},{257,385},{2,130},{1... | collective-permute-start | bytes 589832 | tf_op jit(solution)/shard_map/ppermute | solution.py:15
  205.9 2.6 collective-permute-done.7
  208.8 6.6 conditional.12
  210.2 3.4 fusion.73
  215.4 1.0 copy.82
  216.4 1.9 reshape.637
  218.3 5.6 all-to-all-start.2
  223.9 27.1 %all-to-all-done.2 = bf16[16,2,9216]{2,1,0:T(2,128)(2,1)S(1)} async-done(((bf16[16,2,9216]{2,1,0:T(2,128)(2,1)}), bf16[16,2,9216]{2,1,0:T(2,128)(2,1)S(1)}, u32[]{:S(2)}, u32[]{:S(2)}) %all-to-all-start.2) | async-done | bytes 589856 | tf_op jit(solution)/shard_map/all_to_all | solution.py:122
  253.0 3.8 conditional.13
  254.0 1.5 fusion.15
  255.6 1.2 fusion.22
  257.0 22.3 %all_to_all.146 = bf16[16,64,96]{2,1,0:T(8,128)(2,1)S(1)} all-to-all(bf16[16,64,96]{2,1,0:T(8,128)(2,1)S(1)} %bitcast.206), channel_id=1, replica_groups=mesh['pipe'=4,'ctx'=16,'dp'=8] {'ctx'}, dimensions={0} | all-to-all | bytes 393216 | tf_op jit(solution)/shard_map/all_to_all | solution.py:131
  279.9 1.9 collective-permute-start.8
  281.8 3.8 collective-permute-done.8
  285.9 6.2 conditional.14
  287.3 3.4 fusion.76
  292.1 1.0 copy.87
  293.1 1.9 reshape.639
  295.0 7.6 all-to-all-start.4
  302.6 25.2 %all-to-all-done.4 = bf16[16,2,9216]{2,1,0:T(2,128)(2,1)S(1)} async-done(((bf16[16,2,9216]{2,1,0:T(2,128)(2,1)}), bf16[16,2,9216]{2,1,0:T(2,128)(2,1)S(1)}, u32[]{:S(2)}, u32[]{:S(2)}) %all-to-all-start.4) | async-done | bytes 589856 | tf_op jit(solution)/shard_map/all_to_all | solution.py:122
  329.8 4.0 conditional.15
  331.0 1.5 fusion.29
  332.6 1.2 fusion.36
  334.0 21.9 %all_to_all.147 = bf16[16,64,96]{2,1,0:T(8,128)(2,1)S(1)} all-to-all(bf16[16,64,96]{2,1,0:T(8,128)(2,1)S(1)} %bitcast.207), channel_id=1, replica_groups=mesh['pipe'=4,'ctx'=16,'dp'=8] {'ctx'}, dimensions={0} | all-to-all | bytes 393216 | tf_op jit(solution)/shard_map/all_to_all | solution.py:131
  356.5 5.3 collective-permute-start.9
  361.8 2.6 collective-permute-done.9
  365.8 1.9 reshape.641
  367.7 5.8 all-to-all-start.6
  373.5 25.4 %all-to-all-done.6 = bf16[16,2,9216]{2,1,0:T(2,128)(2,1)S(1)} async-done(((bf16[16,2,9216]{2,1,0:T(2,128)(2,1)}), bf16[16,2,9216]{2,1,0:T(2,128)(2,1)S(1)}, u32[]{:S(2)}, u32[]{:S(2)}) %all-to-all-start.6) | async-done | bytes 589856 | tf_op jit(solution)/shard_map/all_to_all | solution.py:122
  401.1 23.2 %all_to_all.148 = bf16[16,64,96]{2,1,0:T(8,128)(2,1)S(1)} all-to-all(bf16[16,64,96]{2,1,0:T(8,128)(2,1)S(1)} %bitcast.208), channel_id=1, replica_groups=mesh['pipe'=4,'ctx'=16,'dp'=8] {'ctx'}, dimensions={0} | all-to-all | bytes 393216 | tf_op jit(solution)/shard_map/all_to_all | solution.py:131
  425.0 17.2 %collective-permute-start.10 = (bf16[1,64,1536]{2,1,0:T(8,128)(2,1)S(1)}, bf16[1,64,1536]{2,1,0:T(8,128)(2,1)S(1)}, u32[]{:S(2)}, u32[]{:S(2)}) collective-permute-start(bf16[1,64,1536]{2,1,0:T(8,128)(2,1)S(1)} %fusion.97), channel_id=1, source_target_pairs={{0,128},{128,256},{256,384},{1,129},{129,257},{257,385},{2,130},{1... | collective-permute-start | bytes 589832 | tf_op jit(solution)/shard_map/ppermute | solution.py:15
  442.2 2.4 collective-permute-done.10
  446.0 1.9 reshape.643
  447.9 4.7 all-to-all-start.8
  452.5 17.9 %all-to-all-done.8 = bf16[16,2,9216]{2,1,0:T(2,128)(2,1)S(1)} async-done(((bf16[16,2,9216]{2,1,0:T(2,128)(2,1)}), bf16[16,2,9216]{2,1,0:T(2,128)(2,1)S(1)}, u32[]{:S(2)}, u32[]{:S(2)}) %all-to-all-start.8) | async-done | bytes 589856 | tf_op jit(solution)/shard_map/all_to_all | solution.py:122
  473.3 8.0 all-to-all-start.9
  482.0 23.5 %collective-permute-start.12 = (bf16[1536,16]{0,1:T(8,128)(2,1)S(1)}, bf16[1536,16]{0,1:T(8,128)(2,1)S(1)}, u32[]{:S(2)}, u32[]{:S(2)}) collective-permute-start(bf16[1536,16]{0,1:T(8,128)(2,1)S(1)} %copy-done.11), channel_id=1, source_target_pairs={{128,384},{129,385},{130,386},{131,387},{132,388},{133,389},{134,3... | collective-permute-start | bytes 147464 | tf_op jit(solution)/shard_map/ppermute | solution.py:70
  508.0 1.2 copy.110
  509.9 1.3 collective-permute-start.15
  511.9 13.1 %collective-permute-done.15 = f32[2,1,64,16]{2,3,0,1:T(8,128)S(1)} collective-permute-done((f32[2,1,64,16]{2,3,0,1:T(8,128)S(1)}, f32[2,1,64,16]{2,3,0,1:T(8,128)S(1)}, u32[]{:S(2)}, u32[]{:S(2)}) %collective-permute-start.15) | collective-permute-done | bytes 8224 | tf_op jit(solution)/shard_map/ppermute | solution.py:152
  525.6 30.1 %reduce-scatter.4.cloned.1.call-done = f32[192,64]{1,0:T(8,128)} async-done(((f32[1536,64]{1,0:T(8,128)}), f32[192,64]{1,0:T(8,128)}) %reduce-scatter.4.cloned.1.call-update) | async-done | bytes 49168
  556.7 256.2 %psum.7 = f32[192,64]{0,1:T(8,128)S(1)} all-reduce(f32[192,64]{0,1:T(8,128)S(1)} %broadcast_select_fusion.4), channel_id=1, replica_groups=mesh['pipe'=4,'ctx'=16,'dp'=8] {'ctx','pipe'}, use_global_device_ids=true, to_apply=%region_37.39 | all-reduce | flops 12288 | bytes 98304 | tf_op jit(solution)/shard_map/psum | solution.py:156
  (152 shorter events, 39.0 us)
Async XLA Ops:
  7.2 21.3 %copy-start = (bf16[64,1536]{1,0:T(8,128)(2,1)S(1)}, bf16[64,1536]{1,0:T(8,128)(2,1)}, u32[]{:S(2)}) copy-start(bf16[64,1536]{1,0:T(8,128)(2,1)} %param.37) | copy-start | bytes 589828
  7.2 42.3 %copy-start.7 = (bf16[1,192,1536]{2,1,0:T(8,128)(2,1)S(1)}, bf16[1,192,1536]{2,1,0:T(8,128)(2,1)}, u32[]{:S(2)}) copy-start(bf16[1,192,1536]{2,1,0:T(8,128)(2,1)} %param.40) | copy-start | bytes 1769476
  7.2 115.7 %all-gather.3.cloned.1.call-start = ((), (), s32[]{:S(2)}) async-start(), calls=%async_computation.11 | async-start | bytes 5308416 | tf_op jit(solution)/shard_map/all_gather | solution.py:57
  7.9 24.1 %collective-permute-start = (bf16[192,1536]{1,0:T(8,128)(2,1)}, bf16[192,1536]{1,0:T(8,128)(2,1)}, u32[]{:S(2)}, u32[]{:S(2)}) collective-permute-start(bf16[192,1536]{1,0:T(8,128)(2,1)} %bitcast.211), channel_id=1, source_target_pairs={{0,1},{1,2},{2,3},{3,4},{4,5},{5,6},{6,7},{7,0},{8,9},{9,10},{10,1... | collective-permute-start | bytes 1769480 | tf_op jit(solution)/shard_map/ppermute | solution.py:61
  11.9 37.6 %collective-permute-start.1 = (bf16[192,1536]{1,0:T(8,128)(2,1)}, bf16[192,1536]{1,0:T(8,128)(2,1)}, u32[]{:S(2)}, u32[]{:S(2)}) collective-permute-start(bf16[192,1536]{1,0:T(8,128)(2,1)} %bitcast.212), channel_id=1, source_target_pairs={{0,2},{1,3},{2,4},{3,5},{4,6},{5,7},{6,0},{7,1},{8,10},{9,11},{10,... | collective-permute-start | bytes 1769480 | tf_op jit(solution)/shard_map/ppermute | solution.py:61
  16.3 37.1 %collective-permute-start.2 = (bf16[192,1536]{1,0:T(8,128)(2,1)}, bf16[192,1536]{1,0:T(8,128)(2,1)}, u32[]{:S(2)}, u32[]{:S(2)}) collective-permute-start(bf16[192,1536]{1,0:T(8,128)(2,1)} %bitcast.213), channel_id=1, source_target_pairs={{0,3},{1,4},{2,5},{3,6},{4,7},{5,0},{6,1},{7,2},{8,11},{9,12},{10,... | collective-permute-start | bytes 1769480 | tf_op jit(solution)/shard_map/ppermute | solution.py:61
  20.3 63.5 %collective-permute-start.3 = (bf16[192,1536]{1,0:T(8,128)(2,1)}, bf16[192,1536]{1,0:T(8,128)(2,1)S(1)}, u32[]{:S(2)}, u32[]{:S(2)}) collective-permute-start(bf16[192,1536]{1,0:T(8,128)(2,1)} %bitcast.214), channel_id=1, source_target_pairs={{0,4},{1,5},{2,6},{3,7},{4,0},{5,1},{6,2},{7,3},{8,12},{9,13},{10,... | collective-permute-start | bytes 1769480 | tf_op jit(solution)/shard_map/ppermute | solution.py:61
  22.4 62.2 %collective-permute-start.4 = (bf16[192,1536]{1,0:T(8,128)(2,1)}, bf16[192,1536]{1,0:T(8,128)(2,1)S(1)}, u32[]{:S(2)}, u32[]{:S(2)}) collective-permute-start(bf16[192,1536]{1,0:T(8,128)(2,1)} %bitcast.215), channel_id=1, source_target_pairs={{0,5},{1,6},{2,7},{3,0},{4,1},{5,2},{6,3},{7,4},{8,13},{9,14},{10,... | collective-permute-start | bytes 1769480 | tf_op jit(solution)/shard_map/ppermute | solution.py:61
  32.0 64.0 %collective-permute-start.5 = (bf16[192,1536]{1,0:T(8,128)(2,1)}, bf16[192,1536]{1,0:T(8,128)(2,1)S(1)}, u32[]{:S(2)}, u32[]{:S(2)}) collective-permute-start(bf16[192,1536]{1,0:T(8,128)(2,1)} %bitcast.216), channel_id=1, source_target_pairs={{0,6},{1,7},{2,0},{3,1},{4,2},{5,3},{6,4},{7,5},{8,14},{9,15},{10,... | collective-permute-start | bytes 1769480 | tf_op jit(solution)/shard_map/ppermute | solution.py:61
  49.5 55.9 %collective-permute-start.6 = (bf16[192,1536]{1,0:T(8,128)(2,1)S(1)}, bf16[192,1536]{1,0:T(8,128)(2,1)S(1)}, u32[]{:S(2)}, u32[]{:S(2)}) collective-permute-start(bf16[192,1536]{1,0:T(8,128)(2,1)S(1)} %bitcast.217), channel_id=1, source_target_pairs={{0,7},{1,0},{2,1},{3,2},{4,3},{5,4},{6,5},{7,6},{8,15},{9,8},{10,9... | collective-permute-start | bytes 1769480 | tf_op jit(solution)/shard_map/ppermute | solution.py:61
  124.0 41.0 %copy-start.10 = (s32[2,1,1024]{2,1,0:T(1,128)S(1)}, s32[2,1,1024]{2,1,0:T(1,128)}, u32[]{:S(2)}) copy-start(s32[2,1,1024]{2,1,0:T(1,128)} %param.36) | copy-start | bytes 24580
  125.9 37.2 %all-to-all-start = ((bf16[16,2,9216]{2,1,0:T(2,128)(2,1)}), bf16[16,2,9216]{2,1,0:T(2,128)(2,1)S(1)}, u32[]{:S(2)}, u32[]{:S(2)}) async-start(bf16[16,2,9216]{2,1,0:T(2,128)(2,1)} %reshape.635), calls=%async_computation | async-start | bytes 1179648 | tf_op jit(solution)/shard_map/all_to_all | solution.py:122
  191.9 16.6 %collective-permute-start.7 = (bf16[1,64,1536]{2,1,0:T(8,128)(2,1)S(1)}, bf16[1,64,1536]{2,1,0:T(8,128)(2,1)S(1)}, u32[]{:S(2)}, u32[]{:S(2)}) collective-permute-start(bf16[1,64,1536]{2,1,0:T(8,128)(2,1)S(1)} %fusion.105), channel_id=1, source_target_pairs={{0,128},{128,256},{256,384},{1,129},{129,257},{257,385},{2,130},{1... | collective-permute-start | bytes 589832 | tf_op jit(solution)/shard_map/ppermute | solution.py:15
  210.2 3.8 copy-start.3
  218.3 32.7 %all-to-all-start.2 = ((bf16[16,2,9216]{2,1,0:T(2,128)(2,1)}), bf16[16,2,9216]{2,1,0:T(2,128)(2,1)S(1)}, u32[]{:S(2)}, u32[]{:S(2)}) async-start(bf16[16,2,9216]{2,1,0:T(2,128)(2,1)} %reshape.637), calls=%async_computation.2 | async-start | bytes 1179648 | tf_op jit(solution)/shard_map/all_to_all | solution.py:122
  279.9 5.7 collective-permute-start.8
  287.3 3.8 copy-start.4
  295.0 32.8 %all-to-all-start.4 = ((bf16[16,2,9216]{2,1,0:T(2,128)(2,1)}), bf16[16,2,9216]{2,1,0:T(2,128)(2,1)S(1)}, u32[]{:S(2)}, u32[]{:S(2)}) async-start(bf16[16,2,9216]{2,1,0:T(2,128)(2,1)} %reshape.639), calls=%async_computation.4 | async-start | bytes 1179648 | tf_op jit(solution)/shard_map/all_to_all | solution.py:122
  356.5 7.9 collective-permute-start.9
  367.7 31.3 %all-to-all-start.6 = ((bf16[16,2,9216]{2,1,0:T(2,128)(2,1)}), bf16[16,2,9216]{2,1,0:T(2,128)(2,1)S(1)}, u32[]{:S(2)}, u32[]{:S(2)}) async-start(bf16[16,2,9216]{2,1,0:T(2,128)(2,1)} %reshape.641), calls=%async_computation.6 | async-start | bytes 1179648 | tf_op jit(solution)/shard_map/all_to_all | solution.py:122
  425.0 19.6 %collective-permute-start.10 = (bf16[1,64,1536]{2,1,0:T(8,128)(2,1)S(1)}, bf16[1,64,1536]{2,1,0:T(8,128)(2,1)S(1)}, u32[]{:S(2)}, u32[]{:S(2)}) collective-permute-start(bf16[1,64,1536]{2,1,0:T(8,128)(2,1)S(1)} %fusion.97), channel_id=1, source_target_pairs={{0,128},{128,256},{256,384},{1,129},{129,257},{257,385},{2,130},{1... | collective-permute-start | bytes 589832 | tf_op jit(solution)/shard_map/ppermute | solution.py:15
  447.9 22.5 %all-to-all-start.8 = ((bf16[16,2,9216]{2,1,0:T(2,128)(2,1)}), bf16[16,2,9216]{2,1,0:T(2,128)(2,1)S(1)}, u32[]{:S(2)}, u32[]{:S(2)}) async-start(bf16[16,2,9216]{2,1,0:T(2,128)(2,1)} %reshape.643), calls=%async_computation.8 | async-start | bytes 1179648 | tf_op jit(solution)/shard_map/all_to_all | solution.py:122
  472.3 8.9 %copy-start.11 = (bf16[1536,16]{0,1:T(8,128)(2,1)S(1)}, bf16[1536,16]{0,1:T(8,128)(2,1)}, u32[]{:S(2)}) copy-start(bf16[1536,16]{0,1:T(8,128)(2,1)} %param.43) | copy-start | bytes 147460
  472.3 33.8 %copy-start.8 = (f32[2,1,64,64]{3,2,1,0:T(8,128)S(1)}, f32[2,1,64,64]{3,2,1,0:T(8,128)}, u32[]{:S(2)}) copy-start(f32[2,1,64,64]{3,2,1,0:T(8,128)} %param.33) | copy-start | bytes 98308
  472.4 33.9 %copy-start.9 = (f32[2,1,64,64]{3,2,1,0:T(8,128)S(1)}, f32[2,1,64,64]{3,2,1,0:T(8,128)}, u32[]{:S(2)}) copy-start(f32[2,1,64,64]{3,2,1,0:T(8,128)} %param.34) | copy-start | bytes 98308
  472.4 34.8 %copy-start.12 = (f32[1536]{0:T(1024)S(1)}, f32[1536]{0:T(1024)}, u32[]{:S(2)}) copy-start(f32[1536]{0:T(1024)} %param.42) | copy-start | bytes 18436
  473.3 33.1 %all-to-all-start.9 = ((bf16[16,64,96]{2,1,0:T(8,128)(2,1)}), bf16[16,64,96]{2,1,0:T(8,128)(2,1)S(1)}, u32[]{:S(2)}, u32[]{:S(2)}) async-start(bf16[16,64,96]{2,1,0:T(8,128)(2,1)} %bitcast.71), calls=%async_computation.9 | async-start | bytes 524288 | tf_op jit(solution)/shard_map/all_to_all | solution.py:131
  481.2 74.5 %reduce-scatter.4.cloned.1.call-start = ((), (), s32[]{:S(2)}) async-start(), calls=%async_computation.12 | async-start | bytes 884736
  481.3 25.9 %collective-permute-start.11 = (bf16[1536,16]{0,1:T(8,128)(2,1)S(1)}, bf16[1536,16]{0,1:T(8,128)(2,1)S(1)}, u32[]{:S(2)}, u32[]{:S(2)}) collective-permute-start(bf16[1536,16]{0,1:T(8,128)(2,1)S(1)} %copy-done.11), channel_id=1, source_target_pairs={{0,384},{1,385},{2,386},{3,387},{4,388},{5,389},{6,390},{7,391},{8... | collective-permute-start | bytes 147464 | tf_op jit(solution)/shard_map/ppermute | solution.py:70
  482.0 25.2 %collective-permute-start.12 = (bf16[1536,16]{0,1:T(8,128)(2,1)S(1)}, bf16[1536,16]{0,1:T(8,128)(2,1)S(1)}, u32[]{:S(2)}, u32[]{:S(2)}) collective-permute-start(bf16[1536,16]{0,1:T(8,128)(2,1)S(1)} %copy-done.11), channel_id=1, source_target_pairs={{128,384},{129,385},{130,386},{131,387},{132,388},{133,389},{134,3... | collective-permute-start | bytes 147464 | tf_op jit(solution)/shard_map/ppermute | solution.py:70
  505.5 1.7 collective-permute-start.13
  506.3 307.1 %copy-start.1 = (bf16[64,1536]{1,0:T(8,128)(2,1)S(1)}, bf16[64,1536]{1,0:T(8,128)(2,1)}, u32[]{:S(2)}) copy-start(bf16[64,1536]{1,0:T(8,128)(2,1)} %param.37) | copy-start | bytes 589828
  509.2 2.6 collective-permute-start.14
  509.9 15.1 %collective-permute-start.15 = (f32[2,1,64,16]{2,3,0,1:T(8,128)S(1)}, f32[2,1,64,16]{2,3,0,1:T(8,128)S(1)}, u32[]{:S(2)}, u32[]{:S(2)}) collective-permute-start(f32[2,1,64,16]{2,3,0,1:T(8,128)S(1)} %get-tuple-element.325), channel_id=1, source_target_pairs={{384,128},{385,129},{386,130},{387,131},{388,132},{389,133},{390,1... | collective-permute-start | bytes 24584 | tf_op jit(solution)/shard_map/ppermute | solution.py:152
  511.2 13.8 %collective-permute-start.16 = (f32[2,1,64,16]{2,3,0,1:T(8,128)S(1)}, f32[2,1,64,16]{2,3,0,1:T(8,128)S(1)}, u32[]{:S(2)}, u32[]{:S(2)}) collective-permute-start(f32[2,1,64,16]{2,3,0,1:T(8,128)S(1)} %get-tuple-element.326), channel_id=1, source_target_pairs={{384,256},{385,257},{386,258},{387,259},{388,260},{389,261},{390,2... | collective-permute-start | bytes 24584 | tf_op jit(solution)/shard_map/ppermute | solution.py:152
Sparse Core Ops, SparseCore 0:
  10.1 112.7 all-gather.2
  509.3 46.3 reduce-scatter.3

commit v9 on v4

--- a/solution.py
+++ b/solution.py
@@ -119,7 +119,15 @@
             return jnp.zeros((seq_total, local_width), jnp.bfloat16)
 
         mixed_heads = lax.cond(active, run_attention, blank_heads, section_by_heads)
-        mixed = lax.all_to_all(mixed_heads, "ctx", split_axis=0, concat_axis=1, tiled=True)
+        chunk = local_rows * local_width
+        lanes = 128 if chunk % 128 == 0 else chunk
+        outgoing = mixed_heads.reshape(cycle_size, chunk // lanes, lanes)
+        returned = lax.all_to_all(outgoing, "ctx", split_axis=0, concat_axis=0, tiled=True)
+        mixed = (
+            returned.reshape(cycle_size, local_rows, local_width)
+            .transpose(1, 0, 2)
+            .reshape(local_rows, model_width)
+        )
         result = (wide_state + mixed.astype(jnp.float32)[None]).astype(jnp.bfloat16)
         if moment + 1 < moment_count:
             incoming = shifted(result, "pipe", 1)

time: 638 us -> 628 us (0.984)
  no operation moved by 1% of the time
where the time goes in v9:
time: 628 us; the launch traced here: 619 us
  waiting for transfers between devices  271 us (43%)
  blocking collectives  149 us (24%)
  starting transfers between devices  104 us (17%)
  local copies, waits for them, and re-layouts  50.4 us (8%)
  between operations  15.1 us (2%)
  matrix products  14.6 us (2%)
  other arithmetic  14.3 us (2%)
    all_to_all x5, waiting for transfers between devices, on_device(): lax.all_to_all(triple, 'ctx', split_axis=2, concat_axis=1, tiled=True)  127 us
    all_to_all x4, blocking collectives, on_device(): lax.all_to_all(outgoing, 'ctx', split_axis=0, concat_axis=0, tiled=True)  86.2 us
    ppermute x7, waiting for transfers between devices, on_device(): key_blocks.append(lax.ppermute(key_weight[0], 'dp', pairs))  60.5 us
    psum x1, blocking collectives, on_device(): grad_rows = lax.psum(grad_rows, 'ctx')  42.7 us
    unnamed x3, waiting for transfers between devices  41.8 us
    all_to_all x5, starting transfers between devices, on_device(): lax.all_to_all(triple, 'ctx', split_axis=2, concat_axis=1, tiled=True)  36.1 us
    ppermute x4, starting transfers between devices, shifted(): lax.ppermute(value, axis, [(source, source + steps) for source in range(f...  32.8 us
    unnamed x37, local copies, waits for them, and re-layouts  25.5 us
  transfers between devices with their start and end apart: 25, of which 16 were waited for; matrix products, arithmetic and copies ran while one was open for 4% of the time, Pallas kernels for 0%

profile of v9, /device:TPU:1, one launch (start us, length us, event | category | flops | bytes accessed | tf_op | source)
XLA Modules:
  0.0 618.6 jit_solution(9649736871018525663)
XLA Ops:
  7.9 4.0 collective-permute-start
  11.9 4.4 collective-permute-start.1
  16.3 4.1 collective-permute-start.2
  20.3 2.1 collective-permute-start.3
  22.4 3.2 collective-permute-start.4
  28.5 1.2 fusion.88
  29.8 1.9 constant_dynamic-update-slice_fusion
  32.2 3.3 collective-permute-start.5
  35.6 1.9 bitcast_dynamic-update-slice_fusion.6
  37.5 12.0 %collective-permute-done.1 = bf16[192,1536]{1,0:T(8,128)(2,1)} collective-permute-done((bf16[192,1536]{1,0:T(8,128)(2,1)}, bf16[192,1536]{1,0:T(8,128)(2,1)}, u32[]{:S(2)}, u32[]{:S(2)}) %collective-permute-start.1) | collective-permute-done | bytes 589856 | tf_op jit(solution)/shard_map/ppermute | solution.py:61
  49.5 1.9 collective-permute-start.6
  51.4 1.9 bitcast_dynamic-update-slice_fusion.5
  54.2 29.7 %collective-permute-done.3 = bf16[192,1536]{1,0:T(8,128)(2,1)S(1)} collective-permute-done((bf16[192,1536]{1,0:T(8,128)(2,1)}, bf16[192,1536]{1,0:T(8,128)(2,1)S(1)}, u32[]{:S(2)}, u32[]{:S(2)}) %collective-permute-start.3) | collective-permute-done | bytes 589856 | tf_op jit(solution)/shard_map/ppermute | solution.py:61
  85.6 10.5 %collective-permute-done.5 = bf16[192,1536]{1,0:T(8,128)(2,1)S(1)} collective-permute-done((bf16[192,1536]{1,0:T(8,128)(2,1)}, bf16[192,1536]{1,0:T(8,128)(2,1)S(1)}, u32[]{:S(2)}, u32[]{:S(2)}) %collective-permute-start.5) | collective-permute-done | bytes 589856 | tf_op jit(solution)/shard_map/ppermute | solution.py:61
  97.0 8.4 %collective-permute-done.6 = bf16[192,1536]{1,0:T(8,128)(2,1)S(1)} collective-permute-done((bf16[192,1536]{1,0:T(8,128)(2,1)S(1)}, bf16[192,1536]{1,0:T(8,128)(2,1)S(1)}, u32[]{:S(2)}, u32[]{:S(2)}) %collective-permute-start.6) | collective-permute-done | bytes 589856 | tf_op jit(solution)/shard_map/ppermute | solution.py:61
  106.2 5.5 gather_fusion
  111.7 5.1 bitcast_select_fusion
  116.7 6.1 all-gather.3.cloned.1.call-done
  122.9 1.0 copy.34
  124.0 1.8 reshape.651
  125.8 15.6 %all-to-all-start = ((bf16[16,2,9216]{2,1,0:T(2,128)(2,1)}), bf16[16,2,9216]{2,1,0:T(2,128)(2,1)S(1)}, u32[]{:S(2)}, u32[]{:S(2)}) async-start(bf16[16,2,9216]{2,1,0:T(2,128)(2,1)} %reshape.651), calls=%async_computation | async-start | bytes 1179648 | tf_op jit(solution)/shard_map/all_to_all | solution.py:113
  141.5 22.1 %all-to-all-done = bf16[16,2,9216]{2,1,0:T(2,128)(2,1)S(1)} async-done(((bf16[16,2,9216]{2,1,0:T(2,128)(2,1)}), bf16[16,2,9216]{2,1,0:T(2,128)(2,1)S(1)}, u32[]{:S(2)}, u32[]{:S(2)}) %all-to-all-start) | async-done | bytes 589856 | tf_op jit(solution)/shard_map/all_to_all | solution.py:113
  166.1 25.2 %all_to_all.105 = bf16[16,48,128]{2,1,0:T(8,128)(2,1)S(1)} all-to-all(bf16[16,48,128]{2,1,0:T(8,128)(2,1)S(1)} %reshape.619), channel_id=1, replica_groups=mesh['pipe'=4,'ctx'=16,'dp'=8] {'ctx'}, dimensions={0} | all-to-all | bytes 393216 | tf_op jit(solution)/shard_map/all_to_all | solution.py:125
  192.0 12.4 %collective-permute-start.7 = (bf16[1,64,1536]{2,1,0:T(8,128)(2,1)S(1)}, bf16[1,64,1536]{2,1,0:T(8,128)(2,1)S(1)}, u32[]{:S(2)}, u32[]{:S(2)}) collective-permute-start(bf16[1,64,1536]{2,1,0:T(8,128)(2,1)S(1)} %fusion.109), channel_id=1, source_target_pairs={{0,128},{128,256},{256,384},{1,129},{129,257},{257,385},{2,130},{1... | collective-permute-start | bytes 589832 | tf_op jit(solution)/shard_map/ppermute | solution.py:15
  204.5 2.6 collective-permute-done.7
  207.4 5.3 conditional.12
  207.4 3.4 fusion.16
  213.7 1.8 reshape.653
  215.5 4.7 all-to-all-start.2
  220.2 28.1 %all-to-all-done.2 = bf16[16,2,9216]{2,1,0:T(2,128)(2,1)S(1)} async-done(((bf16[16,2,9216]{2,1,0:T(2,128)(2,1)}), bf16[16,2,9216]{2,1,0:T(2,128)(2,1)S(1)}, u32[]{:S(2)}, u32[]{:S(2)}) %all-to-all-start.2) | async-done | bytes 589856 | tf_op jit(solution)/shard_map/all_to_all | solution.py:113
  250.2 3.8 conditional.13
  251.3 1.5 fusion.21
  252.8 1.2 fusion.28
  254.6 20.2 %all_to_all.106 = bf16[16,48,128]{2,1,0:T(8,128)(2,1)S(1)} all-to-all(bf16[16,48,128]{2,1,0:T(8,128)(2,1)S(1)} %reshape.620), channel_id=1, replica_groups=mesh['pipe'=4,'ctx'=16,'dp'=8] {'ctx'}, dimensions={0} | all-to-all | bytes 393216 | tf_op jit(solution)/shard_map/all_to_all | solution.py:125
  275.5 1.9 collective-permute-start.8
  277.5 3.4 collective-permute-done.8
  281.2 4.8 conditional.14
  281.2 3.4 fusion.34
  287.1 1.8 reshape.655
  288.9 7.4 %all-to-all-start.4 = ((bf16[16,2,9216]{2,1,0:T(2,128)(2,1)}), bf16[16,2,9216]{2,1,0:T(2,128)(2,1)S(1)}, u32[]{:S(2)}, u32[]{:S(2)}) async-start(bf16[16,2,9216]{2,1,0:T(2,128)(2,1)} %reshape.655), calls=%async_computation.4 | async-start | bytes 1179648 | tf_op jit(solution)/shard_map/all_to_all | solution.py:113
  296.3 27.0 %all-to-all-done.4 = bf16[16,2,9216]{2,1,0:T(2,128)(2,1)S(1)} async-done(((bf16[16,2,9216]{2,1,0:T(2,128)(2,1)}), bf16[16,2,9216]{2,1,0:T(2,128)(2,1)S(1)}, u32[]{:S(2)}, u32[]{:S(2)}) %all-to-all-start.4) | async-done | bytes 589856 | tf_op jit(solution)/shard_map/all_to_all | solution.py:113
  325.2 4.0 conditional.15
  326.5 1.5 fusion.39
  328.0 1.2 fusion.46
  329.8 20.2 %all_to_all.107 = bf16[16,48,128]{2,1,0:T(8,128)(2,1)S(1)} all-to-all(bf16[16,48,128]{2,1,0:T(8,128)(2,1)S(1)} %reshape.621), channel_id=1, replica_groups=mesh['pipe'=4,'ctx'=16,'dp'=8] {'ctx'}, dimensions={0} | all-to-all | bytes 393216 | tf_op jit(solution)/shard_map/all_to_all | solution.py:125
  350.8 3.5 collective-permute-start.9
  354.3 2.6 collective-permute-done.9
  358.3 1.8 reshape.657
  360.1 4.8 all-to-all-start.6
  364.9 27.5 %all-to-all-done.6 = bf16[16,2,9216]{2,1,0:T(2,128)(2,1)S(1)} async-done(((bf16[16,2,9216]{2,1,0:T(2,128)(2,1)}), bf16[16,2,9216]{2,1,0:T(2,128)(2,1)S(1)}, u32[]{:S(2)}, u32[]{:S(2)}) %all-to-all-start.6) | async-done | bytes 589856 | tf_op jit(solution)/shard_map/all_to_all | solution.py:113
  395.0 20.7 %all_to_all.108 = bf16[16,48,128]{2,1,0:T(8,128)(2,1)S(1)} all-to-all(bf16[16,48,128]{2,1,0:T(8,128)(2,1)S(1)} %reshape.622), channel_id=1, replica_groups=mesh['pipe'=4,'ctx'=16,'dp'=8] {'ctx'}, dimensions={0} | all-to-all | bytes 393216 | tf_op jit(solution)/shard_map/all_to_all | solution.py:125
  416.5 14.9 %collective-permute-start.10 = (bf16[1,64,1536]{2,1,0:T(8,128)(2,1)S(1)}, bf16[1,64,1536]{2,1,0:T(8,128)(2,1)S(1)}, u32[]{:S(2)}, u32[]{:S(2)}) collective-permute-start(bf16[1,64,1536]{2,1,0:T(8,128)(2,1)S(1)} %fusion.101), channel_id=1, source_target_pairs={{0,128},{128,256},{256,384},{1,129},{129,257},{257,385},{2,130},{1... | collective-permute-start | bytes 589832 | tf_op jit(solution)/shard_map/ppermute | solution.py:15
  431.4 2.6 collective-permute-done.10
  435.4 1.8 reshape.659
  437.2 3.6 all-to-all-start.8
  440.8 22.8 %all-to-all-done.8 = bf16[16,2,9216]{2,1,0:T(2,128)(2,1)S(1)} async-done(((bf16[16,2,9216]{2,1,0:T(2,128)(2,1)}), bf16[16,2,9216]{2,1,0:T(2,128)(2,1)S(1)}, u32[]{:S(2)}, u32[]{:S(2)}) %all-to-all-start.8) | async-done | bytes 589856 | tf_op jit(solution)/shard_map/all_to_all | solution.py:113
  466.9 6.6 %all-to-all-start.9 = ((bf16[16,48,128]{2,1,0:T(8,128)(2,1)}), bf16[16,48,128]{2,1,0:T(8,128)(2,1)S(1)}, u32[]{:S(2)}, u32[]{:S(2)}) async-start(bf16[16,48,128]{2,1,0:T(8,128)(2,1)} %reshape.623), calls=%async_computation.9 | async-start | bytes 393216 | tf_op jit(solution)/shard_map/all_to_all | solution.py:125
  473.8 20.0 %all_gather.7 = bf16[1536,64]{0,1:T(8,128)(2,1)S(1)} all-gather(bf16[1536,16]{0,1:T(8,128)(2,1)S(1)} %copy-done.11), channel_id=1, replica_groups=mesh['pipe'=4,'ctx'=16,'dp'=8] {'pipe'}, dimensions={1}, use_global_device_ids=true | all-gather | bytes 245760 | tf_op jit(solution)/shard_map/all_gather | solution.py:65
  495.5 1.2 copy.67
  497.4 1.3 collective-permute-start.12
  499.4 41.2 %reduce-scatter.4.cloned.1.call-done = f32[192,64]{1,0:T(8,128)} async-done(((f32[1536,64]{1,0:T(8,128)}), f32[192,64]{1,0:T(8,128)}) %reduce-scatter.4.cloned.1.call-update) | async-done | bytes 49168
  541.5 42.7 %psum.7 = f32[192,64]{0,1:T(8,128)S(1)} all-reduce(f32[192,64]{0,1:T(8,128)S(1)} %copy.68), channel_id=1, replica_groups=mesh['pipe'=4,'ctx'=16,'dp'=8] {'ctx'}, use_global_device_ids=true, to_apply=%region_37.38 | all-reduce | flops 12288 | bytes 98304 | tf_op jit(solution)/shard_map/psum | solution.py:149
  584.8 1.3 collective-permute-start.15
  587.5 23.4 %collective-permute-done.15 = f32[192,16]{0,1:T(8,128)S(1)} collective-permute-done((f32[192,16]{0,1:T(8,128)S(1)}, f32[192,16]{0,1:T(8,128)S(1)}, u32[]{:S(2)}, u32[]{:S(2)}) %collective-permute-start.15) | collective-permute-done | bytes 12320 | tf_op jit(solution)/shard_map/ppermute | solution.py:156
  (146 shorter events, 41.9 us)
Async XLA Ops:
  7.2 21.3 %copy-start = (bf16[64,1536]{1,0:T(8,128)(2,1)S(1)}, bf16[64,1536]{1,0:T(8,128)(2,1)}, u32[]{:S(2)}) copy-start(bf16[64,1536]{1,0:T(8,128)(2,1)} %param.35) | copy-start | bytes 589828
  7.2 42.3 %copy-start.7 = (bf16[1,192,1536]{2,1,0:T(8,128)(2,1)S(1)}, bf16[1,192,1536]{2,1,0:T(8,128)(2,1)}, u32[]{:S(2)}) copy-start(bf16[1,192,1536]{2,1,0:T(8,128)(2,1)} %param.38) | copy-start | bytes 1769476
  7.2 115.7 %all-gather.3.cloned.1.call-start = ((), (), s32[]{:S(2)}) async-start(), calls=%async_computation.11 | async-start | bytes 5308416 | tf_op jit(solution)/shard_map/all_gather | solution.py:57
  7.9 24.3 %collective-permute-start = (bf16[192,1536]{1,0:T(8,128)(2,1)}, bf16[192,1536]{1,0:T(8,128)(2,1)}, u32[]{:S(2)}, u32[]{:S(2)}) collective-permute-start(bf16[192,1536]{1,0:T(8,128)(2,1)} %bitcast.194), channel_id=1, source_target_pairs={{0,1},{1,2},{2,3},{3,4},{4,5},{5,6},{6,7},{7,0},{8,9},{9,10},{10,1... | collective-permute-start | bytes 1769480 | tf_op jit(solution)/shard_map/ppermute | solution.py:61
  11.9 37.6 %collective-permute-start.1 = (bf16[192,1536]{1,0:T(8,128)(2,1)}, bf16[192,1536]{1,0:T(8,128)(2,1)}, u32[]{:S(2)}, u32[]{:S(2)}) collective-permute-start(bf16[192,1536]{1,0:T(8,128)(2,1)} %bitcast.195), channel_id=1, source_target_pairs={{0,2},{1,3},{2,4},{3,5},{4,6},{5,7},{6,0},{7,1},{8,10},{9,11},{10,... | collective-permute-start | bytes 1769480 | tf_op jit(solution)/shard_map/ppermute | solution.py:61
  16.3 37.1 %collective-permute-start.2 = (bf16[192,1536]{1,0:T(8,128)(2,1)}, bf16[192,1536]{1,0:T(8,128)(2,1)S(1)}, u32[]{:S(2)}, u32[]{:S(2)}) collective-permute-start(bf16[192,1536]{1,0:T(8,128)(2,1)} %bitcast.196), channel_id=1, source_target_pairs={{0,3},{1,4},{2,5},{3,6},{4,7},{5,0},{6,1},{7,2},{8,11},{9,12},{10,... | collective-permute-start | bytes 1769480 | tf_op jit(solution)/shard_map/ppermute | solution.py:61
  20.3 63.5 %collective-permute-start.3 = (bf16[192,1536]{1,0:T(8,128)(2,1)}, bf16[192,1536]{1,0:T(8,128)(2,1)S(1)}, u32[]{:S(2)}, u32[]{:S(2)}) collective-permute-start(bf16[192,1536]{1,0:T(8,128)(2,1)} %bitcast.197), channel_id=1, source_target_pairs={{0,4},{1,5},{2,6},{3,7},{4,0},{5,1},{6,2},{7,3},{8,12},{9,13},{10,... | collective-permute-start | bytes 1769480 | tf_op jit(solution)/shard_map/ppermute | solution.py:61
  22.4 62.2 %collective-permute-start.4 = (bf16[192,1536]{1,0:T(8,128)(2,1)}, bf16[192,1536]{1,0:T(8,128)(2,1)S(1)}, u32[]{:S(2)}, u32[]{:S(2)}) collective-permute-start(bf16[192,1536]{1,0:T(8,128)(2,1)} %bitcast.198), channel_id=1, source_target_pairs={{0,5},{1,6},{2,7},{3,0},{4,1},{5,2},{6,3},{7,4},{8,13},{9,14},{10,... | collective-permute-start | bytes 1769480 | tf_op jit(solution)/shard_map/ppermute | solution.py:61
  32.2 63.8 %collective-permute-start.5 = (bf16[192,1536]{1,0:T(8,128)(2,1)}, bf16[192,1536]{1,0:T(8,128)(2,1)S(1)}, u32[]{:S(2)}, u32[]{:S(2)}) collective-permute-start(bf16[192,1536]{1,0:T(8,128)(2,1)} %bitcast.199), channel_id=1, source_target_pairs={{0,6},{1,7},{2,0},{3,1},{4,2},{5,3},{6,4},{7,5},{8,14},{9,15},{10,... | collective-permute-start | bytes 1769480 | tf_op jit(solution)/shard_map/ppermute | solution.py:61
  49.5 55.9 %collective-permute-start.6 = (bf16[192,1536]{1,0:T(8,128)(2,1)S(1)}, bf16[192,1536]{1,0:T(8,128)(2,1)S(1)}, u32[]{:S(2)}, u32[]{:S(2)}) collective-permute-start(bf16[192,1536]{1,0:T(8,128)(2,1)S(1)} %bitcast.200), channel_id=1, source_target_pairs={{0,7},{1,0},{2,1},{3,2},{4,3},{5,4},{6,5},{7,6},{8,15},{9,8},{10,9... | collective-permute-start | bytes 1769480 | tf_op jit(solution)/shard_map/ppermute | solution.py:61
  124.0 41.5 %copy-start.10 = (s32[2,1,1024]{2,1,0:T(1,128)S(1)}, s32[2,1,1024]{2,1,0:T(1,128)}, u32[]{:S(2)}) copy-start(s32[2,1,1024]{2,1,0:T(1,128)} %param.34) | copy-start | bytes 24580
  125.8 37.7 %all-to-all-start = ((bf16[16,2,9216]{2,1,0:T(2,128)(2,1)}), bf16[16,2,9216]{2,1,0:T(2,128)(2,1)S(1)}, u32[]{:S(2)}, u32[]{:S(2)}) async-start(bf16[16,2,9216]{2,1,0:T(2,128)(2,1)} %reshape.651), calls=%async_computation | async-start | bytes 1179648 | tf_op jit(solution)/shard_map/all_to_all | solution.py:113
  192.0 15.0 %collective-permute-start.7 = (bf16[1,64,1536]{2,1,0:T(8,128)(2,1)S(1)}, bf16[1,64,1536]{2,1,0:T(8,128)(2,1)S(1)}, u32[]{:S(2)}, u32[]{:S(2)}) collective-permute-start(bf16[1,64,1536]{2,1,0:T(8,128)(2,1)S(1)} %fusion.109), channel_id=1, source_target_pairs={{0,128},{128,256},{256,384},{1,129},{129,257},{257,385},{2,130},{1... | collective-permute-start | bytes 589832 | tf_op jit(solution)/shard_map/ppermute | solution.py:15
  207.4 3.8 copy-start.3
  215.5 32.7 %all-to-all-start.2 = ((bf16[16,2,9216]{2,1,0:T(2,128)(2,1)}), bf16[16,2,9216]{2,1,0:T(2,128)(2,1)S(1)}, u32[]{:S(2)}, u32[]{:S(2)}) async-start(bf16[16,2,9216]{2,1,0:T(2,128)(2,1)} %reshape.653), calls=%async_computation.2 | async-start | bytes 1179648 | tf_op jit(solution)/shard_map/all_to_all | solution.py:113
  275.5 5.4 collective-permute-start.8
  281.2 3.8 copy-start.4
  288.9 34.4 %all-to-all-start.4 = ((bf16[16,2,9216]{2,1,0:T(2,128)(2,1)}), bf16[16,2,9216]{2,1,0:T(2,128)(2,1)S(1)}, u32[]{:S(2)}, u32[]{:S(2)}) async-start(bf16[16,2,9216]{2,1,0:T(2,128)(2,1)} %reshape.655), calls=%async_computation.4 | async-start | bytes 1179648 | tf_op jit(solution)/shard_map/all_to_all | solution.py:113
  350.8 6.1 collective-permute-start.9
  360.1 32.3 %all-to-all-start.6 = ((bf16[16,2,9216]{2,1,0:T(2,128)(2,1)}), bf16[16,2,9216]{2,1,0:T(2,128)(2,1)S(1)}, u32[]{:S(2)}, u32[]{:S(2)}) async-start(bf16[16,2,9216]{2,1,0:T(2,128)(2,1)} %reshape.657), calls=%async_computation.6 | async-start | bytes 1179648 | tf_op jit(solution)/shard_map/all_to_all | solution.py:113
  416.5 17.5 %collective-permute-start.10 = (bf16[1,64,1536]{2,1,0:T(8,128)(2,1)S(1)}, bf16[1,64,1536]{2,1,0:T(8,128)(2,1)S(1)}, u32[]{:S(2)}, u32[]{:S(2)}) collective-permute-start(bf16[1,64,1536]{2,1,0:T(8,128)(2,1)S(1)} %fusion.101), channel_id=1, source_target_pairs={{0,128},{128,256},{256,384},{1,129},{129,257},{257,385},{2,130},{1... | collective-permute-start | bytes 589832 | tf_op jit(solution)/shard_map/ppermute | solution.py:15
  437.2 26.4 %all-to-all-start.8 = ((bf16[16,2,9216]{2,1,0:T(2,128)(2,1)}), bf16[16,2,9216]{2,1,0:T(2,128)(2,1)S(1)}, u32[]{:S(2)}, u32[]{:S(2)}) async-start(bf16[16,2,9216]{2,1,0:T(2,128)(2,1)} %reshape.659), calls=%async_computation.8 | async-start | bytes 1179648 | tf_op jit(solution)/shard_map/all_to_all | solution.py:113
  465.6 8.0 %copy-start.8 = (f32[2,1,64,64]{3,2,1,0:T(8,128)S(1)}, f32[2,1,64,64]{3,2,1,0:T(8,128)}, u32[]{:S(2)}) copy-start(f32[2,1,64,64]{3,2,1,0:T(8,128)} %param.31) | copy-start | bytes 98308
  465.6 8.1 %copy-start.9 = (f32[2,1,64,64]{3,2,1,0:T(8,128)S(1)}, f32[2,1,64,64]{3,2,1,0:T(8,128)}, u32[]{:S(2)}) copy-start(f32[2,1,64,64]{3,2,1,0:T(8,128)} %param.32) | copy-start | bytes 98308
  465.6 8.1 %copy-start.11 = (bf16[1536,16]{0,1:T(8,128)(2,1)S(1)}, bf16[1536,16]{0,1:T(8,128)(2,1)}, u32[]{:S(2)}) copy-start(bf16[1536,16]{0,1:T(8,128)(2,1)} %param.41) | copy-start | bytes 147460
  465.7 29.0 %copy-start.12 = (f32[1536]{0:T(1024)S(1)}, f32[1536]{0:T(1024)}, u32[]{:S(2)}) copy-start(f32[1536]{0:T(1024)} %param.40) | copy-start | bytes 18436
  466.9 26.8 %all-to-all-start.9 = ((bf16[16,48,128]{2,1,0:T(8,128)(2,1)}), bf16[16,48,128]{2,1,0:T(8,128)(2,1)S(1)}, u32[]{:S(2)}, u32[]{:S(2)}) async-start(bf16[16,48,128]{2,1,0:T(8,128)(2,1)} %reshape.623), calls=%async_computation.9 | async-start | bytes 393216 | tf_op jit(solution)/shard_map/all_to_all | solution.py:125
  473.5 67.0 %reduce-scatter.4.cloned.1.call-start = ((), (), s32[]{:S(2)}) async-start(), calls=%async_computation.12 | async-start | bytes 884736
  493.7 117.8 %copy-start.1 = (bf16[64,1536]{1,0:T(8,128)(2,1)S(1)}, bf16[64,1536]{1,0:T(8,128)(2,1)}, u32[]{:S(2)}) copy-start(bf16[64,1536]{1,0:T(8,128)(2,1)} %param.35) | copy-start | bytes 589828
  496.7 89.4 %collective-permute-start.11 = (f32[2,1,64,16]{2,3,0,1:T(8,128)S(1)}, f32[2,1,64,16]{2,3,0,1:T(8,128)S(1)}, u32[]{:S(2)}, u32[]{:S(2)}) collective-permute-start(f32[2,1,64,16]{2,3,0,1:T(8,128)S(1)} %get-tuple-element.297), channel_id=1, source_target_pairs={{384,0},{385,1},{386,2},{387,3},{388,4},{389,5},{390,6},{391,7},{3... | collective-permute-start | bytes 24584 | tf_op jit(solution)/shard_map/ppermute | solution.py:155
  497.4 89.4 %collective-permute-start.12 = (f32[2,1,64,16]{2,3,0,1:T(8,128)S(1)}, f32[2,1,64,16]{2,3,0,1:T(8,128)S(1)}, u32[]{:S(2)}, u32[]{:S(2)}) collective-permute-start(f32[2,1,64,16]{2,3,0,1:T(8,128)S(1)} %get-tuple-element.295), channel_id=1, source_target_pairs={{384,128},{385,129},{386,130},{387,131},{388,132},{389,133},{390,1... | collective-permute-start | bytes 24584 | tf_op jit(solution)/shard_map/ppermute | solution.py:155
  498.7 88.1 %collective-permute-start.13 = (f32[2,1,64,16]{2,3,0,1:T(8,128)S(1)}, f32[2,1,64,16]{2,3,0,1:T(8,128)S(1)}, u32[]{:S(2)}, u32[]{:S(2)}) collective-permute-start(f32[2,1,64,16]{2,3,0,1:T(8,128)S(1)} %get-tuple-element.296), channel_id=1, source_target_pairs={{384,256},{385,257},{386,258},{387,259},{388,260},{389,261},{390,2... | collective-permute-start | bytes 24584 | tf_op jit(solution)/shard_map/ppermute | solution.py:155
  584.2 3.3 collective-permute-start.14
  584.8 26.1 %collective-permute-start.15 = (f32[192,16]{0,1:T(8,128)S(1)}, f32[192,16]{0,1:T(8,128)S(1)}, u32[]{:S(2)}, u32[]{:S(2)}) collective-permute-start(f32[192,16]{0,1:T(8,128)S(1)} %get-tuple-element.292), channel_id=1, source_target_pairs={{384,128},{385,129},{386,130},{387,131},{388,132},{389,133},{390,1... | collective-permute-start | bytes 36872 | tf_op jit(solution)/shard_map/ppermute | solution.py:156
  586.2 24.7 %collective-permute-start.16 = (f32[192,16]{0,1:T(8,128)S(1)}, f32[192,16]{0,1:T(8,128)S(1)}, u32[]{:S(2)}, u32[]{:S(2)}) collective-permute-start(f32[192,16]{0,1:T(8,128)S(1)} %get-tuple-element.293), channel_id=1, source_target_pairs={{384,256},{385,257},{386,258},{387,259},{388,260},{389,261},{390,2... | collective-permute-start | bytes 36872 | tf_op jit(solution)/shard_map/ppermute | solution.py:156
Sparse Core Ops, SparseCore 0:
  10.1 112.7 all-gather.2
  496.8 43.6 reduce-scatter.3

commit v10 on v9

--- a/solution.py
+++ b/solution.py
@@ -63,6 +63,7 @@
     source_step = (dp_index - jnp.arange(dp_count, dtype=jnp.int32)) % dp_count
     full_key = jnp.take(by_step, source_step, axis=0).reshape(model_width, model_width)
     head_full = lax.all_gather(head_weight, "pipe", axis=1, tiled=True)
+    full_query, full_key, head_full = lax.optimization_barrier((full_query, full_key, head_full))
     section_gain = norm_gain[0]
 
     def attention(by_heads, frame_row):

time: 628 us -> 650 us (1.035)
  blocking collectives: 149 us -> 211 us
  waiting for transfers between devices: 271 us -> 236 us
    all_gather x1, blocking collectives: 20 us -> 83.1 us  [on_device(): head_full = lax.all_gather(head_weight, 'pipe', axis=1, tiled=True)]
    ppermute x7, waiting for transfers between devices: 60.5 us -> 9.26 us  [on_device(): key_blocks.append(lax.ppermute(key_weight[0], 'dp', pairs))]
    all_to_all x1, waiting for transfers between devices: 0.01 us -> 14.7 us  [on_device(): lax.all_to_all(outgoing, 'ctx', split_axis=0, concat_axis=0, tiled=True)]
    unnamed x37 -> x35, local copies, waits for them, and re-layouts: 25.5 us -> 25.5 us
  transfers between devices with their start and end apart: 25 -> 25, of which waited for: 16 -> 14; matrix products, arithmetic and copies ran while one was open for 4% -> 4% of each run, Pallas kernels for 0% -> 0%
where the time goes in v10:
time: 650 us; the launch traced here: 640 us
  waiting for transfers between devices  236 us (36%)
  blocking collectives  211 us (32%)
  starting transfers between devices  98.3 us (15%)
  local copies, waits for them, and re-layouts  50.4 us (8%)
  between operations  15.1 us (2%)
  matrix products  14.6 us (2%)
  other arithmetic  14.3 us (2%)
    all_to_all x5, waiting for transfers between devices, on_device(): lax.all_to_all(triple, 'ctx', split_axis=2, concat_axis=1, tiled=True)  132 us
    all_to_all x4, blocking collectives, on_device(): lax.all_to_all(outgoing, 'ctx', split_axis=0, concat_axis=0, tiled=True)  84.8 us
    all_gather x1, blocking collectives, on_device(): head_full = lax.all_gather(head_weight, 'pipe', axis=1, tiled=True)  83.1 us
    unnamed x3, waiting for transfers between devices  45.2 us
    psum x1, blocking collectives, on_device(): grad_rows = lax.psum(grad_rows, 'ctx')  42.7 us
    all_to_all x5, starting transfers between devices, on_device(): lax.all_to_all(triple, 'ctx', split_axis=2, concat_axis=1, tiled=True)  35 us
    ppermute x4, starting transfers between devices, shifted(): lax.ppermute(value, axis, [(source, source + steps) for source in range(f...  29.9 us
    unnamed x35, local copies, waits for them, and re-layouts  25.5 us
  transfers between devices with their start and end apart: 25, of which 14 were waited for; matrix products, arithmetic and copies ran while one was open for 4% of the time, Pallas kernels for 0%

profile of v10, /device:TPU:1, one launch (start us, length us, event | category | flops | bytes accessed | tf_op | source)
XLA Modules:
  0.0 640.4 jit_solution(18411379174098207080)
XLA Ops:
  7.9 4.0 collective-permute-start
  11.9 4.4 collective-permute-start.1
  16.3 4.1 collective-permute-start.2
  20.3 2.1 collective-permute-start.3
  22.4 3.2 collective-permute-start.4
  28.5 1.2 fusion.88
  29.9 1.9 constant_dynamic-update-slice_fusion
  31.9 83.1 %all_gather.7 = bf16[1536,64]{0,1:T(8,128)(2,1)S(1)} all-gather(bf16[1536,16]{0,1:T(8,128)(2,1)} %param.41), channel_id=1, replica_groups=mesh['pipe'=4,'ctx'=16,'dp'=8] {'pipe'}, dimensions={1}, use_global_device_ids=true | all-gather | bytes 245760 | tf_op jit(solution)/shard_map/all_gather | solution.py:65
  115.3 1.9 collective-permute-start.5
  117.3 1.9 bitcast_dynamic-update-slice_fusion.6
  119.2 1.9 collective-permute-start.6
  121.1 1.9 bitcast_dynamic-update-slice_fusion.5
  125.7 8.0 %collective-permute-done.5 = bf16[192,1536]{1,0:T(8,128)(2,1)S(1)} collective-permute-done((bf16[192,1536]{1,0:T(8,128)(2,1)}, bf16[192,1536]{1,0:T(8,128)(2,1)S(1)}, u32[]{:S(2)}, u32[]{:S(2)}) %collective-permute-start.5) | collective-permute-done | bytes 589856 | tf_op jit(solution)/shard_map/ppermute | solution.py:61
  134.7 1.2 collective-permute-done.6
  136.7 5.4 gather_fusion
  142.1 5.0 bitcast_select_fusion
  148.3 1.8 reshape.651
  150.1 14.9 %all-to-all-start = ((bf16[16,2,9216]{2,1,0:T(2,128)(2,1)}), bf16[16,2,9216]{2,1,0:T(2,128)(2,1)S(1)}, u32[]{:S(2)}, u32[]{:S(2)}) async-start(bf16[16,2,9216]{2,1,0:T(2,128)(2,1)} %reshape.651), calls=%async_computation | async-start | bytes 1179648 | tf_op jit(solution)/shard_map/all_to_all | solution.py:114
  165.0 22.5 %all-to-all-done = bf16[16,2,9216]{2,1,0:T(2,128)(2,1)S(1)} async-done(((bf16[16,2,9216]{2,1,0:T(2,128)(2,1)}), bf16[16,2,9216]{2,1,0:T(2,128)(2,1)S(1)}, u32[]{:S(2)}, u32[]{:S(2)}) %all-to-all-start) | async-done | bytes 589856 | tf_op jit(solution)/shard_map/all_to_all | solution.py:114
  190.1 25.3 %all_to_all.105 = bf16[16,48,128]{2,1,0:T(8,128)(2,1)S(1)} all-to-all(bf16[16,48,128]{2,1,0:T(8,128)(2,1)S(1)} %reshape.619), channel_id=1, replica_groups=mesh['pipe'=4,'ctx'=16,'dp'=8] {'ctx'}, dimensions={0} | all-to-all | bytes 393216 | tf_op jit(solution)/shard_map/all_to_all | solution.py:126
  216.1 9.6 %collective-permute-start.7 = (bf16[1,64,1536]{2,1,0:T(8,128)(2,1)S(1)}, bf16[1,64,1536]{2,1,0:T(8,128)(2,1)S(1)}, u32[]{:S(2)}, u32[]{:S(2)}) collective-permute-start(bf16[1,64,1536]{2,1,0:T(8,128)(2,1)S(1)} %fusion.109), channel_id=1, source_target_pairs={{0,128},{128,256},{256,384},{1,129},{129,257},{257,385},{2,130},{1... | collective-permute-start | bytes 589832 | tf_op jit(solution)/shard_map/ppermute | solution.py:15
  225.7 2.6 collective-permute-done.7
  228.6 5.2 conditional.12
  229.1 3.4 fusion.16
  233.9 1.0 copy.39
  234.9 1.8 reshape.653
  236.7 4.6 all-to-all-start.2
  241.3 32.0 %all-to-all-done.2 = bf16[16,2,9216]{2,1,0:T(2,128)(2,1)S(1)} async-done(((bf16[16,2,9216]{2,1,0:T(2,128)(2,1)}), bf16[16,2,9216]{2,1,0:T(2,128)(2,1)S(1)}, u32[]{:S(2)}, u32[]{:S(2)}) %all-to-all-start.2) | async-done | bytes 589856 | tf_op jit(solution)/shard_map/all_to_all | solution.py:114
  275.3 3.8 conditional.13
  276.4 1.5 fusion.21
  277.9 1.2 fusion.28
  279.7 18.6 %all_to_all.106 = bf16[16,48,128]{2,1,0:T(8,128)(2,1)S(1)} all-to-all(bf16[16,48,128]{2,1,0:T(8,128)(2,1)S(1)} %reshape.620), channel_id=1, replica_groups=mesh['pipe'=4,'ctx'=16,'dp'=8] {'ctx'}, dimensions={0} | all-to-all | bytes 393216 | tf_op jit(solution)/shard_map/all_to_all | solution.py:126
  299.1 1.9 collective-permute-start.8
  301.1 4.0 collective-permute-done.8
  305.3 4.8 conditional.14
  305.4 3.4 fusion.34
  311.2 1.8 reshape.655
  313.0 7.1 %all-to-all-start.4 = ((bf16[16,2,9216]{2,1,0:T(2,128)(2,1)}), bf16[16,2,9216]{2,1,0:T(2,128)(2,1)S(1)}, u32[]{:S(2)}, u32[]{:S(2)}) async-start(bf16[16,2,9216]{2,1,0:T(2,128)(2,1)} %reshape.655), calls=%async_computation.4 | async-start | bytes 1179648 | tf_op jit(solution)/shard_map/all_to_all | solution.py:114
  320.1 27.0 %all-to-all-done.4 = bf16[16,2,9216]{2,1,0:T(2,128)(2,1)S(1)} async-done(((bf16[16,2,9216]{2,1,0:T(2,128)(2,1)}), bf16[16,2,9216]{2,1,0:T(2,128)(2,1)S(1)}, u32[]{:S(2)}, u32[]{:S(2)}) %all-to-all-start.4) | async-done | bytes 589856 | tf_op jit(solution)/shard_map/all_to_all | solution.py:114
  349.0 4.0 conditional.15
  350.3 1.5 fusion.39
  351.8 1.2 fusion.46
  353.6 20.2 %all_to_all.107 = bf16[16,48,128]{2,1,0:T(8,128)(2,1)S(1)} all-to-all(bf16[16,48,128]{2,1,0:T(8,128)(2,1)S(1)} %reshape.621), channel_id=1, replica_groups=mesh['pipe'=4,'ctx'=16,'dp'=8] {'ctx'}, dimensions={0} | all-to-all | bytes 393216 | tf_op jit(solution)/shard_map/all_to_all | solution.py:126
  374.6 3.5 collective-permute-start.9
  378.1 2.6 collective-permute-done.9
  381.1 1.0 copy.49
  382.1 1.8 reshape.657
  383.9 4.8 all-to-all-start.6
  388.7 27.5 %all-to-all-done.6 = bf16[16,2,9216]{2,1,0:T(2,128)(2,1)S(1)} async-done(((bf16[16,2,9216]{2,1,0:T(2,128)(2,1)}), bf16[16,2,9216]{2,1,0:T(2,128)(2,1)S(1)}, u32[]{:S(2)}, u32[]{:S(2)}) %all-to-all-start.6) | async-done | bytes 589856 | tf_op jit(solution)/shard_map/all_to_all | solution.py:114
  418.8 20.7 %all_to_all.108 = bf16[16,48,128]{2,1,0:T(8,128)(2,1)S(1)} all-to-all(bf16[16,48,128]{2,1,0:T(8,128)(2,1)S(1)} %reshape.622), channel_id=1, replica_groups=mesh['pipe'=4,'ctx'=16,'dp'=8] {'ctx'}, dimensions={0} | all-to-all | bytes 393216 | tf_op jit(solution)/shard_map/all_to_all | solution.py:126
  440.3 14.9 %collective-permute-start.10 = (bf16[1,64,1536]{2,1,0:T(8,128)(2,1)S(1)}, bf16[1,64,1536]{2,1,0:T(8,128)(2,1)S(1)}, u32[]{:S(2)}, u32[]{:S(2)}) collective-permute-start(bf16[1,64,1536]{2,1,0:T(8,128)(2,1)S(1)} %fusion.101), channel_id=1, source_target_pairs={{0,128},{128,256},{256,384},{1,129},{129,257},{257,385},{2,130},{1... | collective-permute-start | bytes 589832 | tf_op jit(solution)/shard_map/ppermute | solution.py:15
  455.2 2.6 collective-permute-done.10
  459.2 1.8 reshape.659
  461.1 3.6 all-to-all-start.8
  464.6 22.8 %all-to-all-done.8 = bf16[16,2,9216]{2,1,0:T(2,128)(2,1)S(1)} async-done(((bf16[16,2,9216]{2,1,0:T(2,128)(2,1)}), bf16[16,2,9216]{2,1,0:T(2,128)(2,1)S(1)}, u32[]{:S(2)}, u32[]{:S(2)}) %all-to-all-start.8) | async-done | bytes 589856 | tf_op jit(solution)/shard_map/all_to_all | solution.py:114
  489.7 1.0 reshape.623
  490.7 6.6 %all-to-all-start.9 = ((bf16[16,48,128]{2,1,0:T(8,128)(2,1)}), bf16[16,48,128]{2,1,0:T(8,128)(2,1)S(1)}, u32[]{:S(2)}, u32[]{:S(2)}) async-start(bf16[16,48,128]{2,1,0:T(8,128)(2,1)} %reshape.623), calls=%async_computation.9 | async-start | bytes 393216 | tf_op jit(solution)/shard_map/all_to_all | solution.py:126
  497.5 14.7 %all-to-all-done.9 = bf16[16,48,128]{2,1,0:T(8,128)(2,1)S(1)} async-done(((bf16[16,48,128]{2,1,0:T(8,128)(2,1)}), bf16[16,48,128]{2,1,0:T(8,128)(2,1)S(1)}, u32[]{:S(2)}, u32[]{:S(2)}) %all-to-all-start.9) | async-done | bytes 196640 | tf_op jit(solution)/shard_map/all_to_all | solution.py:126
  514.0 1.2 copy.67
  515.9 1.3 collective-permute-start.12
  517.9 44.5 %reduce-scatter.4.cloned.1.call-done = f32[192,64]{1,0:T(8,128)} async-done(((f32[1536,64]{1,0:T(8,128)}), f32[192,64]{1,0:T(8,128)}) %reduce-scatter.4.cloned.1.call-update) | async-done | bytes 49168
  563.4 42.7 %psum.7 = f32[192,64]{0,1:T(8,128)S(1)} all-reduce(f32[192,64]{0,1:T(8,128)S(1)} %copy.68), channel_id=1, replica_groups=mesh['pipe'=4,'ctx'=16,'dp'=8] {'ctx'}, use_global_device_ids=true, to_apply=%region_37.38 | all-reduce | flops 12288 | bytes 98304 | tf_op jit(solution)/shard_map/psum | solution.py:150
  606.8 1.3 collective-permute-start.15
  609.4 23.3 %collective-permute-done.15 = f32[192,16]{0,1:T(8,128)S(1)} collective-permute-done((f32[192,16]{0,1:T(8,128)S(1)}, f32[192,16]{0,1:T(8,128)S(1)}, u32[]{:S(2)}, u32[]{:S(2)}) %collective-permute-start.15) | collective-permute-done | bytes 12320 | tf_op jit(solution)/shard_map/ppermute | solution.py:157
  (144 shorter events, 39.8 us)
Async XLA Ops:
  7.2 21.4 %copy-start = (bf16[64,1536]{1,0:T(8,128)(2,1)S(1)}, bf16[64,1536]{1,0:T(8,128)(2,1)}, u32[]{:S(2)}) copy-start(bf16[64,1536]{1,0:T(8,128)(2,1)} %param.35) | copy-start | bytes 589828
  7.2 112.0 %copy-start.7 = (bf16[1,192,1536]{2,1,0:T(8,128)(2,1)S(1)}, bf16[1,192,1536]{2,1,0:T(8,128)(2,1)}, u32[]{:S(2)}) copy-start(bf16[1,192,1536]{2,1,0:T(8,128)(2,1)} %param.38) | copy-start | bytes 1769476
  7.2 140.0 %all-gather.3.cloned.1.call-start = ((), (), s32[]{:S(2)}) async-start(), calls=%async_computation.11 | async-start | bytes 5308416 | tf_op jit(solution)/shard_map/all_gather | solution.py:57
  7.9 107.4 %collective-permute-start = (bf16[192,1536]{1,0:T(8,128)(2,1)}, bf16[192,1536]{1,0:T(8,128)(2,1)}, u32[]{:S(2)}, u32[]{:S(2)}) collective-permute-start(bf16[192,1536]{1,0:T(8,128)(2,1)} %bitcast.194), channel_id=1, source_target_pairs={{0,1},{1,2},{2,3},{3,4},{4,5},{5,6},{6,7},{7,0},{8,9},{9,10},{10,1... | collective-permute-start | bytes 1769480 | tf_op jit(solution)/shard_map/ppermute | solution.py:61
  11.9 107.3 %collective-permute-start.1 = (bf16[192,1536]{1,0:T(8,128)(2,1)}, bf16[192,1536]{1,0:T(8,128)(2,1)}, u32[]{:S(2)}, u32[]{:S(2)}) collective-permute-start(bf16[192,1536]{1,0:T(8,128)(2,1)} %bitcast.195), channel_id=1, source_target_pairs={{0,2},{1,3},{2,4},{3,5},{4,6},{5,7},{6,0},{7,1},{8,10},{9,11},{10,... | collective-permute-start | bytes 1769480 | tf_op jit(solution)/shard_map/ppermute | solution.py:61
  16.3 106.8 %collective-permute-start.2 = (bf16[192,1536]{1,0:T(8,128)(2,1)}, bf16[192,1536]{1,0:T(8,128)(2,1)S(1)}, u32[]{:S(2)}, u32[]{:S(2)}) collective-permute-start(bf16[192,1536]{1,0:T(8,128)(2,1)} %bitcast.196), channel_id=1, source_target_pairs={{0,3},{1,4},{2,5},{3,6},{4,7},{5,0},{6,1},{7,2},{8,11},{9,12},{10,... | collective-permute-start | bytes 1769480 | tf_op jit(solution)/shard_map/ppermute | solution.py:61
  20.3 103.6 %collective-permute-start.3 = (bf16[192,1536]{1,0:T(8,128)(2,1)}, bf16[192,1536]{1,0:T(8,128)(2,1)S(1)}, u32[]{:S(2)}, u32[]{:S(2)}) collective-permute-start(bf16[192,1536]{1,0:T(8,128)(2,1)} %bitcast.197), channel_id=1, source_target_pairs={{0,4},{1,5},{2,6},{3,7},{4,0},{5,1},{6,2},{7,3},{8,12},{9,13},{10,... | collective-permute-start | bytes 1769480 | tf_op jit(solution)/shard_map/ppermute | solution.py:61
  22.4 102.4 %collective-permute-start.4 = (bf16[192,1536]{1,0:T(8,128)(2,1)}, bf16[192,1536]{1,0:T(8,128)(2,1)S(1)}, u32[]{:S(2)}, u32[]{:S(2)}) collective-permute-start(bf16[192,1536]{1,0:T(8,128)(2,1)} %bitcast.198), channel_id=1, source_target_pairs={{0,5},{1,6},{2,7},{3,0},{4,1},{5,2},{6,3},{7,4},{8,13},{9,14},{10,... | collective-permute-start | bytes 1769480 | tf_op jit(solution)/shard_map/ppermute | solution.py:61
  115.3 18.4 %collective-permute-start.5 = (bf16[192,1536]{1,0:T(8,128)(2,1)}, bf16[192,1536]{1,0:T(8,128)(2,1)S(1)}, u32[]{:S(2)}, u32[]{:S(2)}) collective-permute-start(bf16[192,1536]{1,0:T(8,128)(2,1)} %bitcast.199), channel_id=1, source_target_pairs={{0,6},{1,7},{2,0},{3,1},{4,2},{5,3},{6,4},{7,5},{8,14},{9,15},{10,... | collective-permute-start | bytes 1769480 | tf_op jit(solution)/shard_map/ppermute | solution.py:61
  119.2 16.7 %collective-permute-start.6 = (bf16[192,1536]{1,0:T(8,128)(2,1)S(1)}, bf16[192,1536]{1,0:T(8,128)(2,1)S(1)}, u32[]{:S(2)}, u32[]{:S(2)}) collective-permute-start(bf16[192,1536]{1,0:T(8,128)(2,1)S(1)} %bitcast.200), channel_id=1, source_target_pairs={{0,7},{1,0},{2,1},{3,2},{4,3},{5,4},{6,5},{7,6},{8,15},{9,8},{10,9... | collective-permute-start | bytes 1769480 | tf_op jit(solution)/shard_map/ppermute | solution.py:61
  148.3 41.2 %copy-start.10 = (s32[2,1,1024]{2,1,0:T(1,128)S(1)}, s32[2,1,1024]{2,1,0:T(1,128)}, u32[]{:S(2)}) copy-start(s32[2,1,1024]{2,1,0:T(1,128)} %param.34) | copy-start | bytes 24580
  150.1 37.4 %all-to-all-start = ((bf16[16,2,9216]{2,1,0:T(2,128)(2,1)}), bf16[16,2,9216]{2,1,0:T(2,128)(2,1)S(1)}, u32[]{:S(2)}, u32[]{:S(2)}) async-start(bf16[16,2,9216]{2,1,0:T(2,128)(2,1)} %reshape.651), calls=%async_computation | async-start | bytes 1179648 | tf_op jit(solution)/shard_map/all_to_all | solution.py:114
  216.1 12.2 %collective-permute-start.7 = (bf16[1,64,1536]{2,1,0:T(8,128)(2,1)S(1)}, bf16[1,64,1536]{2,1,0:T(8,128)(2,1)S(1)}, u32[]{:S(2)}, u32[]{:S(2)}) collective-permute-start(bf16[1,64,1536]{2,1,0:T(8,128)(2,1)S(1)} %fusion.109), channel_id=1, source_target_pairs={{0,128},{128,256},{256,384},{1,129},{129,257},{257,385},{2,130},{1... | collective-permute-start | bytes 589832 | tf_op jit(solution)/shard_map/ppermute | solution.py:15
  229.1 3.8 copy-start.3
  236.7 36.6 %all-to-all-start.2 = ((bf16[16,2,9216]{2,1,0:T(2,128)(2,1)}), bf16[16,2,9216]{2,1,0:T(2,128)(2,1)S(1)}, u32[]{:S(2)}, u32[]{:S(2)}) async-start(bf16[16,2,9216]{2,1,0:T(2,128)(2,1)} %reshape.653), calls=%async_computation.2 | async-start | bytes 1179648 | tf_op jit(solution)/shard_map/all_to_all | solution.py:114
  299.1 5.9 collective-permute-start.8
  305.4 3.8 copy-start.4
  313.0 34.1 %all-to-all-start.4 = ((bf16[16,2,9216]{2,1,0:T(2,128)(2,1)}), bf16[16,2,9216]{2,1,0:T(2,128)(2,1)S(1)}, u32[]{:S(2)}, u32[]{:S(2)}) async-start(bf16[16,2,9216]{2,1,0:T(2,128)(2,1)} %reshape.655), calls=%async_computation.4 | async-start | bytes 1179648 | tf_op jit(solution)/shard_map/all_to_all | solution.py:114
  374.6 6.1 collective-permute-start.9
  383.9 32.3 %all-to-all-start.6 = ((bf16[16,2,9216]{2,1,0:T(2,128)(2,1)}), bf16[16,2,9216]{2,1,0:T(2,128)(2,1)S(1)}, u32[]{:S(2)}, u32[]{:S(2)}) async-start(bf16[16,2,9216]{2,1,0:T(2,128)(2,1)} %reshape.657), calls=%async_computation.6 | async-start | bytes 1179648 | tf_op jit(solution)/shard_map/all_to_all | solution.py:114
  440.3 17.5 %collective-permute-start.10 = (bf16[1,64,1536]{2,1,0:T(8,128)(2,1)S(1)}, bf16[1,64,1536]{2,1,0:T(8,128)(2,1)S(1)}, u32[]{:S(2)}, u32[]{:S(2)}) collective-permute-start(bf16[1,64,1536]{2,1,0:T(8,128)(2,1)S(1)} %fusion.101), channel_id=1, source_target_pairs={{0,128},{128,256},{256,384},{1,129},{129,257},{257,385},{2,130},{1... | collective-permute-start | bytes 589832 | tf_op jit(solution)/shard_map/ppermute | solution.py:15
  461.1 26.4 %all-to-all-start.8 = ((bf16[16,2,9216]{2,1,0:T(2,128)(2,1)}), bf16[16,2,9216]{2,1,0:T(2,128)(2,1)S(1)}, u32[]{:S(2)}, u32[]{:S(2)}) async-start(bf16[16,2,9216]{2,1,0:T(2,128)(2,1)} %reshape.659), calls=%async_computation.8 | async-start | bytes 1179648 | tf_op jit(solution)/shard_map/all_to_all | solution.py:114
  489.4 8.0 %copy-start.8 = (f32[2,1,64,64]{3,2,1,0:T(8,128)S(1)}, f32[2,1,64,64]{3,2,1,0:T(8,128)}, u32[]{:S(2)}) copy-start(f32[2,1,64,64]{3,2,1,0:T(8,128)} %param.31) | copy-start | bytes 98308
  489.4 8.0 %copy-start.9 = (f32[2,1,64,64]{3,2,1,0:T(8,128)S(1)}, f32[2,1,64,64]{3,2,1,0:T(8,128)}, u32[]{:S(2)}) copy-start(f32[2,1,64,64]{3,2,1,0:T(8,128)} %param.32) | copy-start | bytes 98308
  489.5 23.7 %copy-start.11 = (f32[1536]{0:T(1024)S(1)}, f32[1536]{0:T(1024)}, u32[]{:S(2)}) copy-start(f32[1536]{0:T(1024)} %param.40) | copy-start | bytes 18436
  490.7 21.6 %all-to-all-start.9 = ((bf16[16,48,128]{2,1,0:T(8,128)(2,1)}), bf16[16,48,128]{2,1,0:T(8,128)(2,1)S(1)}, u32[]{:S(2)}, u32[]{:S(2)}) async-start(bf16[16,48,128]{2,1,0:T(8,128)(2,1)} %reshape.623), calls=%async_computation.9 | async-start | bytes 393216 | tf_op jit(solution)/shard_map/all_to_all | solution.py:126
  497.3 65.1 %reduce-scatter.4.cloned.1.call-start = ((), (), s32[]{:S(2)}) async-start(), calls=%async_computation.12 | async-start | bytes 884736
  512.3 121.1 %copy-start.1 = (bf16[64,1536]{1,0:T(8,128)(2,1)S(1)}, bf16[64,1536]{1,0:T(8,128)(2,1)}, u32[]{:S(2)}) copy-start(bf16[64,1536]{1,0:T(8,128)(2,1)} %param.35) | copy-start | bytes 589828
  515.3 92.8 %collective-permute-start.11 = (f32[2,1,64,16]{2,3,0,1:T(8,128)S(1)}, f32[2,1,64,16]{2,3,0,1:T(8,128)S(1)}, u32[]{:S(2)}, u32[]{:S(2)}) collective-permute-start(f32[2,1,64,16]{2,3,0,1:T(8,128)S(1)} %get-tuple-element.303), channel_id=1, source_target_pairs={{384,0},{385,1},{386,2},{387,3},{388,4},{389,5},{390,6},{391,7},{3... | collective-permute-start | bytes 24584 | tf_op jit(solution)/shard_map/ppermute | solution.py:156
  515.9 92.8 %collective-permute-start.12 = (f32[2,1,64,16]{2,3,0,1:T(8,128)S(1)}, f32[2,1,64,16]{2,3,0,1:T(8,128)S(1)}, u32[]{:S(2)}, u32[]{:S(2)}) collective-permute-start(f32[2,1,64,16]{2,3,0,1:T(8,128)S(1)} %get-tuple-element.301), channel_id=1, source_target_pairs={{384,128},{385,129},{386,130},{387,131},{388,132},{389,133},{390,1... | collective-permute-start | bytes 24584 | tf_op jit(solution)/shard_map/ppermute | solution.py:156
  517.2 91.5 %collective-permute-start.13 = (f32[2,1,64,16]{2,3,0,1:T(8,128)S(1)}, f32[2,1,64,16]{2,3,0,1:T(8,128)S(1)}, u32[]{:S(2)}, u32[]{:S(2)}) collective-permute-start(f32[2,1,64,16]{2,3,0,1:T(8,128)S(1)} %get-tuple-element.302), channel_id=1, source_target_pairs={{384,256},{385,257},{386,258},{387,259},{388,260},{389,261},{390,2... | collective-permute-start | bytes 24584 | tf_op jit(solution)/shard_map/ppermute | solution.py:156
  606.1 3.3 collective-permute-start.14
  606.8 26.0 %collective-permute-start.15 = (f32[192,16]{0,1:T(8,128)S(1)}, f32[192,16]{0,1:T(8,128)S(1)}, u32[]{:S(2)}, u32[]{:S(2)}) collective-permute-start(f32[192,16]{0,1:T(8,128)S(1)} %get-tuple-element.298), channel_id=1, source_target_pairs={{384,128},{385,129},{386,130},{387,131},{388,132},{389,133},{390,1... | collective-permute-start | bytes 36872 | tf_op jit(solution)/shard_map/ppermute | solution.py:157
  608.1 24.7 %collective-permute-start.16 = (f32[192,16]{0,1:T(8,128)S(1)}, f32[192,16]{0,1:T(8,128)S(1)}, u32[]{:S(2)}, u32[]{:S(2)}) collective-permute-start(f32[192,16]{0,1:T(8,128)S(1)} %get-tuple-element.299), channel_id=1, source_target_pairs={{384,256},{385,257},{386,258},{387,259},{388,260},{389,261},{390,2... | collective-permute-start | bytes 36872 | tf_op jit(solution)/shard_map/ppermute | solution.py:157
Sparse Core Ops, SparseCore 0:
  10.1 102.7 all-gather.2
  515.4 47.0 reduce-scatter.3

commit v11 on v9

--- a/solution.py
+++ b/solution.py
@@ -62,7 +62,14 @@
     by_step = jnp.stack(key_blocks, axis=0)
     source_step = (dp_index - jnp.arange(dp_count, dtype=jnp.int32)) % dp_count
     full_key = jnp.take(by_step, source_step, axis=0).reshape(model_width, model_width)
-    head_full = lax.all_gather(head_weight, "pipe", axis=1, tiled=True)
+    last_phase = phase_count - 1
+    head_pieces = []
+    for source_phase in range(phase_count):
+        if source_phase == last_phase:
+            head_pieces.append(head_weight)
+        else:
+            head_pieces.append(lax.ppermute(head_weight, "pipe", [(source_phase, last_phase)]))
+    head_full = jnp.concatenate(head_pieces, axis=1)
     section_gain = norm_gain[0]
 
     def attention(by_heads, frame_row):
@@ -134,7 +141,6 @@
         if moment >= phase_count - 1:
             finals.append(result)
     final_state = jnp.stack(finals, axis=0)
-    last_phase = phase_count - 1
     is_last = phase_index == last_phase
     head_cols = head_weight.shape[1]
     final_norm = rms_scale(final_state.astype(jnp.float32), head_gain).astype(jnp.bfloat16)

time: 628 us -> 628 us (level)
  blocking collectives: 149 us -> 129 us
  starting transfers between devices: 104 us -> 123 us
    all_gather x1 -> x0, blocking collectives: 20 us -> none  [on_device(): head_full = lax.all_gather(head_weight, 'pipe', axis=1, tiled=True)]
    ppermute x0 -> x3, starting transfers between devices: none -> 19.6 us  [on_device(): lax.ppermute(head_weight, 'pipe', [(source_phase, last_phase)])]
  transfers between devices with their start and end apart: 25 -> 28, of which waited for: 16 -> 16; matrix products, arithmetic and copies ran while one was open for 4% -> 5% of each run, Pallas kernels for 0% -> 0%
where the time goes in v11:
time: 628 us; the launch traced here: 619 us
  waiting for transfers between devices  271 us (43%)
  blocking collectives  129 us (21%)
  starting transfers between devices  123 us (20%)
  local copies, waits for them, and re-layouts  50.5 us (8%)
  between operations  15.2 us (2%)
  matrix products  14.6 us (2%)
  other arithmetic  14.3 us (2%)
    all_to_all x5, waiting for transfers between devices, on_device(): lax.all_to_all(triple, 'ctx', split_axis=2, concat_axis=1, tiled=True)  127 us
    all_to_all x4, blocking collectives, on_device(): lax.all_to_all(outgoing, 'ctx', split_axis=0, concat_axis=0, tiled=True)  86.2 us
    ppermute x7, waiting for transfers between devices, on_device(): key_blocks.append(lax.ppermute(key_weight[0], 'dp', pairs))  60.4 us
    psum x1, blocking collectives, on_device(): grad_rows = lax.psum(grad_rows, 'ctx')  43 us
    unnamed x3, waiting for transfers between devices  41.8 us
    all_to_all x5, starting transfers between devices, on_device(): lax.all_to_all(triple, 'ctx', split_axis=2, concat_axis=1, tiled=True)  36.1 us
    ppermute x4, starting transfers between devices, shifted(): lax.ppermute(value, axis, [(source, source + steps) for source in range(f...  32.8 us
    unnamed x37, local copies, waits for them, and re-layouts  25.4 us
  transfers between devices with their start and end apart: 28, of which 16 were waited for; matrix products, arithmetic and copies ran while one was open for 5% of the time, Pallas kernels for 0%

profile of v11, /device:TPU:1, one launch (start us, length us, event | category | flops | bytes accessed | tf_op | source)
XLA Modules:
  0.0 618.6 jit_solution(10819170111531097860)
XLA Ops:
  7.9 4.0 collective-permute-start
  11.9 4.4 collective-permute-start.1
  16.3 4.1 collective-permute-start.2
  20.3 2.1 collective-permute-start.3
  22.4 3.2 collective-permute-start.4
  28.5 1.2 fusion.88
  29.8 2.0 constant_dynamic-update-slice_fusion
  32.2 3.3 collective-permute-start.5
  35.6 1.9 bitcast_dynamic-update-slice_fusion.6
  37.5 12.0 %collective-permute-done.1 = bf16[192,1536]{1,0:T(8,128)(2,1)} collective-permute-done((bf16[192,1536]{1,0:T(8,128)(2,1)}, bf16[192,1536]{1,0:T(8,128)(2,1)}, u32[]{:S(2)}, u32[]{:S(2)}) %collective-permute-start.1) | collective-permute-done | bytes 589856 | tf_op jit(solution)/shard_map/ppermute | solution.py:61
  49.5 1.9 collective-permute-start.6
  51.4 1.9 bitcast_dynamic-update-slice_fusion.5
  54.2 29.6 %collective-permute-done.3 = bf16[192,1536]{1,0:T(8,128)(2,1)S(1)} collective-permute-done((bf16[192,1536]{1,0:T(8,128)(2,1)}, bf16[192,1536]{1,0:T(8,128)(2,1)S(1)}, u32[]{:S(2)}, u32[]{:S(2)}) %collective-permute-start.3) | collective-permute-done | bytes 589856 | tf_op jit(solution)/shard_map/ppermute | solution.py:61
  85.6 10.5 %collective-permute-done.5 = bf16[192,1536]{1,0:T(8,128)(2,1)S(1)} collective-permute-done((bf16[192,1536]{1,0:T(8,128)(2,1)}, bf16[192,1536]{1,0:T(8,128)(2,1)S(1)}, u32[]{:S(2)}, u32[]{:S(2)}) %collective-permute-start.5) | collective-permute-done | bytes 589856 | tf_op jit(solution)/shard_map/ppermute | solution.py:61
  97.0 8.4 %collective-permute-done.6 = bf16[192,1536]{1,0:T(8,128)(2,1)S(1)} collective-permute-done((bf16[192,1536]{1,0:T(8,128)(2,1)S(1)}, bf16[192,1536]{1,0:T(8,128)(2,1)S(1)}, u32[]{:S(2)}, u32[]{:S(2)}) %collective-permute-start.6) | collective-permute-done | bytes 589856 | tf_op jit(solution)/shard_map/ppermute | solution.py:61
  106.2 5.5 gather_fusion
  111.7 5.1 bitcast_select_fusion
  116.7 6.2 all-gather.3.cloned.1.call-done
  124.0 1.8 reshape.651
  125.8 15.6 %all-to-all-start = ((bf16[16,2,9216]{2,1,0:T(2,128)(2,1)}), bf16[16,2,9216]{2,1,0:T(2,128)(2,1)S(1)}, u32[]{:S(2)}, u32[]{:S(2)}) async-start(bf16[16,2,9216]{2,1,0:T(2,128)(2,1)} %reshape.651), calls=%async_computation | async-start | bytes 1179648 | tf_op jit(solution)/shard_map/all_to_all | solution.py:120
  141.4 22.1 %all-to-all-done = bf16[16,2,9216]{2,1,0:T(2,128)(2,1)S(1)} async-done(((bf16[16,2,9216]{2,1,0:T(2,128)(2,1)}), bf16[16,2,9216]{2,1,0:T(2,128)(2,1)S(1)}, u32[]{:S(2)}, u32[]{:S(2)}) %all-to-all-start) | async-done | bytes 589856 | tf_op jit(solution)/shard_map/all_to_all | solution.py:120
  166.1 25.1 %all_to_all.105 = bf16[16,48,128]{2,1,0:T(8,128)(2,1)S(1)} all-to-all(bf16[16,48,128]{2,1,0:T(8,128)(2,1)S(1)} %reshape.619), channel_id=1, replica_groups=mesh['pipe'=4,'ctx'=16,'dp'=8] {'ctx'}, dimensions={0} | all-to-all | bytes 393216 | tf_op jit(solution)/shard_map/all_to_all | solution.py:132
  192.0 12.4 %collective-permute-start.7 = (bf16[1,64,1536]{2,1,0:T(8,128)(2,1)S(1)}, bf16[1,64,1536]{2,1,0:T(8,128)(2,1)S(1)}, u32[]{:S(2)}, u32[]{:S(2)}) collective-permute-start(bf16[1,64,1536]{2,1,0:T(8,128)(2,1)S(1)} %fusion.109), channel_id=1, source_target_pairs={{0,128},{128,256},{256,384},{1,129},{129,257},{257,385},{2,130},{1... | collective-permute-start | bytes 589832 | tf_op jit(solution)/shard_map/ppermute | solution.py:15
  204.5 2.6 collective-permute-done.7
  207.4 5.2 conditional.12
  207.4 3.4 fusion.16
  213.7 1.8 reshape.653
  215.5 4.7 all-to-all-start.2
  220.2 28.1 %all-to-all-done.2 = bf16[16,2,9216]{2,1,0:T(2,128)(2,1)S(1)} async-done(((bf16[16,2,9216]{2,1,0:T(2,128)(2,1)}), bf16[16,2,9216]{2,1,0:T(2,128)(2,1)S(1)}, u32[]{:S(2)}, u32[]{:S(2)}) %all-to-all-start.2) | async-done | bytes 589856 | tf_op jit(solution)/shard_map/all_to_all | solution.py:120
  250.2 3.8 conditional.13
  251.3 1.5 fusion.21
  252.8 1.2 fusion.28
  254.6 20.1 %all_to_all.106 = bf16[16,48,128]{2,1,0:T(8,128)(2,1)S(1)} all-to-all(bf16[16,48,128]{2,1,0:T(8,128)(2,1)S(1)} %reshape.620), channel_id=1, replica_groups=mesh['pipe'=4,'ctx'=16,'dp'=8] {'ctx'}, dimensions={0} | all-to-all | bytes 393216 | tf_op jit(solution)/shard_map/all_to_all | solution.py:132
  275.5 1.9 collective-permute-start.8
  277.4 3.4 collective-permute-done.8
  281.2 4.8 conditional.14
  281.2 3.4 fusion.34
  287.0 1.8 reshape.655
  288.9 7.4 %all-to-all-start.4 = ((bf16[16,2,9216]{2,1,0:T(2,128)(2,1)}), bf16[16,2,9216]{2,1,0:T(2,128)(2,1)S(1)}, u32[]{:S(2)}, u32[]{:S(2)}) async-start(bf16[16,2,9216]{2,1,0:T(2,128)(2,1)} %reshape.655), calls=%async_computation.4 | async-start | bytes 1179648 | tf_op jit(solution)/shard_map/all_to_all | solution.py:120
  296.3 27.0 %all-to-all-done.4 = bf16[16,2,9216]{2,1,0:T(2,128)(2,1)S(1)} async-done(((bf16[16,2,9216]{2,1,0:T(2,128)(2,1)}), bf16[16,2,9216]{2,1,0:T(2,128)(2,1)S(1)}, u32[]{:S(2)}, u32[]{:S(2)}) %all-to-all-start.4) | async-done | bytes 589856 | tf_op jit(solution)/shard_map/all_to_all | solution.py:120
  325.2 4.0 conditional.15
  326.4 1.5 fusion.39
  328.0 1.2 fusion.46
  329.7 20.2 %all_to_all.107 = bf16[16,48,128]{2,1,0:T(8,128)(2,1)S(1)} all-to-all(bf16[16,48,128]{2,1,0:T(8,128)(2,1)S(1)} %reshape.621), channel_id=1, replica_groups=mesh['pipe'=4,'ctx'=16,'dp'=8] {'ctx'}, dimensions={0} | all-to-all | bytes 393216 | tf_op jit(solution)/shard_map/all_to_all | solution.py:132
  350.7 3.5 collective-permute-start.9
  354.2 2.6 collective-permute-done.9
  358.3 1.8 reshape.657
  360.1 4.8 all-to-all-start.6
  364.9 27.5 %all-to-all-done.6 = bf16[16,2,9216]{2,1,0:T(2,128)(2,1)S(1)} async-done(((bf16[16,2,9216]{2,1,0:T(2,128)(2,1)}), bf16[16,2,9216]{2,1,0:T(2,128)(2,1)S(1)}, u32[]{:S(2)}, u32[]{:S(2)}) %all-to-all-start.6) | async-done | bytes 589856 | tf_op jit(solution)/shard_map/all_to_all | solution.py:120
  394.9 20.7 %all_to_all.108 = bf16[16,48,128]{2,1,0:T(8,128)(2,1)S(1)} all-to-all(bf16[16,48,128]{2,1,0:T(8,128)(2,1)S(1)} %reshape.622), channel_id=1, replica_groups=mesh['pipe'=4,'ctx'=16,'dp'=8] {'ctx'}, dimensions={0} | all-to-all | bytes 393216 | tf_op jit(solution)/shard_map/all_to_all | solution.py:132
  416.4 14.9 %collective-permute-start.10 = (bf16[1,64,1536]{2,1,0:T(8,128)(2,1)S(1)}, bf16[1,64,1536]{2,1,0:T(8,128)(2,1)S(1)}, u32[]{:S(2)}, u32[]{:S(2)}) collective-permute-start(bf16[1,64,1536]{2,1,0:T(8,128)(2,1)S(1)} %fusion.101), channel_id=1, source_target_pairs={{0,128},{128,256},{256,384},{1,129},{129,257},{257,385},{2,130},{1... | collective-permute-start | bytes 589832 | tf_op jit(solution)/shard_map/ppermute | solution.py:15
  431.4 2.6 collective-permute-done.10
  435.4 1.8 reshape.659
  437.2 3.6 all-to-all-start.8
  440.8 22.8 %all-to-all-done.8 = bf16[16,2,9216]{2,1,0:T(2,128)(2,1)S(1)} async-done(((bf16[16,2,9216]{2,1,0:T(2,128)(2,1)}), bf16[16,2,9216]{2,1,0:T(2,128)(2,1)S(1)}, u32[]{:S(2)}, u32[]{:S(2)}) %all-to-all-start.8) | async-done | bytes 589856 | tf_op jit(solution)/shard_map/all_to_all | solution.py:120
  465.8 1.1 reshape.623
  466.8 6.6 %all-to-all-start.9 = ((bf16[16,48,128]{2,1,0:T(8,128)(2,1)}), bf16[16,48,128]{2,1,0:T(8,128)(2,1)S(1)}, u32[]{:S(2)}, u32[]{:S(2)}) async-start(bf16[16,48,128]{2,1,0:T(8,128)(2,1)} %reshape.623), calls=%async_computation.9 | async-start | bytes 393216 | tf_op jit(solution)/shard_map/all_to_all | solution.py:132
  474.2 18.3 %collective-permute-start.12 = (bf16[1536,16]{0,1:T(8,128)(2,1)S(1)}, bf16[1536,16]{0,1:T(8,128)(2,1)S(1)}, u32[]{:S(2)}, u32[]{:S(2)}) collective-permute-start(bf16[1536,16]{0,1:T(8,128)(2,1)S(1)} %copy-done.11), channel_id=1, source_target_pairs={{128,384},{129,385},{130,386},{131,387},{132,388},{133,389},{134,3... | collective-permute-start | bytes 147464 | tf_op jit(solution)/shard_map/ppermute | solution.py:71
  495.2 1.2 copy.67
  497.1 1.3 collective-permute-start.15
  499.1 41.1 %reduce-scatter.4.cloned.1.call-done = f32[192,64]{1,0:T(8,128)} async-done(((f32[1536,64]{1,0:T(8,128)}), f32[192,64]{1,0:T(8,128)}) %reduce-scatter.4.cloned.1.call-update) | async-done | bytes 49168
  541.2 43.0 %psum.7 = f32[192,64]{0,1:T(8,128)S(1)} all-reduce(f32[192,64]{0,1:T(8,128)S(1)} %copy.68), channel_id=1, replica_groups=mesh['pipe'=4,'ctx'=16,'dp'=8] {'ctx'}, use_global_device_ids=true, to_apply=%region_37.38 | all-reduce | flops 12288 | bytes 98304 | tf_op jit(solution)/shard_map/psum | solution.py:155
  584.8 1.3 collective-permute-start.18
  587.4 23.4 %collective-permute-done.18 = f32[192,16]{0,1:T(8,128)S(1)} collective-permute-done((f32[192,16]{0,1:T(8,128)S(1)}, f32[192,16]{0,1:T(8,128)S(1)}, u32[]{:S(2)}, u32[]{:S(2)}) %collective-permute-start.18) | collective-permute-done | bytes 12320 | tf_op jit(solution)/shard_map/ppermute | solution.py:162
  (151 shorter events, 43.3 us)
Async XLA Ops:
  7.2 21.3 %copy-start = (bf16[64,1536]{1,0:T(8,128)(2,1)S(1)}, bf16[64,1536]{1,0:T(8,128)(2,1)}, u32[]{:S(2)}) copy-start(bf16[64,1536]{1,0:T(8,128)(2,1)} %param.35) | copy-start | bytes 589828
  7.2 42.3 %copy-start.7 = (bf16[1,192,1536]{2,1,0:T(8,128)(2,1)S(1)}, bf16[1,192,1536]{2,1,0:T(8,128)(2,1)}, u32[]{:S(2)}) copy-start(bf16[1,192,1536]{2,1,0:T(8,128)(2,1)} %param.38) | copy-start | bytes 1769476
  7.2 115.7 %all-gather.3.cloned.1.call-start = ((), (), s32[]{:S(2)}) async-start(), calls=%async_computation.11 | async-start | bytes 5308416 | tf_op jit(solution)/shard_map/all_gather | solution.py:57
  7.9 24.3 %collective-permute-start = (bf16[192,1536]{1,0:T(8,128)(2,1)}, bf16[192,1536]{1,0:T(8,128)(2,1)}, u32[]{:S(2)}, u32[]{:S(2)}) collective-permute-start(bf16[192,1536]{1,0:T(8,128)(2,1)} %bitcast.194), channel_id=1, source_target_pairs={{0,1},{1,2},{2,3},{3,4},{4,5},{5,6},{6,7},{7,0},{8,9},{9,10},{10,1... | collective-permute-start | bytes 1769480 | tf_op jit(solution)/shard_map/ppermute | solution.py:61
  11.9 37.6 %collective-permute-start.1 = (bf16[192,1536]{1,0:T(8,128)(2,1)}, bf16[192,1536]{1,0:T(8,128)(2,1)}, u32[]{:S(2)}, u32[]{:S(2)}) collective-permute-start(bf16[192,1536]{1,0:T(8,128)(2,1)} %bitcast.195), channel_id=1, source_target_pairs={{0,2},{1,3},{2,4},{3,5},{4,6},{5,7},{6,0},{7,1},{8,10},{9,11},{10,... | collective-permute-start | bytes 1769480 | tf_op jit(solution)/shard_map/ppermute | solution.py:61
  16.3 37.1 %collective-permute-start.2 = (bf16[192,1536]{1,0:T(8,128)(2,1)}, bf16[192,1536]{1,0:T(8,128)(2,1)S(1)}, u32[]{:S(2)}, u32[]{:S(2)}) collective-permute-start(bf16[192,1536]{1,0:T(8,128)(2,1)} %bitcast.196), channel_id=1, source_target_pairs={{0,3},{1,4},{2,5},{3,6},{4,7},{5,0},{6,1},{7,2},{8,11},{9,12},{10,... | collective-permute-start | bytes 1769480 | tf_op jit(solution)/shard_map/ppermute | solution.py:61
  20.3 63.5 %collective-permute-start.3 = (bf16[192,1536]{1,0:T(8,128)(2,1)}, bf16[192,1536]{1,0:T(8,128)(2,1)S(1)}, u32[]{:S(2)}, u32[]{:S(2)}) collective-permute-start(bf16[192,1536]{1,0:T(8,128)(2,1)} %bitcast.197), channel_id=1, source_target_pairs={{0,4},{1,5},{2,6},{3,7},{4,0},{5,1},{6,2},{7,3},{8,12},{9,13},{10,... | collective-permute-start | bytes 1769480 | tf_op jit(solution)/shard_map/ppermute | solution.py:61
  22.4 62.3 %collective-permute-start.4 = (bf16[192,1536]{1,0:T(8,128)(2,1)}, bf16[192,1536]{1,0:T(8,128)(2,1)S(1)}, u32[]{:S(2)}, u32[]{:S(2)}) collective-permute-start(bf16[192,1536]{1,0:T(8,128)(2,1)} %bitcast.198), channel_id=1, source_target_pairs={{0,5},{1,6},{2,7},{3,0},{4,1},{5,2},{6,3},{7,4},{8,13},{9,14},{10,... | collective-permute-start | bytes 1769480 | tf_op jit(solution)/shard_map/ppermute | solution.py:61
  32.2 63.8 %collective-permute-start.5 = (bf16[192,1536]{1,0:T(8,128)(2,1)}, bf16[192,1536]{1,0:T(8,128)(2,1)S(1)}, u32[]{:S(2)}, u32[]{:S(2)}) collective-permute-start(bf16[192,1536]{1,0:T(8,128)(2,1)} %bitcast.199), channel_id=1, source_target_pairs={{0,6},{1,7},{2,0},{3,1},{4,2},{5,3},{6,4},{7,5},{8,14},{9,15},{10,... | collective-permute-start | bytes 1769480 | tf_op jit(solution)/shard_map/ppermute | solution.py:61
  49.5 55.9 %collective-permute-start.6 = (bf16[192,1536]{1,0:T(8,128)(2,1)S(1)}, bf16[192,1536]{1,0:T(8,128)(2,1)S(1)}, u32[]{:S(2)}, u32[]{:S(2)}) collective-permute-start(bf16[192,1536]{1,0:T(8,128)(2,1)S(1)} %bitcast.200), channel_id=1, source_target_pairs={{0,7},{1,0},{2,1},{3,2},{4,3},{5,4},{6,5},{7,6},{8,15},{9,8},{10,9... | collective-permute-start | bytes 1769480 | tf_op jit(solution)/shard_map/ppermute | solution.py:61
  124.0 41.5 %copy-start.10 = (s32[2,1,1024]{2,1,0:T(1,128)S(1)}, s32[2,1,1024]{2,1,0:T(1,128)}, u32[]{:S(2)}) copy-start(s32[2,1,1024]{2,1,0:T(1,128)} %param.34) | copy-start | bytes 24580
  125.8 37.7 %all-to-all-start = ((bf16[16,2,9216]{2,1,0:T(2,128)(2,1)}), bf16[16,2,9216]{2,1,0:T(2,128)(2,1)S(1)}, u32[]{:S(2)}, u32[]{:S(2)}) async-start(bf16[16,2,9216]{2,1,0:T(2,128)(2,1)} %reshape.651), calls=%async_computation | async-start | bytes 1179648 | tf_op jit(solution)/shard_map/all_to_all | solution.py:120
  192.0 15.0 %collective-permute-start.7 = (bf16[1,64,1536]{2,1,0:T(8,128)(2,1)S(1)}, bf16[1,64,1536]{2,1,0:T(8,128)(2,1)S(1)}, u32[]{:S(2)}, u32[]{:S(2)}) collective-permute-start(bf16[1,64,1536]{2,1,0:T(8,128)(2,1)S(1)} %fusion.109), channel_id=1, source_target_pairs={{0,128},{128,256},{256,384},{1,129},{129,257},{257,385},{2,130},{1... | collective-permute-start | bytes 589832 | tf_op jit(solution)/shard_map/ppermute | solution.py:15
  207.4 3.8 copy-start.3
  215.5 32.7 %all-to-all-start.2 = ((bf16[16,2,9216]{2,1,0:T(2,128)(2,1)}), bf16[16,2,9216]{2,1,0:T(2,128)(2,1)S(1)}, u32[]{:S(2)}, u32[]{:S(2)}) async-start(bf16[16,2,9216]{2,1,0:T(2,128)(2,1)} %reshape.653), calls=%async_computation.2 | async-start | bytes 1179648 | tf_op jit(solution)/shard_map/all_to_all | solution.py:120
  275.5 5.4 collective-permute-start.8
  281.2 3.8 copy-start.4
  288.9 34.4 %all-to-all-start.4 = ((bf16[16,2,9216]{2,1,0:T(2,128)(2,1)}), bf16[16,2,9216]{2,1,0:T(2,128)(2,1)S(1)}, u32[]{:S(2)}, u32[]{:S(2)}) async-start(bf16[16,2,9216]{2,1,0:T(2,128)(2,1)} %reshape.655), calls=%async_computation.4 | async-start | bytes 1179648 | tf_op jit(solution)/shard_map/all_to_all | solution.py:120
  350.7 6.1 collective-permute-start.9
  360.1 32.3 %all-to-all-start.6 = ((bf16[16,2,9216]{2,1,0:T(2,128)(2,1)}), bf16[16,2,9216]{2,1,0:T(2,128)(2,1)S(1)}, u32[]{:S(2)}, u32[]{:S(2)}) async-start(bf16[16,2,9216]{2,1,0:T(2,128)(2,1)} %reshape.657), calls=%async_computation.6 | async-start | bytes 1179648 | tf_op jit(solution)/shard_map/all_to_all | solution.py:120
  416.4 17.5 %collective-permute-start.10 = (bf16[1,64,1536]{2,1,0:T(8,128)(2,1)S(1)}, bf16[1,64,1536]{2,1,0:T(8,128)(2,1)S(1)}, u32[]{:S(2)}, u32[]{:S(2)}) collective-permute-start(bf16[1,64,1536]{2,1,0:T(8,128)(2,1)S(1)} %fusion.101), channel_id=1, source_target_pairs={{0,128},{128,256},{256,384},{1,129},{129,257},{257,385},{2,130},{1... | collective-permute-start | bytes 589832 | tf_op jit(solution)/shard_map/ppermute | solution.py:15
  437.2 26.4 %all-to-all-start.8 = ((bf16[16,2,9216]{2,1,0:T(2,128)(2,1)}), bf16[16,2,9216]{2,1,0:T(2,128)(2,1)S(1)}, u32[]{:S(2)}, u32[]{:S(2)}) async-start(bf16[16,2,9216]{2,1,0:T(2,128)(2,1)} %reshape.659), calls=%async_computation.8 | async-start | bytes 1179648 | tf_op jit(solution)/shard_map/all_to_all | solution.py:120
  465.5 8.0 %copy-start.11 = (bf16[1536,16]{0,1:T(8,128)(2,1)S(1)}, bf16[1536,16]{0,1:T(8,128)(2,1)}, u32[]{:S(2)}) copy-start(bf16[1536,16]{0,1:T(8,128)(2,1)} %param.41) | copy-start | bytes 147460
  465.5 27.6 %copy-start.8 = (f32[2,1,64,64]{3,2,1,0:T(8,128)S(1)}, f32[2,1,64,64]{3,2,1,0:T(8,128)}, u32[]{:S(2)}) copy-start(f32[2,1,64,64]{3,2,1,0:T(8,128)} %param.31) | copy-start | bytes 98308
  465.5 27.7 %copy-start.9 = (f32[2,1,64,64]{3,2,1,0:T(8,128)S(1)}, f32[2,1,64,64]{3,2,1,0:T(8,128)}, u32[]{:S(2)}) copy-start(f32[2,1,64,64]{3,2,1,0:T(8,128)} %param.32) | copy-start | bytes 98308
  465.6 28.8 %copy-start.12 = (f32[1536]{0:T(1024)S(1)}, f32[1536]{0:T(1024)}, u32[]{:S(2)}) copy-start(f32[1536]{0:T(1024)} %param.40) | copy-start | bytes 18436
  466.8 26.5 %all-to-all-start.9 = ((bf16[16,48,128]{2,1,0:T(8,128)(2,1)}), bf16[16,48,128]{2,1,0:T(8,128)(2,1)S(1)}, u32[]{:S(2)}, u32[]{:S(2)}) async-start(bf16[16,48,128]{2,1,0:T(8,128)(2,1)} %reshape.623), calls=%async_computation.9 | async-start | bytes 393216 | tf_op jit(solution)/shard_map/all_to_all | solution.py:132
  473.4 66.7 %reduce-scatter.4.cloned.1.call-start = ((), (), s32[]{:S(2)}) async-start(), calls=%async_computation.12 | async-start | bytes 884736
  473.5 20.8 %collective-permute-start.11 = (bf16[1536,16]{0,1:T(8,128)(2,1)S(1)}, bf16[1536,16]{0,1:T(8,128)(2,1)S(1)}, u32[]{:S(2)}, u32[]{:S(2)}) collective-permute-start(bf16[1536,16]{0,1:T(8,128)(2,1)S(1)} %copy-done.11), channel_id=1, source_target_pairs={{0,384},{1,385},{2,386},{3,387},{4,388},{5,389},{6,390},{7,391},{8... | collective-permute-start | bytes 147464 | tf_op jit(solution)/shard_map/ppermute | solution.py:71
  474.2 20.2 %collective-permute-start.12 = (bf16[1536,16]{0,1:T(8,128)(2,1)S(1)}, bf16[1536,16]{0,1:T(8,128)(2,1)S(1)}, u32[]{:S(2)}, u32[]{:S(2)}) collective-permute-start(bf16[1536,16]{0,1:T(8,128)(2,1)S(1)} %copy-done.11), channel_id=1, source_target_pairs={{128,384},{129,385},{130,386},{131,387},{132,388},{133,389},{134,3... | collective-permute-start | bytes 147464 | tf_op jit(solution)/shard_map/ppermute | solution.py:71
  492.5 1.9 collective-permute-start.13
  493.6 117.9 %copy-start.1 = (bf16[64,1536]{1,0:T(8,128)(2,1)S(1)}, bf16[64,1536]{1,0:T(8,128)(2,1)}, u32[]{:S(2)}) copy-start(bf16[64,1536]{1,0:T(8,128)(2,1)} %param.35) | copy-start | bytes 589828
  496.4 89.7 %collective-permute-start.14 = (f32[2,1,64,16]{2,3,0,1:T(8,128)S(1)}, f32[2,1,64,16]{2,3,0,1:T(8,128)S(1)}, u32[]{:S(2)}, u32[]{:S(2)}) collective-permute-start(f32[2,1,64,16]{2,3,0,1:T(8,128)S(1)} %get-tuple-element.297), channel_id=1, source_target_pairs={{384,0},{385,1},{386,2},{387,3},{388,4},{389,5},{390,6},{391,7},{3... | collective-permute-start | bytes 24584 | tf_op jit(solution)/shard_map/ppermute | solution.py:161
  497.1 89.7 %collective-permute-start.15 = (f32[2,1,64,16]{2,3,0,1:T(8,128)S(1)}, f32[2,1,64,16]{2,3,0,1:T(8,128)S(1)}, u32[]{:S(2)}, u32[]{:S(2)}) collective-permute-start(f32[2,1,64,16]{2,3,0,1:T(8,128)S(1)} %get-tuple-element.295), channel_id=1, source_target_pairs={{384,128},{385,129},{386,130},{387,131},{388,132},{389,133},{390,1... | collective-permute-start | bytes 24584 | tf_op jit(solution)/shard_map/ppermute | solution.py:161
  498.4 88.4 %collective-permute-start.16 = (f32[2,1,64,16]{2,3,0,1:T(8,128)S(1)}, f32[2,1,64,16]{2,3,0,1:T(8,128)S(1)}, u32[]{:S(2)}, u32[]{:S(2)}) collective-permute-start(f32[2,1,64,16]{2,3,0,1:T(8,128)S(1)} %get-tuple-element.296), channel_id=1, source_target_pairs={{384,256},{385,257},{386,258},{387,259},{388,260},{389,261},{390,2... | collective-permute-start | bytes 24584 | tf_op jit(solution)/shard_map/ppermute | solution.py:161
  584.2 3.3 collective-permute-start.17
  584.8 26.1 %collective-permute-start.18 = (f32[192,16]{0,1:T(8,128)S(1)}, f32[192,16]{0,1:T(8,128)S(1)}, u32[]{:S(2)}, u32[]{:S(2)}) collective-permute-start(f32[192,16]{0,1:T(8,128)S(1)} %get-tuple-element.292), channel_id=1, source_target_pairs={{384,128},{385,129},{386,130},{387,131},{388,132},{389,133},{390,1... | collective-permute-start | bytes 36872 | tf_op jit(solution)/shard_map/ppermute | solution.py:162
  586.1 24.7 %collective-permute-start.19 = (f32[192,16]{0,1:T(8,128)S(1)}, f32[192,16]{0,1:T(8,128)S(1)}, u32[]{:S(2)}, u32[]{:S(2)}) collective-permute-start(f32[192,16]{0,1:T(8,128)S(1)} %get-tuple-element.293), channel_id=1, source_target_pairs={{384,256},{385,257},{386,258},{387,259},{388,260},{389,261},{390,2... | collective-permute-start | bytes 36872 | tf_op jit(solution)/shard_map/ppermute | solution.py:162
Sparse Core Ops, SparseCore 0:
  10.1 112.7 all-gather.2
  496.5 43.6 reduce-scatter.3

commit v12 on v11

--- a/solution.py
+++ b/solution.py
@@ -153,14 +153,19 @@
     ) / float(seq_total)
     grad_rows = lax.psum_scatter(grad_all, "dp", scatter_dimension=0, tiled=True)
     grad_rows = lax.psum(grad_rows, "ctx")
-    velocity_in = jnp.zeros(velocity_all.shape[:3] + (head_cols,), jnp.float32)
-    gradient_in = jnp.zeros((grad_rows.shape[0], head_cols), jnp.float32)
+    velocity_shape = velocity_all.shape[:3] + (head_cols,)
+    velocity_size = velocity_all.size // phase_count
+    gradient_shape = (grad_rows.shape[0], head_cols)
+    packed_in = jnp.zeros((velocity_size + grad_rows.size // phase_count,), jnp.float32)
     for target_phase in range(last_phase):
         cols = slice(target_phase * head_cols, (target_phase + 1) * head_cols)
-        pair = [(last_phase, target_phase)]
-        velocity_in = velocity_in + lax.ppermute(velocity_all[..., cols], "pipe", pair)
-        gradient_in = gradient_in + lax.ppermute(grad_rows[:, cols], "pipe", pair)
+        packed = jnp.concatenate(
+            (velocity_all[..., cols].reshape(-1), grad_rows[:, cols].reshape(-1))
+        )
+        packed_in = packed_in + lax.ppermute(packed, "pipe", [(last_phase, target_phase)])
     own_cols = slice(last_phase * head_cols, phase_count * head_cols)
+    velocity_in = packed_in[:velocity_size].reshape(velocity_shape)
+    gradient_in = packed_in[velocity_size:].reshape(gradient_shape)
     velocity = jnp.where(is_last, velocity_all[..., own_cols], velocity_in)
     gradient = jnp.where(is_last, grad_rows[:, own_cols], gradient_in)
     return (velocity, gradient)

time: 628 us -> 628 us (level)
  the two profiles are of different devices: /device:TPU:1 before, /device:TPU:8 now
where the time goes in v12:
time: 628 us; the launch traced here: 618 us
  waiting for transfers between devices  246 us (39%)
  blocking collectives  162 us (26%)
  starting transfers between devices  114 us (18%)
  local copies, waits for them, and re-layouts  51.3 us (8%)
  between operations  15.2 us (2%)
  matrix products  14.6 us (2%)
  other arithmetic  13.8 us (2%)
    all_to_all x5, waiting for transfers between devices, on_device(): lax.all_to_all(triple, 'ctx', split_axis=2, concat_axis=1, tiled=True)  125 us
    all_to_all x4, blocking collectives, on_device(): lax.all_to_all(outgoing, 'ctx', split_axis=0, concat_axis=0, tiled=True)  104 us
    psum x1, blocking collectives, on_device(): grad_rows = lax.psum(grad_rows, 'ctx')  58.2 us
    ppermute x7, waiting for transfers between devices, on_device(): key_blocks.append(lax.ppermute(key_weight[0], 'dp', pairs))  55.9 us
    reduce_scatter x1, waiting for transfers between devices, on_device(): lax.psum_scatter(grad_all, 'dp', scatter_dimension=0, tiled=True)  48.4 us
    all_to_all x5, starting transfers between devices, on_device(): lax.all_to_all(triple, 'ctx', split_axis=2, concat_axis=1, tiled=True)  38.8 us
    unnamed x37, local copies, waits for them, and re-layouts  25.2 us
    ppermute x7, starting transfers between devices, on_device(): key_blocks.append(lax.ppermute(key_weight[0], 'dp', pairs))  24.2 us
  transfers between devices with their start and end apart: 25, of which 17 were waited for; matrix products, arithmetic and copies ran while one was open for 4% of the time, Pallas kernels for 0%

profile of v12, /device:TPU:8, one launch (start us, length us, event | category | flops | bytes accessed | tf_op | source)
XLA Modules:
  0.0 617.9 jit_solution(9341651017741256089)
XLA Ops:
  7.9 3.4 collective-permute-start
  11.3 4.6 collective-permute-start.1
  16.0 6.2 %collective-permute-start.2 = (bf16[192,1536]{1,0:T(8,128)(2,1)}, bf16[192,1536]{1,0:T(8,128)(2,1)S(1)}, u32[]{:S(2)}, u32[]{:S(2)}) collective-permute-start(bf16[192,1536]{1,0:T(8,128)(2,1)} %bitcast.208), channel_id=1, source_target_pairs={{0,3},{1,4},{2,5},{3,6},{4,7},{5,0},{6,1},{7,2},{8,11},{9,12},{10,... | collective-permute-start | bytes 1769480 | tf_op jit(solution)/shard_map/ppermute | solution.py:61
  22.2 1.9 collective-permute-start.3
  24.1 4.2 collective-permute-start.4
  31.2 1.2 fusion.88
  32.5 1.9 constant_dynamic-update-slice_fusion
  34.9 11.7 %collective-permute-done = bf16[192,1536]{1,0:T(8,128)(2,1)} collective-permute-done((bf16[192,1536]{1,0:T(8,128)(2,1)}, bf16[192,1536]{1,0:T(8,128)(2,1)}, u32[]{:S(2)}, u32[]{:S(2)}) %collective-permute-start) | collective-permute-done | bytes 589856 | tf_op jit(solution)/shard_map/ppermute | solution.py:61
  46.6 1.9 collective-permute-start.5
  48.5 1.9 bitcast_dynamic-update-slice_fusion.6
  51.1 1.9 collective-permute-start.6
  53.1 1.9 bitcast_dynamic-update-slice_fusion.5
  55.0 6.0 collective-permute-done.2
  61.9 21.4 %collective-permute-done.3 = bf16[192,1536]{1,0:T(8,128)(2,1)S(1)} collective-permute-done((bf16[192,1536]{1,0:T(8,128)(2,1)}, bf16[192,1536]{1,0:T(8,128)(2,1)S(1)}, u32[]{:S(2)}, u32[]{:S(2)}) %collective-permute-start.3) | collective-permute-done | bytes 589856 | tf_op jit(solution)/shard_map/ppermute | solution.py:61
  85.1 16.0 %collective-permute-done.5 = bf16[192,1536]{1,0:T(8,128)(2,1)S(1)} collective-permute-done((bf16[192,1536]{1,0:T(8,128)(2,1)}, bf16[192,1536]{1,0:T(8,128)(2,1)S(1)}, u32[]{:S(2)}, u32[]{:S(2)}) %collective-permute-start.5) | collective-permute-done | bytes 589856 | tf_op jit(solution)/shard_map/ppermute | solution.py:61
  102.8 5.5 gather_fusion
  108.3 5.1 bitcast_select_fusion
  113.4 7.5 %all-gather.3.cloned.1.call-done = bf16[1,1536,1536]{2,1,0:T(8,128)(2,1)} async-done(((bf16[1,192,1536]{2,1,0:T(8,128)(2,1)}), bf16[1,1536,1536]{2,1,0:T(8,128)(2,1)}) %all-gather.3.cloned.1.call-update) | async-done | bytes 4718608 | tf_op jit(solution)/shard_map/all_gather | solution.py:57
  120.9 4.8 conditional.10
  120.9 3.4 fusion
  125.7 1.0 copy.42
  126.7 1.8 reshape.693
  128.6 16.7 %all-to-all-start = ((bf16[16,2,9216]{2,1,0:T(2,128)(2,1)}), bf16[16,2,9216]{2,1,0:T(2,128)(2,1)S(1)}, u32[]{:S(2)}, u32[]{:S(2)}) async-start(bf16[16,2,9216]{2,1,0:T(2,128)(2,1)} %reshape.693), calls=%async_computation | async-start | bytes 1179648 | tf_op jit(solution)/shard_map/all_to_all | solution.py:120
  145.2 26.7 %all-to-all-done = bf16[16,2,9216]{2,1,0:T(2,128)(2,1)S(1)} async-done(((bf16[16,2,9216]{2,1,0:T(2,128)(2,1)}), bf16[16,2,9216]{2,1,0:T(2,128)(2,1)S(1)}, u32[]{:S(2)}, u32[]{:S(2)}) %all-to-all-start) | async-done | bytes 589856 | tf_op jit(solution)/shard_map/all_to_all | solution.py:120
  173.9 3.8 conditional.11
  175.0 1.5 fusion.3
  176.6 1.2 fusion.10
  178.3 20.1 %all_to_all.105 = bf16[16,48,128]{2,1,0:T(8,128)(2,1)S(1)} all-to-all(bf16[16,48,128]{2,1,0:T(8,128)(2,1)S(1)} %reshape.655), channel_id=1, replica_groups=mesh['pipe'=4,'ctx'=16,'dp'=8] {'ctx'}, dimensions={0} | all-to-all | bytes 393216 | tf_op jit(solution)/shard_map/all_to_all | solution.py:132
  199.2 1.3 collective-permute-start.7
  201.9 5.3 conditional.12
  201.9 3.4 fusion.16
  207.1 1.0 copy.47
  208.2 1.8 reshape.695
  210.0 5.1 all-to-all-start.2
  215.1 25.9 %all-to-all-done.2 = bf16[16,2,9216]{2,1,0:T(2,128)(2,1)S(1)} async-done(((bf16[16,2,9216]{2,1,0:T(2,128)(2,1)}), bf16[16,2,9216]{2,1,0:T(2,128)(2,1)S(1)}, u32[]{:S(2)}, u32[]{:S(2)}) %all-to-all-start.2) | async-done | bytes 589856 | tf_op jit(solution)/shard_map/all_to_all | solution.py:120
  243.0 3.8 conditional.13
  244.0 1.5 fusion.21
  245.6 1.2 fusion.28
  247.3 28.7 %all_to_all.106 = bf16[16,48,128]{2,1,0:T(8,128)(2,1)S(1)} all-to-all(bf16[16,48,128]{2,1,0:T(8,128)(2,1)S(1)} %reshape.656), channel_id=1, replica_groups=mesh['pipe'=4,'ctx'=16,'dp'=8] {'ctx'}, dimensions={0} | all-to-all | bytes 393216 | tf_op jit(solution)/shard_map/all_to_all | solution.py:132
  276.8 1.3 collective-permute-start.8
  279.6 1.0 copy.52
  280.6 1.8 reshape.697
  282.4 6.6 %all-to-all-start.4 = ((bf16[16,2,9216]{2,1,0:T(2,128)(2,1)}), bf16[16,2,9216]{2,1,0:T(2,128)(2,1)S(1)}, u32[]{:S(2)}, u32[]{:S(2)}) async-start(bf16[16,2,9216]{2,1,0:T(2,128)(2,1)} %reshape.697), calls=%async_computation.4 | async-start | bytes 1179648 | tf_op jit(solution)/shard_map/all_to_all | solution.py:120
  289.0 25.6 %all-to-all-done.4 = bf16[16,2,9216]{2,1,0:T(2,128)(2,1)S(1)} async-done(((bf16[16,2,9216]{2,1,0:T(2,128)(2,1)}), bf16[16,2,9216]{2,1,0:T(2,128)(2,1)S(1)}, u32[]{:S(2)}, u32[]{:S(2)}) %all-to-all-start.4) | async-done | bytes 589856 | tf_op jit(solution)/shard_map/all_to_all | solution.py:120
  317.3 25.8 %all_to_all.107 = bf16[16,48,128]{2,1,0:T(8,128)(2,1)S(1)} all-to-all(bf16[16,48,128]{2,1,0:T(8,128)(2,1)S(1)} %reshape.657), channel_id=1, replica_groups=mesh['pipe'=4,'ctx'=16,'dp'=8] {'ctx'}, dimensions={0} | all-to-all | bytes 393216 | tf_op jit(solution)/shard_map/all_to_all | solution.py:132
  343.9 7.5 %collective-permute-start.9 = (bf16[1,64,1536]{2,1,0:T(8,128)(2,1)S(1)}, bf16[1,64,1536]{2,1,0:T(8,128)(2,1)S(1)}, u32[]{:S(2)}, u32[]{:S(2)}) collective-permute-start(bf16[1,64,1536]{2,1,0:T(8,128)(2,1)S(1)} %fusion.97), channel_id=1, source_target_pairs={{0,128},{128,256},{256,384},{1,129},{129,257},{257,385},{2,130},{1... | collective-permute-start | bytes 589832 | tf_op jit(solution)/shard_map/ppermute | solution.py:15
  352.8 1.0 copy.57
  353.8 1.8 reshape.699
  355.7 3.6 all-to-all-start.6
  359.3 25.3 %all-to-all-done.6 = bf16[16,2,9216]{2,1,0:T(2,128)(2,1)S(1)} async-done(((bf16[16,2,9216]{2,1,0:T(2,128)(2,1)}), bf16[16,2,9216]{2,1,0:T(2,128)(2,1)S(1)}, u32[]{:S(2)}, u32[]{:S(2)}) %all-to-all-start.6) | async-done | bytes 589856 | tf_op jit(solution)/shard_map/all_to_all | solution.py:120
  387.1 29.4 %all_to_all.108 = bf16[16,48,128]{2,1,0:T(8,128)(2,1)S(1)} all-to-all(bf16[16,48,128]{2,1,0:T(8,128)(2,1)S(1)} %reshape.658), channel_id=1, replica_groups=mesh['pipe'=4,'ctx'=16,'dp'=8] {'ctx'}, dimensions={0} | all-to-all | bytes 393216 | tf_op jit(solution)/shard_map/all_to_all | solution.py:132
  417.2 1.3 collective-permute-start.10
  420.0 1.0 copy.62
  421.0 1.8 reshape.701
  422.8 6.9 %all-to-all-start.8 = ((bf16[16,2,9216]{2,1,0:T(2,128)(2,1)}), bf16[16,2,9216]{2,1,0:T(2,128)(2,1)S(1)}, u32[]{:S(2)}, u32[]{:S(2)}) async-start(bf16[16,2,9216]{2,1,0:T(2,128)(2,1)} %reshape.701), calls=%async_computation.8 | async-start | bytes 1179648 | tf_op jit(solution)/shard_map/all_to_all | solution.py:120
  429.8 21.5 %all-to-all-done.8 = bf16[16,2,9216]{2,1,0:T(2,128)(2,1)S(1)} async-done(((bf16[16,2,9216]{2,1,0:T(2,128)(2,1)}), bf16[16,2,9216]{2,1,0:T(2,128)(2,1)S(1)}, u32[]{:S(2)}, u32[]{:S(2)}) %all-to-all-start.8) | async-done | bytes 589856 | tf_op jit(solution)/shard_map/all_to_all | solution.py:120
  453.5 1.0 reshape.659
  454.6 14.3 %all-to-all-start.9 = ((bf16[16,48,128]{2,1,0:T(8,128)(2,1)}), bf16[16,48,128]{2,1,0:T(8,128)(2,1)S(1)}, u32[]{:S(2)}, u32[]{:S(2)}) async-start(bf16[16,48,128]{2,1,0:T(8,128)(2,1)} %reshape.659), calls=%async_computation.9 | async-start | bytes 393216 | tf_op jit(solution)/shard_map/all_to_all | solution.py:132
  468.9 20.8 %collective-permute-start.11 = (bf16[1536,16]{0,1:T(8,128)(2,1)S(1)}, bf16[1536,16]{0,1:T(8,128)(2,1)S(1)}, u32[]{:S(2)}, u32[]{:S(2)}) collective-permute-start(bf16[1536,16]{0,1:T(8,128)(2,1)S(1)} %copy-done.11), channel_id=1, source_target_pairs={{0,384},{1,385},{2,386},{3,387},{4,388},{5,389},{6,390},{7,391},{8... | collective-permute-start | bytes 147464 | tf_op jit(solution)/shard_map/ppermute | solution.py:71
  493.2 1.2 copy.81
  494.9 48.4 %reduce-scatter.4.cloned.1.call-done = f32[192,64]{1,0:T(8,128)} async-done(((f32[1536,64]{1,0:T(8,128)}), f32[192,64]{1,0:T(8,128)}) %reduce-scatter.4.cloned.1.call-update) | async-done | bytes 49168 | tf_op jit(solution)/shard_map/reduce_scatter | solution.py:154
  543.3 58.2 %psum.7 = f32[192,64]{1,0:T(8,128)S(1)} all-reduce(f32[192,64]{1,0:T(8,128)} %reduce-scatter.4.cloned.1.call-done), channel_id=1, replica_groups=mesh['pipe'=4,'ctx'=16,'dp'=8] {'ctx'}, use_global_device_ids=true, to_apply=%region_37.38 | all-reduce | flops 12288 | bytes 98304 | tf_op jit(solution)/shard_map/psum | solution.py:155
  602.5 1.3 collective-permute-start.14
  604.6 4.5 collective-permute-done.14
  (163 shorter events, 42.1 us)
Async XLA Ops:
  7.2 24.0 %copy-start = (bf16[64,1536]{1,0:T(8,128)(2,1)S(1)}, bf16[64,1536]{1,0:T(8,128)(2,1)}, u32[]{:S(2)}) copy-start(bf16[64,1536]{1,0:T(8,128)(2,1)} %param.35) | copy-start | bytes 589828
  7.2 44.0 %copy-start.7 = (bf16[1,192,1536]{2,1,0:T(8,128)(2,1)S(1)}, bf16[1,192,1536]{2,1,0:T(8,128)(2,1)}, u32[]{:S(2)}) copy-start(bf16[1,192,1536]{2,1,0:T(8,128)(2,1)} %param.38) | copy-start | bytes 1769476
  7.2 113.7 %all-gather.3.cloned.1.call-start = ((), (), s32[]{:S(2)}) async-start(), calls=%async_computation.11 | async-start | bytes 5308416 | tf_op jit(solution)/shard_map/all_gather | solution.py:57
  7.9 38.6 %collective-permute-start = (bf16[192,1536]{1,0:T(8,128)(2,1)}, bf16[192,1536]{1,0:T(8,128)(2,1)}, u32[]{:S(2)}, u32[]{:S(2)}) collective-permute-start(bf16[192,1536]{1,0:T(8,128)(2,1)} %bitcast.206), channel_id=1, source_target_pairs={{0,1},{1,2},{2,3},{3,4},{4,5},{5,6},{6,7},{7,0},{8,9},{9,10},{10,1... | collective-permute-start | bytes 1769480 | tf_op jit(solution)/shard_map/ppermute | solution.py:61
  11.3 39.8 %collective-permute-start.1 = (bf16[192,1536]{1,0:T(8,128)(2,1)}, bf16[192,1536]{1,0:T(8,128)(2,1)}, u32[]{:S(2)}, u32[]{:S(2)}) collective-permute-start(bf16[192,1536]{1,0:T(8,128)(2,1)} %bitcast.207), channel_id=1, source_target_pairs={{0,2},{1,3},{2,4},{3,5},{4,6},{5,7},{6,0},{7,1},{8,10},{9,11},{10,... | collective-permute-start | bytes 1769480 | tf_op jit(solution)/shard_map/ppermute | solution.py:61
  16.0 45.0 %collective-permute-start.2 = (bf16[192,1536]{1,0:T(8,128)(2,1)}, bf16[192,1536]{1,0:T(8,128)(2,1)S(1)}, u32[]{:S(2)}, u32[]{:S(2)}) collective-permute-start(bf16[192,1536]{1,0:T(8,128)(2,1)} %bitcast.208), channel_id=1, source_target_pairs={{0,3},{1,4},{2,5},{3,6},{4,7},{5,0},{6,1},{7,2},{8,11},{9,12},{10,... | collective-permute-start | bytes 1769480 | tf_op jit(solution)/shard_map/ppermute | solution.py:61
  22.2 61.1 %collective-permute-start.3 = (bf16[192,1536]{1,0:T(8,128)(2,1)}, bf16[192,1536]{1,0:T(8,128)(2,1)S(1)}, u32[]{:S(2)}, u32[]{:S(2)}) collective-permute-start(bf16[192,1536]{1,0:T(8,128)(2,1)} %bitcast.209), channel_id=1, source_target_pairs={{0,4},{1,5},{2,6},{3,7},{4,0},{5,1},{6,2},{7,3},{8,12},{9,13},{10,... | collective-permute-start | bytes 1769480 | tf_op jit(solution)/shard_map/ppermute | solution.py:61
  24.1 60.0 %collective-permute-start.4 = (bf16[192,1536]{1,0:T(8,128)(2,1)}, bf16[192,1536]{1,0:T(8,128)(2,1)S(1)}, u32[]{:S(2)}, u32[]{:S(2)}) collective-permute-start(bf16[192,1536]{1,0:T(8,128)(2,1)} %bitcast.210), channel_id=1, source_target_pairs={{0,5},{1,6},{2,7},{3,0},{4,1},{5,2},{6,3},{7,4},{8,13},{9,14},{10,... | collective-permute-start | bytes 1769480 | tf_op jit(solution)/shard_map/ppermute | solution.py:61
  46.6 54.5 %collective-permute-start.5 = (bf16[192,1536]{1,0:T(8,128)(2,1)}, bf16[192,1536]{1,0:T(8,128)(2,1)S(1)}, u32[]{:S(2)}, u32[]{:S(2)}) collective-permute-start(bf16[192,1536]{1,0:T(8,128)(2,1)} %bitcast.211), channel_id=1, source_target_pairs={{0,6},{1,7},{2,0},{3,1},{4,2},{5,3},{6,4},{7,5},{8,14},{9,15},{10,... | collective-permute-start | bytes 1769480 | tf_op jit(solution)/shard_map/ppermute | solution.py:61
  51.1 50.8 %collective-permute-start.6 = (bf16[192,1536]{1,0:T(8,128)(2,1)S(1)}, bf16[192,1536]{1,0:T(8,128)(2,1)S(1)}, u32[]{:S(2)}, u32[]{:S(2)}) collective-permute-start(bf16[192,1536]{1,0:T(8,128)(2,1)S(1)} %bitcast.212), channel_id=1, source_target_pairs={{0,7},{1,0},{2,1},{3,2},{4,3},{5,4},{6,5},{7,6},{8,15},{9,8},{10,9... | collective-permute-start | bytes 1769480 | tf_op jit(solution)/shard_map/ppermute | solution.py:61
  120.9 3.8 copy-start.2
  126.7 47.2 %copy-start.10 = (s32[2,1,1024]{2,1,0:T(1,128)S(1)}, s32[2,1,1024]{2,1,0:T(1,128)}, u32[]{:S(2)}) copy-start(s32[2,1,1024]{2,1,0:T(1,128)} %param.34) | copy-start | bytes 24580
  128.6 43.4 %all-to-all-start = ((bf16[16,2,9216]{2,1,0:T(2,128)(2,1)}), bf16[16,2,9216]{2,1,0:T(2,128)(2,1)S(1)}, u32[]{:S(2)}, u32[]{:S(2)}) async-start(bf16[16,2,9216]{2,1,0:T(2,128)(2,1)} %reshape.693), calls=%async_computation | async-start | bytes 1179648 | tf_op jit(solution)/shard_map/all_to_all | solution.py:120
  199.2 2.4 collective-permute-start.7
  201.9 3.8 copy-start.3
  210.0 31.0 %all-to-all-start.2 = ((bf16[16,2,9216]{2,1,0:T(2,128)(2,1)}), bf16[16,2,9216]{2,1,0:T(2,128)(2,1)S(1)}, u32[]{:S(2)}, u32[]{:S(2)}) async-start(bf16[16,2,9216]{2,1,0:T(2,128)(2,1)} %reshape.695), calls=%async_computation.2 | async-start | bytes 1179648 | tf_op jit(solution)/shard_map/all_to_all | solution.py:120
  276.8 2.4 collective-permute-start.8
  282.4 32.1 %all-to-all-start.4 = ((bf16[16,2,9216]{2,1,0:T(2,128)(2,1)}), bf16[16,2,9216]{2,1,0:T(2,128)(2,1)S(1)}, u32[]{:S(2)}, u32[]{:S(2)}) async-start(bf16[16,2,9216]{2,1,0:T(2,128)(2,1)} %reshape.697), calls=%async_computation.4 | async-start | bytes 1179648 | tf_op jit(solution)/shard_map/all_to_all | solution.py:120
  343.9 8.5 %collective-permute-start.9 = (bf16[1,64,1536]{2,1,0:T(8,128)(2,1)S(1)}, bf16[1,64,1536]{2,1,0:T(8,128)(2,1)S(1)}, u32[]{:S(2)}, u32[]{:S(2)}) collective-permute-start(bf16[1,64,1536]{2,1,0:T(8,128)(2,1)S(1)} %fusion.97), channel_id=1, source_target_pairs={{0,128},{128,256},{256,384},{1,129},{129,257},{257,385},{2,130},{1... | collective-permute-start | bytes 589832 | tf_op jit(solution)/shard_map/ppermute | solution.py:15
  355.7 28.9 %all-to-all-start.6 = ((bf16[16,2,9216]{2,1,0:T(2,128)(2,1)}), bf16[16,2,9216]{2,1,0:T(2,128)(2,1)S(1)}, u32[]{:S(2)}, u32[]{:S(2)}) async-start(bf16[16,2,9216]{2,1,0:T(2,128)(2,1)} %reshape.699), calls=%async_computation.6 | async-start | bytes 1179648 | tf_op jit(solution)/shard_map/all_to_all | solution.py:120
  417.2 2.4 collective-permute-start.10
  422.8 28.5 %all-to-all-start.8 = ((bf16[16,2,9216]{2,1,0:T(2,128)(2,1)}), bf16[16,2,9216]{2,1,0:T(2,128)(2,1)S(1)}, u32[]{:S(2)}, u32[]{:S(2)}) async-start(bf16[16,2,9216]{2,1,0:T(2,128)(2,1)} %reshape.701), calls=%async_computation.8 | async-start | bytes 1179648 | tf_op jit(solution)/shard_map/all_to_all | solution.py:120
  453.2 15.7 %copy-start.11 = (bf16[1536,16]{0,1:T(8,128)(2,1)S(1)}, bf16[1536,16]{0,1:T(8,128)(2,1)}, u32[]{:S(2)}) copy-start(bf16[1536,16]{0,1:T(8,128)(2,1)} %param.41) | copy-start | bytes 147460
  453.3 37.9 %copy-start.8 = (f32[2,1,64,64]{3,2,1,0:T(8,128)S(1)}, f32[2,1,64,64]{3,2,1,0:T(8,128)}, u32[]{:S(2)}) copy-start(f32[2,1,64,64]{3,2,1,0:T(8,128)} %param.31) | copy-start | bytes 98308
  453.3 38.0 %copy-start.9 = (f32[2,1,64,64]{3,2,1,0:T(8,128)S(1)}, f32[2,1,64,64]{3,2,1,0:T(8,128)}, u32[]{:S(2)}) copy-start(f32[2,1,64,64]{3,2,1,0:T(8,128)} %param.32) | copy-start | bytes 98308
  453.3 39.0 %copy-start.12 = (f32[1536]{0:T(1024)S(1)}, f32[1536]{0:T(1024)}, u32[]{:S(2)}) copy-start(f32[1536]{0:T(1024)} %param.40) | copy-start | bytes 18436
  454.6 36.8 %all-to-all-start.9 = ((bf16[16,48,128]{2,1,0:T(8,128)(2,1)}), bf16[16,48,128]{2,1,0:T(8,128)(2,1)S(1)}, u32[]{:S(2)}, u32[]{:S(2)}) async-start(bf16[16,48,128]{2,1,0:T(8,128)(2,1)} %reshape.659), calls=%async_computation.9 | async-start | bytes 393216 | tf_op jit(solution)/shard_map/all_to_all | solution.py:132
  468.9 74.4 %reduce-scatter.4.cloned.1.call-start = ((), (), s32[]{:S(2)}) async-start(), calls=%async_computation.12 | async-start | bytes 884736 | tf_op jit(solution)/shard_map/reduce_scatter | solution.py:154
  468.9 23.4 %collective-permute-start.11 = (bf16[1536,16]{0,1:T(8,128)(2,1)S(1)}, bf16[1536,16]{0,1:T(8,128)(2,1)S(1)}, u32[]{:S(2)}, u32[]{:S(2)}) collective-permute-start(bf16[1536,16]{0,1:T(8,128)(2,1)S(1)} %copy-done.11), channel_id=1, source_target_pairs={{0,384},{1,385},{2,386},{3,387},{4,388},{5,389},{6,390},{7,391},{8... | collective-permute-start | bytes 147464 | tf_op jit(solution)/shard_map/ppermute | solution.py:71
  489.8 2.5 collective-permute-start.12
  490.5 1.9 collective-permute-start.13
  492.1 118.7 %copy-start.1 = (bf16[64,1536]{1,0:T(8,128)(2,1)S(1)}, bf16[64,1536]{1,0:T(8,128)(2,1)}, u32[]{:S(2)}) copy-start(bf16[64,1536]{1,0:T(8,128)(2,1)} %param.35) | copy-start | bytes 589828
  601.8 2.9 collective-permute-start.15
  602.5 6.6 %collective-permute-start.14 = (f32[5120]{0:T(1024)S(1)}, f32[5120]{0:T(1024)S(1)}, u32[]{:S(2)}, u32[]{:S(2)}) collective-permute-start(f32[5120]{0:T(1024)S(1)} %pad_maximum_fusion.5), channel_id=1, source_target_pairs={{384,0},{385,1},{386,2},{387,3},{388,4},{389,5},{390,6},{391,7},{3... | collective-permute-start | bytes 61448 | tf_op jit(solution)/shard_map/ppermute | solution.py:165
  603.9 5.2 collective-permute-start.16
Sparse Core Ops, SparseCore 0:
  10.1 110.7 all-gather.2
  494.5 48.7 reduce-scatter.3

commit v13 on v12

--- a/solution.py
+++ b/solution.py
@@ -70,6 +70,7 @@
         else:
             head_pieces.append(lax.ppermute(head_weight, "pipe", [(source_phase, last_phase)]))
     head_full = jnp.concatenate(head_pieces, axis=1)
+    full_query, full_key, head_full = lax.optimization_barrier((full_query, full_key, head_full))
     section_gain = norm_gain[0]
 
     def attention(by_heads, frame_row):

time: 628 us -> 645 us (1.027)
  starting transfers between devices: 114 us -> 160 us
  waiting for transfers between devices: 246 us -> 227 us
  blocking collectives: 162 us -> 154 us
    ppermute x7, starting transfers between devices: 24.2 us -> 93.4 us  [on_device(): key_blocks.append(lax.ppermute(key_weight[0], 'dp', pairs))]
    ppermute x7, waiting for transfers between devices: 55.9 us -> 15.5 us  [on_device(): key_blocks.append(lax.ppermute(key_weight[0], 'dp', pairs))]
    ppermute x3, starting transfers between devices: 22.2 us -> 4.41 us  [on_device(): lax.ppermute(head_weight, 'pipe', [(source_phase, last_phase)])]
    all_to_all x1, waiting for transfers between devices: 0.01 us -> 15.7 us  [on_device(): lax.all_to_all(outgoing, 'ctx', split_axis=0, concat_axis=0, tiled=True)]
    all_to_all x5, waiting for transfers between devices: 125 us -> 138 us  [on_device(): lax.all_to_all(triple, 'ctx', split_axis=2, concat_axis=1, tiled=True)]
    all_to_all x4, blocking collectives: 104 us -> 95.6 us  [on_device(): lax.all_to_all(outgoing, 'ctx', split_axis=0, concat_axis=0, tiled=True)]
    all_gather x1, waiting for transfers between devices: 7.54 us -> 0.01 us  [on_device(): full_query = lax.all_gather(query_weight[0], 'dp', axis=0, tiled=True)]
    unnamed x37 -> x35, local copies, waits for them, and re-layouts: 25.2 us -> 23.1 us
  transfers between devices with their start and end apart: 25 -> 25, of which waited for: 17 -> 16; matrix products, arithmetic and copies ran while one was open for 4% -> 4% of each run, Pallas kernels for 0% -> 0%
where the time goes in v13:
time: 645 us; the launch traced here: 636 us
  waiting for transfers between devices  227 us (35%)
  starting transfers between devices  160 us (25%)
  blocking collectives  154 us (24%)
  local copies, waits for them, and re-layouts  49.1 us (8%)
  between operations  15.2 us (2%)
  other arithmetic  14.6 us (2%)
  matrix products  14.6 us (2%)
    all_to_all x5, waiting for transfers between devices, on_device(): lax.all_to_all(triple, 'ctx', split_axis=2, concat_axis=1, tiled=True)  138 us
    all_to_all x4, blocking collectives, on_device(): lax.all_to_all(outgoing, 'ctx', split_axis=0, concat_axis=0, tiled=True)  95.6 us
    ppermute x7, starting transfers between devices, on_device(): key_blocks.append(lax.ppermute(key_weight[0], 'dp', pairs))  93.4 us
    psum x1, blocking collectives, on_device(): grad_rows = lax.psum(grad_rows, 'ctx')  58.2 us
    reduce_scatter x1, waiting for transfers between devices, on_device(): lax.psum_scatter(grad_all, 'dp', scatter_dimension=0, tiled=True)  48.6 us
    all_to_all x5, starting transfers between devices, on_device(): lax.all_to_all(triple, 'ctx', split_axis=2, concat_axis=1, tiled=True)  35.5 us
    unnamed x35, local copies, waits for them, and re-layouts  23.1 us
    all_to_all x1, waiting for transfers between devices, on_device(): lax.all_to_all(outgoing, 'ctx', split_axis=0, concat_axis=0, tiled=True)  15.7 us
  transfers between devices with their start and end apart: 25, of which 16 were waited for; matrix products, arithmetic and copies ran while one was open for 4% of the time, Pallas kernels for 0%

profile of v13, /device:TPU:8, one launch (start us, length us, event | category | flops | bytes accessed | tf_op | source)
XLA Modules:
  0.0 635.5 jit_solution(13360055407728070530)
XLA Ops:
  7.9 3.4 collective-permute-start
  11.3 4.6 collective-permute-start.1
  16.0 3.1 collective-permute-start.7
  23.3 1.2 fusion.88
  24.8 1.9 constant_dynamic-update-slice_fusion
  27.2 4.2 collective-permute-start.2
  31.4 69.8 %collective-permute-start.3 = (bf16[192,1536]{1,0:T(8,128)(2,1)}, bf16[192,1536]{1,0:T(8,128)(2,1)S(1)}, u32[]{:S(2)}, u32[]{:S(2)}) collective-permute-start(bf16[192,1536]{1,0:T(8,128)(2,1)} %bitcast.209), channel_id=1, source_target_pairs={{0,4},{1,5},{2,6},{3,7},{4,0},{5,1},{6,2},{7,3},{8,12},{9,13},{10,... | collective-permute-start | bytes 1769480 | tf_op jit(solution)/shard_map/ppermute | solution.py:61
  101.2 4.8 collective-permute-start.4
  106.9 1.9 collective-permute-start.5
  109.7 4.6 collective-permute-start.6
  116.0 2.9 collective-permute-done.3
  119.7 10.7 %collective-permute-done.4 = bf16[192,1536]{1,0:T(8,128)(2,1)S(1)} collective-permute-done((bf16[192,1536]{1,0:T(8,128)(2,1)}, bf16[192,1536]{1,0:T(8,128)(2,1)S(1)}, u32[]{:S(2)}, u32[]{:S(2)}) %collective-permute-start.4) | collective-permute-done | bytes 589856 | tf_op jit(solution)/shard_map/ppermute | solution.py:61
  132.2 1.9 collective-permute-done.6
  135.0 5.4 gather_fusion
  140.4 5.0 bitcast_select_fusion
  145.4 4.8 conditional.10
  145.4 3.4 fusion
  150.2 1.0 copy.42
  151.3 1.8 reshape.693
  153.1 15.2 %all-to-all-start = ((bf16[16,2,9216]{2,1,0:T(2,128)(2,1)}), bf16[16,2,9216]{2,1,0:T(2,128)(2,1)S(1)}, u32[]{:S(2)}, u32[]{:S(2)}) async-start(bf16[16,2,9216]{2,1,0:T(2,128)(2,1)} %reshape.693), calls=%async_computation | async-start | bytes 1179648 | tf_op jit(solution)/shard_map/all_to_all | solution.py:121
  168.3 25.5 %all-to-all-done = bf16[16,2,9216]{2,1,0:T(2,128)(2,1)S(1)} async-done(((bf16[16,2,9216]{2,1,0:T(2,128)(2,1)}), bf16[16,2,9216]{2,1,0:T(2,128)(2,1)S(1)}, u32[]{:S(2)}, u32[]{:S(2)}) %all-to-all-start) | async-done | bytes 589856 | tf_op jit(solution)/shard_map/all_to_all | solution.py:121
  195.8 3.8 conditional.11
  196.8 1.5 fusion.3
  198.4 1.2 fusion.10
  200.1 20.5 %all_to_all.105 = bf16[16,48,128]{2,1,0:T(8,128)(2,1)S(1)} all-to-all(bf16[16,48,128]{2,1,0:T(8,128)(2,1)S(1)} %reshape.655), channel_id=1, replica_groups=mesh['pipe'=4,'ctx'=16,'dp'=8] {'ctx'}, dimensions={0} | all-to-all | bytes 393216 | tf_op jit(solution)/shard_map/all_to_all | solution.py:133
  221.5 1.3 collective-permute-start.10
  222.8 1.0 collective-permute-done.10
  224.1 5.3 conditional.12
  224.6 3.4 fusion.16
  229.4 1.0 copy.47
  230.4 1.8 reshape.695
  232.3 4.9 all-to-all-start.2
  237.2 31.4 %all-to-all-done.2 = bf16[16,2,9216]{2,1,0:T(2,128)(2,1)S(1)} async-done(((bf16[16,2,9216]{2,1,0:T(2,128)(2,1)}), bf16[16,2,9216]{2,1,0:T(2,128)(2,1)S(1)}, u32[]{:S(2)}, u32[]{:S(2)}) %all-to-all-start.2) | async-done | bytes 589856 | tf_op jit(solution)/shard_map/all_to_all | solution.py:121
  270.5 3.8 conditional.13
  271.6 1.5 fusion.21
  273.2 1.2 fusion.28
  274.9 23.5 %all_to_all.106 = bf16[16,48,128]{2,1,0:T(8,128)(2,1)S(1)} all-to-all(bf16[16,48,128]{2,1,0:T(8,128)(2,1)S(1)} %reshape.656), channel_id=1, replica_groups=mesh['pipe'=4,'ctx'=16,'dp'=8] {'ctx'}, dimensions={0} | all-to-all | bytes 393216 | tf_op jit(solution)/shard_map/all_to_all | solution.py:133
  299.2 1.3 collective-permute-start.11
  302.0 1.0 copy.52
  303.0 1.8 reshape.697
  304.8 5.6 all-to-all-start.4
  310.5 25.6 %all-to-all-done.4 = bf16[16,2,9216]{2,1,0:T(2,128)(2,1)S(1)} async-done(((bf16[16,2,9216]{2,1,0:T(2,128)(2,1)}), bf16[16,2,9216]{2,1,0:T(2,128)(2,1)S(1)}, u32[]{:S(2)}, u32[]{:S(2)}) %all-to-all-start.4) | async-done | bytes 589856 | tf_op jit(solution)/shard_map/all_to_all | solution.py:121
  338.7 25.8 %all_to_all.107 = bf16[16,48,128]{2,1,0:T(8,128)(2,1)S(1)} all-to-all(bf16[16,48,128]{2,1,0:T(8,128)(2,1)S(1)} %reshape.657), channel_id=1, replica_groups=mesh['pipe'=4,'ctx'=16,'dp'=8] {'ctx'}, dimensions={0} | all-to-all | bytes 393216 | tf_op jit(solution)/shard_map/all_to_all | solution.py:133
  365.3 7.5 %collective-permute-start.12 = (bf16[1,64,1536]{2,1,0:T(8,128)(2,1)S(1)}, bf16[1,64,1536]{2,1,0:T(8,128)(2,1)S(1)}, u32[]{:S(2)}, u32[]{:S(2)}) collective-permute-start(bf16[1,64,1536]{2,1,0:T(8,128)(2,1)S(1)} %fusion.97), channel_id=1, source_target_pairs={{0,128},{128,256},{256,384},{1,129},{129,257},{257,385},{2,130},{1... | collective-permute-start | bytes 589832 | tf_op jit(solution)/shard_map/ppermute | solution.py:15
  372.8 1.0 collective-permute-done.12
  374.2 1.0 copy.57
  375.3 1.8 reshape.699
  377.1 3.6 all-to-all-start.6
  380.7 29.6 %all-to-all-done.6 = bf16[16,2,9216]{2,1,0:T(2,128)(2,1)S(1)} async-done(((bf16[16,2,9216]{2,1,0:T(2,128)(2,1)}), bf16[16,2,9216]{2,1,0:T(2,128)(2,1)S(1)}, u32[]{:S(2)}, u32[]{:S(2)}) %all-to-all-start.6) | async-done | bytes 589856 | tf_op jit(solution)/shard_map/all_to_all | solution.py:121
  412.9 25.7 %all_to_all.108 = bf16[16,48,128]{2,1,0:T(8,128)(2,1)S(1)} all-to-all(bf16[16,48,128]{2,1,0:T(8,128)(2,1)S(1)} %reshape.658), channel_id=1, replica_groups=mesh['pipe'=4,'ctx'=16,'dp'=8] {'ctx'}, dimensions={0} | all-to-all | bytes 393216 | tf_op jit(solution)/shard_map/all_to_all | solution.py:133
  439.4 1.3 collective-permute-start.13
  440.7 1.0 collective-permute-done.13
  442.1 1.0 copy.62
  443.2 1.8 reshape.701
  445.0 6.2 all-to-all-start.8
  451.2 25.7 %all-to-all-done.8 = bf16[16,2,9216]{2,1,0:T(2,128)(2,1)S(1)} async-done(((bf16[16,2,9216]{2,1,0:T(2,128)(2,1)}), bf16[16,2,9216]{2,1,0:T(2,128)(2,1)S(1)}, u32[]{:S(2)}, u32[]{:S(2)}) %all-to-all-start.8) | async-done | bytes 589856 | tf_op jit(solution)/shard_map/all_to_all | solution.py:121
  479.1 1.0 reshape.659
  480.2 12.8 %all-to-all-start.9 = ((bf16[16,48,128]{2,1,0:T(8,128)(2,1)}), bf16[16,48,128]{2,1,0:T(8,128)(2,1)S(1)}, u32[]{:S(2)}, u32[]{:S(2)}) async-start(bf16[16,48,128]{2,1,0:T(8,128)(2,1)} %reshape.659), calls=%async_computation.9 | async-start | bytes 393216 | tf_op jit(solution)/shard_map/all_to_all | solution.py:133
  493.2 15.7 %all-to-all-done.9 = bf16[16,48,128]{2,1,0:T(8,128)(2,1)S(1)} async-done(((bf16[16,48,128]{2,1,0:T(8,128)(2,1)}), bf16[16,48,128]{2,1,0:T(8,128)(2,1)S(1)}, u32[]{:S(2)}, u32[]{:S(2)}) %all-to-all-start.9) | async-done | bytes 196640 | tf_op jit(solution)/shard_map/all_to_all | solution.py:133
  510.7 1.2 copy.81
  512.4 48.6 %reduce-scatter.4.cloned.1.call-done = f32[192,64]{1,0:T(8,128)} async-done(((f32[1536,64]{1,0:T(8,128)}), f32[192,64]{1,0:T(8,128)}) %reduce-scatter.4.cloned.1.call-update) | async-done | bytes 49168 | tf_op jit(solution)/shard_map/reduce_scatter | solution.py:155
  561.0 58.2 %psum.7 = f32[192,64]{1,0:T(8,128)S(1)} all-reduce(f32[192,64]{1,0:T(8,128)} %reduce-scatter.4.cloned.1.call-done), channel_id=1, replica_groups=mesh['pipe'=4,'ctx'=16,'dp'=8] {'ctx'}, use_global_device_ids=true, to_apply=%region_37.38 | all-reduce | flops 12288 | bytes 98304 | tf_op jit(solution)/shard_map/psum | solution.py:156
  620.2 1.3 collective-permute-start.14
  622.3 4.5 collective-permute-done.14
  (162 shorter events, 41.0 us)
Async XLA Ops:
  7.2 16.1 %copy-start = (bf16[64,1536]{1,0:T(8,128)(2,1)S(1)}, bf16[64,1536]{1,0:T(8,128)(2,1)}, u32[]{:S(2)}) copy-start(bf16[64,1536]{1,0:T(8,128)(2,1)} %param.35) | copy-start | bytes 589828
  7.2 102.5 %copy-start.7 = (bf16[1,192,1536]{2,1,0:T(8,128)(2,1)S(1)}, bf16[1,192,1536]{2,1,0:T(8,128)(2,1)}, u32[]{:S(2)}) copy-start(bf16[1,192,1536]{2,1,0:T(8,128)(2,1)} %param.38) | copy-start | bytes 1769476
  7.2 138.2 %all-gather.3.cloned.1.call-start = ((), (), s32[]{:S(2)}) async-start(), calls=%async_computation.11 | async-start | bytes 5308416 | tf_op jit(solution)/shard_map/all_gather | solution.py:57
  7.9 98.9 %collective-permute-start = (bf16[192,1536]{1,0:T(8,128)(2,1)}, bf16[192,1536]{1,0:T(8,128)(2,1)S(1)}, u32[]{:S(2)}, u32[]{:S(2)}) collective-permute-start(bf16[192,1536]{1,0:T(8,128)(2,1)} %bitcast.206), channel_id=1, source_target_pairs={{0,1},{1,2},{2,3},{3,4},{4,5},{5,6},{6,7},{7,0},{8,9},{9,10},{10,1... | collective-permute-start | bytes 1769480 | tf_op jit(solution)/shard_map/ppermute | solution.py:61
  11.3 98.3 %collective-permute-start.1 = (bf16[192,1536]{1,0:T(8,128)(2,1)}, bf16[192,1536]{1,0:T(8,128)(2,1)S(1)}, u32[]{:S(2)}, u32[]{:S(2)}) collective-permute-start(bf16[192,1536]{1,0:T(8,128)(2,1)} %bitcast.207), channel_id=1, source_target_pairs={{0,2},{1,3},{2,4},{3,5},{4,6},{5,7},{6,0},{7,1},{8,10},{9,11},{10,... | collective-permute-start | bytes 1769480 | tf_op jit(solution)/shard_map/ppermute | solution.py:61
  16.0 11.2 %collective-permute-start.7 = (bf16[1536,16]{0,1:T(8,128)(2,1)}, bf16[1536,16]{0,1:T(8,128)(2,1)S(1)}, u32[]{:S(2)}, u32[]{:S(2)}) collective-permute-start(bf16[1536,16]{0,1:T(8,128)(2,1)} %param.41), channel_id=1, source_target_pairs={{0,384},{1,385},{2,386},{3,387},{4,388},{5,389},{6,390},{7,391},{8... | collective-permute-start | bytes 147464 | tf_op jit(solution)/shard_map/ppermute | solution.py:71
  19.1 12.3 %collective-permute-start.8 = (bf16[1536,16]{0,1:T(8,128)(2,1)}, bf16[1536,16]{0,1:T(8,128)(2,1)S(1)}, u32[]{:S(2)}, u32[]{:S(2)}) collective-permute-start(bf16[1536,16]{0,1:T(8,128)(2,1)} %param.41), channel_id=1, source_target_pairs={{128,384},{129,385},{130,386},{131,387},{132,388},{133,389},{134,3... | collective-permute-start | bytes 147464 | tf_op jit(solution)/shard_map/ppermute | solution.py:71
  19.7 81.5 %collective-permute-start.9 = (bf16[1536,16]{0,1:T(8,128)(2,1)}, bf16[1536,16]{0,1:T(8,128)(2,1)S(1)}, u32[]{:S(2)}, u32[]{:S(2)}) collective-permute-start(bf16[1536,16]{0,1:T(8,128)(2,1)} %param.41), channel_id=1, source_target_pairs={{256,384},{257,385},{258,386},{259,387},{260,388},{261,389},{262,3... | collective-permute-start | bytes 147464 | tf_op jit(solution)/shard_map/ppermute | solution.py:71
  27.2 88.0 %collective-permute-start.2 = (bf16[192,1536]{1,0:T(8,128)(2,1)}, bf16[192,1536]{1,0:T(8,128)(2,1)S(1)}, u32[]{:S(2)}, u32[]{:S(2)}) collective-permute-start(bf16[192,1536]{1,0:T(8,128)(2,1)} %bitcast.208), channel_id=1, source_target_pairs={{0,3},{1,4},{2,5},{3,6},{4,7},{5,0},{6,1},{7,2},{8,11},{9,12},{10,... | collective-permute-start | bytes 1769480 | tf_op jit(solution)/shard_map/ppermute | solution.py:61
  31.4 87.5 %collective-permute-start.3 = (bf16[192,1536]{1,0:T(8,128)(2,1)}, bf16[192,1536]{1,0:T(8,128)(2,1)S(1)}, u32[]{:S(2)}, u32[]{:S(2)}) collective-permute-start(bf16[192,1536]{1,0:T(8,128)(2,1)} %bitcast.209), channel_id=1, source_target_pairs={{0,4},{1,5},{2,6},{3,7},{4,0},{5,1},{6,2},{7,3},{8,12},{9,13},{10,... | collective-permute-start | bytes 1769480 | tf_op jit(solution)/shard_map/ppermute | solution.py:61
  101.2 29.2 %collective-permute-start.4 = (bf16[192,1536]{1,0:T(8,128)(2,1)}, bf16[192,1536]{1,0:T(8,128)(2,1)S(1)}, u32[]{:S(2)}, u32[]{:S(2)}) collective-permute-start(bf16[192,1536]{1,0:T(8,128)(2,1)} %bitcast.210), channel_id=1, source_target_pairs={{0,5},{1,6},{2,7},{3,0},{4,1},{5,2},{6,3},{7,4},{8,13},{9,14},{10,... | collective-permute-start | bytes 1769480 | tf_op jit(solution)/shard_map/ppermute | solution.py:61
  106.9 24.4 %collective-permute-start.5 = (bf16[192,1536]{1,0:T(8,128)(2,1)}, bf16[192,1536]{1,0:T(8,128)(2,1)S(1)}, u32[]{:S(2)}, u32[]{:S(2)}) collective-permute-start(bf16[192,1536]{1,0:T(8,128)(2,1)} %bitcast.211), channel_id=1, source_target_pairs={{0,6},{1,7},{2,0},{3,1},{4,2},{5,3},{6,4},{7,5},{8,14},{9,15},{10,... | collective-permute-start | bytes 1769480 | tf_op jit(solution)/shard_map/ppermute | solution.py:61
  109.7 24.5 %collective-permute-start.6 = (bf16[192,1536]{1,0:T(8,128)(2,1)S(1)}, bf16[192,1536]{1,0:T(8,128)(2,1)S(1)}, u32[]{:S(2)}, u32[]{:S(2)}) collective-permute-start(bf16[192,1536]{1,0:T(8,128)(2,1)S(1)} %bitcast.212), channel_id=1, source_target_pairs={{0,7},{1,0},{2,1},{3,2},{4,3},{5,4},{6,5},{7,6},{8,15},{9,8},{10,9... | collective-permute-start | bytes 1769480 | tf_op jit(solution)/shard_map/ppermute | solution.py:61
  145.4 3.8 copy-start.2
  151.3 44.5 %copy-start.10 = (s32[2,1,1024]{2,1,0:T(1,128)S(1)}, s32[2,1,1024]{2,1,0:T(1,128)}, u32[]{:S(2)}) copy-start(s32[2,1,1024]{2,1,0:T(1,128)} %param.34) | copy-start | bytes 24580
  153.1 40.7 %all-to-all-start = ((bf16[16,2,9216]{2,1,0:T(2,128)(2,1)}), bf16[16,2,9216]{2,1,0:T(2,128)(2,1)S(1)}, u32[]{:S(2)}, u32[]{:S(2)}) async-start(bf16[16,2,9216]{2,1,0:T(2,128)(2,1)} %reshape.693), calls=%async_computation | async-start | bytes 1179648 | tf_op jit(solution)/shard_map/all_to_all | solution.py:121
  221.5 2.4 collective-permute-start.10
  224.6 3.8 copy-start.3
  232.3 36.3 %all-to-all-start.2 = ((bf16[16,2,9216]{2,1,0:T(2,128)(2,1)}), bf16[16,2,9216]{2,1,0:T(2,128)(2,1)S(1)}, u32[]{:S(2)}, u32[]{:S(2)}) async-start(bf16[16,2,9216]{2,1,0:T(2,128)(2,1)} %reshape.695), calls=%async_computation.2 | async-start | bytes 1179648 | tf_op jit(solution)/shard_map/all_to_all | solution.py:121
  299.2 2.4 collective-permute-start.11
  304.8 31.2 %all-to-all-start.4 = ((bf16[16,2,9216]{2,1,0:T(2,128)(2,1)}), bf16[16,2,9216]{2,1,0:T(2,128)(2,1)S(1)}, u32[]{:S(2)}, u32[]{:S(2)}) async-start(bf16[16,2,9216]{2,1,0:T(2,128)(2,1)} %reshape.697), calls=%async_computation.4 | async-start | bytes 1179648 | tf_op jit(solution)/shard_map/all_to_all | solution.py:121
  365.3 8.5 %collective-permute-start.12 = (bf16[1,64,1536]{2,1,0:T(8,128)(2,1)S(1)}, bf16[1,64,1536]{2,1,0:T(8,128)(2,1)S(1)}, u32[]{:S(2)}, u32[]{:S(2)}) collective-permute-start(bf16[1,64,1536]{2,1,0:T(8,128)(2,1)S(1)} %fusion.97), channel_id=1, source_target_pairs={{0,128},{128,256},{256,384},{1,129},{129,257},{257,385},{2,130},{1... | collective-permute-start | bytes 589832 | tf_op jit(solution)/shard_map/ppermute | solution.py:15
  377.1 33.2 %all-to-all-start.6 = ((bf16[16,2,9216]{2,1,0:T(2,128)(2,1)}), bf16[16,2,9216]{2,1,0:T(2,128)(2,1)S(1)}, u32[]{:S(2)}, u32[]{:S(2)}) async-start(bf16[16,2,9216]{2,1,0:T(2,128)(2,1)} %reshape.699), calls=%async_computation.6 | async-start | bytes 1179648 | tf_op jit(solution)/shard_map/all_to_all | solution.py:121
  439.4 2.4 collective-permute-start.13
  445.0 31.9 %all-to-all-start.8 = ((bf16[16,2,9216]{2,1,0:T(2,128)(2,1)}), bf16[16,2,9216]{2,1,0:T(2,128)(2,1)S(1)}, u32[]{:S(2)}, u32[]{:S(2)}) async-start(bf16[16,2,9216]{2,1,0:T(2,128)(2,1)} %reshape.701), calls=%async_computation.8 | async-start | bytes 1179648 | tf_op jit(solution)/shard_map/all_to_all | solution.py:121
  478.9 14.1 %copy-start.8 = (f32[2,1,64,64]{3,2,1,0:T(8,128)S(1)}, f32[2,1,64,64]{3,2,1,0:T(8,128)}, u32[]{:S(2)}) copy-start(f32[2,1,64,64]{3,2,1,0:T(8,128)} %param.31) | copy-start | bytes 98308
  478.9 14.2 %copy-start.9 = (f32[2,1,64,64]{3,2,1,0:T(8,128)S(1)}, f32[2,1,64,64]{3,2,1,0:T(8,128)}, u32[]{:S(2)}) copy-start(f32[2,1,64,64]{3,2,1,0:T(8,128)} %param.32) | copy-start | bytes 98308
  478.9 30.9 %copy-start.11 = (f32[1536]{0:T(1024)S(1)}, f32[1536]{0:T(1024)}, u32[]{:S(2)}) copy-start(f32[1536]{0:T(1024)} %param.40) | copy-start | bytes 18436
  480.2 28.7 %all-to-all-start.9 = ((bf16[16,48,128]{2,1,0:T(8,128)(2,1)}), bf16[16,48,128]{2,1,0:T(8,128)(2,1)S(1)}, u32[]{:S(2)}, u32[]{:S(2)}) async-start(bf16[16,48,128]{2,1,0:T(8,128)(2,1)} %reshape.659), calls=%async_computation.9 | async-start | bytes 393216 | tf_op jit(solution)/shard_map/all_to_all | solution.py:133
  492.9 68.0 %reduce-scatter.4.cloned.1.call-start = ((), (), s32[]{:S(2)}) async-start(), calls=%async_computation.12 | async-start | bytes 884736 | tf_op jit(solution)/shard_map/reduce_scatter | solution.py:155
  509.4 119.1 %copy-start.1 = (bf16[64,1536]{1,0:T(8,128)(2,1)S(1)}, bf16[64,1536]{1,0:T(8,128)(2,1)}, u32[]{:S(2)}) copy-start(bf16[64,1536]{1,0:T(8,128)(2,1)} %param.35) | copy-start | bytes 589828
  619.4 2.9 collective-permute-start.15
  620.2 6.6 %collective-permute-start.14 = (f32[5120]{0:T(1024)S(1)}, f32[5120]{0:T(1024)S(1)}, u32[]{:S(2)}, u32[]{:S(2)}) collective-permute-start(f32[5120]{0:T(1024)S(1)} %pad_maximum_fusion.6), channel_id=1, source_target_pairs={{384,0},{385,1},{386,2},{387,3},{388,4},{389,5},{390,6},{391,7},{3... | collective-permute-start | bytes 61448 | tf_op jit(solution)/shard_map/ppermute | solution.py:166
  621.6 5.2 collective-permute-start.16
Sparse Core Ops, SparseCore 0:
  10.1 87.3 all-gather.2
  512.0 48.9 reduce-scatter.3

commit v14 on v11

--- a/solution.py
+++ b/solution.py
@@ -116,8 +116,18 @@
         def blank_triple(source):
             return jnp.zeros((3,) + source.shape, jnp.bfloat16)
 
-        triple = lax.cond(active, project, blank_triple, normed)
-        section_by_heads = lax.all_to_all(triple, "ctx", split_axis=2, concat_axis=1, tiled=True)
+        if moment == 0:
+            value_heads = lax.all_to_all(
+                normed[None], "ctx", split_axis=2, concat_axis=1, tiled=True
+            )
+            pair = lax.cond(active, project, blank_triple, normed)[:2]
+            pair_heads = lax.all_to_all(pair, "ctx", split_axis=2, concat_axis=1, tiled=True)
+            section_by_heads = jnp.concatenate((pair_heads, value_heads), axis=0)
+        else:
+            triple = lax.cond(active, project, blank_triple, normed)
+            section_by_heads = lax.all_to_all(
+                triple, "ctx", split_axis=2, concat_axis=1, tiled=True
+            )
 
         def run_attention(arrived):
             return attention(arrived, frame_row)

time: 628 us -> 618 us (0.984)
  waiting for transfers between devices: 271 us -> 235 us
  starting transfers between devices: 123 us -> 139 us
  other arithmetic: 14.3 us -> 23.1 us
    all_to_all x0 -> x2, starting transfers between devices: none -> 29.8 us  [the longest x1 14.9 us: on_device(): lax.all_to_all(normed[None], 'ctx', split_axis=2, concat_axis=1, tiled=True)]
    ppermute x7, waiting for transfers between devices: 60.4 us -> 36.8 us  [on_device(): key_blocks.append(lax.ppermute(key_weight[0], 'dp', pairs))]
    all_to_all x5 -> x4, waiting for transfers between devices: 127 us -> 105 us  [on_device(): lax.all_to_all(triple, 'ctx', split_axis=2, concat_axis=1, tiled=True)]
    all_to_all x5 -> x4, starting transfers between devices: 36.1 us -> 20.5 us  [on_device(): lax.all_to_all(triple, 'ctx', split_axis=2, concat_axis=1, tiled=True)]
    all_to_all x0 -> x2, waiting for transfers between devices: none -> 13.4 us  [the longest x1 13.4 us: on_device(): lax.all_to_all(pair, 'ctx', split_axis=2, concat_axis=1, tiled=True)]
    unnamed x2 -> x3, other arithmetic: 1.33 us -> 10.1 us
    unnamed x37 -> x41, local copies, waits for them, and re-layouts: 25.4 us -> 28 us
  transfers between devices with their start and end apart: 28 -> 29, of which waited for: 16 -> 15; matrix products, arithmetic and copies ran while one was open for 5% -> 7% of each run, Pallas kernels for 0% -> 0%
where the time goes in v14:
time: 618 us; the launch traced here: 609 us
  waiting for transfers between devices  235 us (38%)
  starting transfers between devices  139 us (22%)
  blocking collectives  128 us (21%)
  local copies, waits for them, and re-layouts  52.8 us (9%)
  other arithmetic  23.1 us (4%)
  between operations  15.2 us (2%)
  matrix products  14.6 us (2%)
    all_to_all x4, waiting for transfers between devices, on_device(): lax.all_to_all(triple, 'ctx', split_axis=2, concat_axis=1, tiled=True)  105 us
    all_to_all x4, blocking collectives, on_device(): lax.all_to_all(outgoing, 'ctx', split_axis=0, concat_axis=0, tiled=True)  85.6 us
    psum x1, blocking collectives, on_device(): grad_rows = lax.psum(grad_rows, 'ctx')  42.7 us
    unnamed x3, waiting for transfers between devices  42 us
    ppermute x7, waiting for transfers between devices, on_device(): key_blocks.append(lax.ppermute(key_weight[0], 'dp', pairs))  36.8 us
    ppermute x4, starting transfers between devices, shifted(): lax.ppermute(value, axis, [(source, source + steps) for source in range(f...  32.8 us
    unnamed x41, local copies, waits for them, and re-layouts  28 us
    ppermute x7, starting transfers between devices, on_device(): key_blocks.append(lax.ppermute(key_weight[0], 'dp', pairs))  24.4 us
  transfers between devices with their start and end apart: 29, of which 15 were waited for; matrix products, arithmetic and copies ran while one was open for 7% of the time, Pallas kernels for 0%

profile of v14, /device:TPU:1, one launch (start us, length us, event | category | flops | bytes accessed | tf_op | source)
XLA Modules:
  0.0 608.5 jit_solution(6330334581896447720)
XLA Ops:
  7.9 4.0 collective-permute-start
  11.9 4.4 collective-permute-start.1
  16.3 4.1 collective-permute-start.2
  20.3 2.1 collective-permute-start.3
  22.4 3.2 collective-permute-start.4
  31.0 8.8 %reduce.37 = bf16[1536,64]{1,0:T(8,128)(2,1)S(1)} reduce(bf16[1536,1,64]{2,1,0:T(2,128)(2,1)S(1)} %bitcast.189, bf16[]{:T(256)} %broadcast.437), dimensions={1}, to_apply=%bitcast.133.reduce_sub_computation | reduce | bytes 393218
  40.7 14.9 %all-to-all-start.1 = ((bf16[16,2,3072]{2,1,0:T(2,128)(2,1)}), bf16[16,2,3072]{2,1,0:T(2,128)(2,1)S(1)}, u32[]{:S(2)}, u32[]{:S(2)}) async-start(bf16[16,2,3072]{2,1,0:T(2,128)(2,1)} %reshape.652), calls=%async_computation.1 | async-start | bytes 393216 | tf_op jit(solution)/shard_map/all_to_all | solution.py:120
  56.9 3.3 collective-permute-start.5
  60.2 1.9 bitcast_dynamic-update-slice_fusion.6
  62.2 3.3 collective-permute-start.6
  65.5 1.9 bitcast_dynamic-update-slice_fusion.5
  67.5 1.9 bitcast_dynamic-update-slice_fusion.4
  69.4 19.2 %collective-permute-done.3 = bf16[192,1536]{1,0:T(8,128)(2,1)} collective-permute-done((bf16[192,1536]{1,0:T(8,128)(2,1)}, bf16[192,1536]{1,0:T(8,128)(2,1)}, u32[]{:S(2)}, u32[]{:S(2)}) %collective-permute-start.3) | collective-permute-done | bytes 589856 | tf_op jit(solution)/shard_map/ppermute | solution.py:61
  88.6 1.9 bitcast_dynamic-update-slice_fusion.3
  91.4 2.3 collective-permute-done.5
  94.6 15.3 %collective-permute-done.6 = bf16[192,1536]{1,0:T(8,128)(2,1)S(1)} collective-permute-done((bf16[192,1536]{1,0:T(8,128)(2,1)S(1)}, bf16[192,1536]{1,0:T(8,128)(2,1)S(1)}, u32[]{:S(2)}, u32[]{:S(2)}) %collective-permute-start.6) | collective-permute-done | bytes 589856 | tf_op jit(solution)/shard_map/ppermute | solution.py:61
  110.8 5.5 gather_fusion
  116.2 5.1 bitcast_select_fusion
  121.3 2.7 all-gather.3.cloned.1.call-done
  124.7 1.3 reshape.650
  126.0 14.9 %all-to-all-start = ((bf16[16,2,6144]{2,1,0:T(2,128)(2,1)}), bf16[16,2,6144]{2,1,0:T(2,128)(2,1)S(1)}, u32[]{:S(2)}, u32[]{:S(2)}) async-start(bf16[16,2,6144]{2,1,0:T(2,128)(2,1)} %reshape.650), calls=%async_computation | async-start | bytes 786432 | tf_op jit(solution)/shard_map/all_to_all | solution.py:124
  142.0 13.4 %all-to-all-done = bf16[16,2,6144]{2,1,0:T(2,128)(2,1)S(1)} async-done(((bf16[16,2,6144]{2,1,0:T(2,128)(2,1)}), bf16[16,2,6144]{2,1,0:T(2,128)(2,1)S(1)}, u32[]{:S(2)}, u32[]{:S(2)}) %all-to-all-start) | async-done | bytes 393248 | tf_op jit(solution)/shard_map/all_to_all | solution.py:124
  157.3 24.0 %all_to_all.121 = bf16[16,48,128]{2,1,0:T(8,128)(2,1)S(1)} all-to-all(bf16[16,48,128]{2,1,0:T(8,128)(2,1)S(1)} %reshape.618), channel_id=1, replica_groups=mesh['pipe'=4,'ctx'=16,'dp'=8] {'ctx'}, dimensions={0} | all-to-all | bytes 393216 | tf_op jit(solution)/shard_map/all_to_all | solution.py:142
  182.2 12.8 %collective-permute-start.7 = (bf16[1,64,1536]{2,1,0:T(8,128)(2,1)S(1)}, bf16[1,64,1536]{2,1,0:T(8,128)(2,1)S(1)}, u32[]{:S(2)}, u32[]{:S(2)}) collective-permute-start(bf16[1,64,1536]{2,1,0:T(8,128)(2,1)S(1)} %fusion.109), channel_id=1, source_target_pairs={{0,128},{128,256},{256,384},{1,129},{129,257},{257,385},{2,130},{1... | collective-permute-start | bytes 589832 | tf_op jit(solution)/shard_map/ppermute | solution.py:15
  194.9 2.6 collective-permute-done.7
  197.8 4.8 conditional.12
  197.9 3.4 fusion.16
  203.7 1.8 reshape.654
  205.5 4.7 all-to-all-start.3
  210.2 28.1 %all-to-all-done.3 = bf16[16,2,9216]{2,1,0:T(2,128)(2,1)S(1)} async-done(((bf16[16,2,9216]{2,1,0:T(2,128)(2,1)}), bf16[16,2,9216]{2,1,0:T(2,128)(2,1)S(1)}, u32[]{:S(2)}, u32[]{:S(2)}) %all-to-all-start.3) | async-done | bytes 589856 | tf_op jit(solution)/shard_map/all_to_all | solution.py:128
  240.2 3.8 conditional.13
  241.2 1.5 fusion.21
  242.8 1.2 fusion.28
  244.6 20.6 %all_to_all.122 = bf16[16,48,128]{2,1,0:T(8,128)(2,1)S(1)} all-to-all(bf16[16,48,128]{2,1,0:T(8,128)(2,1)S(1)} %reshape.619), channel_id=1, replica_groups=mesh['pipe'=4,'ctx'=16,'dp'=8] {'ctx'}, dimensions={0} | all-to-all | bytes 393216 | tf_op jit(solution)/shard_map/all_to_all | solution.py:142
  265.9 1.9 collective-permute-start.8
  267.8 3.3 collective-permute-done.8
  271.5 4.8 conditional.14
  271.5 3.4 fusion.34
  277.3 1.8 reshape.656
  279.1 7.5 %all-to-all-start.5 = ((bf16[16,2,9216]{2,1,0:T(2,128)(2,1)}), bf16[16,2,9216]{2,1,0:T(2,128)(2,1)S(1)}, u32[]{:S(2)}, u32[]{:S(2)}) async-start(bf16[16,2,9216]{2,1,0:T(2,128)(2,1)} %reshape.656), calls=%async_computation.5 | async-start | bytes 1179648 | tf_op jit(solution)/shard_map/all_to_all | solution.py:128
  286.6 27.0 %all-to-all-done.5 = bf16[16,2,9216]{2,1,0:T(2,128)(2,1)S(1)} async-done(((bf16[16,2,9216]{2,1,0:T(2,128)(2,1)}), bf16[16,2,9216]{2,1,0:T(2,128)(2,1)S(1)}, u32[]{:S(2)}, u32[]{:S(2)}) %all-to-all-start.5) | async-done | bytes 589856 | tf_op jit(solution)/shard_map/all_to_all | solution.py:128
  315.5 3.8 conditional.15
  316.6 1.5 fusion.39
  318.2 1.2 fusion.46
  319.9 20.2 %all_to_all.123 = bf16[16,48,128]{2,1,0:T(8,128)(2,1)S(1)} all-to-all(bf16[16,48,128]{2,1,0:T(8,128)(2,1)S(1)} %reshape.620), channel_id=1, replica_groups=mesh['pipe'=4,'ctx'=16,'dp'=8] {'ctx'}, dimensions={0} | all-to-all | bytes 393216 | tf_op jit(solution)/shard_map/all_to_all | solution.py:142
  340.9 3.5 collective-permute-start.9
  344.4 2.6 collective-permute-done.9
  348.4 1.8 reshape.658
  350.2 4.8 all-to-all-start.7
  355.0 27.5 %all-to-all-done.7 = bf16[16,2,9216]{2,1,0:T(2,128)(2,1)S(1)} async-done(((bf16[16,2,9216]{2,1,0:T(2,128)(2,1)}), bf16[16,2,9216]{2,1,0:T(2,128)(2,1)S(1)}, u32[]{:S(2)}, u32[]{:S(2)}) %all-to-all-start.7) | async-done | bytes 589856 | tf_op jit(solution)/shard_map/all_to_all | solution.py:128
  385.3 20.9 %all_to_all.124 = bf16[16,48,128]{2,1,0:T(8,128)(2,1)S(1)} all-to-all(bf16[16,48,128]{2,1,0:T(8,128)(2,1)S(1)} %reshape.621), channel_id=1, replica_groups=mesh['pipe'=4,'ctx'=16,'dp'=8] {'ctx'}, dimensions={0} | all-to-all | bytes 393216 | tf_op jit(solution)/shard_map/all_to_all | solution.py:142
  406.9 14.6 %collective-permute-start.10 = (bf16[1,64,1536]{2,1,0:T(8,128)(2,1)S(1)}, bf16[1,64,1536]{2,1,0:T(8,128)(2,1)S(1)}, u32[]{:S(2)}, u32[]{:S(2)}) collective-permute-start(bf16[1,64,1536]{2,1,0:T(8,128)(2,1)S(1)} %fusion.101), channel_id=1, source_target_pairs={{0,128},{128,256},{256,384},{1,129},{129,257},{257,385},{2,130},{1... | collective-permute-start | bytes 589832 | tf_op jit(solution)/shard_map/ppermute | solution.py:15
  421.5 2.6 collective-permute-done.10
  425.5 1.8 reshape.660
  427.3 3.6 all-to-all-start.9
  430.9 22.6 %all-to-all-done.9 = bf16[16,2,9216]{2,1,0:T(2,128)(2,1)S(1)} async-done(((bf16[16,2,9216]{2,1,0:T(2,128)(2,1)}), bf16[16,2,9216]{2,1,0:T(2,128)(2,1)S(1)}, u32[]{:S(2)}, u32[]{:S(2)}) %all-to-all-start.9) | async-done | bytes 589856 | tf_op jit(solution)/shard_map/all_to_all | solution.py:128
  456.8 6.7 %all-to-all-start.10 = ((bf16[16,48,128]{2,1,0:T(8,128)(2,1)}), bf16[16,48,128]{2,1,0:T(8,128)(2,1)S(1)}, u32[]{:S(2)}, u32[]{:S(2)}) async-start(bf16[16,48,128]{2,1,0:T(8,128)(2,1)} %reshape.622), calls=%async_computation.10 | async-start | bytes 393216 | tf_op jit(solution)/shard_map/all_to_all | solution.py:142
  464.3 18.3 %collective-permute-start.12 = (bf16[1536,16]{0,1:T(8,128)(2,1)S(1)}, bf16[1536,16]{0,1:T(8,128)(2,1)S(1)}, u32[]{:S(2)}, u32[]{:S(2)}) collective-permute-start(bf16[1536,16]{0,1:T(8,128)(2,1)S(1)} %copy-done.11), channel_id=1, source_target_pairs={{128,384},{129,385},{130,386},{131,387},{132,388},{133,389},{134,3... | collective-permute-start | bytes 147464 | tf_op jit(solution)/shard_map/ppermute | solution.py:71
  485.4 1.2 copy.102
  487.2 1.3 collective-permute-start.15
  489.2 41.3 %reduce-scatter.4.cloned.1.call-done = f32[192,64]{1,0:T(8,128)} async-done(((f32[1536,64]{1,0:T(8,128)}), f32[192,64]{1,0:T(8,128)}) %reduce-scatter.4.cloned.1.call-update) | async-done | bytes 49168
  531.5 42.7 %psum.7 = f32[192,64]{0,1:T(8,128)S(1)} all-reduce(f32[192,64]{0,1:T(8,128)S(1)} %copy.103), channel_id=1, replica_groups=mesh['pipe'=4,'ctx'=16,'dp'=8] {'ctx'}, use_global_device_ids=true, to_apply=%region_37.38 | all-reduce | flops 12288 | bytes 98304 | tf_op jit(solution)/shard_map/psum | solution.py:165
  574.8 1.3 collective-permute-start.18
  577.4 23.4 %collective-permute-done.18 = f32[192,16]{0,1:T(8,128)S(1)} collective-permute-done((f32[192,16]{0,1:T(8,128)S(1)}, f32[192,16]{0,1:T(8,128)S(1)}, u32[]{:S(2)}, u32[]{:S(2)}) %collective-permute-start.18) | collective-permute-done | bytes 12320 | tf_op jit(solution)/shard_map/ppermute | solution.py:172
  (161 shorter events, 46.8 us)
Async XLA Ops:
  7.2 21.3 %copy-start = (bf16[64,1536]{1,0:T(8,128)(2,1)S(1)}, bf16[64,1536]{1,0:T(8,128)(2,1)}, u32[]{:S(2)}) copy-start(bf16[64,1536]{1,0:T(8,128)(2,1)} %param.35) | copy-start | bytes 589828
  7.2 48.5 %copy-start.7 = (bf16[1,192,1536]{2,1,0:T(8,128)(2,1)S(1)}, bf16[1,192,1536]{2,1,0:T(8,128)(2,1)}, u32[]{:S(2)}) copy-start(bf16[1,192,1536]{2,1,0:T(8,128)(2,1)} %param.38) | copy-start | bytes 1769476
  7.2 116.8 %all-gather.3.cloned.1.call-start = ((), (), s32[]{:S(2)}) async-start(), calls=%async_computation.12 | async-start | bytes 5308416 | tf_op jit(solution)/shard_map/all_gather | solution.py:57
  7.9 48.9 %collective-permute-start = (bf16[192,1536]{1,0:T(8,128)(2,1)}, bf16[192,1536]{1,0:T(8,128)(2,1)}, u32[]{:S(2)}, u32[]{:S(2)}) collective-permute-start(bf16[192,1536]{1,0:T(8,128)(2,1)} %bitcast.200), channel_id=1, source_target_pairs={{0,1},{1,2},{2,3},{3,4},{4,5},{5,6},{6,7},{7,0},{8,9},{9,10},{10,1... | collective-permute-start | bytes 1769480 | tf_op jit(solution)/shard_map/ppermute | solution.py:61
  11.9 50.3 %collective-permute-start.1 = (bf16[192,1536]{1,0:T(8,128)(2,1)}, bf16[192,1536]{1,0:T(8,128)(2,1)}, u32[]{:S(2)}, u32[]{:S(2)}) collective-permute-start(bf16[192,1536]{1,0:T(8,128)(2,1)} %bitcast.201), channel_id=1, source_target_pairs={{0,2},{1,3},{2,4},{3,5},{4,6},{5,7},{6,0},{7,1},{8,10},{9,11},{10,... | collective-permute-start | bytes 1769480 | tf_op jit(solution)/shard_map/ppermute | solution.py:61
  16.3 51.2 %collective-permute-start.2 = (bf16[192,1536]{1,0:T(8,128)(2,1)}, bf16[192,1536]{1,0:T(8,128)(2,1)}, u32[]{:S(2)}, u32[]{:S(2)}) collective-permute-start(bf16[192,1536]{1,0:T(8,128)(2,1)} %bitcast.202), channel_id=1, source_target_pairs={{0,3},{1,4},{2,5},{3,6},{4,7},{5,0},{6,1},{7,2},{8,11},{9,12},{10,... | collective-permute-start | bytes 1769480 | tf_op jit(solution)/shard_map/ppermute | solution.py:61
  20.3 68.2 %collective-permute-start.3 = (bf16[192,1536]{1,0:T(8,128)(2,1)}, bf16[192,1536]{1,0:T(8,128)(2,1)}, u32[]{:S(2)}, u32[]{:S(2)}) collective-permute-start(bf16[192,1536]{1,0:T(8,128)(2,1)} %bitcast.203), channel_id=1, source_target_pairs={{0,4},{1,5},{2,6},{3,7},{4,0},{5,1},{6,2},{7,3},{8,12},{9,13},{10,... | collective-permute-start | bytes 1769480 | tf_op jit(solution)/shard_map/ppermute | solution.py:61
  22.4 68.1 %collective-permute-start.4 = (bf16[192,1536]{1,0:T(8,128)(2,1)}, bf16[192,1536]{1,0:T(8,128)(2,1)S(1)}, u32[]{:S(2)}, u32[]{:S(2)}) collective-permute-start(bf16[192,1536]{1,0:T(8,128)(2,1)} %bitcast.204), channel_id=1, source_target_pairs={{0,5},{1,6},{2,7},{3,0},{4,1},{5,2},{6,3},{7,4},{8,13},{9,14},{10,... | collective-permute-start | bytes 1769480 | tf_op jit(solution)/shard_map/ppermute | solution.py:61
  40.7 85.3 %all-to-all-start.1 = ((bf16[16,2,3072]{2,1,0:T(2,128)(2,1)}), bf16[16,2,3072]{2,1,0:T(2,128)(2,1)S(1)}, u32[]{:S(2)}, u32[]{:S(2)}) async-start(bf16[16,2,3072]{2,1,0:T(2,128)(2,1)} %reshape.652), calls=%async_computation.1 | async-start | bytes 393216 | tf_op jit(solution)/shard_map/all_to_all | solution.py:120
  56.9 36.8 %collective-permute-start.5 = (bf16[192,1536]{1,0:T(8,128)(2,1)S(1)}, bf16[192,1536]{1,0:T(8,128)(2,1)S(1)}, u32[]{:S(2)}, u32[]{:S(2)}) collective-permute-start(bf16[192,1536]{1,0:T(8,128)(2,1)S(1)} %bitcast.205), channel_id=1, source_target_pairs={{0,6},{1,7},{2,0},{3,1},{4,2},{5,3},{6,4},{7,5},{8,14},{9,15},{10,... | collective-permute-start | bytes 1769480 | tf_op jit(solution)/shard_map/ppermute | solution.py:61
  62.2 47.8 %collective-permute-start.6 = (bf16[192,1536]{1,0:T(8,128)(2,1)S(1)}, bf16[192,1536]{1,0:T(8,128)(2,1)S(1)}, u32[]{:S(2)}, u32[]{:S(2)}) collective-permute-start(bf16[192,1536]{1,0:T(8,128)(2,1)S(1)} %bitcast.206), channel_id=1, source_target_pairs={{0,7},{1,0},{2,1},{3,2},{4,3},{5,4},{6,5},{7,6},{8,15},{9,8},{10,9... | collective-permute-start | bytes 1769480 | tf_op jit(solution)/shard_map/ppermute | solution.py:61
  124.1 32.5 %copy-start.10 = (s32[2,1,1024]{2,1,0:T(1,128)S(1)}, s32[2,1,1024]{2,1,0:T(1,128)}, u32[]{:S(2)}) copy-start(s32[2,1,1024]{2,1,0:T(1,128)} %param.34) | copy-start | bytes 24580
  126.0 29.4 %all-to-all-start = ((bf16[16,2,6144]{2,1,0:T(2,128)(2,1)}), bf16[16,2,6144]{2,1,0:T(2,128)(2,1)S(1)}, u32[]{:S(2)}, u32[]{:S(2)}) async-start(bf16[16,2,6144]{2,1,0:T(2,128)(2,1)} %reshape.650), calls=%async_computation | async-start | bytes 786432 | tf_op jit(solution)/shard_map/all_to_all | solution.py:124
  182.2 15.4 %collective-permute-start.7 = (bf16[1,64,1536]{2,1,0:T(8,128)(2,1)S(1)}, bf16[1,64,1536]{2,1,0:T(8,128)(2,1)S(1)}, u32[]{:S(2)}, u32[]{:S(2)}) collective-permute-start(bf16[1,64,1536]{2,1,0:T(8,128)(2,1)S(1)} %fusion.109), channel_id=1, source_target_pairs={{0,128},{128,256},{256,384},{1,129},{129,257},{257,385},{2,130},{1... | collective-permute-start | bytes 589832 | tf_op jit(solution)/shard_map/ppermute | solution.py:15
  197.8 3.8 copy-start.3
  205.5 32.7 %all-to-all-start.3 = ((bf16[16,2,9216]{2,1,0:T(2,128)(2,1)}), bf16[16,2,9216]{2,1,0:T(2,128)(2,1)S(1)}, u32[]{:S(2)}, u32[]{:S(2)}) async-start(bf16[16,2,9216]{2,1,0:T(2,128)(2,1)} %reshape.654), calls=%async_computation.3 | async-start | bytes 1179648 | tf_op jit(solution)/shard_map/all_to_all | solution.py:128
  265.9 5.3 collective-permute-start.8
  271.5 3.8 copy-start.4
  279.1 34.4 %all-to-all-start.5 = ((bf16[16,2,9216]{2,1,0:T(2,128)(2,1)}), bf16[16,2,9216]{2,1,0:T(2,128)(2,1)S(1)}, u32[]{:S(2)}, u32[]{:S(2)}) async-start(bf16[16,2,9216]{2,1,0:T(2,128)(2,1)} %reshape.656), calls=%async_computation.5 | async-start | bytes 1179648 | tf_op jit(solution)/shard_map/all_to_all | solution.py:128
  340.9 6.1 %collective-permute-start.9 = (bf16[1,64,1536]{2,1,0:T(8,128)(2,1)S(1)}, bf16[1,64,1536]{2,1,0:T(8,128)(2,1)S(1)}, u32[]{:S(2)}, u32[]{:S(2)}) collective-permute-start(bf16[1,64,1536]{2,1,0:T(8,128)(2,1)S(1)} %fusion.97), channel_id=1, source_target_pairs={{0,128},{128,256},{256,384},{1,129},{129,257},{257,385},{2,130},{1... | collective-permute-start | bytes 589832 | tf_op jit(solution)/shard_map/ppermute | solution.py:15
  350.2 32.3 %all-to-all-start.7 = ((bf16[16,2,9216]{2,1,0:T(2,128)(2,1)}), bf16[16,2,9216]{2,1,0:T(2,128)(2,1)S(1)}, u32[]{:S(2)}, u32[]{:S(2)}) async-start(bf16[16,2,9216]{2,1,0:T(2,128)(2,1)} %reshape.658), calls=%async_computation.7 | async-start | bytes 1179648 | tf_op jit(solution)/shard_map/all_to_all | solution.py:128
  406.9 17.2 %collective-permute-start.10 = (bf16[1,64,1536]{2,1,0:T(8,128)(2,1)S(1)}, bf16[1,64,1536]{2,1,0:T(8,128)(2,1)S(1)}, u32[]{:S(2)}, u32[]{:S(2)}) collective-permute-start(bf16[1,64,1536]{2,1,0:T(8,128)(2,1)S(1)} %fusion.101), channel_id=1, source_target_pairs={{0,128},{128,256},{256,384},{1,129},{129,257},{257,385},{2,130},{1... | collective-permute-start | bytes 589832 | tf_op jit(solution)/shard_map/ppermute | solution.py:15
  427.3 26.2 %all-to-all-start.9 = ((bf16[16,2,9216]{2,1,0:T(2,128)(2,1)}), bf16[16,2,9216]{2,1,0:T(2,128)(2,1)S(1)}, u32[]{:S(2)}, u32[]{:S(2)}) async-start(bf16[16,2,9216]{2,1,0:T(2,128)(2,1)} %reshape.660), calls=%async_computation.9 | async-start | bytes 1179648 | tf_op jit(solution)/shard_map/all_to_all | solution.py:128
  455.5 8.1 %copy-start.11 = (bf16[1536,16]{0,1:T(8,128)(2,1)S(1)}, bf16[1536,16]{0,1:T(8,128)(2,1)}, u32[]{:S(2)}) copy-start(bf16[1536,16]{0,1:T(8,128)(2,1)} %param.41) | copy-start | bytes 147460
  455.5 27.8 %copy-start.8 = (f32[2,1,64,64]{3,2,1,0:T(8,128)S(1)}, f32[2,1,64,64]{3,2,1,0:T(8,128)}, u32[]{:S(2)}) copy-start(f32[2,1,64,64]{3,2,1,0:T(8,128)} %param.31) | copy-start | bytes 98308
  455.5 27.9 %copy-start.9 = (f32[2,1,64,64]{3,2,1,0:T(8,128)S(1)}, f32[2,1,64,64]{3,2,1,0:T(8,128)}, u32[]{:S(2)}) copy-start(f32[2,1,64,64]{3,2,1,0:T(8,128)} %param.32) | copy-start | bytes 98308
  455.6 28.9 %copy-start.12 = (f32[1536]{0:T(1024)S(1)}, f32[1536]{0:T(1024)}, u32[]{:S(2)}) copy-start(f32[1536]{0:T(1024)} %param.40) | copy-start | bytes 18436
  456.8 26.7 %all-to-all-start.10 = ((bf16[16,48,128]{2,1,0:T(8,128)(2,1)}), bf16[16,48,128]{2,1,0:T(8,128)(2,1)S(1)}, u32[]{:S(2)}, u32[]{:S(2)}) async-start(bf16[16,48,128]{2,1,0:T(8,128)(2,1)} %reshape.622), calls=%async_computation.10 | async-start | bytes 393216 | tf_op jit(solution)/shard_map/all_to_all | solution.py:142
  463.6 66.9 %reduce-scatter.4.cloned.1.call-start = ((), (), s32[]{:S(2)}) async-start(), calls=%async_computation.13 | async-start | bytes 884736
  463.6 20.9 %collective-permute-start.11 = (bf16[1536,16]{0,1:T(8,128)(2,1)S(1)}, bf16[1536,16]{0,1:T(8,128)(2,1)S(1)}, u32[]{:S(2)}, u32[]{:S(2)}) collective-permute-start(bf16[1536,16]{0,1:T(8,128)(2,1)S(1)} %copy-done.11), channel_id=1, source_target_pairs={{0,384},{1,385},{2,386},{3,387},{4,388},{5,389},{6,390},{7,391},{8... | collective-permute-start | bytes 147464 | tf_op jit(solution)/shard_map/ppermute | solution.py:71
  464.3 20.2 %collective-permute-start.12 = (bf16[1536,16]{0,1:T(8,128)(2,1)S(1)}, bf16[1536,16]{0,1:T(8,128)(2,1)S(1)}, u32[]{:S(2)}, u32[]{:S(2)}) collective-permute-start(bf16[1536,16]{0,1:T(8,128)(2,1)S(1)} %copy-done.11), channel_id=1, source_target_pairs={{128,384},{129,385},{130,386},{131,387},{132,388},{133,389},{134,3... | collective-permute-start | bytes 147464 | tf_op jit(solution)/shard_map/ppermute | solution.py:71
  482.7 1.9 collective-permute-start.13
  483.7 117.8 %copy-start.1 = (bf16[64,1536]{1,0:T(8,128)(2,1)S(1)}, bf16[64,1536]{1,0:T(8,128)(2,1)}, u32[]{:S(2)}) copy-start(bf16[64,1536]{1,0:T(8,128)(2,1)} %param.35) | copy-start | bytes 589828
  486.6 89.6 %collective-permute-start.14 = (f32[2,1,64,16]{2,3,0,1:T(8,128)S(1)}, f32[2,1,64,16]{2,3,0,1:T(8,128)S(1)}, u32[]{:S(2)}, u32[]{:S(2)}) collective-permute-start(f32[2,1,64,16]{2,3,0,1:T(8,128)S(1)} %get-tuple-element.322), channel_id=1, source_target_pairs={{384,0},{385,1},{386,2},{387,3},{388,4},{389,5},{390,6},{391,7},{3... | collective-permute-start | bytes 24584 | tf_op jit(solution)/shard_map/ppermute | solution.py:171
  487.2 89.6 %collective-permute-start.15 = (f32[2,1,64,16]{2,3,0,1:T(8,128)S(1)}, f32[2,1,64,16]{2,3,0,1:T(8,128)S(1)}, u32[]{:S(2)}, u32[]{:S(2)}) collective-permute-start(f32[2,1,64,16]{2,3,0,1:T(8,128)S(1)} %get-tuple-element.320), channel_id=1, source_target_pairs={{384,128},{385,129},{386,130},{387,131},{388,132},{389,133},{390,1... | collective-permute-start | bytes 24584 | tf_op jit(solution)/shard_map/ppermute | solution.py:171
  488.5 88.3 %collective-permute-start.16 = (f32[2,1,64,16]{2,3,0,1:T(8,128)S(1)}, f32[2,1,64,16]{2,3,0,1:T(8,128)S(1)}, u32[]{:S(2)}, u32[]{:S(2)}) collective-permute-start(f32[2,1,64,16]{2,3,0,1:T(8,128)S(1)} %get-tuple-element.321), channel_id=1, source_target_pairs={{384,256},{385,257},{386,258},{387,259},{388,260},{389,261},{390,2... | collective-permute-start | bytes 24584 | tf_op jit(solution)/shard_map/ppermute | solution.py:171
  574.2 3.3 collective-permute-start.17
  574.8 26.0 %collective-permute-start.18 = (f32[192,16]{0,1:T(8,128)S(1)}, f32[192,16]{0,1:T(8,128)S(1)}, u32[]{:S(2)}, u32[]{:S(2)}) collective-permute-start(f32[192,16]{0,1:T(8,128)S(1)} %get-tuple-element.317), channel_id=1, source_target_pairs={{384,128},{385,129},{386,130},{387,131},{388,132},{389,133},{390,1... | collective-permute-start | bytes 36872 | tf_op jit(solution)/shard_map/ppermute | solution.py:172
  576.1 24.7 %collective-permute-start.19 = (f32[192,16]{0,1:T(8,128)S(1)}, f32[192,16]{0,1:T(8,128)S(1)}, u32[]{:S(2)}, u32[]{:S(2)}) collective-permute-start(f32[192,16]{0,1:T(8,128)S(1)} %get-tuple-element.318), channel_id=1, source_target_pairs={{384,256},{385,257},{386,258},{387,259},{388,260},{389,261},{390,2... | collective-permute-start | bytes 36872 | tf_op jit(solution)/shard_map/ppermute | solution.py:172
Sparse Core Ops, SparseCore 0:
  10.1 113.8 all-gather.2
  486.7 43.7 reduce-scatter.3

commit v15 on v14

--- a/solution.py
+++ b/solution.py
@@ -108,9 +108,17 @@
             queries = jnp.dot(source, full_query, preferred_element_type=jnp.float32).astype(
                 jnp.bfloat16
             )
-            keys = jnp.dot(source, full_key, preferred_element_type=jnp.float32).astype(
-                jnp.bfloat16
-            )
+            if moment == 0:
+                block_rows = model_width // dp_count
+                by_block = source.reshape(local_rows, dp_count, block_rows)
+                in_step_order = jnp.take(by_block, source_step, axis=1).reshape(
+                    local_rows, model_width
+                )
+                step_key = by_step.reshape(model_width, model_width)
+                keys = jnp.dot(in_step_order, step_key, preferred_element_type=jnp.float32)
+            else:
+                keys = jnp.dot(source, full_key, preferred_element_type=jnp.float32)
+            keys = keys.astype(jnp.bfloat16)
             return jnp.stack((queries, keys, source), axis=0)
 
         def blank_triple(source):

time: 618 us -> 623 us (level)
  blocking collectives: 128 us -> 103 us
  waiting for transfers between devices: 235 us -> 252 us
  starting transfers between devices: 139 us -> 151 us
    all_to_all x4 -> x3, blocking collectives: 85.6 us -> 60.4 us  [on_device(): lax.all_to_all(outgoing, 'ctx', split_axis=0, concat_axis=0, tiled=True)]
    all_gather x1, waiting for transfers between devices: 2.71 us -> 13.2 us  [on_device(): full_query = lax.all_gather(query_weight[0], 'dp', axis=0, tiled=True)]
    all_to_all x1 -> x2, starting transfers between devices: 6.75 us -> 15.9 us  [on_device(): lax.all_to_all(outgoing, 'ctx', split_axis=0, concat_axis=0, tiled=True)]
    all_to_all x1 -> x2, waiting for transfers between devices: 0.01 us -> 6.69 us  [on_device(): lax.all_to_all(outgoing, 'ctx', split_axis=0, concat_axis=0, tiled=True)]
  transfers between devices with their start and end apart: 29 -> 30, of which waited for: 15 -> 15; matrix products, arithmetic and copies ran while one was open for 7% -> 7% of each run, Pallas kernels for 0% -> 0%
where the time goes in v15:
time: 623 us; the launch traced here: 614 us
  waiting for transfers between devices  252 us (40%)
  starting transfers between devices  151 us (24%)
  blocking collectives  103 us (17%)
  local copies, waits for them, and re-layouts  53.5 us (9%)
  other arithmetic  23.1 us (4%)
  between operations  15.2 us (2%)
  matrix products  14.6 us (2%)
    all_to_all x4, waiting for transfers between devices, on_device(): lax.all_to_all(triple, 'ctx', split_axis=2, concat_axis=1, tiled=True)  108 us
    all_to_all x3, blocking collectives, on_device(): lax.all_to_all(outgoing, 'ctx', split_axis=0, concat_axis=0, tiled=True)  60.4 us
    psum x1, blocking collectives, on_device(): grad_rows = lax.psum(grad_rows, 'ctx')  42.8 us
    unnamed x3, waiting for transfers between devices  42.1 us
    ppermute x7, waiting for transfers between devices, on_device(): key_blocks.append(lax.ppermute(key_weight[0], 'dp', pairs))  37 us
    ppermute x4, starting transfers between devices, shifted(): lax.ppermute(value, axis, [(source, source + steps) for source in range(f...  35.2 us
    unnamed x41, local copies, waits for them, and re-layouts  28 us
    ppermute x7, starting transfers between devices, on_device(): key_blocks.append(lax.ppermute(key_weight[0], 'dp', pairs))  24.4 us
  transfers between devices with their start and end apart: 30, of which 15 were waited for; matrix products, arithmetic and copies ran while one was open for 7% of the time, Pallas kernels for 0%

profile of v15, /device:TPU:1, one launch (start us, length us, event | category | flops | bytes accessed | tf_op | source)
XLA Modules:
  0.0 613.8 jit_solution(7331022444867417601)
XLA Ops:
  7.9 4.0 collective-permute-start
  11.9 4.4 collective-permute-start.1
  16.3 4.1 collective-permute-start.2
  20.3 2.1 collective-permute-start.3
  22.4 3.2 collective-permute-start.4
  31.0 8.8 %reduce.37 = bf16[1536,64]{1,0:T(8,128)(2,1)S(1)} reduce(bf16[1536,1,64]{2,1,0:T(2,128)(2,1)S(1)} %bitcast.197, bf16[]{:T(256)} %broadcast.466), dimensions={1}, to_apply=%bitcast.142.reduce_sub_computation | reduce | bytes 393218
  40.7 14.9 %all-to-all-start.1 = ((bf16[16,2,3072]{2,1,0:T(2,128)(2,1)}), bf16[16,2,3072]{2,1,0:T(2,128)(2,1)S(1)}, u32[]{:S(2)}, u32[]{:S(2)}) async-start(bf16[16,2,3072]{2,1,0:T(2,128)(2,1)} %reshape.669), calls=%async_computation.1 | async-start | bytes 393216 | tf_op jit(solution)/shard_map/all_to_all | solution.py:128
  56.7 3.3 collective-permute-start.5
  60.0 1.9 bitcast_dynamic-update-slice_fusion.6
  62.0 3.4 collective-permute-start.6
  65.3 1.9 bitcast_dynamic-update-slice_fusion.5
  67.3 1.9 bitcast_dynamic-update-slice_fusion.4
  69.2 19.4 %collective-permute-done.3 = bf16[192,1536]{1,0:T(8,128)(2,1)} collective-permute-done((bf16[192,1536]{1,0:T(8,128)(2,1)}, bf16[192,1536]{1,0:T(8,128)(2,1)}, u32[]{:S(2)}, u32[]{:S(2)}) %collective-permute-start.3) | collective-permute-done | bytes 589856 | tf_op jit(solution)/shard_map/ppermute | solution.py:61
  88.6 1.9 bitcast_dynamic-update-slice_fusion.3
  91.4 2.4 collective-permute-done.5
  94.7 15.3 %collective-permute-done.6 = bf16[192,1536]{1,0:T(8,128)(2,1)S(1)} collective-permute-done((bf16[192,1536]{1,0:T(8,128)(2,1)S(1)}, bf16[192,1536]{1,0:T(8,128)(2,1)S(1)}, u32[]{:S(2)}, u32[]{:S(2)}) %collective-permute-start.6) | collective-permute-done | bytes 589856 | tf_op jit(solution)/shard_map/ppermute | solution.py:61
  110.8 13.2 %all-gather.3.cloned.1.call-done = bf16[1,1536,1536]{2,1,0:T(8,128)(2,1)} async-done(((bf16[1,192,1536]{2,1,0:T(8,128)(2,1)}), bf16[1,1536,1536]{2,1,0:T(8,128)(2,1)}) %all-gather.3.cloned.1.call-update) | async-done | bytes 4718608 | tf_op jit(solution)/shard_map/all_gather | solution.py:57
  124.7 1.3 reshape.667
  126.0 14.9 %all-to-all-start = ((bf16[16,2,6144]{2,1,0:T(2,128)(2,1)}), bf16[16,2,6144]{2,1,0:T(2,128)(2,1)S(1)}, u32[]{:S(2)}, u32[]{:S(2)}) async-start(bf16[16,2,6144]{2,1,0:T(2,128)(2,1)} %reshape.667), calls=%async_computation | async-start | bytes 786432 | tf_op jit(solution)/shard_map/all_to_all | solution.py:132
  142.0 13.6 %all-to-all-done = bf16[16,2,6144]{2,1,0:T(2,128)(2,1)S(1)} async-done(((bf16[16,2,6144]{2,1,0:T(2,128)(2,1)}), bf16[16,2,6144]{2,1,0:T(2,128)(2,1)S(1)}, u32[]{:S(2)}, u32[]{:S(2)}) %all-to-all-start) | async-done | bytes 393248 | tf_op jit(solution)/shard_map/all_to_all | solution.py:132
  158.2 9.3 %all-to-all-start.2 = ((bf16[16,48,128]{2,1,0:T(8,128)(2,1)}), bf16[16,48,128]{2,1,0:T(8,128)(2,1)S(1)}, u32[]{:S(2)}, u32[]{:S(2)}) async-start(bf16[16,48,128]{2,1,0:T(8,128)(2,1)} %reshape.625), calls=%async_computation.2 | async-start | bytes 393216 | tf_op jit(solution)/shard_map/all_to_all | solution.py:150
  167.7 5.4 gather_fusion.1
  173.1 6.7 %all-to-all-done.2 = bf16[16,48,128]{2,1,0:T(8,128)(2,1)S(1)} async-done(((bf16[16,48,128]{2,1,0:T(8,128)(2,1)}), bf16[16,48,128]{2,1,0:T(8,128)(2,1)S(1)}, u32[]{:S(2)}, u32[]{:S(2)}) %all-to-all-start.2) | async-done | bytes 196640 | tf_op jit(solution)/shard_map/all_to_all | solution.py:150
  180.6 15.2 %collective-permute-start.7 = (bf16[1,64,1536]{2,1,0:T(8,128)(2,1)S(1)}, bf16[1,64,1536]{2,1,0:T(8,128)(2,1)S(1)}, u32[]{:S(2)}, u32[]{:S(2)}) collective-permute-start(bf16[1,64,1536]{2,1,0:T(8,128)(2,1)S(1)} %fusion.115), channel_id=1, source_target_pairs={{0,128},{128,256},{256,384},{1,129},{129,257},{257,385},{2,130},{1... | collective-permute-start | bytes 589832 | tf_op jit(solution)/shard_map/ppermute | solution.py:15
  195.8 5.0 bitcast_select_fusion
  201.1 4.8 conditional.12
  201.2 3.4 fusion.14
  207.0 1.8 reshape.671
  208.8 4.7 all-to-all-start.3
  213.5 30.1 %all-to-all-done.3 = bf16[16,2,9216]{2,1,0:T(2,128)(2,1)S(1)} async-done(((bf16[16,2,9216]{2,1,0:T(2,128)(2,1)}), bf16[16,2,9216]{2,1,0:T(2,128)(2,1)S(1)}, u32[]{:S(2)}, u32[]{:S(2)}) %all-to-all-start.3) | async-done | bytes 589856 | tf_op jit(solution)/shard_map/all_to_all | solution.py:136
  245.5 4.0 conditional.13
  246.6 1.5 fusion.19
  248.2 1.2 fusion.26
  250.1 19.4 %all_to_all.121 = bf16[16,48,128]{2,1,0:T(8,128)(2,1)S(1)} all-to-all(bf16[16,48,128]{2,1,0:T(8,128)(2,1)S(1)} %reshape.626), channel_id=1, replica_groups=mesh['pipe'=4,'ctx'=16,'dp'=8] {'ctx'}, dimensions={0} | all-to-all | bytes 393216 | tf_op jit(solution)/shard_map/all_to_all | solution.py:150
  270.3 1.9 collective-permute-start.8
  272.3 3.5 collective-permute-done.8
  276.1 4.8 conditional.14
  276.1 3.4 fusion.32
  282.0 1.8 reshape.673
  283.8 7.5 %all-to-all-start.5 = ((bf16[16,2,9216]{2,1,0:T(2,128)(2,1)}), bf16[16,2,9216]{2,1,0:T(2,128)(2,1)S(1)}, u32[]{:S(2)}, u32[]{:S(2)}) async-start(bf16[16,2,9216]{2,1,0:T(2,128)(2,1)} %reshape.673), calls=%async_computation.5 | async-start | bytes 1179648 | tf_op jit(solution)/shard_map/all_to_all | solution.py:136
  291.3 27.0 %all-to-all-done.5 = bf16[16,2,9216]{2,1,0:T(2,128)(2,1)S(1)} async-done(((bf16[16,2,9216]{2,1,0:T(2,128)(2,1)}), bf16[16,2,9216]{2,1,0:T(2,128)(2,1)S(1)}, u32[]{:S(2)}, u32[]{:S(2)}) %all-to-all-start.5) | async-done | bytes 589856 | tf_op jit(solution)/shard_map/all_to_all | solution.py:136
  320.1 3.8 conditional.15
  321.2 1.5 fusion.37
  322.8 1.2 fusion.44
  324.5 20.2 %all_to_all.122 = bf16[16,48,128]{2,1,0:T(8,128)(2,1)S(1)} all-to-all(bf16[16,48,128]{2,1,0:T(8,128)(2,1)S(1)} %reshape.627), channel_id=1, replica_groups=mesh['pipe'=4,'ctx'=16,'dp'=8] {'ctx'}, dimensions={0} | all-to-all | bytes 393216 | tf_op jit(solution)/shard_map/all_to_all | solution.py:150
  345.5 3.5 collective-permute-start.9
  349.0 2.6 collective-permute-done.9
  353.0 1.8 reshape.675
  354.9 5.2 all-to-all-start.7
  360.0 27.6 %all-to-all-done.7 = bf16[16,2,9216]{2,1,0:T(2,128)(2,1)S(1)} async-done(((bf16[16,2,9216]{2,1,0:T(2,128)(2,1)}), bf16[16,2,9216]{2,1,0:T(2,128)(2,1)S(1)}, u32[]{:S(2)}, u32[]{:S(2)}) %all-to-all-start.7) | async-done | bytes 589856 | tf_op jit(solution)/shard_map/all_to_all | solution.py:136
  390.2 20.8 %all_to_all.123 = bf16[16,48,128]{2,1,0:T(8,128)(2,1)S(1)} all-to-all(bf16[16,48,128]{2,1,0:T(8,128)(2,1)S(1)} %reshape.628), channel_id=1, replica_groups=mesh['pipe'=4,'ctx'=16,'dp'=8] {'ctx'}, dimensions={0} | all-to-all | bytes 393216 | tf_op jit(solution)/shard_map/all_to_all | solution.py:150
  411.7 14.6 %collective-permute-start.10 = (bf16[1,64,1536]{2,1,0:T(8,128)(2,1)S(1)}, bf16[1,64,1536]{2,1,0:T(8,128)(2,1)S(1)}, u32[]{:S(2)}, u32[]{:S(2)}) collective-permute-start(bf16[1,64,1536]{2,1,0:T(8,128)(2,1)S(1)} %fusion.107), channel_id=1, source_target_pairs={{0,128},{128,256},{256,384},{1,129},{129,257},{257,385},{2,130},{1... | collective-permute-start | bytes 589832 | tf_op jit(solution)/shard_map/ppermute | solution.py:15
  426.3 2.6 collective-permute-done.10
  430.3 1.8 reshape.677
  432.2 3.6 all-to-all-start.9
  435.7 22.8 %all-to-all-done.9 = bf16[16,2,9216]{2,1,0:T(2,128)(2,1)S(1)} async-done(((bf16[16,2,9216]{2,1,0:T(2,128)(2,1)}), bf16[16,2,9216]{2,1,0:T(2,128)(2,1)S(1)}, u32[]{:S(2)}, u32[]{:S(2)}) %all-to-all-start.9) | async-done | bytes 589856 | tf_op jit(solution)/shard_map/all_to_all | solution.py:136
  462.0 6.6 %all-to-all-start.10 = ((bf16[16,48,128]{2,1,0:T(8,128)(2,1)}), bf16[16,48,128]{2,1,0:T(8,128)(2,1)S(1)}, u32[]{:S(2)}, u32[]{:S(2)}) async-start(bf16[16,48,128]{2,1,0:T(8,128)(2,1)} %reshape.629), calls=%async_computation.10 | async-start | bytes 393216 | tf_op jit(solution)/shard_map/all_to_all | solution.py:150
  469.3 18.3 %collective-permute-start.12 = (bf16[1536,16]{0,1:T(8,128)(2,1)S(1)}, bf16[1536,16]{0,1:T(8,128)(2,1)S(1)}, u32[]{:S(2)}, u32[]{:S(2)}) collective-permute-start(bf16[1536,16]{0,1:T(8,128)(2,1)S(1)} %copy-done.11), channel_id=1, source_target_pairs={{128,384},{129,385},{130,386},{131,387},{132,388},{133,389},{134,3... | collective-permute-start | bytes 147464 | tf_op jit(solution)/shard_map/ppermute | solution.py:71
  490.4 1.2 copy.124
  492.2 1.3 collective-permute-start.15
  494.2 41.4 %reduce-scatter.4.cloned.1.call-done = f32[192,64]{1,0:T(8,128)} async-done(((f32[1536,64]{1,0:T(8,128)}), f32[192,64]{1,0:T(8,128)}) %reduce-scatter.4.cloned.1.call-update) | async-done | bytes 49168
  536.6 42.8 %psum.7 = f32[192,64]{0,1:T(8,128)S(1)} all-reduce(f32[192,64]{0,1:T(8,128)S(1)} %copy.125), channel_id=1, replica_groups=mesh['pipe'=4,'ctx'=16,'dp'=8] {'ctx'}, use_global_device_ids=true, to_apply=%region_37.38 | all-reduce | flops 12288 | bytes 98304 | tf_op jit(solution)/shard_map/psum | solution.py:173
  580.1 1.3 collective-permute-start.18
  582.7 23.4 %collective-permute-done.18 = f32[192,16]{0,1:T(8,128)S(1)} collective-permute-done((f32[192,16]{0,1:T(8,128)S(1)}, f32[192,16]{0,1:T(8,128)S(1)}, u32[]{:S(2)}, u32[]{:S(2)}) %collective-permute-start.18) | collective-permute-done | bytes 12320 | tf_op jit(solution)/shard_map/ppermute | solution.py:180
  (163 shorter events, 47.5 us)
Async XLA Ops:
  7.2 21.3 %copy-start = (bf16[64,1536]{1,0:T(8,128)(2,1)S(1)}, bf16[64,1536]{1,0:T(8,128)(2,1)}, u32[]{:S(2)}) copy-start(bf16[64,1536]{1,0:T(8,128)(2,1)} %param.35) | copy-start | bytes 589828
  7.2 48.5 %copy-start.7 = (bf16[1,192,1536]{2,1,0:T(8,128)(2,1)S(1)}, bf16[1,192,1536]{2,1,0:T(8,128)(2,1)}, u32[]{:S(2)}) copy-start(bf16[1,192,1536]{2,1,0:T(8,128)(2,1)} %param.38) | copy-start | bytes 1769476
  7.2 116.8 %all-gather.3.cloned.1.call-start = ((), (), s32[]{:S(2)}) async-start(), calls=%async_computation.12 | async-start | bytes 5308416 | tf_op jit(solution)/shard_map/all_gather | solution.py:57
  7.9 48.8 %collective-permute-start = (bf16[192,1536]{1,0:T(8,128)(2,1)}, bf16[192,1536]{1,0:T(8,128)(2,1)}, u32[]{:S(2)}, u32[]{:S(2)}) collective-permute-start(bf16[192,1536]{1,0:T(8,128)(2,1)} %bitcast.208), channel_id=1, source_target_pairs={{0,1},{1,2},{2,3},{3,4},{4,5},{5,6},{6,7},{7,0},{8,9},{9,10},{10,1... | collective-permute-start | bytes 1769480 | tf_op jit(solution)/shard_map/ppermute | solution.py:61
  11.9 50.1 %collective-permute-start.1 = (bf16[192,1536]{1,0:T(8,128)(2,1)}, bf16[192,1536]{1,0:T(8,128)(2,1)}, u32[]{:S(2)}, u32[]{:S(2)}) collective-permute-start(bf16[192,1536]{1,0:T(8,128)(2,1)} %bitcast.209), channel_id=1, source_target_pairs={{0,2},{1,3},{2,4},{3,5},{4,6},{5,7},{6,0},{7,1},{8,10},{9,11},{10,... | collective-permute-start | bytes 1769480 | tf_op jit(solution)/shard_map/ppermute | solution.py:61
  16.3 51.0 %collective-permute-start.2 = (bf16[192,1536]{1,0:T(8,128)(2,1)}, bf16[192,1536]{1,0:T(8,128)(2,1)}, u32[]{:S(2)}, u32[]{:S(2)}) collective-permute-start(bf16[192,1536]{1,0:T(8,128)(2,1)} %bitcast.210), channel_id=1, source_target_pairs={{0,3},{1,4},{2,5},{3,6},{4,7},{5,0},{6,1},{7,2},{8,11},{9,12},{10,... | collective-permute-start | bytes 1769480 | tf_op jit(solution)/shard_map/ppermute | solution.py:61
  20.3 68.2 %collective-permute-start.3 = (bf16[192,1536]{1,0:T(8,128)(2,1)}, bf16[192,1536]{1,0:T(8,128)(2,1)}, u32[]{:S(2)}, u32[]{:S(2)}) collective-permute-start(bf16[192,1536]{1,0:T(8,128)(2,1)} %bitcast.211), channel_id=1, source_target_pairs={{0,4},{1,5},{2,6},{3,7},{4,0},{5,1},{6,2},{7,3},{8,12},{9,13},{10,... | collective-permute-start | bytes 1769480 | tf_op jit(solution)/shard_map/ppermute | solution.py:61
  22.4 68.1 %collective-permute-start.4 = (bf16[192,1536]{1,0:T(8,128)(2,1)}, bf16[192,1536]{1,0:T(8,128)(2,1)S(1)}, u32[]{:S(2)}, u32[]{:S(2)}) collective-permute-start(bf16[192,1536]{1,0:T(8,128)(2,1)} %bitcast.212), channel_id=1, source_target_pairs={{0,5},{1,6},{2,7},{3,0},{4,1},{5,2},{6,3},{7,4},{8,13},{9,14},{10,... | collective-permute-start | bytes 1769480 | tf_op jit(solution)/shard_map/ppermute | solution.py:61
  40.7 85.3 %all-to-all-start.1 = ((bf16[16,2,3072]{2,1,0:T(2,128)(2,1)}), bf16[16,2,3072]{2,1,0:T(2,128)(2,1)S(1)}, u32[]{:S(2)}, u32[]{:S(2)}) async-start(bf16[16,2,3072]{2,1,0:T(2,128)(2,1)} %reshape.669), calls=%async_computation.1 | async-start | bytes 393216 | tf_op jit(solution)/shard_map/all_to_all | solution.py:128
  56.7 37.1 %collective-permute-start.5 = (bf16[192,1536]{1,0:T(8,128)(2,1)S(1)}, bf16[192,1536]{1,0:T(8,128)(2,1)S(1)}, u32[]{:S(2)}, u32[]{:S(2)}) collective-permute-start(bf16[192,1536]{1,0:T(8,128)(2,1)S(1)} %bitcast.213), channel_id=1, source_target_pairs={{0,6},{1,7},{2,0},{3,1},{4,2},{5,3},{6,4},{7,5},{8,14},{9,15},{10,... | collective-permute-start | bytes 1769480 | tf_op jit(solution)/shard_map/ppermute | solution.py:61
  62.0 48.0 %collective-permute-start.6 = (bf16[192,1536]{1,0:T(8,128)(2,1)S(1)}, bf16[192,1536]{1,0:T(8,128)(2,1)S(1)}, u32[]{:S(2)}, u32[]{:S(2)}) collective-permute-start(bf16[192,1536]{1,0:T(8,128)(2,1)S(1)} %bitcast.214), channel_id=1, source_target_pairs={{0,7},{1,0},{2,1},{3,2},{4,3},{5,4},{6,5},{7,6},{8,15},{9,8},{10,9... | collective-permute-start | bytes 1769480 | tf_op jit(solution)/shard_map/ppermute | solution.py:61
  124.1 32.6 %copy-start.10 = (s32[2,1,1024]{2,1,0:T(1,128)S(1)}, s32[2,1,1024]{2,1,0:T(1,128)}, u32[]{:S(2)}) copy-start(s32[2,1,1024]{2,1,0:T(1,128)} %param.34) | copy-start | bytes 24580
  126.0 29.6 %all-to-all-start = ((bf16[16,2,6144]{2,1,0:T(2,128)(2,1)}), bf16[16,2,6144]{2,1,0:T(2,128)(2,1)S(1)}, u32[]{:S(2)}, u32[]{:S(2)}) async-start(bf16[16,2,6144]{2,1,0:T(2,128)(2,1)} %reshape.667), calls=%async_computation | async-start | bytes 786432 | tf_op jit(solution)/shard_map/all_to_all | solution.py:132
  158.2 21.6 %all-to-all-start.2 = ((bf16[16,48,128]{2,1,0:T(8,128)(2,1)}), bf16[16,48,128]{2,1,0:T(8,128)(2,1)S(1)}, u32[]{:S(2)}, u32[]{:S(2)}) async-start(bf16[16,48,128]{2,1,0:T(8,128)(2,1)} %reshape.625), calls=%async_computation.2 | async-start | bytes 393216 | tf_op jit(solution)/shard_map/all_to_all | solution.py:150
  180.6 20.3 %collective-permute-start.7 = (bf16[1,64,1536]{2,1,0:T(8,128)(2,1)S(1)}, bf16[1,64,1536]{2,1,0:T(8,128)(2,1)S(1)}, u32[]{:S(2)}, u32[]{:S(2)}) collective-permute-start(bf16[1,64,1536]{2,1,0:T(8,128)(2,1)S(1)} %fusion.115), channel_id=1, source_target_pairs={{0,128},{128,256},{256,384},{1,129},{129,257},{257,385},{2,130},{1... | collective-permute-start | bytes 589832 | tf_op jit(solution)/shard_map/ppermute | solution.py:15
  201.2 3.8 copy-start.2
  208.8 34.8 %all-to-all-start.3 = ((bf16[16,2,9216]{2,1,0:T(2,128)(2,1)}), bf16[16,2,9216]{2,1,0:T(2,128)(2,1)S(1)}, u32[]{:S(2)}, u32[]{:S(2)}) async-start(bf16[16,2,9216]{2,1,0:T(2,128)(2,1)} %reshape.671), calls=%async_computation.3 | async-start | bytes 1179648 | tf_op jit(solution)/shard_map/all_to_all | solution.py:136
  270.3 5.5 collective-permute-start.8
  276.1 3.8 copy-start.3
  283.8 34.4 %all-to-all-start.5 = ((bf16[16,2,9216]{2,1,0:T(2,128)(2,1)}), bf16[16,2,9216]{2,1,0:T(2,128)(2,1)S(1)}, u32[]{:S(2)}, u32[]{:S(2)}) async-start(bf16[16,2,9216]{2,1,0:T(2,128)(2,1)} %reshape.673), calls=%async_computation.5 | async-start | bytes 1179648 | tf_op jit(solution)/shard_map/all_to_all | solution.py:136
  345.5 6.1 collective-permute-start.9
  354.9 32.8 %all-to-all-start.7 = ((bf16[16,2,9216]{2,1,0:T(2,128)(2,1)}), bf16[16,2,9216]{2,1,0:T(2,128)(2,1)S(1)}, u32[]{:S(2)}, u32[]{:S(2)}) async-start(bf16[16,2,9216]{2,1,0:T(2,128)(2,1)} %reshape.675), calls=%async_computation.7 | async-start | bytes 1179648 | tf_op jit(solution)/shard_map/all_to_all | solution.py:136
  411.7 17.2 %collective-permute-start.10 = (bf16[1,64,1536]{2,1,0:T(8,128)(2,1)S(1)}, bf16[1,64,1536]{2,1,0:T(8,128)(2,1)S(1)}, u32[]{:S(2)}, u32[]{:S(2)}) collective-permute-start(bf16[1,64,1536]{2,1,0:T(8,128)(2,1)S(1)} %fusion.107), channel_id=1, source_target_pairs={{0,128},{128,256},{256,384},{1,129},{129,257},{257,385},{2,130},{1... | collective-permute-start | bytes 589832 | tf_op jit(solution)/shard_map/ppermute | solution.py:15
  432.2 26.4 %all-to-all-start.9 = ((bf16[16,2,9216]{2,1,0:T(2,128)(2,1)}), bf16[16,2,9216]{2,1,0:T(2,128)(2,1)S(1)}, u32[]{:S(2)}, u32[]{:S(2)}) async-start(bf16[16,2,9216]{2,1,0:T(2,128)(2,1)} %reshape.677), calls=%async_computation.9 | async-start | bytes 1179648 | tf_op jit(solution)/shard_map/all_to_all | solution.py:136
  460.5 8.2 %copy-start.11 = (bf16[1536,16]{0,1:T(8,128)(2,1)S(1)}, bf16[1536,16]{0,1:T(8,128)(2,1)}, u32[]{:S(2)}) copy-start(bf16[1536,16]{0,1:T(8,128)(2,1)} %param.41) | copy-start | bytes 147460
  460.5 27.8 %copy-start.8 = (f32[2,1,64,64]{3,2,1,0:T(8,128)S(1)}, f32[2,1,64,64]{3,2,1,0:T(8,128)}, u32[]{:S(2)}) copy-start(f32[2,1,64,64]{3,2,1,0:T(8,128)} %param.31) | copy-start | bytes 98308
  460.5 27.9 %copy-start.9 = (f32[2,1,64,64]{3,2,1,0:T(8,128)S(1)}, f32[2,1,64,64]{3,2,1,0:T(8,128)}, u32[]{:S(2)}) copy-start(f32[2,1,64,64]{3,2,1,0:T(8,128)} %param.32) | copy-start | bytes 98308
  460.7 28.8 %copy-start.12 = (f32[1536]{0:T(1024)S(1)}, f32[1536]{0:T(1024)}, u32[]{:S(2)}) copy-start(f32[1536]{0:T(1024)} %param.40) | copy-start | bytes 18436
  462.0 26.6 %all-to-all-start.10 = ((bf16[16,48,128]{2,1,0:T(8,128)(2,1)}), bf16[16,48,128]{2,1,0:T(8,128)(2,1)S(1)}, u32[]{:S(2)}, u32[]{:S(2)}) async-start(bf16[16,48,128]{2,1,0:T(8,128)(2,1)} %reshape.629), calls=%async_computation.10 | async-start | bytes 393216 | tf_op jit(solution)/shard_map/all_to_all | solution.py:150
  468.6 67.0 %reduce-scatter.4.cloned.1.call-start = ((), (), s32[]{:S(2)}) async-start(), calls=%async_computation.13 | async-start | bytes 884736
  468.6 20.8 %collective-permute-start.11 = (bf16[1536,16]{0,1:T(8,128)(2,1)S(1)}, bf16[1536,16]{0,1:T(8,128)(2,1)S(1)}, u32[]{:S(2)}, u32[]{:S(2)}) collective-permute-start(bf16[1536,16]{0,1:T(8,128)(2,1)S(1)} %copy-done.11), channel_id=1, source_target_pairs={{0,384},{1,385},{2,386},{3,387},{4,388},{5,389},{6,390},{7,391},{8... | collective-permute-start | bytes 147464 | tf_op jit(solution)/shard_map/ppermute | solution.py:71
  469.3 20.2 %collective-permute-start.12 = (bf16[1536,16]{0,1:T(8,128)(2,1)S(1)}, bf16[1536,16]{0,1:T(8,128)(2,1)S(1)}, u32[]{:S(2)}, u32[]{:S(2)}) collective-permute-start(bf16[1536,16]{0,1:T(8,128)(2,1)S(1)} %copy-done.11), channel_id=1, source_target_pairs={{128,384},{129,385},{130,386},{131,387},{132,388},{133,389},{134,3... | collective-permute-start | bytes 147464 | tf_op jit(solution)/shard_map/ppermute | solution.py:71
  487.6 1.9 collective-permute-start.13
  488.7 118.0 %copy-start.1 = (bf16[64,1536]{1,0:T(8,128)(2,1)S(1)}, bf16[64,1536]{1,0:T(8,128)(2,1)}, u32[]{:S(2)}) copy-start(bf16[64,1536]{1,0:T(8,128)(2,1)} %param.35) | copy-start | bytes 589828
  491.6 89.8 %collective-permute-start.14 = (f32[2,1,64,16]{2,3,0,1:T(8,128)S(1)}, f32[2,1,64,16]{2,3,0,1:T(8,128)S(1)}, u32[]{:S(2)}, u32[]{:S(2)}) collective-permute-start(f32[2,1,64,16]{2,3,0,1:T(8,128)S(1)} %get-tuple-element.343), channel_id=1, source_target_pairs={{384,0},{385,1},{386,2},{387,3},{388,4},{389,5},{390,6},{391,7},{3... | collective-permute-start | bytes 24584 | tf_op jit(solution)/shard_map/ppermute | solution.py:179
  492.2 89.8 %collective-permute-start.15 = (f32[2,1,64,16]{2,3,0,1:T(8,128)S(1)}, f32[2,1,64,16]{2,3,0,1:T(8,128)S(1)}, u32[]{:S(2)}, u32[]{:S(2)}) collective-permute-start(f32[2,1,64,16]{2,3,0,1:T(8,128)S(1)} %get-tuple-element.341), channel_id=1, source_target_pairs={{384,128},{385,129},{386,130},{387,131},{388,132},{389,133},{390,1... | collective-permute-start | bytes 24584 | tf_op jit(solution)/shard_map/ppermute | solution.py:179
  493.5 88.5 %collective-permute-start.16 = (f32[2,1,64,16]{2,3,0,1:T(8,128)S(1)}, f32[2,1,64,16]{2,3,0,1:T(8,128)S(1)}, u32[]{:S(2)}, u32[]{:S(2)}) collective-permute-start(f32[2,1,64,16]{2,3,0,1:T(8,128)S(1)} %get-tuple-element.342), channel_id=1, source_target_pairs={{384,256},{385,257},{386,258},{387,259},{388,260},{389,261},{390,2... | collective-permute-start | bytes 24584 | tf_op jit(solution)/shard_map/ppermute | solution.py:179
  579.4 3.3 collective-permute-start.17
  580.1 26.1 %collective-permute-start.18 = (f32[192,16]{0,1:T(8,128)S(1)}, f32[192,16]{0,1:T(8,128)S(1)}, u32[]{:S(2)}, u32[]{:S(2)}) collective-permute-start(f32[192,16]{0,1:T(8,128)S(1)} %get-tuple-element.338), channel_id=1, source_target_pairs={{384,128},{385,129},{386,130},{387,131},{388,132},{389,133},{390,1... | collective-permute-start | bytes 36872 | tf_op jit(solution)/shard_map/ppermute | solution.py:180
  581.4 24.8 %collective-permute-start.19 = (f32[192,16]{0,1:T(8,128)S(1)}, f32[192,16]{0,1:T(8,128)S(1)}, u32[]{:S(2)}, u32[]{:S(2)}) collective-permute-start(f32[192,16]{0,1:T(8,128)S(1)} %get-tuple-element.339), channel_id=1, source_target_pairs={{384,256},{385,257},{386,258},{387,259},{388,260},{389,261},{390,2... | collective-permute-start | bytes 36872 | tf_op jit(solution)/shard_map/ppermute | solution.py:180
Sparse Core Ops, SparseCore 0:
  10.1 113.8 all-gather.2
  491.7 43.8 reduce-scatter.3

commit v16 on v14

--- a/solution.py
+++ b/solution.py
@@ -120,9 +120,21 @@
             value_heads = lax.all_to_all(
                 normed[None], "ctx", split_axis=2, concat_axis=1, tiled=True
             )
-            pair = lax.cond(active, project, blank_triple, normed)[:2]
-            pair_heads = lax.all_to_all(pair, "ctx", split_axis=2, concat_axis=1, tiled=True)
-            section_by_heads = jnp.concatenate((pair_heads, value_heads), axis=0)
+            def project_one(source, weight):
+                return jnp.dot(source, weight, preferred_element_type=jnp.float32).astype(
+                    jnp.bfloat16
+                )[None]
+
+            def blank_one(source, weight):
+                return jnp.zeros((1,) + source.shape, jnp.bfloat16)
+
+            query_rows = lax.cond(active, project_one, blank_one, normed, full_query)
+            query_heads = lax.all_to_all(
+                query_rows, "ctx", split_axis=2, concat_axis=1, tiled=True
+            )
+            key_rows = lax.cond(active, project_one, blank_one, normed, full_key)
+            key_heads = lax.all_to_all(key_rows, "ctx", split_axis=2, concat_axis=1, tiled=True)
+            section_by_heads = jnp.concatenate((query_heads, key_heads, value_heads), axis=0)
         else:
             triple = lax.cond(active, project, blank_triple, normed)
             section_by_heads = lax.all_to_all(

time: 618 us -> 636 us (1.029)
  other arithmetic: 23.1 us -> 40.8 us
    unnamed x3 -> x5, other arithmetic: 10.1 us -> 27.9 us
    all_to_all x1 -> x2, starting transfers between devices: 14.9 us -> 22.6 us  [the longest x1 13.1 us: on_device(): lax.all_to_all(key_rows, 'ctx', split_axis=2, concat_axis=1, tiled=True)]
    ppermute x4, waiting for transfers between devices: 11.1 us -> 18.1 us  [shifted(): lax.ppermute(value, axis, [(source, source + steps) for source in range(f...]
    all_to_all x1 -> x2, waiting for transfers between devices: 13.4 us -> 12.1 us  [the longest x1 10.1 us: on_device(): lax.all_to_all(query_rows, 'ctx', split_axis=2, concat_axis=1, tiled=True)]
    unnamed x41 -> x42, local copies, waits for them, and re-layouts: 28 us -> 28.3 us
  transfers between devices with their start and end apart: 29 -> 30, of which waited for: 15 -> 15; matrix products, arithmetic and copies ran while one was open for 7% -> 10% of each run, Pallas kernels for 0% -> 0%
where the time goes in v16:
time: 636 us; the launch traced here: 628 us
  waiting for transfers between devices  233 us (37%)
  starting transfers between devices  143 us (22%)
  blocking collectives  126 us (20%)
  local copies, waits for them, and re-layouts  55 us (9%)
  other arithmetic  40.8 us (6%)
  between operations  15.2 us (2%)
  matrix products  14.6 us (2%)
    all_to_all x4, waiting for transfers between devices, on_device(): lax.all_to_all(triple, 'ctx', split_axis=2, concat_axis=1, tiled=True)  104 us
    all_to_all x4, blocking collectives, on_device(): lax.all_to_all(outgoing, 'ctx', split_axis=0, concat_axis=0, tiled=True)  82.7 us
    psum x1, blocking collectives, on_device(): grad_rows = lax.psum(grad_rows, 'ctx')  42.9 us
    ppermute x7, waiting for transfers between devices, on_device(): key_blocks.append(lax.ppermute(key_weight[0], 'dp', pairs))  38.1 us
    unnamed x3, waiting for transfers between devices  36.9 us
    ppermute x4, starting transfers between devices, shifted(): lax.ppermute(value, axis, [(source, source + steps) for source in range(f...  30.2 us
    unnamed x42, local copies, waits for them, and re-layouts  28.3 us
    unnamed x5, other arithmetic  27.9 us
  transfers between devices with their start and end apart: 30, of which 15 were waited for; matrix products, arithmetic and copies ran while one was open for 10% of the time, Pallas kernels for 0%

profile of v16, /device:TPU:1, one launch (start us, length us, event | category | flops | bytes accessed | tf_op | source)
XLA Modules:
  0.0 628.3 jit_solution(8502125076571135832)
XLA Ops:
  7.2 4.1 collective-permute-start
  11.3 4.4 collective-permute-start.1
  15.7 4.1 collective-permute-start.2
  19.8 2.1 collective-permute-start.3
  21.9 3.2 collective-permute-start.4
  30.6 8.8 %reduce.39 = bf16[1536,64]{1,0:T(8,128)(2,1)S(1)} reduce(bf16[1536,1,64]{2,1,0:T(2,128)(2,1)S(1)} %bitcast.189, bf16[]{:T(256)} %broadcast.453), dimensions={1}, to_apply=%bitcast.135.reduce_sub_computation | reduce | bytes 393218
  40.3 14.9 %all-to-all-start.2 = ((bf16[16,2,3072]{2,1,0:T(2,128)(2,1)}), bf16[16,2,3072]{2,1,0:T(2,128)(2,1)S(1)}, u32[]{:S(2)}, u32[]{:S(2)}) async-start(bf16[16,2,3072]{2,1,0:T(2,128)(2,1)} %reshape.652), calls=%async_computation.2 | async-start | bytes 393216 | tf_op jit(solution)/shard_map/all_to_all | solution.py:120
  56.4 3.3 collective-permute-start.5
  59.8 1.9 bitcast_dynamic-update-slice_fusion.6
  61.7 3.4 collective-permute-start.6
  65.1 1.9 bitcast_dynamic-update-slice_fusion.5
  67.0 1.9 bitcast_dynamic-update-slice_fusion.4
  68.9 11.5 %collective-permute-done.3 = bf16[192,1536]{1,0:T(8,128)(2,1)} collective-permute-done((bf16[192,1536]{1,0:T(8,128)(2,1)}, bf16[192,1536]{1,0:T(8,128)(2,1)}, u32[]{:S(2)}, u32[]{:S(2)}) %collective-permute-start.3) | collective-permute-done | bytes 589856 | tf_op jit(solution)/shard_map/ppermute | solution.py:61
  80.4 1.9 bitcast_dynamic-update-slice_fusion.3
  83.3 7.1 %collective-permute-done.5 = bf16[192,1536]{1,0:T(8,128)(2,1)S(1)} collective-permute-done((bf16[192,1536]{1,0:T(8,128)(2,1)S(1)}, bf16[192,1536]{1,0:T(8,128)(2,1)S(1)}, u32[]{:S(2)}, u32[]{:S(2)}) %collective-permute-start.5) | collective-permute-done | bytes 589856 | tf_op jit(solution)/shard_map/ppermute | solution.py:61
  91.3 19.5 %collective-permute-done.6 = bf16[192,1536]{1,0:T(8,128)(2,1)S(1)} collective-permute-done((bf16[192,1536]{1,0:T(8,128)(2,1)S(1)}, bf16[192,1536]{1,0:T(8,128)(2,1)S(1)}, u32[]{:S(2)}, u32[]{:S(2)}) %collective-permute-start.6) | collective-permute-done | bytes 589856 | tf_op jit(solution)/shard_map/ppermute | solution.py:61
  111.6 5.4 gather_fusion
  117.1 5.1 bitcast_select_fusion
  123.2 8.8 %reduce.38 = bf16[1536,64]{1,0:T(8,128)(2,1)S(1)} reduce(bf16[1536,1,64]{2,1,0:T(2,128)(2,1)S(1)} %bitcast.191, bf16[]{:T(256)} %broadcast.453), dimensions={1}, to_apply=%bitcast.133.reduce_sub_computation | reduce | bytes 393218
  133.0 13.1 %all-to-all-start.1 = ((bf16[16,2,3072]{2,1,0:T(2,128)(2,1)}), bf16[16,2,3072]{2,1,0:T(2,128)(2,1)S(1)}, u32[]{:S(2)}, u32[]{:S(2)}) async-start(bf16[16,2,3072]{2,1,0:T(2,128)(2,1)} %reshape.650), calls=%async_computation.1 | async-start | bytes 393216 | tf_op jit(solution)/shard_map/all_to_all | solution.py:136
  146.7 8.8 %reduce.37 = bf16[1536,64]{1,0:T(8,128)(2,1)S(1)} reduce(bf16[1536,1,64]{2,1,0:T(2,128)(2,1)S(1)} %bitcast.190, bf16[]{:T(256)} %broadcast.453), dimensions={1}, to_apply=%bitcast.131.reduce_sub_computation | reduce | bytes 393218
  156.5 2.0 all-to-all-done.1
  158.5 9.5 %all-to-all-start = ((bf16[16,2,3072]{2,1,0:T(2,128)(2,1)}), bf16[16,2,3072]{2,1,0:T(2,128)(2,1)S(1)}, u32[]{:S(2)}, u32[]{:S(2)}) async-start(bf16[16,2,3072]{2,1,0:T(2,128)(2,1)} %reshape.648), calls=%async_computation | async-start | bytes 393216 | tf_op jit(solution)/shard_map/all_to_all | solution.py:132
  170.2 10.1 %all-to-all-done = bf16[16,2,3072]{2,1,0:T(2,128)(2,1)S(1)} async-done(((bf16[16,2,3072]{2,1,0:T(2,128)(2,1)}), bf16[16,2,3072]{2,1,0:T(2,128)(2,1)S(1)}, u32[]{:S(2)}, u32[]{:S(2)}) %all-to-all-start) | async-done | bytes 196640 | tf_op jit(solution)/shard_map/all_to_all | solution.py:132
  182.2 17.0 %all_to_all.137 = bf16[16,48,128]{2,1,0:T(8,128)(2,1)S(1)} all-to-all(bf16[16,48,128]{2,1,0:T(8,128)(2,1)S(1)} %reshape.616), channel_id=1, replica_groups=mesh['pipe'=4,'ctx'=16,'dp'=8] {'ctx'}, dimensions={0} | all-to-all | bytes 393216 | tf_op jit(solution)/shard_map/all_to_all | solution.py:154
  200.0 11.0 %collective-permute-start.7 = (bf16[1,64,1536]{2,1,0:T(8,128)(2,1)S(1)}, bf16[1,64,1536]{2,1,0:T(8,128)(2,1)S(1)}, u32[]{:S(2)}, u32[]{:S(2)}) collective-permute-start(bf16[1,64,1536]{2,1,0:T(8,128)(2,1)S(1)} %fusion.109), channel_id=1, source_target_pairs={{0,128},{128,256},{256,384},{1,129},{129,257},{257,385},{2,130},{1... | collective-permute-start | bytes 589832 | tf_op jit(solution)/shard_map/ppermute | solution.py:15
  211.0 8.0 %collective-permute-done.7 = bf16[1,64,1536]{2,1,0:T(8,128)(2,1)S(1)} collective-permute-done((bf16[1,64,1536]{2,1,0:T(8,128)(2,1)S(1)}, bf16[1,64,1536]{2,1,0:T(8,128)(2,1)S(1)}, u32[]{:S(2)}, u32[]{:S(2)}) %collective-permute-start.7) | collective-permute-done | bytes 196640 | tf_op jit(solution)/shard_map/ppermute | solution.py:15
  219.3 4.8 conditional.14
  219.3 3.4 fusion.16
  225.1 1.8 reshape.654
  227.0 4.8 all-to-all-start.4
  231.7 26.1 %all-to-all-done.4 = bf16[16,2,9216]{2,1,0:T(2,128)(2,1)S(1)} async-done(((bf16[16,2,9216]{2,1,0:T(2,128)(2,1)}), bf16[16,2,9216]{2,1,0:T(2,128)(2,1)S(1)}, u32[]{:S(2)}, u32[]{:S(2)}) %all-to-all-start.4) | async-done | bytes 589856 | tf_op jit(solution)/shard_map/all_to_all | solution.py:140
  259.8 3.8 conditional.15
  260.8 1.5 fusion.21
  264.2 25.0 %all_to_all.138 = bf16[16,48,128]{2,1,0:T(8,128)(2,1)S(1)} all-to-all(bf16[16,48,128]{2,1,0:T(8,128)(2,1)S(1)} %reshape.617), channel_id=1, replica_groups=mesh['pipe'=4,'ctx'=16,'dp'=8] {'ctx'}, dimensions={0} | all-to-all | bytes 393216 | tf_op jit(solution)/shard_map/all_to_all | solution.py:154
  290.0 1.9 collective-permute-start.8
  291.9 4.9 collective-permute-done.8
  297.1 4.8 conditional.16
  297.2 3.4 fusion.34
  303.0 1.8 reshape.656
  304.8 6.5 %all-to-all-start.6 = ((bf16[16,2,9216]{2,1,0:T(2,128)(2,1)}), bf16[16,2,9216]{2,1,0:T(2,128)(2,1)S(1)}, u32[]{:S(2)}, u32[]{:S(2)}) async-start(bf16[16,2,9216]{2,1,0:T(2,128)(2,1)} %reshape.656), calls=%async_computation.6 | async-start | bytes 1179648 | tf_op jit(solution)/shard_map/all_to_all | solution.py:140
  311.3 27.0 %all-to-all-done.6 = bf16[16,2,9216]{2,1,0:T(2,128)(2,1)S(1)} async-done(((bf16[16,2,9216]{2,1,0:T(2,128)(2,1)}), bf16[16,2,9216]{2,1,0:T(2,128)(2,1)S(1)}, u32[]{:S(2)}, u32[]{:S(2)}) %all-to-all-start.6) | async-done | bytes 589856 | tf_op jit(solution)/shard_map/all_to_all | solution.py:140
  340.2 3.8 conditional.17
  341.3 1.5 fusion.39
  342.8 1.2 fusion.46
  344.6 20.2 %all_to_all.139 = bf16[16,48,128]{2,1,0:T(8,128)(2,1)S(1)} all-to-all(bf16[16,48,128]{2,1,0:T(8,128)(2,1)S(1)} %reshape.618), channel_id=1, replica_groups=mesh['pipe'=4,'ctx'=16,'dp'=8] {'ctx'}, dimensions={0} | all-to-all | bytes 393216 | tf_op jit(solution)/shard_map/all_to_all | solution.py:154
  365.6 2.7 collective-permute-start.9
  368.3 2.6 collective-permute-done.9
  372.4 1.8 reshape.658
  374.2 4.8 all-to-all-start.8
  378.9 28.0 %all-to-all-done.8 = bf16[16,2,9216]{2,1,0:T(2,128)(2,1)S(1)} async-done(((bf16[16,2,9216]{2,1,0:T(2,128)(2,1)}), bf16[16,2,9216]{2,1,0:T(2,128)(2,1)S(1)}, u32[]{:S(2)}, u32[]{:S(2)}) %all-to-all-start.8) | async-done | bytes 589856 | tf_op jit(solution)/shard_map/all_to_all | solution.py:140
  409.7 20.4 %all_to_all.140 = bf16[16,48,128]{2,1,0:T(8,128)(2,1)S(1)} all-to-all(bf16[16,48,128]{2,1,0:T(8,128)(2,1)S(1)} %reshape.619), channel_id=1, replica_groups=mesh['pipe'=4,'ctx'=16,'dp'=8] {'ctx'}, dimensions={0} | all-to-all | bytes 393216 | tf_op jit(solution)/shard_map/all_to_all | solution.py:154
  430.9 14.5 %collective-permute-start.10 = (bf16[1,64,1536]{2,1,0:T(8,128)(2,1)S(1)}, bf16[1,64,1536]{2,1,0:T(8,128)(2,1)S(1)}, u32[]{:S(2)}, u32[]{:S(2)}) collective-permute-start(bf16[1,64,1536]{2,1,0:T(8,128)(2,1)S(1)} %fusion.101), channel_id=1, source_target_pairs={{0,128},{128,256},{256,384},{1,129},{129,257},{257,385},{2,130},{1... | collective-permute-start | bytes 589832 | tf_op jit(solution)/shard_map/ppermute | solution.py:15
  445.4 2.6 collective-permute-done.10
  449.4 1.8 reshape.660
  451.3 3.6 all-to-all-start.10
  454.9 22.9 %all-to-all-done.10 = bf16[16,2,9216]{2,1,0:T(2,128)(2,1)S(1)} async-done(((bf16[16,2,9216]{2,1,0:T(2,128)(2,1)}), bf16[16,2,9216]{2,1,0:T(2,128)(2,1)S(1)}, u32[]{:S(2)}, u32[]{:S(2)}) %all-to-all-start.10) | async-done | bytes 589856 | tf_op jit(solution)/shard_map/all_to_all | solution.py:140
  481.1 7.0 %all-to-all-start.11 = ((bf16[16,48,128]{2,1,0:T(8,128)(2,1)}), bf16[16,48,128]{2,1,0:T(8,128)(2,1)S(1)}, u32[]{:S(2)}, u32[]{:S(2)}) async-start(bf16[16,48,128]{2,1,0:T(8,128)(2,1)} %reshape.620), calls=%async_computation.11 | async-start | bytes 393216 | tf_op jit(solution)/shard_map/all_to_all | solution.py:154
  488.8 17.8 %collective-permute-start.12 = (bf16[1536,16]{0,1:T(8,128)(2,1)S(1)}, bf16[1536,16]{0,1:T(8,128)(2,1)S(1)}, u32[]{:S(2)}, u32[]{:S(2)}) collective-permute-start(bf16[1536,16]{0,1:T(8,128)(2,1)S(1)} %copy-done.10), channel_id=1, source_target_pairs={{128,384},{129,385},{130,386},{131,387},{132,388},{133,389},{134,3... | collective-permute-start | bytes 147464 | tf_op jit(solution)/shard_map/ppermute | solution.py:71
  511.1 1.3 collective-permute-start.15
  513.1 36.9 %reduce-scatter.4.cloned.1.call-done = f32[192,64]{1,0:T(8,128)} async-done(((f32[1536,64]{1,0:T(8,128)}), f32[192,64]{1,0:T(8,128)}) %reduce-scatter.4.cloned.1.call-update) | async-done | bytes 49168
  551.0 42.9 %psum.7 = f32[192,64]{0,1:T(8,128)S(1)} all-reduce(f32[192,64]{0,1:T(8,128)S(1)} %copy.109), channel_id=1, replica_groups=mesh['pipe'=4,'ctx'=16,'dp'=8] {'ctx'}, use_global_device_ids=true, to_apply=%region_39.40 | all-reduce | flops 12288 | bytes 98304 | tf_op jit(solution)/shard_map/psum | solution.py:177
  594.6 1.3 collective-permute-start.18
  597.2 23.4 %collective-permute-done.18 = f32[192,16]{0,1:T(8,128)S(1)} collective-permute-done((f32[192,16]{0,1:T(8,128)S(1)}, f32[192,16]{0,1:T(8,128)S(1)}, u32[]{:S(2)}, u32[]{:S(2)}) %collective-permute-start.18) | collective-permute-done | bytes 12320 | tf_op jit(solution)/shard_map/ppermute | solution.py:184
  (172 shorter events, 52.5 us)
Async XLA Ops:
  7.2 20.8 %copy-start = (bf16[64,1536]{1,0:T(8,128)(2,1)S(1)}, bf16[64,1536]{1,0:T(8,128)(2,1)}, u32[]{:S(2)}) copy-start(bf16[64,1536]{1,0:T(8,128)(2,1)} %param.37) | copy-start | bytes 589828
  7.2 48.1 %copy-start.6 = (bf16[1,192,1536]{2,1,0:T(8,128)(2,1)S(1)}, bf16[1,192,1536]{2,1,0:T(8,128)(2,1)}, u32[]{:S(2)}) copy-start(bf16[1,192,1536]{2,1,0:T(8,128)(2,1)} %param.40) | copy-start | bytes 1769476
  7.2 138.9 %all-gather.3.cloned.1.call-start = ((), (), s32[]{:S(2)}) async-start(), calls=%async_computation.13 | async-start | bytes 5308416 | tf_op jit(solution)/shard_map/all_gather | solution.py:57
  7.2 49.2 %collective-permute-start = (bf16[192,1536]{1,0:T(8,128)(2,1)}, bf16[192,1536]{1,0:T(8,128)(2,1)}, u32[]{:S(2)}, u32[]{:S(2)}) collective-permute-start(bf16[192,1536]{1,0:T(8,128)(2,1)} %bitcast.205), channel_id=1, source_target_pairs={{0,1},{1,2},{2,3},{3,4},{4,5},{5,6},{6,7},{7,0},{8,9},{9,10},{10,1... | collective-permute-start | bytes 1769480 | tf_op jit(solution)/shard_map/ppermute | solution.py:61
  11.3 50.4 %collective-permute-start.1 = (bf16[192,1536]{1,0:T(8,128)(2,1)}, bf16[192,1536]{1,0:T(8,128)(2,1)}, u32[]{:S(2)}, u32[]{:S(2)}) collective-permute-start(bf16[192,1536]{1,0:T(8,128)(2,1)} %bitcast.206), channel_id=1, source_target_pairs={{0,2},{1,3},{2,4},{3,5},{4,6},{5,7},{6,0},{7,1},{8,10},{9,11},{10,... | collective-permute-start | bytes 1769480 | tf_op jit(solution)/shard_map/ppermute | solution.py:61
  15.7 51.3 %collective-permute-start.2 = (bf16[192,1536]{1,0:T(8,128)(2,1)}, bf16[192,1536]{1,0:T(8,128)(2,1)}, u32[]{:S(2)}, u32[]{:S(2)}) collective-permute-start(bf16[192,1536]{1,0:T(8,128)(2,1)} %bitcast.207), channel_id=1, source_target_pairs={{0,3},{1,4},{2,5},{3,6},{4,7},{5,0},{6,1},{7,2},{8,11},{9,12},{10,... | collective-permute-start | bytes 1769480 | tf_op jit(solution)/shard_map/ppermute | solution.py:61
  19.8 60.7 %collective-permute-start.3 = (bf16[192,1536]{1,0:T(8,128)(2,1)}, bf16[192,1536]{1,0:T(8,128)(2,1)}, u32[]{:S(2)}, u32[]{:S(2)}) collective-permute-start(bf16[192,1536]{1,0:T(8,128)(2,1)} %bitcast.208), channel_id=1, source_target_pairs={{0,4},{1,5},{2,6},{3,7},{4,0},{5,1},{6,2},{7,3},{8,12},{9,13},{10,... | collective-permute-start | bytes 1769480 | tf_op jit(solution)/shard_map/ppermute | solution.py:61
  21.9 60.5 %collective-permute-start.4 = (bf16[192,1536]{1,0:T(8,128)(2,1)}, bf16[192,1536]{1,0:T(8,128)(2,1)S(1)}, u32[]{:S(2)}, u32[]{:S(2)}) collective-permute-start(bf16[192,1536]{1,0:T(8,128)(2,1)} %bitcast.209), channel_id=1, source_target_pairs={{0,5},{1,6},{2,7},{3,0},{4,1},{5,2},{6,3},{7,4},{8,13},{9,14},{10,... | collective-permute-start | bytes 1769480 | tf_op jit(solution)/shard_map/ppermute | solution.py:61
  40.3 92.6 %all-to-all-start.2 = ((bf16[16,2,3072]{2,1,0:T(2,128)(2,1)}), bf16[16,2,3072]{2,1,0:T(2,128)(2,1)S(1)}, u32[]{:S(2)}, u32[]{:S(2)}) async-start(bf16[16,2,3072]{2,1,0:T(2,128)(2,1)} %reshape.652), calls=%async_computation.2 | async-start | bytes 393216 | tf_op jit(solution)/shard_map/all_to_all | solution.py:120
  56.4 33.9 %collective-permute-start.5 = (bf16[192,1536]{1,0:T(8,128)(2,1)S(1)}, bf16[192,1536]{1,0:T(8,128)(2,1)S(1)}, u32[]{:S(2)}, u32[]{:S(2)}) collective-permute-start(bf16[192,1536]{1,0:T(8,128)(2,1)S(1)} %bitcast.210), channel_id=1, source_target_pairs={{0,6},{1,7},{2,0},{3,1},{4,2},{5,3},{6,4},{7,5},{8,14},{9,15},{10,... | collective-permute-start | bytes 1769480 | tf_op jit(solution)/shard_map/ppermute | solution.py:61
  61.7 49.1 %collective-permute-start.6 = (bf16[192,1536]{1,0:T(8,128)(2,1)S(1)}, bf16[192,1536]{1,0:T(8,128)(2,1)S(1)}, u32[]{:S(2)}, u32[]{:S(2)}) collective-permute-start(bf16[192,1536]{1,0:T(8,128)(2,1)S(1)} %bitcast.211), channel_id=1, source_target_pairs={{0,7},{1,0},{2,1},{3,2},{4,3},{5,4},{6,5},{7,6},{8,15},{9,8},{10,9... | collective-permute-start | bytes 1769480 | tf_op jit(solution)/shard_map/ppermute | solution.py:61
  133.0 25.5 %all-to-all-start.1 = ((bf16[16,2,3072]{2,1,0:T(2,128)(2,1)}), bf16[16,2,3072]{2,1,0:T(2,128)(2,1)S(1)}, u32[]{:S(2)}, u32[]{:S(2)}) async-start(bf16[16,2,3072]{2,1,0:T(2,128)(2,1)} %reshape.650), calls=%async_computation.1 | async-start | bytes 393216 | tf_op jit(solution)/shard_map/all_to_all | solution.py:136
  155.6 25.9 %copy-start.9 = (s32[2,1,1024]{2,1,0:T(1,128)S(1)}, s32[2,1,1024]{2,1,0:T(1,128)}, u32[]{:S(2)}) copy-start(s32[2,1,1024]{2,1,0:T(1,128)} %param.36) | copy-start | bytes 24580
  158.5 21.8 %all-to-all-start = ((bf16[16,2,3072]{2,1,0:T(2,128)(2,1)}), bf16[16,2,3072]{2,1,0:T(2,128)(2,1)S(1)}, u32[]{:S(2)}, u32[]{:S(2)}) async-start(bf16[16,2,3072]{2,1,0:T(2,128)(2,1)} %reshape.648), calls=%async_computation | async-start | bytes 393216 | tf_op jit(solution)/shard_map/all_to_all | solution.py:132
  200.0 19.0 %collective-permute-start.7 = (bf16[1,64,1536]{2,1,0:T(8,128)(2,1)S(1)}, bf16[1,64,1536]{2,1,0:T(8,128)(2,1)S(1)}, u32[]{:S(2)}, u32[]{:S(2)}) collective-permute-start(bf16[1,64,1536]{2,1,0:T(8,128)(2,1)S(1)} %fusion.109), channel_id=1, source_target_pairs={{0,128},{128,256},{256,384},{1,129},{129,257},{257,385},{2,130},{1... | collective-permute-start | bytes 589832 | tf_op jit(solution)/shard_map/ppermute | solution.py:15
  219.3 3.8 copy-start.2
  227.0 30.9 %all-to-all-start.4 = ((bf16[16,2,9216]{2,1,0:T(2,128)(2,1)}), bf16[16,2,9216]{2,1,0:T(2,128)(2,1)S(1)}, u32[]{:S(2)}, u32[]{:S(2)}) async-start(bf16[16,2,9216]{2,1,0:T(2,128)(2,1)} %reshape.654), calls=%async_computation.4 | async-start | bytes 1179648 | tf_op jit(solution)/shard_map/all_to_all | solution.py:140
  290.0 6.9 %collective-permute-start.8 = (bf16[1,64,1536]{2,1,0:T(8,128)(2,1)S(1)}, bf16[1,64,1536]{2,1,0:T(8,128)(2,1)S(1)}, u32[]{:S(2)}, u32[]{:S(2)}) collective-permute-start(bf16[1,64,1536]{2,1,0:T(8,128)(2,1)S(1)} %fusion.93), channel_id=1, source_target_pairs={{0,128},{128,256},{256,384},{1,129},{129,257},{257,385},{2,130},{1... | collective-permute-start | bytes 589832 | tf_op jit(solution)/shard_map/ppermute | solution.py:15
  297.2 3.8 copy-start.3
  304.8 33.5 %all-to-all-start.6 = ((bf16[16,2,9216]{2,1,0:T(2,128)(2,1)}), bf16[16,2,9216]{2,1,0:T(2,128)(2,1)S(1)}, u32[]{:S(2)}, u32[]{:S(2)}) async-start(bf16[16,2,9216]{2,1,0:T(2,128)(2,1)} %reshape.656), calls=%async_computation.6 | async-start | bytes 1179648 | tf_op jit(solution)/shard_map/all_to_all | solution.py:140
  365.6 5.3 collective-permute-start.9
  374.2 32.8 %all-to-all-start.8 = ((bf16[16,2,9216]{2,1,0:T(2,128)(2,1)}), bf16[16,2,9216]{2,1,0:T(2,128)(2,1)S(1)}, u32[]{:S(2)}, u32[]{:S(2)}) async-start(bf16[16,2,9216]{2,1,0:T(2,128)(2,1)} %reshape.658), calls=%async_computation.8 | async-start | bytes 1179648 | tf_op jit(solution)/shard_map/all_to_all | solution.py:140
  430.9 17.1 %collective-permute-start.10 = (bf16[1,64,1536]{2,1,0:T(8,128)(2,1)S(1)}, bf16[1,64,1536]{2,1,0:T(8,128)(2,1)S(1)}, u32[]{:S(2)}, u32[]{:S(2)}) collective-permute-start(bf16[1,64,1536]{2,1,0:T(8,128)(2,1)S(1)} %fusion.101), channel_id=1, source_target_pairs={{0,128},{128,256},{256,384},{1,129},{129,257},{257,385},{2,130},{1... | collective-permute-start | bytes 589832 | tf_op jit(solution)/shard_map/ppermute | solution.py:15
  451.3 26.5 %all-to-all-start.10 = ((bf16[16,2,9216]{2,1,0:T(2,128)(2,1)}), bf16[16,2,9216]{2,1,0:T(2,128)(2,1)S(1)}, u32[]{:S(2)}, u32[]{:S(2)}) async-start(bf16[16,2,9216]{2,1,0:T(2,128)(2,1)} %reshape.660), calls=%async_computation.10 | async-start | bytes 1179648 | tf_op jit(solution)/shard_map/all_to_all | solution.py:140
  479.7 8.4 %copy-start.10 = (bf16[1536,16]{0,1:T(8,128)(2,1)S(1)}, bf16[1536,16]{0,1:T(8,128)(2,1)}, u32[]{:S(2)}) copy-start(bf16[1536,16]{0,1:T(8,128)(2,1)} %param.43) | copy-start | bytes 147460
  479.8 27.5 %copy-start.7 = (f32[2,1,64,64]{3,2,1,0:T(8,128)S(1)}, f32[2,1,64,64]{3,2,1,0:T(8,128)}, u32[]{:S(2)}) copy-start(f32[2,1,64,64]{3,2,1,0:T(8,128)} %param.33) | copy-start | bytes 98308
  479.8 27.6 %copy-start.8 = (f32[2,1,64,64]{3,2,1,0:T(8,128)S(1)}, f32[2,1,64,64]{3,2,1,0:T(8,128)}, u32[]{:S(2)}) copy-start(f32[2,1,64,64]{3,2,1,0:T(8,128)} %param.34) | copy-start | bytes 98308
  479.8 28.6 %copy-start.11 = (f32[1536]{0:T(1024)S(1)}, f32[1536]{0:T(1024)}, u32[]{:S(2)}) copy-start(f32[1536]{0:T(1024)} %param.42) | copy-start | bytes 18436
  481.1 26.4 %all-to-all-start.11 = ((bf16[16,48,128]{2,1,0:T(8,128)(2,1)}), bf16[16,48,128]{2,1,0:T(8,128)(2,1)S(1)}, u32[]{:S(2)}, u32[]{:S(2)}) async-start(bf16[16,48,128]{2,1,0:T(8,128)(2,1)} %reshape.620), calls=%async_computation.11 | async-start | bytes 393216 | tf_op jit(solution)/shard_map/all_to_all | solution.py:154
  488.0 61.9 %reduce-scatter.4.cloned.1.call-start = ((), (), s32[]{:S(2)}) async-start(), calls=%async_computation.14 | async-start | bytes 884736
  488.1 20.3 %collective-permute-start.11 = (bf16[1536,16]{0,1:T(8,128)(2,1)S(1)}, bf16[1536,16]{0,1:T(8,128)(2,1)S(1)}, u32[]{:S(2)}, u32[]{:S(2)}) collective-permute-start(bf16[1536,16]{0,1:T(8,128)(2,1)S(1)} %copy-done.10), channel_id=1, source_target_pairs={{0,384},{1,385},{2,386},{3,387},{4,388},{5,389},{6,390},{7,391},{8... | collective-permute-start | bytes 147464 | tf_op jit(solution)/shard_map/ppermute | solution.py:71
  488.8 19.6 %collective-permute-start.12 = (bf16[1536,16]{0,1:T(8,128)(2,1)S(1)}, bf16[1536,16]{0,1:T(8,128)(2,1)S(1)}, u32[]{:S(2)}, u32[]{:S(2)}) collective-permute-start(bf16[1536,16]{0,1:T(8,128)(2,1)S(1)} %copy-done.10), channel_id=1, source_target_pairs={{128,384},{129,385},{130,386},{131,387},{132,388},{133,389},{134,3... | collective-permute-start | bytes 147464 | tf_op jit(solution)/shard_map/ppermute | solution.py:71
  506.6 1.9 collective-permute-start.13
  507.6 113.6 %copy-start.1 = (bf16[64,1536]{1,0:T(8,128)(2,1)S(1)}, bf16[64,1536]{1,0:T(8,128)(2,1)}, u32[]{:S(2)}) copy-start(bf16[64,1536]{1,0:T(8,128)(2,1)} %param.37) | copy-start | bytes 589828
  510.5 85.4 %collective-permute-start.14 = (f32[2,1,64,16]{2,3,0,1:T(8,128)S(1)}, f32[2,1,64,16]{2,3,0,1:T(8,128)S(1)}, u32[]{:S(2)}, u32[]{:S(2)}) collective-permute-start(f32[2,1,64,16]{2,3,0,1:T(8,128)S(1)} %get-tuple-element.332), channel_id=1, source_target_pairs={{384,0},{385,1},{386,2},{387,3},{388,4},{389,5},{390,6},{391,7},{3... | collective-permute-start | bytes 24584 | tf_op jit(solution)/shard_map/ppermute | solution.py:183
  511.1 85.4 %collective-permute-start.15 = (f32[2,1,64,16]{2,3,0,1:T(8,128)S(1)}, f32[2,1,64,16]{2,3,0,1:T(8,128)S(1)}, u32[]{:S(2)}, u32[]{:S(2)}) collective-permute-start(f32[2,1,64,16]{2,3,0,1:T(8,128)S(1)} %get-tuple-element.330), channel_id=1, source_target_pairs={{384,128},{385,129},{386,130},{387,131},{388,132},{389,133},{390,1... | collective-permute-start | bytes 24584 | tf_op jit(solution)/shard_map/ppermute | solution.py:183
  512.4 84.1 %collective-permute-start.16 = (f32[2,1,64,16]{2,3,0,1:T(8,128)S(1)}, f32[2,1,64,16]{2,3,0,1:T(8,128)S(1)}, u32[]{:S(2)}, u32[]{:S(2)}) collective-permute-start(f32[2,1,64,16]{2,3,0,1:T(8,128)S(1)} %get-tuple-element.331), channel_id=1, source_target_pairs={{384,256},{385,257},{386,258},{387,259},{388,260},{389,261},{390,2... | collective-permute-start | bytes 24584 | tf_op jit(solution)/shard_map/ppermute | solution.py:183
  593.9 3.3 collective-permute-start.17
  594.6 26.0 %collective-permute-start.18 = (f32[192,16]{0,1:T(8,128)S(1)}, f32[192,16]{0,1:T(8,128)S(1)}, u32[]{:S(2)}, u32[]{:S(2)}) collective-permute-start(f32[192,16]{0,1:T(8,128)S(1)} %get-tuple-element.327), channel_id=1, source_target_pairs={{384,128},{385,129},{386,130},{387,131},{388,132},{389,133},{390,1... | collective-permute-start | bytes 36872 | tf_op jit(solution)/shard_map/ppermute | solution.py:184
  595.9 24.7 %collective-permute-start.19 = (f32[192,16]{0,1:T(8,128)S(1)}, f32[192,16]{0,1:T(8,128)S(1)}, u32[]{:S(2)}, u32[]{:S(2)}) collective-permute-start(f32[192,16]{0,1:T(8,128)S(1)} %get-tuple-element.328), channel_id=1, source_target_pairs={{384,256},{385,257},{386,258},{387,259},{388,260},{389,261},{390,2... | collective-permute-start | bytes 36872 | tf_op jit(solution)/shard_map/ppermute | solution.py:184
Sparse Core Ops, SparseCore 0:
  25.2 98.1 all-gather.2
  510.6 39.3 reduce-scatter.3
